TPU v7x, 128 devices: a whole 4x4x4 slice. The times are simulated.
128 devices in a mesh: grp: 16 (over y, z), lag: 8 (over x, core).
Axes of the slice: x: 4, y: 4, z: 4, core: 2. Of those that a mesh axis runs over, the one named last changes fastest.
Arguments:
- history: float32 [16, 512, 32, 128], P('lag', 'grp'), may hold values from -6 to 6
- tiles: bfloat16 [65536, 128, 128], P(('grp', 'lag')), may hold values from -0.01171875 to 0.01171875
- tile_src: int32 [65536], P(('grp', 'lag')), may hold values from 0 to 511
- tile_obs: int32 [65536], P(('grp', 'lag')), may hold values from 0 to 32
- tile_lag: int32 [65536], P(('grp', 'lag')), may hold values from 0 to 1
- incident: float32 [32, 32, 128], P('grp', 'lag'), may hold values from -6 to 6
- near_inverse: bfloat16 [32, 128, 128], P('grp'), may hold values from -0.5 to 0.5
Outputs:
- field: float32 [32, 32, 128], P('grp', 'lag')
- new_current: float32 [32, 32, 128], P('grp', 'lag')
Inputs may be any that keep to these rules, and one draw needn't show every extreme that they name: `tile_obs`: a value of 32 marks a padded tile.
All inputs are finite; a program needn't handle non-finite values.
Results may differ from a plain program's by a relative error of at most 0.0035.
Values may be sent and summed in bfloat16 or wider, within the bound.
No kernel may reach another device: no remote copies, remote signals or barrier semaphores. Data moves between devices by JAX's collectives and lax.ppermute only.
A program may use at most 128 MiB of HBM per device.

v0:
```python
import jax
import jax.numpy as jnp
from jax import lax
from jax.sharding import PartitionSpec as P

OBS_DEV = 2


def body(history, tiles, tile_src, tile_obs, tile_lag, incident, near_inverse):
    hist16 = history.astype(jnp.bfloat16)
    gathered = lax.all_gather(hist16, "grp", axis=1, tiled=True)
    lag_count = gathered.shape[0]
    source_count = gathered.shape[1]
    flat = gathered.reshape(lag_count * source_count, gathered.shape[2], gathered.shape[3])
    picked = flat[tile_lag * source_count + tile_src]
    terms = jnp.einsum("kas,kos->kao", picked, tiles, preferred_element_type=jnp.float32)
    observers = OBS_DEV * lax.axis_size("grp")
    partial_field = jax.ops.segment_sum(terms, tile_obs, num_segments=observers)
    angle_part = incident.shape[1]
    summed = lax.psum(partial_field, "lag")
    mine = lax.psum_scatter(summed, "grp", scatter_dimension=0, tiled=True)
    field = lax.dynamic_slice_in_dim(mine, lax.axis_index("lag") * angle_part, angle_part, 1)
    rhs = (incident - field).astype(jnp.bfloat16)
    new_current = jnp.einsum("oag,ohg->oah", rhs, near_inverse, preferred_element_type=jnp.float32)
    return (field, new_current)


def solution(mesh):
    return jax.shard_map(
        body,
        mesh=mesh,
        in_specs=(
            P("lag", "grp", None, None),
            P(("grp", "lag"), None, None),
            P(("grp", "lag")),
            P(("grp", "lag")),
            P(("grp", "lag")),
            P("grp", "lag", None),
            P("grp", None, None),
        ),
        out_specs=(P("grp", "lag", None), P("grp", "lag", None)),
        check_vma=False,
    )
```

profile of v0, /device:TPU:1, one launch (start us, length us, event | category | flops | bytes accessed | tf_op | source)
XLA Modules:
  0.0 253.0 jit_solution(2422170448194656881)
XLA Ops:
  7.2 0.0 copy-start
  7.2 0.0 all-gather.2.cloned.1.call-start
  7.2 2.2 convert_element_type.6
  9.4 0.0 all-gather.2.cloned.1.call-update
  9.4 0.0 reduce-scatter.2.cloned.1.call-start
  9.5 0.7 compare_select_fusion
  10.2 74.2 %all-gather.2.cloned.1.call-done = bf16[2,512,32,128]{3,2,1,0:T(8,128)(2,1)} async-done(((bf16[2,32,32,128]{3,2,1,0:T(8,128)(2,1)}), bf16[2,512,32,128]{3,2,1,0:T(8,128)(2,1)}) %all-gather.2.cloned.1.call-update) | async-done | bytes 8388624 | tf_op jit(solution)/shard_map/all_gather | solution.py:11
  84.3 6.5 %gather_fusion = bf16[512,32,128]{2,1,0:T(8,128)(2,1)} fusion(bf16[1024,32,128]{2,1,0:T(8,128)(2,1)} %bitcast.4, s32[1024]{0:T(1024)S(1)} %pad_clamp_fusion), kind=kCustom, calls=%fused_computation | custom fusion | bytes 8390656 | tf_op jit(solution)/shard_map/gather | solution.py:15
  90.9 0.0 copy-start.4
  90.9 15.0 %fusion.1 = f32[512,32,128]{2,1,0:T(8,128)} fusion(bf16[512,32,128]{2,1,0:T(8,128)(2,1)} %gather_fusion, bf16[512,128,128]{2,1,0:T(8,128)(2,1)} %param.8), kind=kOutput, calls=%fused_computation.7 | convolution fusion | flops 536870912 | bytes 29360128 | tf_op jit(solution)/shard_map/kas,kos->kao/dot_general | solution.py:16
  105.9 0.0 copy-done.4
  105.9 0.0 copy-start.3
  105.9 44.7 %scatter_fusion = f32[32,32,128]{2,1,0:T(8,128)S(1)} fusion(f32[32,32,128]{2,1,0:T(8,128)S(1)} %broadcast_in_dim.9, s32[512]{0:T(512)S(1)} %copy-done.4, f32[512,32,128]{2,1,0:T(8,128)} %fusion.1), kind=kCustom, calls=%fused_computation.1 | custom fusion | flops 2097152 | bytes 25167872 | tf_op jit(solution)/shard_map/scatter-add | solution.py:18
  150.6 0.0 copy-start.1
  150.6 0.8 copy-done.1
  151.4 0.0 reduce-scatter.2.cloned.1.call-update
  151.5 70.5 %reduce-scatter.2.cloned.1.call-done = f32[2,32,128]{2,1,0:T(8,128)} async-done(((f32[32,32,128]{2,1,0:T(8,128)}), f32[2,32,128]{2,1,0:T(8,128)}) %reduce-scatter.2.cloned.1.call-update) | async-done | bytes 32784 | tf_op jit(solution)/shard_map/reduce_scatter | solution.py:21
  222.0 23.4 %psum.8 = f32[2,32,128]{2,1,0:T(8,128)S(1)} all-reduce(f32[2,32,128]{2,1,0:T(8,128)} %reduce-scatter.2.cloned.1.call-done), channel_id=1, replica_groups=mesh['grp'=16,'lag'=8] {'lag'}, use_global_device_ids=true, to_apply=%region_1.0 | all-reduce | flops 8192 | bytes 65536 | tf_op jit(solution)/shard_map/psum | solution.py:20
  245.4 0.0 copy-done
  245.4 0.0 copy-done.3
  245.4 0.0 copy-start.2
  245.4 0.7 fusion
  246.2 0.0 copy-done.2
  (3 shorter events, 0.1 us)
Async XLA Ops:
  7.2 238.2 %copy-start = (bf16[2,128,128]{2,1,0:T(8,128)(2,1)S(1)}, bf16[2,128,128]{2,1,0:T(8,128)(2,1)}, u32[]{:S(2)}) copy-start(bf16[2,128,128]{2,1,0:T(8,128)(2,1)} %param.13) | copy-start | bytes 196612
  7.2 77.2 %all-gather.2.cloned.1.call-start = ((), (), s32[]{:S(2)}) async-start(), calls=%async_computation.1 | async-start | bytes 8912896 | tf_op jit(solution)/shard_map/all_gather | solution.py:11
  9.4 212.6 %reduce-scatter.2.cloned.1.call-start = ((), (), s32[]{:S(2)}) async-start(), calls=%async_computation.2 | async-start | bytes 557056 | tf_op jit(solution)/shard_map/reduce_scatter | solution.py:21
  90.9 15.0 %copy-start.4 = (s32[512]{0:T(512)S(1)}, s32[512]{0:T(512)}, u32[]{:S(2)}) copy-start(s32[512]{0:T(512)} %param.10) | copy-start | bytes 6148
  105.9 139.5 %copy-start.3 = (f32[2,4,128]{2,1,0:T(4,128)S(1)}, f32[2,4,128]{2,1,0:T(4,128)}, u32[]{:S(2)}) copy-start(f32[2,4,128]{2,1,0:T(4,128)} %param.12) | copy-start | bytes 12292
  150.6 0.8 copy-start.1
  245.4 0.8 copy-start.2
Sparse Core Ops, SparseCore 0:
  10.2 74.0 all-gather.1
  151.6 70.3 reduce-scatter.1
where the time goes:
time: 256 us; the launch traced here: 253 us
  waiting for transfers between devices  145 us (57%)
  other arithmetic  47.6 us (19%)
  blocking collectives  23.4 us (9%)
  matrix products  15.7 us (6%)
  between operations  14.1 us (6%)
  local copies, waits for them, and re-layouts  7.41 us (3%)
    all_gather x1, waiting for transfers between devices, body(): gathered = lax.all_gather(hist16, 'grp', axis=1, tiled=True)  74.2 us
    reduce_scatter x1, waiting for transfers between devices, body(): mine = lax.psum_scatter(summed, 'grp', scatter_dimension=0, tiled=True)  70.5 us
    scatter-add x1, other arithmetic, body(): partial_field = jax.ops.segment_sum(terms, tile_obs, num_segments=observers)  44.7 us
    psum x1, blocking collectives, body(): summed = lax.psum(partial_field, 'lag')  23.4 us
    dot_general x1, matrix products, body(): jnp.einsum('kas,kos->kao', picked, tiles, preferred_element_type=jnp.floa...  15 us
    gather x1, local copies, waits for them, and re-layouts, body(): picked = flat[tile_lag * source_count + tile_src]  6.55 us
  transfers between devices with their start and end apart: 2, of which 2 were waited for; matrix products, arithmetic and copies ran while one was open for 0% of the time, Pallas kernels for 0%

commit v1 on v0

--- a/solution.py
+++ b/solution.py
@@ -3,10 +3,12 @@
 from jax import lax
 from jax.sharding import PartitionSpec as P
 
-OBS_DEV = 2
-
 
 def body(history, tiles, tile_src, tile_obs, tile_lag, incident, near_inverse):
+    n_grp = lax.axis_size("grp")
+    n_lag = lax.axis_size("lag")
+    obs_dev, ang_dev, width = incident.shape
+    observers = obs_dev * n_grp
     hist16 = history.astype(jnp.bfloat16)
     gathered = lax.all_gather(hist16, "grp", axis=1, tiled=True)
     lag_count = gathered.shape[0]
@@ -14,12 +16,12 @@
     flat = gathered.reshape(lag_count * source_count, gathered.shape[2], gathered.shape[3])
     picked = flat[tile_lag * source_count + tile_src]
     terms = jnp.einsum("kas,kos->kao", picked, tiles, preferred_element_type=jnp.float32)
-    observers = OBS_DEV * lax.axis_size("grp")
-    partial_field = jax.ops.segment_sum(terms, tile_obs, num_segments=observers)
-    angle_part = incident.shape[1]
-    summed = lax.psum(partial_field, "lag")
-    mine = lax.psum_scatter(summed, "grp", scatter_dimension=0, tiled=True)
-    field = lax.dynamic_slice_in_dim(mine, lax.axis_index("lag") * angle_part, angle_part, 1)
+    onehot = (tile_obs[:, None] == jnp.arange(observers, dtype=tile_obs.dtype)[None, :]).astype(jnp.float32)
+    partial = jnp.einsum("kg,kao->gao", onehot, terms, precision=lax.Precision.HIGHEST,
+                         preferred_element_type=jnp.float32)
+    partial = partial.reshape(n_grp, obs_dev, n_lag, ang_dev, width)
+    partial = partial.transpose(0, 2, 1, 3, 4).reshape(n_grp * n_lag, obs_dev, ang_dev, width)
+    field = lax.psum_scatter(partial, ("grp", "lag"), scatter_dimension=0, tiled=True)[0]
     rhs = (incident - field).astype(jnp.bfloat16)
     new_current = jnp.einsum("oag,ohg->oah", rhs, near_inverse, preferred_element_type=jnp.float32)
     return (field, new_current)

time: 256 us -> 266 us (1.039); the launches traced: 253 us -> 266 us
  waiting for transfers between devices: 145 us -> 219 us
  other arithmetic: 47.6 us -> 2.86 us
  blocking collectives: 23.4 us -> 0 us
  matrix products: 15.7 us -> 21.4 us
    unnamed x2 -> x3, waiting for transfers between devices: 0.03 us -> 145 us
    reduce_scatter x1 -> x0, waiting for transfers between devices: 70.5 us -> none  [body(): mine = lax.psum_scatter(summed, 'grp', scatter_dimension=0, tiled=True)]
    scatter-add x1 -> x0, other arithmetic: 44.7 us -> none  [body(): partial_field = jax.ops.segment_sum(terms, tile_obs, num_segments=observers)]
    psum x1 -> x0, blocking collectives: 23.4 us -> none  [body(): summed = lax.psum(partial_field, 'lag')]
    dot_general x0 -> x1, matrix products: none -> 7.72 us  [body(): jnp.einsum('kg,kao->gao', onehot, terms, precision=lax.Precision.HIGHEST,...]
where the time goes in v1:
time: 266 us
  waiting for transfers between devices  219 us (82%)
  matrix products  21.4 us (8%)
  between operations  14.1 us (5%)
  local copies, waits for them, and re-layouts  8.4 us (3%)
  other arithmetic  2.86 us (1%)
    unnamed x3, waiting for transfers between devices  145 us
    all_gather x1, waiting for transfers between devices, body(): gathered = lax.all_gather(hist16, 'grp', axis=1, tiled=True)  74.2 us
    dot_general x1, matrix products, body(): jnp.einsum('kas,kos->kao', picked, tiles, preferred_element_type=jnp.floa...  13 us
    dot_general x1, matrix products, body(): jnp.einsum('kg,kao->gao', onehot, terms, precision=lax.Precision.HIGHEST,...  7.72 us
    gather x1, local copies, waits for them, and re-layouts, body(): picked = flat[tile_lag * source_count + tile_src]  6.56 us
  transfers between devices with their start and end apart: 2, of which 2 were waited for; matrix products, arithmetic and copies ran while one was open for 0% of the time, Pallas kernels for 0%

profile of v1, /device:TPU:1, one launch (start us, length us, event | category | flops | bytes accessed | tf_op | source)
XLA Modules:
  0.0 266.0 jit_solution(15926588088370661575)
XLA Ops:
  7.2 0.0 copy-start
  7.2 0.0 all-gather.2.cloned.1.call-start
  7.2 2.1 convert_element_type.7
  9.4 0.0 all-gather.2.cloned.1.call-update
  9.4 0.0 all-reduce.3.cloned.1.call-start
  9.4 0.7 compare_select_fusion
  10.2 74.2 %all-gather.2.cloned.1.call-done = bf16[2,512,32,128]{3,2,1,0:T(8,128)(2,1)} async-done(((bf16[2,32,32,128]{3,2,1,0:T(8,128)(2,1)}), bf16[2,512,32,128]{3,2,1,0:T(8,128)(2,1)}) %all-gather.2.cloned.1.call-update) | async-done | bytes 8388624 | tf_op jit(solution)/shard_map/all_gather | solution.py:13
  84.3 6.6 %gather_fusion = bf16[512,32,128]{2,1,0:T(8,128)(2,1)} fusion(bf16[1024,32,128]{2,1,0:T(8,128)(2,1)} %bitcast.13, s32[1024]{0:T(1024)S(1)} %pad_clamp_fusion), kind=kCustom, calls=%fused_computation | custom fusion | bytes 8390656 | tf_op jit(solution)/shard_map/gather | solution.py:17
  90.9 0.0 copy-start.3
  90.9 13.0 %fusion.6 = f32[512,32,128]{2,1,0:T(8,128)S(1)} fusion(bf16[512,32,128]{2,1,0:T(8,128)(2,1)} %gather_fusion, bf16[512,128,128]{2,1,0:T(8,128)(2,1)} %param.8), kind=kOutput, calls=%fused_computation.11 | convolution fusion | flops 536870912 | bytes 29360128 | tf_op jit(solution)/shard_map/kas,kos->kao/dot_general | solution.py:18
  103.9 0.0 copy-done.3
  103.9 0.0 copy-start.2
  103.9 7.7 %fusion = f32[32,32,128]{2,0,1:T(8,128)S(1)} fusion(f32[512,32,128]{2,1,0:T(8,128)S(1)} %fusion.6, s32[512]{0:T(512)S(1)} %copy-done.3), kind=kOutput, calls=%fused_computation.1 | convolution fusion | flops 805322752 | bytes 8914944 | tf_op jit(solution)/shard_map/kg,kao->gao/dot_general | solution.py:20
  111.6 1.1 copy.10
  112.7 0.0 all-reduce.3.cloned.1.call-update
  112.8 145.0 %all-reduce.3.cloned.1.call-done = f32[128,2,4,128]{3,2,1,0:T(4,128)} async-done(((f32[128,2,4,128]{3,2,1,0:T(4,128)}), f32[128,2,4,128]{3,2,1,0:T(4,128)}) %all-reduce.3.cloned.1.call-update) | async-done | bytes 524304
  257.8 0.7 dynamic-slice_bitcast_fusion
  258.4 0.0 copy-done
  258.4 0.0 copy-done.2
  258.4 0.0 copy-start.1
  258.4 0.7 fusion.5
  259.2 0.0 copy-done.1
  (1 shorter events, 0.0 us)
Async XLA Ops:
  7.2 251.3 %copy-start = (bf16[2,128,128]{2,1,0:T(8,128)(2,1)S(1)}, bf16[2,128,128]{2,1,0:T(8,128)(2,1)}, u32[]{:S(2)}) copy-start(bf16[2,128,128]{2,1,0:T(8,128)(2,1)} %param.13) | copy-start | bytes 196612
  7.2 77.2 %all-gather.2.cloned.1.call-start = ((), (), s32[]{:S(2)}) async-start(), calls=%async_computation | async-start | bytes 8912896 | tf_op jit(solution)/shard_map/all_gather | solution.py:13
  9.4 248.4 %all-reduce.3.cloned.1.call-start = ((), (), s32[]{:S(2)}) async-start(), calls=%async_computation.1 | async-start | bytes 1048576
  90.9 13.0 %copy-start.3 = (s32[512]{0:T(512)S(1)}, s32[512]{0:T(512)}, u32[]{:S(2)}) copy-start(s32[512]{0:T(512)} %param.10) | copy-start | bytes 6148
  103.9 154.6 %copy-start.2 = (f32[2,4,128]{2,1,0:T(4,128)S(1)}, f32[2,4,128]{2,1,0:T(4,128)}, u32[]{:S(2)}) copy-start(f32[2,4,128]{2,1,0:T(4,128)} %param.12) | copy-start | bytes 12292
  258.4 0.7 copy-start.1
Sparse Core Ops, SparseCore 0:
  10.2 74.0 all-gather.1
  112.9 144.8 all-reduce.2

commit v2 on v1

--- a/solution.py
+++ b/solution.py
@@ -21,7 +21,8 @@
                          preferred_element_type=jnp.float32)
     partial = partial.reshape(n_grp, obs_dev, n_lag, ang_dev, width)
     partial = partial.transpose(0, 2, 1, 3, 4).reshape(n_grp * n_lag, obs_dev, ang_dev, width)
-    field = lax.psum_scatter(partial, ("grp", "lag"), scatter_dimension=0, tiled=True)[0]
+    received = lax.all_to_all(partial, ("grp", "lag"), 0, 0, tiled=True)
+    field = jnp.sum(received, axis=0)
     rhs = (incident - field).astype(jnp.bfloat16)
     new_current = jnp.einsum("oag,ohg->oah", rhs, near_inverse, preferred_element_type=jnp.float32)
     return (field, new_current)

time: 266 us -> 142 us (0.53)
  waiting for transfers between devices: 219 us -> 74.2 us
  blocking collectives: 0 us -> 21.4 us
    unnamed x3 -> x1, waiting for transfers between devices: 145 us -> 0.02 us
    all_to_all x0 -> x1, blocking collectives: none -> 21.4 us  [body(): received = lax.all_to_all(partial, ('grp', 'lag'), 0, 0, tiled=True)]
  transfers between devices with their start and end apart: 2 -> 1, of which waited for: 2 -> 1; matrix products, arithmetic and copies ran while one was open for 0% -> 1% of each run, Pallas kernels for 0% -> 0%
where the time goes in v2:
time: 142 us; the launch traced here: 141 us
  waiting for transfers between devices  74.2 us (52%)
  matrix products  21.4 us (15%)
  blocking collectives  21.4 us (15%)
  between operations  14.1 us (10%)
  local copies, waits for them, and re-layouts  7.22 us (5%)
  other arithmetic  3.02 us (2%)
    all_gather x1, waiting for transfers between devices, body(): gathered = lax.all_gather(hist16, 'grp', axis=1, tiled=True)  74.2 us
    all_to_all x1, blocking collectives, body(): received = lax.all_to_all(partial, ('grp', 'lag'), 0, 0, tiled=True)  21.4 us
    dot_general x1, matrix products, body(): jnp.einsum('kas,kos->kao', picked, tiles, preferred_element_type=jnp.floa...  13 us
    dot_general x1, matrix products, body(): jnp.einsum('kg,kao->gao', onehot, terms, precision=lax.Precision.HIGHEST,...  7.72 us
    gather x1, local copies, waits for them, and re-layouts, body(): picked = flat[tile_lag * source_count + tile_src]  6.53 us
  transfers between devices with their start and end apart: 1, of which 1 were waited for; matrix products, arithmetic and copies ran while one was open for 1% of the time, Pallas kernels for 0%

profile of v2, /device:TPU:1, one launch (start us, length us, event | category | flops | bytes accessed | tf_op | source)
XLA Modules:
  0.0 141.4 jit_solution(16144967134915029307)
XLA Ops:
  7.2 0.0 copy-start
  7.2 0.0 all-gather.2.cloned.1.call-start
  7.2 2.2 %convert_element_type.7 = bf16[2,32,32,128]{3,2,1,0:T(8,128)(2,1)} convert(f32[2,32,32,128]{3,2,1,0:T(8,128)} %param.7) | non-fusion elementwise | flops 262144 | bytes 1572864 | tf_op jit(solution)/shard_map/convert_element_type | solution.py:12
  9.4 0.0 all-gather.2.cloned.1.call-update
  9.4 0.7 compare_select_fusion
  10.1 74.2 %all-gather.2.cloned.1.call-done = bf16[2,512,32,128]{3,2,1,0:T(8,128)(2,1)} async-done(((bf16[2,32,32,128]{3,2,1,0:T(8,128)(2,1)}), bf16[2,512,32,128]{3,2,1,0:T(8,128)(2,1)}) %all-gather.2.cloned.1.call-update) | async-done | bytes 8388624 | tf_op jit(solution)/shard_map/all_gather | solution.py:13
  84.3 6.5 %gather_fusion = bf16[512,32,128]{2,1,0:T(8,128)(2,1)} fusion(bf16[1024,32,128]{2,1,0:T(8,128)(2,1)} %bitcast.13, s32[1024]{0:T(1024)S(1)} %pad_clamp_fusion), kind=kCustom, calls=%fused_computation | custom fusion | bytes 8390656 | tf_op jit(solution)/shard_map/gather | solution.py:17
  90.9 0.0 copy-start.3
  90.9 13.0 %fusion.6 = f32[512,32,128]{2,1,0:T(8,128)S(1)} fusion(bf16[512,32,128]{2,1,0:T(8,128)(2,1)} %gather_fusion, bf16[512,128,128]{2,1,0:T(8,128)(2,1)} %param.8), kind=kOutput, calls=%fused_computation.11 | convolution fusion | flops 536870912 | bytes 29360128 | tf_op jit(solution)/shard_map/kas,kos->kao/dot_general | solution.py:18
  103.8 0.0 copy-done.3
  103.8 0.0 copy-start.2
  103.9 7.7 %fusion = f32[32,32,128]{2,0,1:T(8,128)S(1)} fusion(f32[512,32,128]{2,1,0:T(8,128)S(1)} %fusion.6, s32[512]{0:T(512)S(1)} %copy-done.3), kind=kOutput, calls=%fused_computation.1 | convolution fusion | flops 805322752 | bytes 8914944 | tf_op jit(solution)/shard_map/kg,kao->gao/dot_general | solution.py:20
  111.6 0.3 copy.16
  111.9 0.3 copy.12
  112.3 21.4 %all_to_all.5 = f32[128,2,4,128]{3,2,1,0:T(4,128)S(1)} all-to-all(f32[128,2,4,128]{3,2,1,0:T(4,128)S(1)} %copy.12), channel_id=1, replica_groups=mesh['grp'=16,'lag'=8] {'grp','lag'}, dimensions={0} | all-to-all | bytes 1048576 | tf_op jit(solution)/shard_map/all_to_all | solution.py:24
  133.7 0.1 reduce_sum.9
  133.8 0.0 copy-done
  133.8 0.0 copy-done.2
  133.8 0.0 copy-start.1
  133.8 0.7 fusion.5
  134.6 0.0 copy-done.1
  (1 shorter events, 0.0 us)
Async XLA Ops:
  7.2 126.6 %copy-start = (bf16[2,128,128]{2,1,0:T(8,128)(2,1)S(1)}, bf16[2,128,128]{2,1,0:T(8,128)(2,1)}, u32[]{:S(2)}) copy-start(bf16[2,128,128]{2,1,0:T(8,128)(2,1)} %param.13) | copy-start | bytes 196612
  7.2 77.2 %all-gather.2.cloned.1.call-start = ((), (), s32[]{:S(2)}) async-start(), calls=%async_computation.1 | async-start | bytes 8912896 | tf_op jit(solution)/shard_map/all_gather | solution.py:13
  90.9 13.0 %copy-start.3 = (s32[512]{0:T(512)S(1)}, s32[512]{0:T(512)}, u32[]{:S(2)}) copy-start(s32[512]{0:T(512)} %param.10) | copy-start | bytes 6148
  103.8 30.0 %copy-start.2 = (f32[2,4,128]{2,1,0:T(4,128)S(1)}, f32[2,4,128]{2,1,0:T(4,128)}, u32[]{:S(2)}) copy-start(f32[2,4,128]{2,1,0:T(4,128)} %param.12) | copy-start | bytes 12292
  133.8 0.8 copy-start.1
Sparse Core Ops, SparseCore 0:
  10.2 74.0 all-gather.1

commit v3 on v1

v3 whole, which is shorter than its diff:
```python
import jax
import jax.numpy as jnp
from jax import lax
from jax.sharding import PartitionSpec as P

CHUNKS = 2


def chunk_field(hist16, tile_index, tiles, onehot, n_grp, n_lag, obs_dev):
    gathered = lax.all_gather(hist16, "grp", axis=1, tiled=True)
    lag_count, source_count, angles, width = gathered.shape
    flat = gathered.reshape(lag_count * source_count, angles, width)
    picked = flat[tile_index]
    terms = jnp.einsum("kas,kos->kao", picked, tiles, preferred_element_type=jnp.float32)
    partial = jnp.einsum("kg,kao->gao", onehot, terms, precision=lax.Precision.HIGHEST,
                         preferred_element_type=jnp.float32)
    per_lag = angles // n_lag
    partial = partial.reshape(n_grp, obs_dev, n_lag, per_lag, width)
    partial = partial.transpose(0, 2, 1, 3, 4).reshape(n_grp * n_lag, obs_dev, per_lag, width)
    received = lax.all_to_all(partial, ("grp", "lag"), 0, 0, tiled=True)
    return jnp.sum(received, axis=0)


def body(history, tiles, tile_src, tile_obs, tile_lag, incident, near_inverse):
    n_grp = lax.axis_size("grp")
    n_lag = lax.axis_size("lag")
    obs_dev, ang_dev, width = incident.shape
    observers = obs_dev * n_grp
    lag_count, src_dev, angles, _ = history.shape
    source_count = src_dev * n_grp
    tile_index = tile_lag * source_count + tile_src
    onehot = (tile_obs[:, None] == jnp.arange(observers, dtype=tile_obs.dtype)[None, :]).astype(jnp.float32)
    split = history.reshape(lag_count, src_dev, n_lag, CHUNKS, ang_dev // CHUNKS, width)
    fields = []
    for c in range(CHUNKS):
        part = split[:, :, :, c].reshape(lag_count, src_dev, angles // CHUNKS, width)
        fields.append(chunk_field(part.astype(jnp.bfloat16), tile_index, tiles, onehot, n_grp, n_lag, obs_dev))
    field = jnp.concatenate(fields, axis=1)
    rhs = (incident - field).astype(jnp.bfloat16)
    new_current = jnp.einsum("oag,ohg->oah", rhs, near_inverse, preferred_element_type=jnp.float32)
    return (field, new_current)


def solution(mesh):
    return jax.shard_map(
        body,
        mesh=mesh,
        in_specs=(
            P("lag", "grp", None, None),
            P(("grp", "lag"), None, None),
            P(("grp", "lag")),
            P(("grp", "lag")),
            P(("grp", "lag")),
            P("grp", "lag", None),
            P("grp", None, None),
        ),
        out_specs=(P("grp", "lag", None), P("grp", "lag", None)),
        check_vma=False,
    )
```

time: 266 us -> 164 us (0.62)
  waiting for transfers between devices: 219 us -> 92.9 us
  starting transfers between devices: 0.08 us -> 15.1 us
  matrix products: 21.4 us -> 29.6 us
    unnamed x3 -> x2, waiting for transfers between devices: 145 us -> 0.71 us
    all_to_all x0 -> x2, starting transfers between devices: none -> 15 us  [chunk_field(): received = lax.all_to_all(partial, ('grp', 'lag'), 0, 0, tiled=True)]
    all_to_all x0 -> x2, waiting for transfers between devices: none -> 10.8 us  [chunk_field(): received = lax.all_to_all(partial, ('grp', 'lag'), 0, 0, tiled=True)]
    dot_general x2 -> x4, matrix products: 20.7 us -> 28.9 us  [the longest x2 23.4 us: chunk_field(): jnp.einsum('kas,kos->kao', picked, tiles, preferred_element_type=jnp.floa...]
    all_gather x1 -> x2, waiting for transfers between devices: 74.2 us -> 81.4 us  [chunk_field(): gathered = lax.all_gather(hist16, 'grp', axis=1, tiled=True)]
    gather x1 -> x2, local copies, waits for them, and re-layouts: 6.56 us -> 6.75 us  [chunk_field(): picked = flat[tile_index]]
  transfers between devices with their start and end apart: 2 -> 4, of which waited for: 2 -> 3; matrix products, arithmetic and copies ran while one was open for 0% -> 23% of each run, Pallas kernels for 0% -> 0%
where the time goes in v3:
time: 164 us
  waiting for transfers between devices  92.9 us (57%)
  matrix products  29.6 us (18%)
  starting transfers between devices  15.1 us (9%)
  between operations  14.1 us (9%)
  local copies, waits for them, and re-layouts  10.1 us (6%)
  other arithmetic  2.34 us (1%)
    all_gather x2, waiting for transfers between devices, chunk_field(): gathered = lax.all_gather(hist16, 'grp', axis=1, tiled=True)  81.4 us
    dot_general x2, matrix products, chunk_field(): jnp.einsum('kas,kos->kao', picked, tiles, preferred_element_type=jnp.floa...  23.4 us
    all_to_all x2, starting transfers between devices, chunk_field(): received = lax.all_to_all(partial, ('grp', 'lag'), 0, 0, tiled=True)  15 us
    all_to_all x2, waiting for transfers between devices, chunk_field(): received = lax.all_to_all(partial, ('grp', 'lag'), 0, 0, tiled=True)  10.8 us
    gather x2, local copies, waits for them, and re-layouts, chunk_field(): picked = flat[tile_index]  6.75 us
    dot_general x2, matrix products, chunk_field(): jnp.einsum('kg,kao->gao', onehot, terms, precision=lax.Precision.HIGHEST,...  5.42 us
  transfers between devices with their start and end apart: 4, of which 3 were waited for; matrix products, arithmetic and copies ran while one was open for 23% of the time, Pallas kernels for 0%

profile of v3, /device:TPU:1, one launch (start us, length us, event | category | flops | bytes accessed | tf_op | source)
XLA Modules:
  0.0 164.2 jit_solution(12016228070089195481)
XLA Ops:
  7.2 0.0 copy-start
  7.2 0.0 all-gather.3.cloned.1.call-start
  7.2 1.3 convert.5
  8.5 1.2 fusion.10
  9.7 0.0 all-gather.3.cloned.1.call-update
  9.8 0.0 all-gather.5.cloned.1.call-start
  9.8 0.7 all-gather.5.cloned.1.call-update
  10.5 0.7 compare_select_fusion
  11.2 53.9 %all-gather.3.cloned.1.call-done = bf16[2,512,16,128]{3,2,1,0:T(8,128)(2,1)} async-done(((bf16[2,32,16,128]{3,2,1,0:T(8,128)(2,1)}), bf16[2,512,16,128]{3,2,1,0:T(8,128)(2,1)}) %all-gather.3.cloned.1.call-update) | async-done | bytes 4194320 | tf_op jit(solution)/shard_map/all_gather | solution.py:10
  65.2 3.4 %gather_fusion = bf16[512,16,128]{2,1,0:T(8,128)(2,1)S(1)} fusion(bf16[1024,16,128]{2,1,0:T(8,128)(2,1)} %bitcast.32, s32[1024]{0:T(1024)S(1)} %pad_clamp_fusion), kind=kCustom, calls=%fused_computation | custom fusion | bytes 4196352 | tf_op jit(solution)/shard_map/gather | solution.py:13
  68.5 0.0 copy-start.2
  68.6 11.7 %fusion.11 = f32[512,16,128]{2,1,0:T(8,128)S(1)} fusion(bf16[512,16,128]{2,1,0:T(8,128)(2,1)S(1)} %gather_fusion, bf16[512,128,128]{2,1,0:T(8,128)(2,1)} %param.8), kind=kOutput, calls=%fused_computation.18 | convolution fusion | flops 268435456 | bytes 23068672 | tf_op jit(solution)/shard_map/kas,kos->kao/dot_general | solution.py:14
  80.3 0.0 copy-done.2
  80.3 2.7 %fusion.2 = f32[32,16,128]{2,0,1:T(8,128)S(1)} fusion(f32[512,16,128]{2,1,0:T(8,128)S(1)} %fusion.11, s32[512]{0:T(512)S(1)} %copy-done.2), kind=kOutput, calls=%fused_computation.4 | convolution fusion | flops 402669568 | bytes 4458496 | tf_op jit(solution)/shard_map/kg,kao->gao/dot_general | solution.py:15
  83.0 0.2 copy.24
  83.2 0.9 copy.13
  84.1 7.9 %all-to-all-start = ((f32[128,2,2,128]{3,2,1,0:T(2,128)}), f32[128,2,2,128]{3,2,1,0:T(2,128)S(1)}, u32[]{:S(2)}, u32[]{:S(2)}) async-start(f32[128,2,2,128]{3,2,1,0:T(2,128)} %copy.13), calls=%async_computation | async-start | bytes 524288 | tf_op jit(solution)/shard_map/all_to_all | solution.py:20
  91.9 27.5 %all-gather.5.cloned.1.call-done = bf16[2,512,16,128]{3,2,1,0:T(8,128)(2,1)} async-done(((bf16[2,32,16,128]{3,2,1,0:T(8,128)(2,1)}), bf16[2,512,16,128]{3,2,1,0:T(8,128)(2,1)}) %all-gather.5.cloned.1.call-update) | async-done | bytes 4194320 | tf_op jit(solution)/shard_map/all_gather | solution.py:10
  119.4 3.4 %gather_fusion.1 = bf16[512,16,128]{2,1,0:T(8,128)(2,1)S(1)} fusion(bf16[1024,16,128]{2,1,0:T(8,128)(2,1)} %bitcast.31, s32[1024]{0:T(1024)S(1)} %pad_clamp_fusion), kind=kCustom, calls=%fused_computation.1 | custom fusion | bytes 4196352 | tf_op jit(solution)/shard_map/gather | solution.py:13
  122.8 11.7 %fusion.12 = f32[512,16,128]{2,1,0:T(8,128)S(1)} fusion(bf16[512,16,128]{2,1,0:T(8,128)(2,1)S(1)} %gather_fusion.1, bf16[512,128,128]{2,1,0:T(8,128)(2,1)} %param.8), kind=kOutput, calls=%fused_computation.19 | convolution fusion | flops 268435456 | bytes 23068672 | tf_op jit(solution)/shard_map/kas,kos->kao/dot_general | solution.py:14
  134.5 0.0 copy-start.3
  134.5 2.7 %fusion = f32[32,16,128]{2,0,1:T(8,128)S(1)} fusion(f32[512,16,128]{2,1,0:T(8,128)S(1)} %fusion.12, s32[512]{0:T(512)S(1)} %copy-done.2), kind=kOutput, calls=%fused_computation.2 | convolution fusion | flops 402669568 | bytes 4458496 | tf_op jit(solution)/shard_map/kg,kao->gao/dot_general | solution.py:15
  137.3 0.2 copy.23
  137.4 0.9 copy.16
  138.3 0.0 all-to-all-done
  138.3 7.1 %all-to-all-start.1 = ((f32[128,2,2,128]{3,2,1,0:T(2,128)}), f32[128,2,2,128]{3,2,1,0:T(2,128)S(1)}, u32[]{:S(2)}, u32[]{:S(2)}) async-start(f32[128,2,2,128]{3,2,1,0:T(2,128)} %copy.16), calls=%async_computation.1 | async-start | bytes 524288 | tf_op jit(solution)/shard_map/all_to_all | solution.py:20
  145.5 0.1 reduce_sum.18
  145.6 10.8 %all-to-all-done.1 = f32[128,2,2,128]{3,2,1,0:T(2,128)S(1)} async-done(((f32[128,2,2,128]{3,2,1,0:T(2,128)}), f32[128,2,2,128]{3,2,1,0:T(2,128)S(1)}, u32[]{:S(2)}, u32[]{:S(2)}) %all-to-all-start.1) | async-done | bytes 262176 | tf_op jit(solution)/shard_map/all_to_all | solution.py:20
  156.4 0.1 reduce_sum.19
  156.6 0.0 copy-done
  156.6 0.0 copy-done.3
  156.6 0.0 copy-start.1
  156.6 0.7 fusion.9
  157.3 0.0 copy-done.1
  (2 shorter events, 0.0 us)
Async XLA Ops:
  7.2 149.4 %copy-start = (bf16[2,128,128]{2,1,0:T(8,128)(2,1)S(1)}, bf16[2,128,128]{2,1,0:T(8,128)(2,1)}, u32[]{:S(2)}) copy-start(bf16[2,128,128]{2,1,0:T(8,128)(2,1)} %param.13) | copy-start | bytes 196612
  7.2 58.0 %all-gather.3.cloned.1.call-start = ((), (), s32[]{:S(2)}) async-start(), calls=%async_computation.2 | async-start | bytes 4456448 | tf_op jit(solution)/shard_map/all_gather | solution.py:10
  9.8 109.7 %all-gather.5.cloned.1.call-start = ((), (), s32[]{:S(2)}) async-start(), calls=%async_computation.3 | async-start | bytes 4456448 | tf_op jit(solution)/shard_map/all_gather | solution.py:10
  68.5 11.7 %copy-start.2 = (s32[512]{0:T(512)S(1)}, s32[512]{0:T(512)}, u32[]{:S(2)}) copy-start(s32[512]{0:T(512)} %param.10) | copy-start | bytes 6148
  84.1 54.3 %all-to-all-start = ((f32[128,2,2,128]{3,2,1,0:T(2,128)}), f32[128,2,2,128]{3,2,1,0:T(2,128)S(1)}, u32[]{:S(2)}, u32[]{:S(2)}) async-start(f32[128,2,2,128]{3,2,1,0:T(2,128)} %copy.13), calls=%async_computation | async-start | bytes 524288 | tf_op jit(solution)/shard_map/all_to_all | solution.py:20
  134.5 22.0 %copy-start.3 = (f32[2,4,128]{2,1,0:T(4,128)S(1)}, f32[2,4,128]{2,1,0:T(4,128)}, u32[]{:S(2)}) copy-start(f32[2,4,128]{2,1,0:T(4,128)} %param.12) | copy-start | bytes 12292
  138.3 18.1 %all-to-all-start.1 = ((f32[128,2,2,128]{3,2,1,0:T(2,128)}), f32[128,2,2,128]{3,2,1,0:T(2,128)S(1)}, u32[]{:S(2)}, u32[]{:S(2)}) async-start(f32[128,2,2,128]{3,2,1,0:T(2,128)} %copy.16), calls=%async_computation.1 | async-start | bytes 524288 | tf_op jit(solution)/shard_map/all_to_all | solution.py:20
  156.6 0.8 copy-start.1
Sparse Core Ops, SparseCore 0:
  10.2 54.9 all-gather.2
  67.4 52.0 all-gather.4

commit v4 on v2

--- a/solution.py
+++ b/solution.py
@@ -2,6 +2,31 @@
 import jax.numpy as jnp
 from jax import lax
 from jax.sharding import PartitionSpec as P
+
+
+def shift_pairs(rows, cols, step, along_cols):
+    pairs = []
+    for a in range(rows):
+        for b in range(cols):
+            if along_cols:
+                pairs.append((a * cols + b, a * cols + (b + step) % cols))
+            else:
+                pairs.append((a * cols + b, ((a + step) % rows) * cols + b))
+    return pairs
+
+
+def ring_gather(x, rows, cols, along_cols):
+    n = cols if along_cols else rows
+    plus = shift_pairs(rows, cols, 1, along_cols)
+    minus = shift_pairs(rows, cols, -1, along_cols)
+    from_behind = lax.ppermute(x, "grp", plus)
+    from_ahead = lax.ppermute(x, "grp", minus)
+    assert n == 4
+    half = x.shape[0] // 2
+    far_a = lax.ppermute(from_behind[:half], "grp", plus)
+    far_b = lax.ppermute(from_ahead[half:], "grp", minus)
+    far = jnp.concatenate([far_a, far_b], axis=0)
+    return jnp.stack([x, from_ahead, far, from_behind])
 
 
 def body(history, tiles, tile_src, tile_obs, tile_lag, incident, near_inverse):
@@ -10,11 +35,22 @@
     obs_dev, ang_dev, width = incident.shape
     observers = obs_dev * n_grp
     hist16 = history.astype(jnp.bfloat16)
-    gathered = lax.all_gather(hist16, "grp", axis=1, tiled=True)
-    lag_count = gathered.shape[0]
-    source_count = gathered.shape[1]
-    flat = gathered.reshape(lag_count * source_count, gathered.shape[2], gathered.shape[3])
-    picked = flat[tile_lag * source_count + tile_src]
+    lag_count, src_dev, angles, _ = hist16.shape
+    rows = 4
+    cols = n_grp // rows
+    assert lag_count == 2 and rows * cols == n_grp
+    first = ring_gather(ring_gather(hist16[0], rows, cols, True), rows, cols, False)
+    second = ring_gather(ring_gather(hist16[1], rows, cols, False), rows, cols, True)
+    per_lag = n_grp * src_dev
+    flat = jnp.concatenate([first.reshape(per_lag, angles, width), second.reshape(per_lag, angles, width)])
+    me = lax.axis_index("grp")
+    owner = tile_src // src_dev
+    local = tile_src % src_dev
+    dy = (owner // cols - me // cols + rows) % rows
+    dz = (owner % cols - me % cols + cols) % cols
+    index_first = (dy * cols + dz) * src_dev + local
+    index_second = per_lag + (dz * rows + dy) * src_dev + local
+    picked = flat[jnp.where(tile_lag == 0, index_first, index_second)]
     terms = jnp.einsum("kas,kos->kao", picked, tiles, preferred_element_type=jnp.float32)
     onehot = (tile_obs[:, None] == jnp.arange(observers, dtype=tile_obs.dtype)[None, :]).astype(jnp.float32)
     partial = jnp.einsum("kg,kao->gao", onehot, terms, precision=lax.Precision.HIGHEST,

time: 142 us -> 153 us (1.077)
  waiting for transfers between devices: 74.2 us -> 49.2 us
  starting transfers between devices: 0.04 us -> 24 us
  other arithmetic: 3.02 us -> 17.5 us
  between operations: 14.1 us -> 0.87 us
  blocking collectives: 21.4 us -> 27.2 us
  local copies, waits for them, and re-layouts: 7.22 us -> 12.3 us
    all_gather x1 -> x0, waiting for transfers between devices: 74.2 us -> none  [body(): gathered = lax.all_gather(hist16, 'grp', axis=1, tiled=True)]
    ppermute x0 -> x16, waiting for transfers between devices: none -> 49.2 us  [the longest x4 26.1 us: ring_gather(): far_a = lax.ppermute(from_behind[:half], 'grp', plus)]
    ppermute x0 -> x16, starting transfers between devices: none -> 24 us  [the longest x4 9.86 us: ring_gather(): far_b = lax.ppermute(from_ahead[half:], 'grp', minus)]
    another operation x0 -> x8, other arithmetic: none -> 8.5 us  [ring_gather(): return jnp.stack([x, from_ahead, far, from_behind])]
    concatenate x0 -> x1, other arithmetic: none -> 7.43 us  [body(): jnp.concatenate([first.reshape(per_lag, angles, width), second.reshape(pe...]
    all_to_all x1, blocking collectives: 21.4 us -> 27.2 us  [body(): received = lax.all_to_all(partial, ('grp', 'lag'), 0, 0, tiled=True)]
    slice x0 -> x9, local copies, waits for them, and re-layouts: none -> 4.03 us  [the longest x4 1.95 us: ring_gather(): far_b = lax.ppermute(from_ahead[half:], 'grp', minus)]
  transfers between devices with their start and end apart: 1 -> 16, of which waited for: 1 -> 6; matrix products, arithmetic and copies ran while one was open for 1% -> 6% of each run, Pallas kernels for 0% -> 0%
where the time goes in v4:
time: 153 us
  waiting for transfers between devices  49.2 us (32%)
  blocking collectives  27.2 us (18%)
  starting transfers between devices  24 us (16%)
  matrix products  21.6 us (14%)
  other arithmetic  17.5 us (11%)
  local copies, waits for them, and re-layouts  12.3 us (8%)
    all_to_all x1, blocking collectives, body(): received = lax.all_to_all(partial, ('grp', 'lag'), 0, 0, tiled=True)  27.2 us
    ppermute x4, waiting for transfers between devices, ring_gather(): far_a = lax.ppermute(from_behind[:half], 'grp', plus)  26.1 us
    ppermute x4, waiting for transfers between devices, ring_gather(): from_behind = lax.ppermute(x, 'grp', plus)  23 us
    dot_general x1, matrix products, body(): jnp.einsum('kas,kos->kao', picked, tiles, preferred_element_type=jnp.floa...  13.1 us
    ppermute x4, starting transfers between devices, ring_gather(): far_b = lax.ppermute(from_ahead[half:], 'grp', minus)  9.86 us
    another operation x8, other arithmetic, ring_gather(): return jnp.stack([x, from_ahead, far, from_behind])  8.5 us
    ppermute x4, starting transfers between devices, ring_gather(): from_ahead = lax.ppermute(x, 'grp', minus)  8.17 us
    dot_general x1, matrix products, body(): jnp.einsum('kg,kao->gao', onehot, terms, precision=lax.Precision.HIGHEST,...  7.72 us
  transfers between devices with their start and end apart: 16, of which 6 were waited for; matrix products, arithmetic and copies ran while one was open for 6% of the time, Pallas kernels for 0%

profile of v4, /device:TPU:1, one launch (start us, length us, event | category | flops | bytes accessed | tf_op | source)
XLA Modules:
  0.0 152.6 jit_solution(15778627769312142424)
XLA Ops:
  0.6 0.0 copy-start
  0.6 1.3 convert_element_type.7
  2.0 0.1 fusion.16
  2.1 2.5 %collective-permute-start.1 = (bf16[32,32,128]{2,1,0:T(8,128)(2,1)S(1)}, bf16[32,32,128]{2,1,0:T(8,128)(2,1)S(1)}, u32[]{:S(2)}, u32[]{:S(2)}) collective-permute-start(bf16[32,32,128]{2,1,0:T(8,128)(2,1)S(1)} %get-tuple-element.7), channel_id=1, source_target_pairs={{0,8},{8,16},{16,24},{24,0},{32,40},{40,48},{48,56},{56,32},{64,72... | collective-permute-start | bytes 786440 | tf_op jit(solution)/shard_map/ppermute | solution.py:22
  4.7 2.2 %collective-permute-start = (bf16[32,32,128]{2,1,0:T(8,128)(2,1)S(1)}, bf16[32,32,128]{2,1,0:T(8,128)(2,1)S(1)}, u32[]{:S(2)}, u32[]{:S(2)}) collective-permute-start(bf16[32,32,128]{2,1,0:T(8,128)(2,1)S(1)} %get-tuple-element.7), channel_id=1, source_target_pairs={{0,24},{8,0},{16,8},{24,16},{32,56},{40,32},{48,40},{56,48},{64,88... | collective-permute-start | bytes 786440 | tf_op jit(solution)/shard_map/ppermute | solution.py:23
  6.9 6.0 %collective-permute-done.1 = bf16[32,32,128]{2,1,0:T(8,128)(2,1)S(1)} collective-permute-done((bf16[32,32,128]{2,1,0:T(8,128)(2,1)S(1)}, bf16[32,32,128]{2,1,0:T(8,128)(2,1)S(1)}, u32[]{:S(2)}, u32[]{:S(2)}) %collective-permute-start.1) | collective-permute-done | bytes 262176 | tf_op jit(solution)/shard_map/ppermute | solution.py:22
  12.8 0.1 collective-permute-start.2
  13.0 2.7 %collective-permute-start.3 = (bf16[16,32,128]{2,1,0:T(8,128)(2,1)S(1)}, bf16[16,32,128]{2,1,0:T(8,128)(2,1)S(1)}, u32[]{:S(2)}, u32[]{:S(2)}) collective-permute-start(bf16[16,32,128]{2,1,0:T(8,128)(2,1)S(1)} %slice.44), channel_id=1, source_target_pairs={{0,24},{8,0},{16,8},{24,16},{32,56},{40,32},{48,40},{56,48},{64,88... | collective-permute-start | bytes 393224 | tf_op jit(solution)/shard_map/ppermute | solution.py:27
  15.7 1.3 collective-permute-start.9
  17.0 1.4 collective-permute-start.8
  18.4 0.0 copy-start.6
  18.5 0.0 copy-start.7
  18.5 0.2 fusion.15
  18.7 0.9 collective-permute-start.5
  19.5 1.9 %collective-permute-start.4 = (bf16[4,32,32,128]{3,2,1,0:T(8,128)(2,1)S(1)}, bf16[4,32,32,128]{3,2,1,0:T(8,128)(2,1)S(1)}, u32[]{:S(2)}, u32[]{:S(2)}) collective-permute-start(bf16[4,32,32,128]{3,2,1,0:T(8,128)(2,1)S(1)} %get-tuple-element.3), channel_id=1, source_target_pairs={{0,96},{8,104},{16,112},{24,120},{32,0},{40,8},{48,16},{56,24},{64... | collective-permute-start | bytes 3145736 | tf_op jit(solution)/shard_map/ppermute | solution.py:23
  21.4 1.6 %collective-permute-done.9 = bf16[32,32,128]{2,1,0:T(8,128)(2,1)S(1)} collective-permute-done((bf16[32,32,128]{2,1,0:T(8,128)(2,1)S(1)}, bf16[32,32,128]{2,1,0:T(8,128)(2,1)S(1)}, u32[]{:S(2)}, u32[]{:S(2)}) %collective-permute-start.9) | collective-permute-done | bytes 262176 | tf_op jit(solution)/shard_map/ppermute | solution.py:22
  23.0 0.1 collective-permute-start.10
  23.1 2.7 %collective-permute-start.11 = (bf16[16,32,128]{2,1,0:T(8,128)(2,1)S(1)}, bf16[16,32,128]{2,1,0:T(8,128)(2,1)S(1)}, u32[]{:S(2)}, u32[]{:S(2)}) collective-permute-start(bf16[16,32,128]{2,1,0:T(8,128)(2,1)S(1)} %slice.49), channel_id=1, source_target_pairs={{0,96},{8,104},{16,112},{24,120},{32,0},{40,8},{48,16},{56,24},{64... | collective-permute-start | bytes 393224 | tf_op jit(solution)/shard_map/ppermute | solution.py:27
  25.9 22.4 %collective-permute-done.10 = bf16[16,32,128]{2,1,0:T(8,128)(2,1)S(1)} collective-permute-done((bf16[16,32,128]{2,1,0:T(8,128)(2,1)S(1)}, bf16[16,32,128]{2,1,0:T(8,128)(2,1)S(1)}, u32[]{:S(2)}, u32[]{:S(2)}) %collective-permute-start.10) | collective-permute-done | bytes 131104 | tf_op jit(solution)/shard_map/ppermute | solution.py:26
  48.3 1.2 fusion.14
  49.5 2.7 %collective-permute-start.12 = (bf16[4,32,32,128]{3,2,1,0:T(8,128)(2,1)}, bf16[4,32,32,128]{3,2,1,0:T(8,128)(2,1)}, u32[]{:S(2)}, u32[]{:S(2)}) collective-permute-start(bf16[4,32,32,128]{3,2,1,0:T(8,128)(2,1)} %get-tuple-element.5), channel_id=1, source_target_pairs={{0,24},{8,0},{16,8},{24,16},{32,56},{40,32},{48,40},{56,48},{64,88... | collective-permute-start | bytes 3145736 | tf_op jit(solution)/shard_map/ppermute | solution.py:23
  52.2 0.8 slice.45
  53.0 1.0 collective-permute-start.6
  54.0 1.0 copy-done.1
  55.0 0.9 slice.46
  55.8 1.7 %collective-permute-start.7 = (bf16[2,32,32,128]{3,2,1,0:T(8,128)(2,1)}, bf16[2,32,32,128]{3,2,1,0:T(8,128)(2,1)}, u32[]{:S(2)}, u32[]{:S(2)}) collective-permute-start(bf16[2,32,32,128]{3,2,1,0:T(8,128)(2,1)} %slice.46), channel_id=1, source_target_pairs={{0,96},{8,104},{16,112},{24,120},{32,0},{40,8},{48,16},{56,24},{64... | collective-permute-start | bytes 1572872 | tf_op jit(solution)/shard_map/ppermute | solution.py:27
  57.6 15.4 %collective-permute-done.13 = bf16[4,32,32,128]{3,2,1,0:T(8,128)(2,1)} collective-permute-done((bf16[4,32,32,128]{3,2,1,0:T(8,128)(2,1)}, bf16[4,32,32,128]{3,2,1,0:T(8,128)(2,1)}, u32[]{:S(2)}, u32[]{:S(2)}) %collective-permute-start.13) | collective-permute-done | bytes 1048608 | tf_op jit(solution)/shard_map/ppermute | solution.py:22
  73.0 1.1 slice.50
  74.1 0.1 collective-permute-start.14
  74.2 1.1 slice.51
  75.3 2.7 %collective-permute-start.15 = (bf16[2,32,32,128]{3,2,1,0:T(8,128)(2,1)S(1)}, bf16[2,32,32,128]{3,2,1,0:T(8,128)(2,1)S(1)}, u32[]{:S(2)}, u32[]{:S(2)}) collective-permute-start(bf16[2,32,32,128]{3,2,1,0:T(8,128)(2,1)S(1)} %slice.51), channel_id=1, source_target_pairs={{0,24},{8,0},{16,8},{24,16},{32,56},{40,32},{48,40},{56,48},{64,88... | collective-permute-start | bytes 1572872 | tf_op jit(solution)/shard_map/ppermute | solution.py:27
  78.0 1.3 maximum_bitcast_fusion
  79.3 2.3 %pad_maximum_fusion.1 = bf16[4,4,32,32,128]{4,3,2,1,0:T(8,128)(2,1)} fusion(bf16[1,4,32,32,128]{4,3,2,1,0:T(8,128)(2,1)S(1)} %bitcast.40, bf16[1,4,32,32,128]{4,3,2,1,0:T(8,128)(2,1)S(1)} %maximum_bitcast_fusion, bf16[1,4,32,32,128]{4,3,2,1,0:T(8,128)(2,1)S(1)} %bitcast.41, bf16[1,4,32,32,128]{4,3,2,1,0:T(8,128)(2,1)S(1)} %get-tuple-element.2), kind=kLoop, calls=%fused_computation.4 | loop fusion | flops 6291456 | bytes 8388608 | tf_op jit(solution)/shard_map/stack | solution.py:29
  81.6 3.6 %collective-permute-done.14 = bf16[2,32,32,128]{3,2,1,0:T(8,128)(2,1)S(1)} collective-permute-done((bf16[2,32,32,128]{3,2,1,0:T(8,128)(2,1)S(1)}, bf16[2,32,32,128]{3,2,1,0:T(8,128)(2,1)S(1)}, u32[]{:S(2)}, u32[]{:S(2)}) %collective-permute-start.14) | collective-permute-done | bytes 524320 | tf_op jit(solution)/shard_map/ppermute | solution.py:26
  85.2 0.1 collective-permute-done.15
  85.3 0.1 maximum_bitcast_fusion.1
  85.4 3.5 %pad_maximum_fusion.2 = bf16[4,4,32,32,128]{4,3,2,1,0:T(8,128)(2,1)} fusion(bf16[1,4,32,32,128]{4,3,2,1,0:T(8,128)(2,1)} %bitcast.17, bf16[1,4,32,32,128]{4,3,2,1,0:T(8,128)(2,1)S(1)} %maximum_bitcast_fusion.1, bf16[1,4,32,32,128]{4,3,2,1,0:T(8,128)(2,1)} %bitcast.15, bf16[1,4,32,32,128]{4,3,2,1,0:T(8,128)(2,1)S(1)} %get-tuple-element.4), kind=kLoop, calls=%fused_computation.5 | loop fusion | flops 6291456 | bytes 8388608 | tf_op jit(solution)/shard_map/stack | solution.py:29
  88.9 7.4 %pad_maximum_fusion = bf16[1024,32,128]{2,1,0:T(8,128)(2,1)} fusion(bf16[512,32,128]{2,1,0:T(8,128)(2,1)} %bitcast.39, bf16[512,32,128]{2,1,0:T(8,128)(2,1)} %bitcast.38), kind=kLoop, calls=%fused_computation.1 | loop fusion | flops 4194304 | bytes 16777216 | tf_op jit(solution)/shard_map/concatenate | solution.py:45
  96.3 6.6 %gather_fusion = bf16[512,32,128]{2,1,0:T(8,128)(2,1)} fusion(bf16[1024,32,128]{2,1,0:T(8,128)(2,1)} %pad_maximum_fusion, s32[1024]{0:T(1024)S(1)} %pad_clamp_fusion), kind=kCustom, calls=%fused_computation | custom fusion | bytes 8390656 | tf_op jit(solution)/shard_map/gather | solution.py:53
  102.9 13.1 %fusion.17 = f32[512,32,128]{2,1,0:T(8,128)S(1)} fusion(bf16[512,32,128]{2,1,0:T(8,128)(2,1)} %gather_fusion, bf16[512,128,128]{2,1,0:T(8,128)(2,1)} %param.8), kind=kOutput, calls=%fused_computation.51 | convolution fusion | flops 536870912 | bytes 29360128 | tf_op jit(solution)/shard_map/kas,kos->kao/dot_general | solution.py:54
  116.0 0.0 copy-start.4
  116.0 7.7 %fusion = f32[32,32,128]{2,0,1:T(8,128)S(1)} fusion(f32[512,32,128]{2,1,0:T(8,128)S(1)} %fusion.17, s32[512]{0:T(512)S(1)} %copy-done.5), kind=kOutput, calls=%fused_computation.2 | convolution fusion | flops 805322752 | bytes 8914944 | tf_op jit(solution)/shard_map/kg,kao->gao/dot_general | solution.py:56
  123.8 0.3 copy.16
  124.1 0.3 copy.12
  124.4 27.2 %all_to_all.5 = f32[128,2,4,128]{3,2,1,0:T(4,128)S(1)} all-to-all(f32[128,2,4,128]{3,2,1,0:T(4,128)S(1)} %copy.12), channel_id=1, replica_groups=mesh['grp'=16,'lag'=8] {'grp','lag'}, dimensions={0} | all-to-all | bytes 1048576 | tf_op jit(solution)/shard_map/all_to_all | solution.py:60
  151.6 0.1 reduce_sum.9
  151.8 0.0 copy-start.3
  151.8 0.7 fusion.11
  (29 shorter events, 0.2 us)
Async XLA Ops:
  0.6 151.2 %copy-start = (bf16[2,128,128]{2,1,0:T(8,128)(2,1)S(1)}, bf16[2,128,128]{2,1,0:T(8,128)(2,1)}, u32[]{:S(2)}) copy-start(bf16[2,128,128]{2,1,0:T(8,128)(2,1)} %param.13) | copy-start | bytes 196612
  2.1 10.7 %collective-permute-start.1 = (bf16[32,32,128]{2,1,0:T(8,128)(2,1)S(1)}, bf16[32,32,128]{2,1,0:T(8,128)(2,1)S(1)}, u32[]{:S(2)}, u32[]{:S(2)}) collective-permute-start(bf16[32,32,128]{2,1,0:T(8,128)(2,1)S(1)} %get-tuple-element.7), channel_id=1, source_target_pairs={{0,8},{8,16},{16,24},{24,0},{32,40},{40,48},{48,56},{56,32},{64,72... | collective-permute-start | bytes 786440 | tf_op jit(solution)/shard_map/ppermute | solution.py:22
  4.7 8.3 %collective-permute-start = (bf16[32,32,128]{2,1,0:T(8,128)(2,1)S(1)}, bf16[32,32,128]{2,1,0:T(8,128)(2,1)S(1)}, u32[]{:S(2)}, u32[]{:S(2)}) collective-permute-start(bf16[32,32,128]{2,1,0:T(8,128)(2,1)S(1)} %get-tuple-element.7), channel_id=1, source_target_pairs={{0,24},{8,0},{16,8},{24,16},{32,56},{40,32},{48,40},{56,48},{64,88... | collective-permute-start | bytes 786440 | tf_op jit(solution)/shard_map/ppermute | solution.py:23
  12.8 5.6 %collective-permute-start.2 = (bf16[16,32,128]{2,1,0:T(8,128)(2,1)S(1)}, bf16[16,32,128]{2,1,0:T(8,128)(2,1)S(1)}, u32[]{:S(2)}, u32[]{:S(2)}) collective-permute-start(bf16[16,32,128]{2,1,0:T(8,128)(2,1)S(1)} %slice.43), channel_id=1, source_target_pairs={{0,8},{8,16},{16,24},{24,0},{32,40},{40,48},{48,56},{56,32},{64,72... | collective-permute-start | bytes 393224 | tf_op jit(solution)/shard_map/ppermute | solution.py:26
  13.0 5.5 %collective-permute-start.3 = (bf16[16,32,128]{2,1,0:T(8,128)(2,1)S(1)}, bf16[16,32,128]{2,1,0:T(8,128)(2,1)S(1)}, u32[]{:S(2)}, u32[]{:S(2)}) collective-permute-start(bf16[16,32,128]{2,1,0:T(8,128)(2,1)S(1)} %slice.44), channel_id=1, source_target_pairs={{0,24},{8,0},{16,8},{24,16},{32,56},{40,32},{48,40},{56,48},{64,88... | collective-permute-start | bytes 393224 | tf_op jit(solution)/shard_map/ppermute | solution.py:27
  15.7 7.3 %collective-permute-start.9 = (bf16[32,32,128]{2,1,0:T(8,128)(2,1)S(1)}, bf16[32,32,128]{2,1,0:T(8,128)(2,1)S(1)}, u32[]{:S(2)}, u32[]{:S(2)}) collective-permute-start(bf16[32,32,128]{2,1,0:T(8,128)(2,1)S(1)} %get-tuple-element.8), channel_id=1, source_target_pairs={{0,32},{8,40},{16,48},{24,56},{32,64},{40,72},{48,80},{56,88},{64,... | collective-permute-start | bytes 786440 | tf_op jit(solution)/shard_map/ppermute | solution.py:22
  17.0 6.1 %collective-permute-start.8 = (bf16[32,32,128]{2,1,0:T(8,128)(2,1)S(1)}, bf16[32,32,128]{2,1,0:T(8,128)(2,1)S(1)}, u32[]{:S(2)}, u32[]{:S(2)}) collective-permute-start(bf16[32,32,128]{2,1,0:T(8,128)(2,1)S(1)} %get-tuple-element.8), channel_id=1, source_target_pairs={{0,96},{8,104},{16,112},{24,120},{32,0},{40,8},{48,16},{56,24},{64... | collective-permute-start | bytes 786440 | tf_op jit(solution)/shard_map/ppermute | solution.py:23
  18.4 39.1 %copy-start.6 = (s32[512]{0:T(512)S(1)}, s32[512]{0:T(512)}, u32[]{:S(2)}) copy-start(s32[512]{0:T(512)} %param.9) | copy-start | bytes 6148
  18.5 39.1 %copy-start.7 = (s32[512]{0:T(512)S(1)}, s32[512]{0:T(512)}, u32[]{:S(2)}) copy-start(s32[512]{0:T(512)} %param.11) | copy-start | bytes 6148
  18.7 33.5 %collective-permute-start.5 = (bf16[4,32,32,128]{3,2,1,0:T(8,128)(2,1)S(1)}, bf16[4,32,32,128]{3,2,1,0:T(8,128)(2,1)S(1)}, u32[]{:S(2)}, u32[]{:S(2)}) collective-permute-start(bf16[4,32,32,128]{3,2,1,0:T(8,128)(2,1)S(1)} %get-tuple-element.3), channel_id=1, source_target_pairs={{0,32},{8,40},{16,48},{24,56},{32,64},{40,72},{48,80},{56,88},{64,... | collective-permute-start | bytes 3145736 | tf_op jit(solution)/shard_map/ppermute | solution.py:22
  19.5 34.5 %collective-permute-start.4 = (bf16[4,32,32,128]{3,2,1,0:T(8,128)(2,1)S(1)}, bf16[4,32,32,128]{3,2,1,0:T(8,128)(2,1)S(1)}, u32[]{:S(2)}, u32[]{:S(2)}) collective-permute-start(bf16[4,32,32,128]{3,2,1,0:T(8,128)(2,1)S(1)} %get-tuple-element.3), channel_id=1, source_target_pairs={{0,96},{8,104},{16,112},{24,120},{32,0},{40,8},{48,16},{56,24},{64... | collective-permute-start | bytes 3145736 | tf_op jit(solution)/shard_map/ppermute | solution.py:23
  23.0 25.3 %collective-permute-start.10 = (bf16[16,32,128]{2,1,0:T(8,128)(2,1)S(1)}, bf16[16,32,128]{2,1,0:T(8,128)(2,1)S(1)}, u32[]{:S(2)}, u32[]{:S(2)}) collective-permute-start(bf16[16,32,128]{2,1,0:T(8,128)(2,1)S(1)} %slice.48), channel_id=1, source_target_pairs={{0,32},{8,40},{16,48},{24,56},{32,64},{40,72},{48,80},{56,88},{64,... | collective-permute-start | bytes 393224 | tf_op jit(solution)/shard_map/ppermute | solution.py:26
  23.1 25.2 %collective-permute-start.11 = (bf16[16,32,128]{2,1,0:T(8,128)(2,1)S(1)}, bf16[16,32,128]{2,1,0:T(8,128)(2,1)S(1)}, u32[]{:S(2)}, u32[]{:S(2)}) collective-permute-start(bf16[16,32,128]{2,1,0:T(8,128)(2,1)S(1)} %slice.49), channel_id=1, source_target_pairs={{0,96},{8,104},{16,112},{24,120},{32,0},{40,8},{48,16},{56,24},{64... | collective-permute-start | bytes 393224 | tf_op jit(solution)/shard_map/ppermute | solution.py:27
  49.5 23.5 %collective-permute-start.13 = (bf16[4,32,32,128]{3,2,1,0:T(8,128)(2,1)}, bf16[4,32,32,128]{3,2,1,0:T(8,128)(2,1)}, u32[]{:S(2)}, u32[]{:S(2)}) collective-permute-start(bf16[4,32,32,128]{3,2,1,0:T(8,128)(2,1)} %get-tuple-element.5), channel_id=1, source_target_pairs={{0,8},{8,16},{16,24},{24,0},{32,40},{40,48},{48,56},{56,32},{64,72... | collective-permute-start | bytes 3145736 | tf_op jit(solution)/shard_map/ppermute | solution.py:22
  49.5 24.7 %collective-permute-start.12 = (bf16[4,32,32,128]{3,2,1,0:T(8,128)(2,1)}, bf16[4,32,32,128]{3,2,1,0:T(8,128)(2,1)}, u32[]{:S(2)}, u32[]{:S(2)}) collective-permute-start(bf16[4,32,32,128]{3,2,1,0:T(8,128)(2,1)} %get-tuple-element.5), channel_id=1, source_target_pairs={{0,24},{8,0},{16,8},{24,16},{32,56},{40,32},{48,40},{56,48},{64,88... | collective-permute-start | bytes 3145736 | tf_op jit(solution)/shard_map/ppermute | solution.py:23
  53.0 25.0 %collective-permute-start.6 = (bf16[2,32,32,128]{3,2,1,0:T(8,128)(2,1)}, bf16[2,32,32,128]{3,2,1,0:T(8,128)(2,1)}, u32[]{:S(2)}, u32[]{:S(2)}) collective-permute-start(bf16[2,32,32,128]{3,2,1,0:T(8,128)(2,1)} %slice.45), channel_id=1, source_target_pairs={{0,32},{8,40},{16,48},{24,56},{32,64},{40,72},{48,80},{56,88},{64,... | collective-permute-start | bytes 1572872 | tf_op jit(solution)/shard_map/ppermute | solution.py:26
  54.0 1.0 copy-start.1
  55.8 22.2 %collective-permute-start.7 = (bf16[2,32,32,128]{3,2,1,0:T(8,128)(2,1)}, bf16[2,32,32,128]{3,2,1,0:T(8,128)(2,1)}, u32[]{:S(2)}, u32[]{:S(2)}) collective-permute-start(bf16[2,32,32,128]{3,2,1,0:T(8,128)(2,1)} %slice.46), channel_id=1, source_target_pairs={{0,96},{8,104},{16,112},{24,120},{32,0},{40,8},{48,16},{56,24},{64... | collective-permute-start | bytes 1572872 | tf_op jit(solution)/shard_map/ppermute | solution.py:27
  57.5 21.8 %copy-start.2 = (bf16[4,32,32,128]{3,2,1,0:T(8,128)(2,1)S(1)}, bf16[4,32,32,128]{3,2,1,0:T(8,128)(2,1)}, u32[]{:S(2)}) copy-start(bf16[4,32,32,128]{3,2,1,0:T(8,128)(2,1)} %copy-done.1) | copy-start | bytes 3145732
  74.1 11.1 %collective-permute-start.14 = (bf16[2,32,32,128]{3,2,1,0:T(8,128)(2,1)S(1)}, bf16[2,32,32,128]{3,2,1,0:T(8,128)(2,1)S(1)}, u32[]{:S(2)}, u32[]{:S(2)}) collective-permute-start(bf16[2,32,32,128]{3,2,1,0:T(8,128)(2,1)S(1)} %slice.50), channel_id=1, source_target_pairs={{0,8},{8,16},{16,24},{24,0},{32,40},{40,48},{48,56},{56,32},{64,72... | collective-permute-start | bytes 1572872 | tf_op jit(solution)/shard_map/ppermute | solution.py:26
  75.3 10.1 %collective-permute-start.15 = (bf16[2,32,32,128]{3,2,1,0:T(8,128)(2,1)S(1)}, bf16[2,32,32,128]{3,2,1,0:T(8,128)(2,1)S(1)}, u32[]{:S(2)}, u32[]{:S(2)}) collective-permute-start(bf16[2,32,32,128]{3,2,1,0:T(8,128)(2,1)S(1)} %slice.51), channel_id=1, source_target_pairs={{0,24},{8,0},{16,8},{24,16},{32,56},{40,32},{48,40},{56,48},{64,88... | collective-permute-start | bytes 1572872 | tf_op jit(solution)/shard_map/ppermute | solution.py:27
  102.9 13.1 %copy-start.5 = (s32[512]{0:T(512)S(1)}, s32[512]{0:T(512)}, u32[]{:S(2)}) copy-start(s32[512]{0:T(512)} %param.10) | copy-start | bytes 6148
  116.0 35.8 %copy-start.4 = (f32[2,4,128]{2,1,0:T(4,128)S(1)}, f32[2,4,128]{2,1,0:T(4,128)}, u32[]{:S(2)}) copy-start(f32[2,4,128]{2,1,0:T(4,128)} %param.12) | copy-start | bytes 12292
  151.8 0.8 copy-start.3

commit v5 on v1

--- a/solution.py
+++ b/solution.py
@@ -16,12 +16,16 @@
     flat = gathered.reshape(lag_count * source_count, gathered.shape[2], gathered.shape[3])
     picked = flat[tile_lag * source_count + tile_src]
     terms = jnp.einsum("kas,kos->kao", picked, tiles, preferred_element_type=jnp.float32)
-    onehot = (tile_obs[:, None] == jnp.arange(observers, dtype=tile_obs.dtype)[None, :]).astype(jnp.float32)
-    partial = jnp.einsum("kg,kao->gao", onehot, terms, precision=lax.Precision.HIGHEST,
-                         preferred_element_type=jnp.float32)
+    onehot = (tile_obs[:, None] == jnp.arange(observers, dtype=tile_obs.dtype)[None, :]).astype(jnp.bfloat16)
+    high = terms.astype(jnp.bfloat16)
+    low = (terms - high.astype(jnp.float32)).astype(jnp.bfloat16)
+    partial = (jnp.einsum("kg,kao->gao", onehot, high, preferred_element_type=jnp.float32)
+               + jnp.einsum("kg,kao->gao", onehot, low, preferred_element_type=jnp.float32))
     partial = partial.reshape(n_grp, obs_dev, n_lag, ang_dev, width)
-    partial = partial.transpose(0, 2, 1, 3, 4).reshape(n_grp * n_lag, obs_dev, ang_dev, width)
-    field = lax.psum_scatter(partial, ("grp", "lag"), scatter_dimension=0, tiled=True)[0]
+    by_grp = lax.all_to_all(partial, "grp", 0, 0, tiled=True)
+    partial = jnp.sum(by_grp, axis=0).transpose(1, 0, 2, 3)
+    by_lag = lax.all_to_all(partial, "lag", 0, 0, tiled=True)
+    field = jnp.sum(by_lag, axis=0)
     rhs = (incident - field).astype(jnp.bfloat16)
     new_current = jnp.einsum("oag,ohg->oah", rhs, near_inverse, preferred_element_type=jnp.float32)
     return (field, new_current)

time: 266 us -> 144 us (0.54)
  waiting for transfers between devices: 219 us -> 74.2 us
  blocking collectives: 0 us -> 26 us
    unnamed x3 -> x1, waiting for transfers between devices: 145 us -> 0.02 us
    all_to_all x0 -> x2, blocking collectives: none -> 26 us  [the longest x1 15.1 us: body(): by_grp = lax.all_to_all(partial, 'grp', 0, 0, tiled=True)]
    dot_general x1 -> x2, matrix products: 7.72 us -> 4.87 us  [the longest x1 3.52 us: body(): jnp.einsum('kg,kao->gao', onehot, low, preferred_element_type=jnp.float32)]
  transfers between devices with their start and end apart: 2 -> 1, of which waited for: 2 -> 1; matrix products, arithmetic and copies ran while one was open for 0% -> 0% of each run, Pallas kernels for 0% -> 0%
where the time goes in v5:
time: 144 us
  waiting for transfers between devices  74.2 us (52%)
  blocking collectives  26 us (18%)
  matrix products  19.9 us (14%)
  between operations  14.1 us (10%)
  local copies, waits for them, and re-layouts  6.85 us (5%)
  other arithmetic  3.05 us (2%)
    all_gather x1, waiting for transfers between devices, body(): gathered = lax.all_gather(hist16, 'grp', axis=1, tiled=True)  74.2 us
    all_to_all x1, blocking collectives, body(): by_grp = lax.all_to_all(partial, 'grp', 0, 0, tiled=True)  15.1 us
    dot_general x1, matrix products, body(): jnp.einsum('kas,kos->kao', picked, tiles, preferred_element_type=jnp.floa...  14.3 us
    all_to_all x1, blocking collectives, body(): by_lag = lax.all_to_all(partial, 'lag', 0, 0, tiled=True)  10.9 us
    gather x1, local copies, waits for them, and re-layouts, body(): picked = flat[tile_lag * source_count + tile_src]  6.55 us
    dot_general x1, matrix products, body(): jnp.einsum('kg,kao->gao', onehot, low, preferred_element_type=jnp.float32)  3.52 us
  transfers between devices with their start and end apart: 1, of which 1 were waited for; matrix products, arithmetic and copies ran while one was open for 0% of the time, Pallas kernels for 0%

profile of v5, /device:TPU:1, one launch (start us, length us, event | category | flops | bytes accessed | tf_op | source)
XLA Modules:
  0.0 144.2 jit_solution(1609621045576208696)
XLA Ops:
  7.2 0.0 copy-start
  7.2 0.0 all-gather.2.cloned.1.call-start
  7.2 2.2 %convert_element_type.16 = bf16[2,32,32,128]{3,2,1,0:T(8,128)(2,1)} convert(f32[2,32,32,128]{3,2,1,0:T(8,128)} %param.7) | non-fusion elementwise | flops 262144 | bytes 1572864 | tf_op jit(solution)/shard_map/convert_element_type | solution.py:12
  9.4 0.0 all-gather.2.cloned.1.call-update
  9.4 0.7 compare_select_fusion
  10.1 74.2 %all-gather.2.cloned.1.call-done = bf16[2,512,32,128]{3,2,1,0:T(8,128)(2,1)} async-done(((bf16[2,32,32,128]{3,2,1,0:T(8,128)(2,1)}), bf16[2,512,32,128]{3,2,1,0:T(8,128)(2,1)}) %all-gather.2.cloned.1.call-update) | async-done | bytes 8388624 | tf_op jit(solution)/shard_map/all_gather | solution.py:13
  84.3 6.5 %gather_fusion = bf16[512,32,128]{2,1,0:T(8,128)(2,1)} fusion(bf16[1024,32,128]{2,1,0:T(8,128)(2,1)} %bitcast.10, s32[1024]{0:T(1024)S(1)} %pad_clamp_fusion), kind=kCustom, calls=%fused_computation | custom fusion | bytes 8390656 | tf_op jit(solution)/shard_map/gather | solution.py:17
  90.9 0.0 copy-start.2
  90.9 14.3 %subtract_convert_fusion = (bf16[512,32,128]{2,1,0:T(8,128)(2,1)}, bf16[512,32,128]{2,1,0:T(8,128)(2,1)S(1)}) fusion(bf16[512,32,128]{2,1,0:T(8,128)(2,1)} %gather_fusion, bf16[512,128,128]{2,1,0:T(8,128)(2,1)} %param.8), kind=kOutput, calls=%fused_computation.1 | convolution fusion | flops 545259520 | bytes 29360128 | tf_op jit(solution)/shard_map/kas,kos->kao/dot_general | solution.py:18
  105.2 0.0 copy-done.2
  105.2 3.5 %fusion = f32[32,32,128]{2,0,1:T(8,128)S(1)} fusion(bf16[512,32,128]{2,1,0:T(8,128)(2,1)} %get-tuple-element.2, s32[512]{0:T(512)S(1)} %copy-done.2), kind=kOutput, calls=%fused_computation.2 | convolution fusion | flops 134234112 | bytes 4720640 | tf_op jit(solution)/shard_map/kg,kao->gao/dot_general | solution.py:23
  108.7 0.0 copy-start.3
  108.7 1.4 fusion.4
  110.1 0.3 copy.13
  110.4 15.1 %all_to_all.10 = f32[16,2,8,4,128]{4,1,3,2,0:T(2,128)S(1)} all-to-all(f32[16,2,8,4,128]{4,1,3,2,0:T(2,128)S(1)} %copy.13), channel_id=1, replica_groups=mesh['grp'=16,'lag'=8] {'grp'}, dimensions={0} | all-to-all | bytes 1048576 | tf_op jit(solution)/shard_map/all_to_all | solution.py:25
  125.5 0.2 reduce_sum.18
  125.6 10.9 %all_to_all.11 = f32[8,2,4,128]{3,2,1,0:T(4,128)S(1)} all-to-all(f32[8,2,4,128]{3,2,1,0:T(4,128)S(1)} %copy.15), channel_id=1, replica_groups=mesh['grp'=16,'lag'=8] {'lag'}, dimensions={0} | all-to-all | bytes 65536 | tf_op jit(solution)/shard_map/all_to_all | solution.py:27
  136.6 0.0 copy-done
  136.6 0.0 copy-done.3
  136.6 0.0 copy-start.1
  136.6 0.7 fusion.12
  137.3 0.0 copy-done.1
  (3 shorter events, 0.0 us)
Async XLA Ops:
  7.2 129.4 %copy-start = (bf16[2,128,128]{2,1,0:T(8,128)(2,1)S(1)}, bf16[2,128,128]{2,1,0:T(8,128)(2,1)}, u32[]{:S(2)}) copy-start(bf16[2,128,128]{2,1,0:T(8,128)(2,1)} %param.13) | copy-start | bytes 196612
  7.2 77.2 %all-gather.2.cloned.1.call-start = ((), (), s32[]{:S(2)}) async-start(), calls=%async_computation.2 | async-start | bytes 8912896 | tf_op jit(solution)/shard_map/all_gather | solution.py:13
  90.9 14.3 %copy-start.2 = (s32[512]{0:T(512)S(1)}, s32[512]{0:T(512)}, u32[]{:S(2)}) copy-start(s32[512]{0:T(512)} %param.10) | copy-start | bytes 6148
  108.7 27.9 %copy-start.3 = (f32[2,4,128]{2,1,0:T(4,128)S(1)}, f32[2,4,128]{2,1,0:T(4,128)}, u32[]{:S(2)}) copy-start(f32[2,4,128]{2,1,0:T(4,128)} %param.12) | copy-start | bytes 12292
  136.6 0.8 copy-start.1
Sparse Core Ops, SparseCore 0:
  10.2 74.0 all-gather.1

commit v6 on v2

--- a/solution.py
+++ b/solution.py
@@ -17,7 +17,7 @@
     picked = flat[tile_lag * source_count + tile_src]
     terms = jnp.einsum("kas,kos->kao", picked, tiles, preferred_element_type=jnp.float32)
     onehot = (tile_obs[:, None] == jnp.arange(observers, dtype=tile_obs.dtype)[None, :]).astype(jnp.float32)
-    partial = jnp.einsum("kg,kao->gao", onehot, terms, precision=lax.Precision.HIGHEST,
+    partial = jnp.einsum("kg,kao->gao", onehot, terms, precision=lax.Precision.HIGH,
                          preferred_element_type=jnp.float32)
     partial = partial.reshape(n_grp, obs_dev, n_lag, ang_dev, width)
     partial = partial.transpose(0, 2, 1, 3, 4).reshape(n_grp * n_lag, obs_dev, ang_dev, width)

time: 142 us -> 140 us (0.986)
  matrix products: 21.4 us -> 19.9 us
    dot_general x1, matrix products: 7.72 us -> 6.16 us  [body(): jnp.einsum('kg,kao->gao', onehot, terms, precision=lax.Precision.HIGH, pr...]
where the time goes in v6:
time: 140 us
  waiting for transfers between devices  74.2 us (53%)
  blocking collectives  21.4 us (15%)
  matrix products  19.9 us (14%)
  between operations  14.1 us (10%)
  local copies, waits for them, and re-layouts  7.22 us (5%)
  other arithmetic  3.02 us (2%)
    all_gather x1, waiting for transfers between devices, body(): gathered = lax.all_gather(hist16, 'grp', axis=1, tiled=True)  74.2 us
    all_to_all x1, blocking collectives, body(): received = lax.all_to_all(partial, ('grp', 'lag'), 0, 0, tiled=True)  21.4 us
    dot_general x1, matrix products, body(): jnp.einsum('kas,kos->kao', picked, tiles, preferred_element_type=jnp.floa...  13 us
    gather x1, local copies, waits for them, and re-layouts, body(): picked = flat[tile_lag * source_count + tile_src]  6.53 us
    dot_general x1, matrix products, body(): jnp.einsum('kg,kao->gao', onehot, terms, precision=lax.Precision.HIGH, pr...  6.16 us
  transfers between devices with their start and end apart: 1, of which 1 were waited for; matrix products, arithmetic and copies ran while one was open for 1% of the time, Pallas kernels for 0%

profile of v6, /device:TPU:1, one launch (start us, length us, event | category | flops | bytes accessed | tf_op | source)
XLA Modules:
  0.0 139.9 jit_solution(7365229820921487209)
XLA Ops:
  7.2 0.0 copy-start
  7.2 0.0 all-gather.2.cloned.1.call-start
  7.2 2.2 %convert_element_type.7 = bf16[2,32,32,128]{3,2,1,0:T(8,128)(2,1)} convert(f32[2,32,32,128]{3,2,1,0:T(8,128)} %param.7) | non-fusion elementwise | flops 262144 | bytes 1572864 | tf_op jit(solution)/shard_map/convert_element_type | solution.py:12
  9.4 0.0 all-gather.2.cloned.1.call-update
  9.4 0.7 compare_select_fusion
  10.1 74.2 %all-gather.2.cloned.1.call-done = bf16[2,512,32,128]{3,2,1,0:T(8,128)(2,1)} async-done(((bf16[2,32,32,128]{3,2,1,0:T(8,128)(2,1)}), bf16[2,512,32,128]{3,2,1,0:T(8,128)(2,1)}) %all-gather.2.cloned.1.call-update) | async-done | bytes 8388624 | tf_op jit(solution)/shard_map/all_gather | solution.py:13
  84.3 6.5 %gather_fusion = bf16[512,32,128]{2,1,0:T(8,128)(2,1)} fusion(bf16[1024,32,128]{2,1,0:T(8,128)(2,1)} %bitcast.13, s32[1024]{0:T(1024)S(1)} %pad_clamp_fusion), kind=kCustom, calls=%fused_computation | custom fusion | bytes 8390656 | tf_op jit(solution)/shard_map/gather | solution.py:17
  90.9 0.0 copy-start.3
  90.9 13.0 %fusion.6 = f32[512,32,128]{2,1,0:T(8,128)S(1)} fusion(bf16[512,32,128]{2,1,0:T(8,128)(2,1)} %gather_fusion, bf16[512,128,128]{2,1,0:T(8,128)(2,1)} %param.8), kind=kOutput, calls=%fused_computation.11 | convolution fusion | flops 536870912 | bytes 29360128 | tf_op jit(solution)/shard_map/kas,kos->kao/dot_general | solution.py:18
  103.8 0.0 copy-done.3
  103.8 0.0 copy-start.2
  103.9 6.2 %fusion = f32[32,32,128]{2,0,1:T(8,128)S(1)} fusion(f32[512,32,128]{2,1,0:T(8,128)S(1)} %fusion.6, s32[512]{0:T(512)S(1)} %copy-done.3), kind=kOutput, calls=%fused_computation.1 | convolution fusion | flops 402669568 | bytes 8914944 | tf_op jit(solution)/shard_map/kg,kao->gao/dot_general | solution.py:20
  110.0 0.3 copy.16
  110.4 0.3 copy.12
  110.7 21.4 %all_to_all.5 = f32[128,2,4,128]{3,2,1,0:T(4,128)S(1)} all-to-all(f32[128,2,4,128]{3,2,1,0:T(4,128)S(1)} %copy.12), channel_id=1, replica_groups=mesh['grp'=16,'lag'=8] {'grp','lag'}, dimensions={0} | all-to-all | bytes 1048576 | tf_op jit(solution)/shard_map/all_to_all | solution.py:24
  132.1 0.1 reduce_sum.9
  132.2 0.0 copy-done
  132.2 0.0 copy-done.2
  132.3 0.0 copy-start.1
  132.3 0.7 fusion.5
  133.0 0.0 copy-done.1
  (1 shorter events, 0.0 us)
Async XLA Ops:
  7.2 125.1 %copy-start = (bf16[2,128,128]{2,1,0:T(8,128)(2,1)S(1)}, bf16[2,128,128]{2,1,0:T(8,128)(2,1)}, u32[]{:S(2)}) copy-start(bf16[2,128,128]{2,1,0:T(8,128)(2,1)} %param.13) | copy-start | bytes 196612
  7.2 77.2 %all-gather.2.cloned.1.call-start = ((), (), s32[]{:S(2)}) async-start(), calls=%async_computation.1 | async-start | bytes 8912896 | tf_op jit(solution)/shard_map/all_gather | solution.py:13
  90.9 13.0 %copy-start.3 = (s32[512]{0:T(512)S(1)}, s32[512]{0:T(512)}, u32[]{:S(2)}) copy-start(s32[512]{0:T(512)} %param.10) | copy-start | bytes 6148
  103.8 28.4 %copy-start.2 = (f32[2,4,128]{2,1,0:T(4,128)S(1)}, f32[2,4,128]{2,1,0:T(4,128)}, u32[]{:S(2)}) copy-start(f32[2,4,128]{2,1,0:T(4,128)} %param.12) | copy-start | bytes 12292
  132.3 0.8 copy-start.1
Sparse Core Ops, SparseCore 0:
  10.2 74.0 all-gather.1

commit v7 on v6

--- a/solution.py
+++ b/solution.py
@@ -1,7 +1,76 @@
 import jax
 import jax.numpy as jnp
 from jax import lax
+from jax.experimental import pallas as pl
+from jax.experimental.pallas import tpu as pltpu
 from jax.sharding import PartitionSpec as P
+
+BLOCK = 32
+
+
+def field_kernel(index_ref, obs_ref, table_ref, tiles_ref, out_ref, rows, acc, sems):
+    step = pl.program_id(0)
+    steps = pl.num_programs(0)
+    block = tiles_ref.shape[0]
+
+    def fetch(which, slot):
+        for t in range(block):
+            pltpu.make_async_copy(table_ref.at[index_ref[which * block + t]], rows.at[slot, t], sems.at[slot]).start()
+
+    def wait(slot):
+        for t in range(block):
+            pltpu.make_async_copy(table_ref.at[0], rows.at[slot, t], sems.at[slot]).wait()
+
+    slot = step % 2
+
+    @pl.when(step == 0)
+    def _():
+        acc[...] = jnp.zeros_like(acc)
+        fetch(0, 0)
+
+    wait(slot)
+
+    @pl.when(step + 1 < steps)
+    def _():
+        fetch(step + 1, 1 - slot)
+
+    def one(t, carry):
+        term = lax.dot_general(rows[slot, t], tiles_ref[t], (((1,), (1,)), ((), ())),
+                               preferred_element_type=jnp.float32)
+        o = obs_ref[step * block + t]
+        acc[o] = acc[o] + term
+        return carry
+
+    lax.fori_loop(0, block, one, 0, unroll=8)
+
+    @pl.when(step == steps - 1)
+    def _():
+        out_ref[...] = acc[: out_ref.shape[0]]
+
+
+def field_partial(table, tile_index, tile_obs, tiles, observers):
+    count, angles, width = table.shape
+    n_tiles = tiles.shape[0]
+    grid_spec = pltpu.PrefetchScalarGridSpec(
+        num_scalar_prefetch=2,
+        grid=(n_tiles // BLOCK,),
+        in_specs=[
+            pl.BlockSpec(memory_space=pl.ANY),
+            pl.BlockSpec((BLOCK,) + tiles.shape[1:], lambda i, *_: (i, 0, 0)),
+        ],
+        out_specs=pl.BlockSpec((observers, angles, width), lambda i, *_: (0, 0, 0)),
+        scratch_shapes=[
+            pltpu.VMEM((2, BLOCK, angles, width), table.dtype),
+            pltpu.VMEM((observers + 1, angles, width), jnp.float32),
+            pltpu.SemaphoreType.DMA((2,)),
+        ],
+    )
+    return pl.pallas_call(
+        field_kernel,
+        grid_spec=grid_spec,
+        out_shape=jax.ShapeDtypeStruct((observers, angles, width), jnp.float32),
+        compiler_params=pltpu.CompilerParams(dimension_semantics=("arbitrary",)),
+    )(tile_index, tile_obs, table, tiles)
 
 
 def body(history, tiles, tile_src, tile_obs, tile_lag, incident, near_inverse):
@@ -14,11 +83,8 @@
     lag_count = gathered.shape[0]
     source_count = gathered.shape[1]
     flat = gathered.reshape(lag_count * source_count, gathered.shape[2], gathered.shape[3])
-    picked = flat[tile_lag * source_count + tile_src]
-    terms = jnp.einsum("kas,kos->kao", picked, tiles, preferred_element_type=jnp.float32)
-    onehot = (tile_obs[:, None] == jnp.arange(observers, dtype=tile_obs.dtype)[None, :]).astype(jnp.float32)
-    partial = jnp.einsum("kg,kao->gao", onehot, terms, precision=lax.Precision.HIGH,
-                         preferred_element_type=jnp.float32)
+    tile_index = tile_lag * source_count + tile_src
+    partial = field_partial(flat, tile_index, tile_obs, tiles, observers)
     partial = partial.reshape(n_grp, obs_dev, n_lag, ang_dev, width)
     partial = partial.transpose(0, 2, 1, 3, 4).reshape(n_grp * n_lag, obs_dev, ang_dev, width)
     received = lax.all_to_all(partial, ("grp", "lag"), 0, 0, tiled=True)

time: 140 us -> 138 us (0.986)
  Pallas kernels: 0 us -> 22.2 us
  matrix products: 19.9 us -> 0.74 us
  local copies, waits for them, and re-layouts: 7.22 us -> 1.44 us
    pallas_call x0 -> x1, Pallas kernels: none -> 22.2 us  [field_partial(): pl.pallas_call(field_kernel, grid_spec=grid_spec, out_shape=jax.ShapeDtyp...]
    dot_general x2 -> x0, matrix products: 19.1 us -> none  [the longest x1 13 us: body(): jnp.einsum('kas,kos->kao', picked, tiles, preferred_element_type=jnp.floa...]
    gather x1 -> x0, local copies, waits for them, and re-layouts: 6.53 us -> none  [body(): picked = flat[tile_lag * source_count + tile_src]]
where the time goes in v7:
time: 138 us; the launch traced here: 137 us
  waiting for transfers between devices  73.7 us (53%)
  Pallas kernels  22.2 us (16%)
  blocking collectives  21.4 us (16%)
  between operations  14.1 us (10%)
  other arithmetic  3.58 us (3%)
  local copies, waits for them, and re-layouts  1.44 us (1%)
    all_gather x1, waiting for transfers between devices, body(): gathered = lax.all_gather(hist16, 'grp', axis=1, tiled=True)  73.7 us
    pallas_call x1, Pallas kernels, field_partial(): pl.pallas_call(field_kernel, grid_spec=grid_spec, out_shape=jax.ShapeDtyp...  22.2 us
    all_to_all x1, blocking collectives, body(): received = lax.all_to_all(partial, ('grp', 'lag'), 0, 0, tiled=True)  21.4 us
  transfers between devices with their start and end apart: 1, of which 1 were waited for; matrix products, arithmetic and copies ran while one was open for 1% of the time, Pallas kernels for 0%

profile of v7, /device:TPU:1, one launch (start us, length us, event | category | flops | bytes accessed | tf_op | source)
XLA Modules:
  0.0 137.1 jit_solution(1955329440009007138)
XLA Ops:
  7.2 0.0 copy-start
  7.2 0.0 copy-start.2
  7.2 0.0 all-gather.2.cloned.1.call-start
  7.2 2.1 %convert_element_type.6 = bf16[2,32,32,128]{3,2,1,0:T(8,128)(2,1)} convert(f32[2,32,32,128]{3,2,1,0:T(8,128)} %param.7) | non-fusion elementwise | flops 262144 | bytes 1572864 | tf_op jit(solution)/shard_map/convert_element_type | solution.py:81
  9.4 0.0 all-gather.2.cloned.1.call-update
  9.4 1.3 multiply_add_fusion.index_ref
  10.7 73.7 %all-gather.2.cloned.1.call-done = bf16[2,512,32,128]{3,2,1,0:T(8,128)(2,1)} async-done(((bf16[2,32,32,128]{3,2,1,0:T(8,128)(2,1)}), bf16[2,512,32,128]{3,2,1,0:T(8,128)(2,1)}) %all-gather.2.cloned.1.call-update) | async-done | bytes 8388624 | tf_op jit(solution)/shard_map/all_gather | solution.py:82
  84.3 22.2 %shard_map.86 = f32[32,32,128]{2,1,0:T(8,128)} custom-call(s32[512]{0:T(512)} %multiply_add_fusion.index_ref, s32[512]{0:T(512)} %obs_ref.1, bf16[1024,32,128]{2,1,0:T(8,128)(2,1)} %bitcast.8, bf16[512,128,128]{2,1,0:T(8,128)(2,1)} %tiles_ref.1), custom_call_target="tpu_custom_call" | custom-call | tf_op jit(solution)/shard_map/pallas_call | solution.py:68
  106.5 1.1 copy.13
  107.6 0.3 copy.11
  107.9 21.4 %all_to_all.5 = f32[128,2,4,128]{3,2,1,0:T(4,128)S(1)} all-to-all(f32[128,2,4,128]{3,2,1,0:T(4,128)S(1)} %copy.11), channel_id=1, replica_groups=mesh['grp'=16,'lag'=8] {'grp','lag'}, dimensions={0} | all-to-all | bytes 1048576 | tf_op jit(solution)/shard_map/all_to_all | solution.py:90
  129.3 0.1 reduce_sum.9
  129.5 0.0 copy-done
  129.5 0.0 copy-done.2
  129.5 0.0 copy-start.1
  129.5 0.7 fusion
  130.3 0.0 copy-done.1
Async XLA Ops:
  7.2 122.3 %copy-start = (bf16[2,128,128]{2,1,0:T(8,128)(2,1)S(1)}, bf16[2,128,128]{2,1,0:T(8,128)(2,1)}, u32[]{:S(2)}) copy-start(bf16[2,128,128]{2,1,0:T(8,128)(2,1)} %param.13) | copy-start | bytes 196612
  7.2 122.3 %copy-start.2 = (f32[2,4,128]{2,1,0:T(4,128)S(1)}, f32[2,4,128]{2,1,0:T(4,128)}, u32[]{:S(2)}) copy-start(f32[2,4,128]{2,1,0:T(4,128)} %param.12) | copy-start | bytes 12292
  7.2 77.2 %all-gather.2.cloned.1.call-start = ((), (), s32[]{:S(2)}) async-start(), calls=%async_computation.1 | async-start | bytes 8912896 | tf_op jit(solution)/shard_map/all_gather | solution.py:82
  129.5 0.8 copy-start.1
Sparse Core Ops, SparseCore 0:
  10.2 74.0 all-gather.1

commit v8 on v7

--- a/solution.py
+++ b/solution.py
@@ -5,7 +5,7 @@
 from jax.experimental.pallas import tpu as pltpu
 from jax.sharding import PartitionSpec as P
 
-BLOCK = 32
+BLOCK = 128
 
 
 def field_kernel(index_ref, obs_ref, table_ref, tiles_ref, out_ref, rows, acc, sems):
@@ -41,7 +41,7 @@
         acc[o] = acc[o] + term
         return carry
 
-    lax.fori_loop(0, block, one, 0, unroll=8)
+    lax.fori_loop(0, block, one, 0, unroll=32)
 
     @pl.when(step == steps - 1)
     def _():
@@ -79,11 +79,10 @@
     obs_dev, ang_dev, width = incident.shape
     observers = obs_dev * n_grp
     hist16 = history.astype(jnp.bfloat16)
-    gathered = lax.all_gather(hist16, "grp", axis=1, tiled=True)
-    lag_count = gathered.shape[0]
-    source_count = gathered.shape[1]
-    flat = gathered.reshape(lag_count * source_count, gathered.shape[2], gathered.shape[3])
-    tile_index = tile_lag * source_count + tile_src
+    lag_count, src_dev, angles, _ = hist16.shape
+    flat = lax.all_gather(hist16.reshape(lag_count * src_dev, angles, width), "grp", axis=0, tiled=True)
+    owner = tile_src // src_dev
+    tile_index = (owner * lag_count + tile_lag) * src_dev + tile_src % src_dev
     partial = field_partial(flat, tile_index, tile_obs, tiles, observers)
     partial = partial.reshape(n_grp, obs_dev, n_lag, ang_dev, width)
     partial = partial.transpose(0, 2, 1, 3, 4).reshape(n_grp * n_lag, obs_dev, ang_dev, width)

time: 138 us -> 132 us (0.957)
  Pallas kernels: 22.2 us -> 17 us
    pallas_call x1, Pallas kernels: 22.2 us -> 17 us  [field_partial(): pl.pallas_call(field_kernel, grid_spec=grid_spec, out_shape=jax.ShapeDtyp...]
where the time goes in v8:
time: 132 us
  waiting for transfers between devices  73.6 us (56%)
  blocking collectives  21.4 us (16%)
  Pallas kernels  17 us (13%)
  between operations  14.1 us (11%)
  other arithmetic  3.59 us (3%)
  local copies, waits for them, and re-layouts  1.44 us (1%)
    all_gather x1, waiting for transfers between devices, body(): lax.all_gather(hist16.reshape(lag_count * src_dev, angles, width), 'grp',...  73.6 us
    all_to_all x1, blocking collectives, body(): received = lax.all_to_all(partial, ('grp', 'lag'), 0, 0, tiled=True)  21.4 us
    pallas_call x1, Pallas kernels, field_partial(): pl.pallas_call(field_kernel, grid_spec=grid_spec, out_shape=jax.ShapeDtyp...  17 us
  transfers between devices with their start and end apart: 1, of which 1 were waited for; matrix products, arithmetic and copies ran while one was open for 1% of the time, Pallas kernels for 0%

profile of v8, /device:TPU:1, one launch (start us, length us, event | category | flops | bytes accessed | tf_op | source)
XLA Modules:
  0.0 131.8 jit_solution(5693769173871313649)
XLA Ops:
  7.2 0.0 copy-start
  7.2 0.0 copy-start.2
  7.2 0.0 all-gather.2.cloned.1.call-start
  7.2 2.1 %convert_element_type.6 = bf16[2,32,32,128]{3,2,1,0:T(8,128)(2,1)} convert(f32[2,32,32,128]{3,2,1,0:T(8,128)} %param.7) | non-fusion elementwise | flops 262144 | bytes 1572864 | tf_op jit(solution)/shard_map/convert_element_type | solution.py:81
  9.4 0.0 all-gather.2.cloned.1.call-update
  9.4 1.3 fusion.3.index_ref
  10.7 73.6 %all-gather.2.cloned.1.call-done.table_ref = bf16[1024,32,128]{2,1,0:T(8,128)(2,1)} async-done(((bf16[64,32,128]{2,1,0:T(8,128)(2,1)}), bf16[1024,32,128]{2,1,0:T(8,128)(2,1)}) %all-gather.2.cloned.1.call-update) | async-done | bytes 8388624 | tf_op jit(solution)/shard_map/all_gather | solution.py:83
  84.3 17.0 %shard_map.86 = f32[32,32,128]{2,1,0:T(8,128)} custom-call(s32[512]{0:T(512)} %fusion.3.index_ref, s32[512]{0:T(512)} %obs_ref.1, bf16[1024,32,128]{2,1,0:T(8,128)(2,1)} %all-gather.2.cloned.1.call-done.table_ref, bf16[512,128,128]{2,1,0:T(8,128)(2,1)} %tiles_ref.1), custom_call_target="tpu_custom_call" | custom-call | tf_op jit(solution)/shard_map/pallas_call | solution.py:68
  101.3 1.1 copy.13
  102.3 0.3 copy.11
  102.7 21.4 %all_to_all.5 = f32[128,2,4,128]{3,2,1,0:T(4,128)S(1)} all-to-all(f32[128,2,4,128]{3,2,1,0:T(4,128)S(1)} %copy.11), channel_id=1, replica_groups=mesh['grp'=16,'lag'=8] {'grp','lag'}, dimensions={0} | all-to-all | bytes 1048576 | tf_op jit(solution)/shard_map/all_to_all | solution.py:89
  124.1 0.1 reduce_sum.9
  124.2 0.0 copy-done
  124.2 0.0 copy-done.2
  124.2 0.0 copy-start.1
  124.3 0.7 fusion.4
  125.0 0.0 copy-done.1
Async XLA Ops:
  7.2 117.1 %copy-start = (bf16[2,128,128]{2,1,0:T(8,128)(2,1)S(1)}, bf16[2,128,128]{2,1,0:T(8,128)(2,1)}, u32[]{:S(2)}) copy-start(bf16[2,128,128]{2,1,0:T(8,128)(2,1)} %param.13) | copy-start | bytes 196612
  7.2 117.1 %copy-start.2 = (f32[2,4,128]{2,1,0:T(4,128)S(1)}, f32[2,4,128]{2,1,0:T(4,128)}, u32[]{:S(2)}) copy-start(f32[2,4,128]{2,1,0:T(4,128)} %param.12) | copy-start | bytes 12292
  7.2 77.1 %all-gather.2.cloned.1.call-start = ((), (), s32[]{:S(2)}) async-start(), calls=%async_computation.1 | async-start | bytes 8912896 | tf_op jit(solution)/shard_map/all_gather | solution.py:83
  124.2 0.8 copy-start.1
Sparse Core Ops, SparseCore 0:
  10.2 74.0 all-gather.1

commit v9 on v8

--- a/solution.py
+++ b/solution.py
@@ -8,18 +8,34 @@
 BLOCK = 128
 
 
-def field_kernel(index_ref, obs_ref, table_ref, tiles_ref, out_ref, rows, acc, sems):
+def field_kernel(index_ref, lag_ref, obs_ref, table_ref, other_ref, tiles_ref, out_ref, rows, acc, sems):
     step = pl.program_id(0)
     steps = pl.num_programs(0)
     block = tiles_ref.shape[0]
 
     def fetch(which, slot):
-        for t in range(block):
-            pltpu.make_async_copy(table_ref.at[index_ref[which * block + t]], rows.at[slot, t], sems.at[slot]).start()
+        def issue(t, carry):
+            r = which * block + t
+            i = index_ref[r]
+
+            @pl.when(lag_ref[r] == 0)
+            def _():
+                pltpu.make_async_copy(table_ref.at[i], rows.at[slot, t], sems.at[slot]).start()
+
+            @pl.when(lag_ref[r] != 0)
+            def _():
+                pltpu.make_async_copy(other_ref.at[i], rows.at[slot, t], sems.at[slot]).start()
+
+            return carry
+
+        lax.fori_loop(0, block, issue, 0, unroll=8)
 
     def wait(slot):
-        for t in range(block):
+        def one_wait(t, carry):
             pltpu.make_async_copy(table_ref.at[0], rows.at[slot, t], sems.at[slot]).wait()
+            return carry
+
+        lax.fori_loop(0, block, one_wait, 0, unroll=8)
 
     slot = step % 2
 
@@ -48,13 +64,14 @@
         out_ref[...] = acc[: out_ref.shape[0]]
 
 
-def field_partial(table, tile_index, tile_obs, tiles, observers):
+def field_partial(table, other, tile_index, tile_lag, tile_obs, tiles, observers):
     count, angles, width = table.shape
     n_tiles = tiles.shape[0]
     grid_spec = pltpu.PrefetchScalarGridSpec(
-        num_scalar_prefetch=2,
+        num_scalar_prefetch=3,
         grid=(n_tiles // BLOCK,),
         in_specs=[
+            pl.BlockSpec(memory_space=pl.ANY),
             pl.BlockSpec(memory_space=pl.ANY),
             pl.BlockSpec((BLOCK,) + tiles.shape[1:], lambda i, *_: (i, 0, 0)),
         ],
@@ -70,7 +87,32 @@
         grid_spec=grid_spec,
         out_shape=jax.ShapeDtypeStruct((observers, angles, width), jnp.float32),
         compiler_params=pltpu.CompilerParams(dimension_semantics=("arbitrary",)),
-    )(tile_index, tile_obs, table, tiles)
+    )(tile_index, tile_lag, tile_obs, table, other, tiles)
+
+
+def shift_pairs(rows, cols, step, along_cols):
+    pairs = []
+    for a in range(rows):
+        for b in range(cols):
+            if along_cols:
+                pairs.append((a * cols + b, a * cols + (b + step) % cols))
+            else:
+                pairs.append((a * cols + b, ((a + step) % rows) * cols + b))
+    return pairs
+
+
+def ring_gather(x, rows, cols, along_cols):
+    n = cols if along_cols else rows
+    plus = shift_pairs(rows, cols, 1, along_cols)
+    minus = shift_pairs(rows, cols, -1, along_cols)
+    from_behind = lax.ppermute(x, "grp", plus)
+    from_ahead = lax.ppermute(x, "grp", minus)
+    assert n == 4
+    half = x.shape[0] // 2
+    far_a = lax.ppermute(from_behind[:half], "grp", plus)
+    far_b = lax.ppermute(from_ahead[half:], "grp", minus)
+    far = jnp.concatenate([far_a, far_b], axis=0)
+    return jnp.stack([x, from_ahead, far, from_behind])
 
 
 def body(history, tiles, tile_src, tile_obs, tile_lag, incident, near_inverse):
@@ -80,10 +122,19 @@
     observers = obs_dev * n_grp
     hist16 = history.astype(jnp.bfloat16)
     lag_count, src_dev, angles, _ = hist16.shape
-    flat = lax.all_gather(hist16.reshape(lag_count * src_dev, angles, width), "grp", axis=0, tiled=True)
+    rows = 4
+    cols = n_grp // rows
+    assert lag_count == 2 and rows * cols == n_grp
+    table = lax.all_gather(hist16[0], "grp", axis=0, tiled=True)
+    other = ring_gather(ring_gather(hist16[1], rows, cols, True), rows, cols, False)
+    other = other.reshape(n_grp * src_dev, angles, width)
+    me = lax.axis_index("grp")
     owner = tile_src // src_dev
-    tile_index = (owner * lag_count + tile_lag) * src_dev + tile_src % src_dev
-    partial = field_partial(flat, tile_index, tile_obs, tiles, observers)
+    dy = (owner // cols - me // cols + rows) % rows
+    dz = (owner % cols - me % cols + cols) % cols
+    other_index = (dy * cols + dz) * src_dev + tile_src % src_dev
+    tile_index = jnp.where(tile_lag == 0, tile_src, other_index)
+    partial = field_partial(table, other, tile_index, tile_lag, tile_obs, tiles, observers)
     partial = partial.reshape(n_grp, obs_dev, n_lag, ang_dev, width)
     partial = partial.transpose(0, 2, 1, 3, 4).reshape(n_grp * n_lag, obs_dev, ang_dev, width)
     received = lax.all_to_all(partial, ("grp", "lag"), 0, 0, tiled=True)

time: 132 us -> 139 us (1.053)
  waiting for transfers between devices: 73.6 us -> 55.2 us
  starting transfers between devices: 0.04 us -> 14.4 us
  local copies, waits for them, and re-layouts: 1.44 us -> 8.24 us
  blocking collectives: 21.4 us -> 24.5 us
  Pallas kernels: 17 us -> 18.4 us
    all_gather x1, waiting for transfers between devices: 73.6 us -> 0.01 us  [body(): table = lax.all_gather(hist16[0], 'grp', axis=0, tiled=True)]
    ppermute x0 -> x8, waiting for transfers between devices: none -> 55.2 us  [the longest x2 34.2 us: ring_gather(): from_behind = lax.ppermute(x, 'grp', plus)]
    ppermute x0 -> x8, starting transfers between devices: none -> 14.4 us  [the longest x2 6.24 us: ring_gather(): far_b = lax.ppermute(from_ahead[half:], 'grp', minus)]
    slice x0 -> x5, local copies, waits for them, and re-layouts: none -> 3.79 us  [the longest x1 2.04 us: body(): hist16[1]]
    all_to_all x1, blocking collectives: 21.4 us -> 24.5 us  [body(): received = lax.all_to_all(partial, ('grp', 'lag'), 0, 0, tiled=True)]
    another operation x0 -> x1, local copies, waits for them, and re-layouts: none -> 3 us  [ring_gather(): return jnp.stack([x, from_ahead, far, from_behind])]
    convert_element_type x1 -> x0, other arithmetic: 2.15 us -> none  [body(): hist16 = history.astype(jnp.bfloat16)]
    another operation x0 -> x4, other arithmetic: none -> 2.04 us  [ring_gather(): return jnp.stack([x, from_ahead, far, from_behind])]
  transfers between devices with their start and end apart: 1 -> 9, of which waited for: 1 -> 6; matrix products, arithmetic and copies ran while one was open for 1% -> 5% of each run, Pallas kernels for 0% -> 0%
where the time goes in v9:
time: 139 us; the launch traced here: 138 us
  waiting for transfers between devices  55.2 us (40%)
  blocking collectives  24.5 us (18%)
  Pallas kernels  18.4 us (13%)
  starting transfers between devices  14.4 us (10%)
  between operations  14.1 us (10%)
  local copies, waits for them, and re-layouts  8.24 us (6%)
  other arithmetic  2.8 us (2%)
    ppermute x2, waiting for transfers between devices, ring_gather(): from_behind = lax.ppermute(x, 'grp', plus)  34.2 us
    all_to_all x1, blocking collectives, body(): received = lax.all_to_all(partial, ('grp', 'lag'), 0, 0, tiled=True)  24.5 us
    ppermute x2, waiting for transfers between devices, ring_gather(): far_a = lax.ppermute(from_behind[:half], 'grp', plus)  19.3 us
    pallas_call x1, Pallas kernels, field_partial(): pl.pallas_call(field_kernel, grid_spec=grid_spec, out_shape=jax.ShapeDtyp...  18.4 us
    ppermute x2, starting transfers between devices, ring_gather(): far_b = lax.ppermute(from_ahead[half:], 'grp', minus)  6.24 us
    ppermute x2, starting transfers between devices, ring_gather(): from_ahead = lax.ppermute(x, 'grp', minus)  4.54 us
    ppermute x2, starting transfers between devices, ring_gather(): from_behind = lax.ppermute(x, 'grp', plus)  3.51 us
    another operation x1, local copies, waits for them, and re-layouts, ring_gather(): return jnp.stack([x, from_ahead, far, from_behind])  3 us
  transfers between devices with their start and end apart: 9, of which 6 were waited for; matrix products, arithmetic and copies ran while one was open for 5% of the time, Pallas kernels for 0%

profile of v9, /device:TPU:1, one launch (start us, length us, event | category | flops | bytes accessed | tf_op | source)
XLA Modules:
  0.0 138.5 jit_solution(427805940806690555)
XLA Ops:
  7.2 0.0 copy-start
  7.2 0.0 copy-start.2
  7.2 0.0 copy-start.4
  7.2 0.0 all-gather.3.cloned.1.call-start
  7.2 2.0 %fusion.15 = (bf16[1,32,32,128]{3,2,0,1:T(8,128)(2,1)S(1)}, bf16[32,32,128]{2,1,0:T(8,128)(2,1)S(1)}, bf16[1,32,32,128]{3,2,0,1:T(8,128)(2,1)}) fusion(f32[2,32,32,128]{3,2,1,0:T(8,128)} %param.7), kind=kLoop, calls=%fused_computation.41 | loop fusion | bytes 1310720 | tf_op jit(solution)/shard_map/slice | solution.py:129
  9.3 0.0 all-gather.3.cloned.1.call-update
  9.3 2.5 %collective-permute-start.1 = (bf16[32,32,128]{2,1,0:T(8,128)(2,1)S(1)}, bf16[32,32,128]{2,1,0:T(8,128)(2,1)S(1)}, u32[]{:S(2)}, u32[]{:S(2)}) collective-permute-start(bf16[32,32,128]{2,1,0:T(8,128)(2,1)S(1)} %get-tuple-element.5), channel_id=1, source_target_pairs={{0,8},{8,16},{16,24},{24,0},{32,40},{40,48},{48,56},{56,32},{64,72... | collective-permute-start | bytes 786440 | tf_op jit(solution)/shard_map/ppermute | solution.py:108
  11.8 2.2 %collective-permute-start = (bf16[32,32,128]{2,1,0:T(8,128)(2,1)S(1)}, bf16[32,32,128]{2,1,0:T(8,128)(2,1)S(1)}, u32[]{:S(2)}, u32[]{:S(2)}) collective-permute-start(bf16[32,32,128]{2,1,0:T(8,128)(2,1)S(1)} %get-tuple-element.5), channel_id=1, source_target_pairs={{0,24},{8,0},{16,8},{24,16},{32,56},{40,32},{48,40},{56,48},{64,88... | collective-permute-start | bytes 786440 | tf_op jit(solution)/shard_map/ppermute | solution.py:109
  14.1 6.0 %collective-permute-done.1 = bf16[32,32,128]{2,1,0:T(8,128)(2,1)S(1)} collective-permute-done((bf16[32,32,128]{2,1,0:T(8,128)(2,1)S(1)}, bf16[32,32,128]{2,1,0:T(8,128)(2,1)S(1)}, u32[]{:S(2)}, u32[]{:S(2)}) %collective-permute-start.1) | collective-permute-done | bytes 262176 | tf_op jit(solution)/shard_map/ppermute | solution.py:108
  20.0 0.1 collective-permute-start.2
  20.1 0.0 collective-permute-done
  20.1 2.7 %collective-permute-start.3 = (bf16[16,32,128]{2,1,0:T(8,128)(2,1)S(1)}, bf16[16,32,128]{2,1,0:T(8,128)(2,1)S(1)}, u32[]{:S(2)}, u32[]{:S(2)}) collective-permute-start(bf16[16,32,128]{2,1,0:T(8,128)(2,1)S(1)} %slice.27), channel_id=1, source_target_pairs={{0,24},{8,0},{16,8},{24,16},{32,56},{40,32},{48,40},{56,48},{64,88... | collective-permute-start | bytes 393224 | tf_op jit(solution)/shard_map/ppermute | solution.py:113
  22.8 2.3 %collective-permute-done.2 = bf16[16,32,128]{2,1,0:T(8,128)(2,1)S(1)} collective-permute-done((bf16[16,32,128]{2,1,0:T(8,128)(2,1)S(1)}, bf16[16,32,128]{2,1,0:T(8,128)(2,1)S(1)}, u32[]{:S(2)}, u32[]{:S(2)}) %collective-permute-start.2) | collective-permute-done | bytes 131104 | tf_op jit(solution)/shard_map/ppermute | solution.py:112
  25.1 0.4 collective-permute-done.3
  25.5 0.2 fusion.14
  25.7 1.0 collective-permute-start.5
  26.7 2.3 %collective-permute-start.4 = (bf16[4,32,32,128]{3,2,0,1:T(8,128)(2,1)S(1)}, bf16[4,32,32,128]{3,2,0,1:T(8,128)(2,1)S(1)}, u32[]{:S(2)}, u32[]{:S(2)}) collective-permute-start(bf16[4,32,32,128]{3,2,0,1:T(8,128)(2,1)S(1)} %get-tuple-element.3), channel_id=1, source_target_pairs={{0,96},{8,104},{16,112},{24,120},{32,0},{40,8},{48,16},{56,24},{64... | collective-permute-start | bytes 3145736 | tf_op jit(solution)/shard_map/ppermute | solution.py:109
  29.0 28.2 %collective-permute-done.5 = bf16[4,32,32,128]{3,2,0,1:T(8,128)(2,1)S(1)} collective-permute-done((bf16[4,32,32,128]{3,2,0,1:T(8,128)(2,1)S(1)}, bf16[4,32,32,128]{3,2,0,1:T(8,128)(2,1)S(1)}, u32[]{:S(2)}, u32[]{:S(2)}) %collective-permute-start.5) | collective-permute-done | bytes 1048608 | tf_op jit(solution)/shard_map/ppermute | solution.py:108
  57.2 0.9 slice.28
  58.1 0.0 collective-permute-start.6
  58.1 1.3 collective-permute-done.4
  59.4 0.9 slice.29
  60.3 3.5 %collective-permute-start.7 = (bf16[2,32,32,128]{3,2,0,1:T(8,128)(2,1)}, bf16[2,32,32,128]{3,2,0,1:T(8,128)(2,1)}, u32[]{:S(2)}, u32[]{:S(2)}) collective-permute-start(bf16[2,32,32,128]{3,2,0,1:T(8,128)(2,1)} %slice.29), channel_id=1, source_target_pairs={{0,96},{8,104},{16,112},{24,120},{32,0},{40,8},{48,16},{56,24},{64... | collective-permute-start | bytes 1572872 | tf_op jit(solution)/shard_map/ppermute | solution.py:113
  63.8 0.0 copy-done.2
  63.8 0.0 copy-done.4
  63.8 0.6 fusion.7.index_ref
  64.4 17.0 %collective-permute-done.6 = bf16[2,32,32,128]{3,2,0,1:T(8,128)(2,1)} collective-permute-done((bf16[2,32,32,128]{3,2,0,1:T(8,128)(2,1)}, bf16[2,32,32,128]{3,2,0,1:T(8,128)(2,1)}, u32[]{:S(2)}, u32[]{:S(2)}) %collective-permute-start.6) | collective-permute-done | bytes 524320 | tf_op jit(solution)/shard_map/ppermute | solution.py:112
  81.4 0.0 collective-permute-done.7
  81.4 1.3 maximum_bitcast_fusion
  82.7 0.6 pad_maximum_fusion
  83.3 3.0 %copy.13 = bf16[4,4,32,32,128]{4,3,2,1,0:T(8,128)(2,1)} copy(bf16[4,4,32,32,128]{4,3,1,2,0:T(8,128)(2,1)S(1)} %pad_maximum_fusion) | data formatting | bytes 8388608 | tf_op jit(solution)/shard_map/stack | solution.py:115
  86.3 0.0 all-gather.3.cloned.1.call-done
  86.3 0.0 copy-start.3
  86.3 18.4 %shard_map.86 = f32[32,32,128]{2,1,0:T(8,128)} custom-call(s32[512]{0:T(512)} %fusion.7.index_ref, s32[512]{0:T(512)} %lag_ref.1, s32[512]{0:T(512)} %obs_ref.1, bf16[512,32,128]{2,1,0:T(8,128)(2,1)} %bitcast.26, bf16[512,32,128]{2,1,0:T(8,128)(2,1)} %bitcast.25, bf16[512,128,128]{2,1,0:T(8,128)(2,1)} %tiles_ref.1), custom_call_target="tpu_custom_call" | custom-call | tf_op jit(solution)/shard_map/pallas_call | solution.py:85
  104.8 1.1 copy.21
  105.8 0.3 copy.15
  106.2 24.5 %all_to_all.5 = f32[128,2,4,128]{3,2,1,0:T(4,128)S(1)} all-to-all(f32[128,2,4,128]{3,2,1,0:T(4,128)S(1)} %copy.15), channel_id=1, replica_groups=mesh['grp'=16,'lag'=8] {'grp','lag'}, dimensions={0} | all-to-all | bytes 1048576 | tf_op jit(solution)/shard_map/all_to_all | solution.py:140
  130.7 0.1 reduce_sum.9
  130.9 0.0 copy-done
  130.9 0.0 copy-done.3
  130.9 0.0 copy-start.1
  130.9 0.7 fusion.11
  131.6 0.0 copy-done.1
  (3 shorter events, 0.0 us)
Async XLA Ops:
  7.2 123.7 %copy-start = (bf16[2,128,128]{2,1,0:T(8,128)(2,1)S(1)}, bf16[2,128,128]{2,1,0:T(8,128)(2,1)}, u32[]{:S(2)}) copy-start(bf16[2,128,128]{2,1,0:T(8,128)(2,1)} %param.13) | copy-start | bytes 196612
  7.2 56.6 %copy-start.2 = (s32[512]{0:T(512)S(1)}, s32[512]{0:T(512)}, u32[]{:S(2)}) copy-start(s32[512]{0:T(512)} %lag_ref.1) | copy-start | bytes 6148
  7.2 56.6 %copy-start.4 = (s32[512]{0:T(512)S(1)}, s32[512]{0:T(512)}, u32[]{:S(2)}) copy-start(s32[512]{0:T(512)} %param.9) | copy-start | bytes 6148
  7.2 79.1 %all-gather.3.cloned.1.call-start = ((), (), s32[]{:S(2)}) async-start(), calls=%async_computation.1 | async-start | bytes 4456448 | tf_op jit(solution)/shard_map/all_gather | solution.py:128
  9.3 10.7 %collective-permute-start.1 = (bf16[32,32,128]{2,1,0:T(8,128)(2,1)S(1)}, bf16[32,32,128]{2,1,0:T(8,128)(2,1)S(1)}, u32[]{:S(2)}, u32[]{:S(2)}) collective-permute-start(bf16[32,32,128]{2,1,0:T(8,128)(2,1)S(1)} %get-tuple-element.5), channel_id=1, source_target_pairs={{0,8},{8,16},{16,24},{24,0},{32,40},{40,48},{48,56},{56,32},{64,72... | collective-permute-start | bytes 786440 | tf_op jit(solution)/shard_map/ppermute | solution.py:108
  11.8 8.3 %collective-permute-start = (bf16[32,32,128]{2,1,0:T(8,128)(2,1)S(1)}, bf16[32,32,128]{2,1,0:T(8,128)(2,1)S(1)}, u32[]{:S(2)}, u32[]{:S(2)}) collective-permute-start(bf16[32,32,128]{2,1,0:T(8,128)(2,1)S(1)} %get-tuple-element.5), channel_id=1, source_target_pairs={{0,24},{8,0},{16,8},{24,16},{32,56},{40,32},{48,40},{56,48},{64,88... | collective-permute-start | bytes 786440 | tf_op jit(solution)/shard_map/ppermute | solution.py:109
  20.0 5.1 %collective-permute-start.2 = (bf16[16,32,128]{2,1,0:T(8,128)(2,1)S(1)}, bf16[16,32,128]{2,1,0:T(8,128)(2,1)S(1)}, u32[]{:S(2)}, u32[]{:S(2)}) collective-permute-start(bf16[16,32,128]{2,1,0:T(8,128)(2,1)S(1)} %slice.26), channel_id=1, source_target_pairs={{0,8},{8,16},{16,24},{24,0},{32,40},{40,48},{48,56},{56,32},{64,72... | collective-permute-start | bytes 393224 | tf_op jit(solution)/shard_map/ppermute | solution.py:112
  20.1 5.4 %collective-permute-start.3 = (bf16[16,32,128]{2,1,0:T(8,128)(2,1)S(1)}, bf16[16,32,128]{2,1,0:T(8,128)(2,1)S(1)}, u32[]{:S(2)}, u32[]{:S(2)}) collective-permute-start(bf16[16,32,128]{2,1,0:T(8,128)(2,1)S(1)} %slice.27), channel_id=1, source_target_pairs={{0,24},{8,0},{16,8},{24,16},{32,56},{40,32},{48,40},{56,48},{64,88... | collective-permute-start | bytes 393224 | tf_op jit(solution)/shard_map/ppermute | solution.py:113
  25.7 31.5 %collective-permute-start.5 = (bf16[4,32,32,128]{3,2,0,1:T(8,128)(2,1)S(1)}, bf16[4,32,32,128]{3,2,0,1:T(8,128)(2,1)S(1)}, u32[]{:S(2)}, u32[]{:S(2)}) collective-permute-start(bf16[4,32,32,128]{3,2,0,1:T(8,128)(2,1)S(1)} %get-tuple-element.3), channel_id=1, source_target_pairs={{0,32},{8,40},{16,48},{24,56},{32,64},{40,72},{48,80},{56,88},{64,... | collective-permute-start | bytes 3145736 | tf_op jit(solution)/shard_map/ppermute | solution.py:108
  26.7 32.8 %collective-permute-start.4 = (bf16[4,32,32,128]{3,2,0,1:T(8,128)(2,1)S(1)}, bf16[4,32,32,128]{3,2,0,1:T(8,128)(2,1)S(1)}, u32[]{:S(2)}, u32[]{:S(2)}) collective-permute-start(bf16[4,32,32,128]{3,2,0,1:T(8,128)(2,1)S(1)} %get-tuple-element.3), channel_id=1, source_target_pairs={{0,96},{8,104},{16,112},{24,120},{32,0},{40,8},{48,16},{56,24},{64... | collective-permute-start | bytes 3145736 | tf_op jit(solution)/shard_map/ppermute | solution.py:109
  58.1 23.3 %collective-permute-start.6 = (bf16[2,32,32,128]{3,2,0,1:T(8,128)(2,1)}, bf16[2,32,32,128]{3,2,0,1:T(8,128)(2,1)}, u32[]{:S(2)}, u32[]{:S(2)}) collective-permute-start(bf16[2,32,32,128]{3,2,0,1:T(8,128)(2,1)} %slice.28), channel_id=1, source_target_pairs={{0,32},{8,40},{16,48},{24,56},{32,64},{40,72},{48,80},{56,88},{64,... | collective-permute-start | bytes 1572872 | tf_op jit(solution)/shard_map/ppermute | solution.py:112
  60.3 21.2 %collective-permute-start.7 = (bf16[2,32,32,128]{3,2,0,1:T(8,128)(2,1)}, bf16[2,32,32,128]{3,2,0,1:T(8,128)(2,1)}, u32[]{:S(2)}, u32[]{:S(2)}) collective-permute-start(bf16[2,32,32,128]{3,2,0,1:T(8,128)(2,1)} %slice.29), channel_id=1, source_target_pairs={{0,96},{8,104},{16,112},{24,120},{32,0},{40,8},{48,16},{56,24},{64... | collective-permute-start | bytes 1572872 | tf_op jit(solution)/shard_map/ppermute | solution.py:113
  86.3 44.6 %copy-start.3 = (f32[2,4,128]{2,1,0:T(4,128)S(1)}, f32[2,4,128]{2,1,0:T(4,128)}, u32[]{:S(2)}) copy-start(f32[2,4,128]{2,1,0:T(4,128)} %param.12) | copy-start | bytes 12292
  130.9 0.8 copy-start.1
Sparse Core Ops, SparseCore 0:
  10.2 70.1 all-gather.2

commit v10 on v9

--- a/solution.py
+++ b/solution.py
@@ -125,15 +125,16 @@
     rows = 4
     cols = n_grp // rows
     assert lag_count == 2 and rows * cols == n_grp
-    table = lax.all_gather(hist16[0], "grp", axis=0, tiled=True)
-    other = ring_gather(ring_gather(hist16[1], rows, cols, True), rows, cols, False)
+    table = ring_gather(ring_gather(hist16[0], rows, cols, True), rows, cols, False)
+    table = table.reshape(n_grp * src_dev, angles, width)
+    other = ring_gather(ring_gather(hist16[1], rows, cols, False), rows, cols, True)
     other = other.reshape(n_grp * src_dev, angles, width)
     me = lax.axis_index("grp")
     owner = tile_src // src_dev
+    local = tile_src % src_dev
     dy = (owner // cols - me // cols + rows) % rows
     dz = (owner % cols - me % cols + cols) % cols
-    other_index = (dy * cols + dz) * src_dev + tile_src % src_dev
-    tile_index = jnp.where(tile_lag == 0, tile_src, other_index)
+    tile_index = jnp.where(tile_lag == 0, (dy * cols + dz) * src_dev + local, (dz * rows + dy) * src_dev + local)
     partial = field_partial(table, other, tile_index, tile_lag, tile_obs, tiles, observers)
     partial = partial.reshape(n_grp, obs_dev, n_lag, ang_dev, width)
     partial = partial.transpose(0, 2, 1, 3, 4).reshape(n_grp * n_lag, obs_dev, ang_dev, width)

time: 139 us -> 112 us (0.81)
  waiting for transfers between devices: 55.2 us -> 24.4 us
  between operations: 14.1 us -> 0.82 us
  starting transfers between devices: 14.4 us -> 24.3 us
  other arithmetic: 2.8 us -> 10.6 us
  local copies, waits for them, and re-layouts: 8.24 us -> 6.5 us
    ppermute x2 -> x4, waiting for transfers between devices: 19.3 us -> 2.19 us  [ring_gather(): far_a = lax.ppermute(from_behind[:half], 'grp', plus)]
    ppermute x2 -> x4, waiting for transfers between devices: 34.2 us -> 20.8 us  [ring_gather(): from_behind = lax.ppermute(x, 'grp', plus)]
    another operation x4 -> x8, other arithmetic: 2.04 us -> 8.45 us  [ring_gather(): return jnp.stack([x, from_ahead, far, from_behind])]
    ppermute x2 -> x4, starting transfers between devices: 4.54 us -> 8.98 us  [ring_gather(): from_ahead = lax.ppermute(x, 'grp', minus)]
    ppermute x2 -> x4, starting transfers between devices: 6.24 us -> 10.1 us  [ring_gather(): far_b = lax.ppermute(from_ahead[half:], 'grp', minus)]
    another operation x1 -> x0, local copies, waits for them, and re-layouts: 3 us -> none  [ring_gather(): return jnp.stack([x, from_ahead, far, from_behind])]
    slice x1, local copies, waits for them, and re-layouts: 2.04 us -> 0.16 us  [body(): hist16[1]]
    ppermute x2 -> x4, starting transfers between devices: 3.51 us -> 3.91 us  [ring_gather(): from_behind = lax.ppermute(x, 'grp', plus)]
  transfers between devices with their start and end apart: 9 -> 16, of which waited for: 6 -> 6; matrix products, arithmetic and copies ran while one was open for 5% -> 9% of each run, Pallas kernels for 0% -> 0%
where the time goes in v10:
time: 112 us
  blocking collectives  25.7 us (23%)
  waiting for transfers between devices  24.4 us (22%)
  starting transfers between devices  24.3 us (22%)
  Pallas kernels  18.5 us (17%)
  other arithmetic  10.6 us (9%)
  local copies, waits for them, and re-layouts  6.5 us (6%)
    all_to_all x1, blocking collectives, body(): received = lax.all_to_all(partial, ('grp', 'lag'), 0, 0, tiled=True)  25.7 us
    ppermute x4, waiting for transfers between devices, ring_gather(): from_behind = lax.ppermute(x, 'grp', plus)  20.8 us
    pallas_call x1, Pallas kernels, field_partial(): pl.pallas_call(field_kernel, grid_spec=grid_spec, out_shape=jax.ShapeDtyp...  18.5 us
    ppermute x4, starting transfers between devices, ring_gather(): far_b = lax.ppermute(from_ahead[half:], 'grp', minus)  10.1 us
    ppermute x4, starting transfers between devices, ring_gather(): from_ahead = lax.ppermute(x, 'grp', minus)  8.98 us
    another operation x8, other arithmetic, ring_gather(): return jnp.stack([x, from_ahead, far, from_behind])  8.45 us
    ppermute x4, starting transfers between devices, ring_gather(): from_behind = lax.ppermute(x, 'grp', plus)  3.91 us
  transfers between devices with their start and end apart: 16, of which 6 were waited for; matrix products, arithmetic and copies ran while one was open for 9% of the time, Pallas kernels for 0%

profile of v10, /device:TPU:1, one launch (start us, length us, event | category | flops | bytes accessed | tf_op | source)
XLA Modules:
  0.0 111.6 jit_solution(12756874031802106899)
XLA Ops:
  0.6 0.0 copy-start
  0.6 1.3 %convert_element_type.6 = bf16[2,32,32,128]{3,2,1,0:T(8,128)(2,1)S(1)} convert(f32[2,32,32,128]{3,2,1,0:T(8,128)} %param.7) | non-fusion elementwise | flops 262144 | bytes 1572864 | tf_op jit(solution)/shard_map/convert_element_type | solution.py:123
  2.0 0.2 fusion.11
  2.2 2.2 %collective-permute-start.9 = (bf16[32,32,128]{2,1,0:T(8,128)(2,1)S(1)}, bf16[32,32,128]{2,1,0:T(8,128)(2,1)S(1)}, u32[]{:S(2)}, u32[]{:S(2)}) collective-permute-start(bf16[32,32,128]{2,1,0:T(8,128)(2,1)S(1)} %get-tuple-element.8), channel_id=1, source_target_pairs={{0,32},{8,40},{16,48},{24,56},{32,64},{40,72},{48,80},{56,88},{64,... | collective-permute-start | bytes 786440 | tf_op jit(solution)/shard_map/ppermute | solution.py:108
  4.4 1.5 %collective-permute-start.8 = (bf16[32,32,128]{2,1,0:T(8,128)(2,1)S(1)}, bf16[32,32,128]{2,1,0:T(8,128)(2,1)S(1)}, u32[]{:S(2)}, u32[]{:S(2)}) collective-permute-start(bf16[32,32,128]{2,1,0:T(8,128)(2,1)S(1)} %get-tuple-element.8), channel_id=1, source_target_pairs={{0,96},{8,104},{16,112},{24,120},{32,0},{40,8},{48,16},{56,24},{64... | collective-permute-start | bytes 786440 | tf_op jit(solution)/shard_map/ppermute | solution.py:109
  5.9 1.6 %collective-permute-start.1 = (bf16[32,32,128]{2,1,0:T(8,128)(2,1)S(1)}, bf16[32,32,128]{2,1,0:T(8,128)(2,1)S(1)}, u32[]{:S(2)}, u32[]{:S(2)}) collective-permute-start(bf16[32,32,128]{2,1,0:T(8,128)(2,1)S(1)} %get-tuple-element.7), channel_id=1, source_target_pairs={{0,8},{8,16},{16,24},{24,0},{32,40},{40,48},{48,56},{56,32},{64,72... | collective-permute-start | bytes 786440 | tf_op jit(solution)/shard_map/ppermute | solution.py:108
  7.5 2.1 %collective-permute-start = (bf16[32,32,128]{2,1,0:T(8,128)(2,1)S(1)}, bf16[32,32,128]{2,1,0:T(8,128)(2,1)S(1)}, u32[]{:S(2)}, u32[]{:S(2)}) collective-permute-start(bf16[32,32,128]{2,1,0:T(8,128)(2,1)S(1)} %get-tuple-element.7), channel_id=1, source_target_pairs={{0,24},{8,0},{16,8},{24,16},{32,56},{40,32},{48,40},{56,48},{64,88... | collective-permute-start | bytes 786440 | tf_op jit(solution)/shard_map/ppermute | solution.py:109
  9.6 2.0 %collective-permute-done.9 = bf16[32,32,128]{2,1,0:T(8,128)(2,1)S(1)} collective-permute-done((bf16[32,32,128]{2,1,0:T(8,128)(2,1)S(1)}, bf16[32,32,128]{2,1,0:T(8,128)(2,1)S(1)}, u32[]{:S(2)}, u32[]{:S(2)}) %collective-permute-start.9) | collective-permute-done | bytes 262176 | tf_op jit(solution)/shard_map/ppermute | solution.py:108
  11.7 0.1 collective-permute-start.10
  11.8 0.0 collective-permute-done.8
  11.8 2.7 %collective-permute-start.11 = (bf16[16,32,128]{2,1,0:T(8,128)(2,1)S(1)}, bf16[16,32,128]{2,1,0:T(8,128)(2,1)S(1)}, u32[]{:S(2)}, u32[]{:S(2)}) collective-permute-start(bf16[16,32,128]{2,1,0:T(8,128)(2,1)S(1)} %slice.47), channel_id=1, source_target_pairs={{0,96},{8,104},{16,112},{24,120},{32,0},{40,8},{48,16},{56,24},{64... | collective-permute-start | bytes 393224 | tf_op jit(solution)/shard_map/ppermute | solution.py:113
  14.5 0.7 collective-permute-done.1
  15.2 1.0 collective-permute-start.2
  16.1 0.0 collective-permute-done
  16.2 2.2 %collective-permute-start.3 = (bf16[16,32,128]{2,1,0:T(8,128)(2,1)S(1)}, bf16[16,32,128]{2,1,0:T(8,128)(2,1)S(1)}, u32[]{:S(2)}, u32[]{:S(2)}) collective-permute-start(bf16[16,32,128]{2,1,0:T(8,128)(2,1)S(1)} %slice.42), channel_id=1, source_target_pairs={{0,24},{8,0},{16,8},{24,16},{32,56},{40,32},{48,40},{56,48},{64,88... | collective-permute-start | bytes 393224 | tf_op jit(solution)/shard_map/ppermute | solution.py:113
  18.4 0.2 fusion.9
  18.6 0.0 copy-start.4
  18.6 0.0 copy-start.6
  18.6 0.1 collective-permute-start.13
  18.7 2.7 %collective-permute-start.12 = (bf16[4,32,32,128]{3,2,1,0:T(8,128)(2,1)S(1)}, bf16[4,32,32,128]{3,2,1,0:T(8,128)(2,1)S(1)}, u32[]{:S(2)}, u32[]{:S(2)}) collective-permute-start(bf16[4,32,32,128]{3,2,1,0:T(8,128)(2,1)S(1)} %get-tuple-element.3), channel_id=1, source_target_pairs={{0,24},{8,0},{16,8},{24,16},{32,56},{40,32},{48,40},{56,48},{64,88... | collective-permute-start | bytes 3145736 | tf_op jit(solution)/shard_map/ppermute | solution.py:109
  21.4 0.0 collective-permute-done.2
  21.4 1.2 %fusion.10 = (bf16[1,4,32,32,128]{4,3,2,1,0:T(8,128)(2,1)S(1)}, bf16[4,32,32,128]{3,2,1,0:T(8,128)(2,1)}) fusion(bf16[1,32,32,128]{3,2,1,0:T(8,128)(2,1)S(1)} %bitcast.39, bf16[1,32,32,128]{3,2,1,0:T(8,128)(2,1)S(1)} %maximum_bitcast_fusion.2, bf16[1,32,32,128]{3,2,1,0:T(8,128)(2,1)S(1)} %bitcast.40, bf16[1,32,32,128]{3,2,1,0:T(8,128)(2,1)S(1)} %get-tuple-element.9), kind=kLoop, calls=%fused_computation.41 | loop fusion | flops 1572864 | bytes 3145728 | tf_op jit(solution)/shard_map/stack | solution.py:115
  22.6 2.7 %collective-permute-start.4 = (bf16[4,32,32,128]{3,2,1,0:T(8,128)(2,1)}, bf16[4,32,32,128]{3,2,1,0:T(8,128)(2,1)}, u32[]{:S(2)}, u32[]{:S(2)}) collective-permute-start(bf16[4,32,32,128]{3,2,1,0:T(8,128)(2,1)} %get-tuple-element.5), channel_id=1, source_target_pairs={{0,96},{8,104},{16,112},{24,120},{32,0},{40,8},{48,16},{56,24},{64... | collective-permute-start | bytes 3145736 | tf_op jit(solution)/shard_map/ppermute | solution.py:109
  25.2 18.1 %collective-permute-done.13 = bf16[4,32,32,128]{3,2,1,0:T(8,128)(2,1)S(1)} collective-permute-done((bf16[4,32,32,128]{3,2,1,0:T(8,128)(2,1)S(1)}, bf16[4,32,32,128]{3,2,1,0:T(8,128)(2,1)S(1)}, u32[]{:S(2)}, u32[]{:S(2)}) %collective-permute-start.13) | collective-permute-done | bytes 1048608 | tf_op jit(solution)/shard_map/ppermute | solution.py:108
  43.4 0.8 slice.48
  44.2 0.2 collective-permute-start.14
  44.4 1.0 copy-done.1
  45.4 0.8 slice.49
  46.2 2.5 %collective-permute-start.15 = (bf16[2,32,32,128]{3,2,1,0:T(8,128)(2,1)}, bf16[2,32,32,128]{3,2,1,0:T(8,128)(2,1)}, u32[]{:S(2)}, u32[]{:S(2)}) collective-permute-start(bf16[2,32,32,128]{3,2,1,0:T(8,128)(2,1)} %slice.49), channel_id=1, source_target_pairs={{0,24},{8,0},{16,8},{24,16},{32,56},{40,32},{48,40},{56,48},{64,88... | collective-permute-start | bytes 1572872 | tf_op jit(solution)/shard_map/ppermute | solution.py:113
  48.7 1.2 %slice.43 = bf16[2,32,32,128]{3,2,1,0:T(8,128)(2,1)S(1)} slice(bf16[4,32,32,128]{3,2,1,0:T(8,128)(2,1)} %collective-permute-done.5), slice={[0:2], [0:32], [0:32], [0:128]} | slice | bytes 1048576 | tf_op jit(solution)/shard_map/slice | solution.py:112
  49.9 0.1 collective-permute-start.6
  50.0 1.1 slice.44
  51.0 2.7 %collective-permute-start.7 = (bf16[2,32,32,128]{3,2,1,0:T(8,128)(2,1)S(1)}, bf16[2,32,32,128]{3,2,1,0:T(8,128)(2,1)S(1)}, u32[]{:S(2)}, u32[]{:S(2)}) collective-permute-start(bf16[2,32,32,128]{3,2,1,0:T(8,128)(2,1)S(1)} %slice.44), channel_id=1, source_target_pairs={{0,96},{8,104},{16,112},{24,120},{32,0},{40,8},{48,16},{56,24},{64... | collective-permute-start | bytes 1572872 | tf_op jit(solution)/shard_map/ppermute | solution.py:113
  53.8 0.6 add_select_fusion.6.index_ref
  54.4 2.2 %collective-permute-done.14 = bf16[2,32,32,128]{3,2,1,0:T(8,128)(2,1)} collective-permute-done((bf16[2,32,32,128]{3,2,1,0:T(8,128)(2,1)}, bf16[2,32,32,128]{3,2,1,0:T(8,128)(2,1)}, u32[]{:S(2)}, u32[]{:S(2)}) %collective-permute-start.14) | collective-permute-done | bytes 524320 | tf_op jit(solution)/shard_map/ppermute | solution.py:112
  56.6 1.3 %collective-permute-done.15 = bf16[2,32,32,128]{3,2,1,0:T(8,128)(2,1)} collective-permute-done((bf16[2,32,32,128]{3,2,1,0:T(8,128)(2,1)}, bf16[2,32,32,128]{3,2,1,0:T(8,128)(2,1)}, u32[]{:S(2)}, u32[]{:S(2)}) %collective-permute-start.15) | collective-permute-done | bytes 524320 | tf_op jit(solution)/shard_map/ppermute | solution.py:113
  57.8 1.3 %maximum_bitcast_fusion.1 = bf16[1,4,32,32,128]{4,3,2,1,0:T(8,128)(2,1)S(1)} fusion(bf16[2,32,32,128]{3,2,1,0:T(8,128)(2,1)} %collective-permute-done.15, bf16[2,32,32,128]{3,2,1,0:T(8,128)(2,1)} %collective-permute-done.14), kind=kLoop, calls=%fused_computation.5 | loop fusion | flops 524288 | bytes 2097152 | tf_op jit(solution)/shard_map/stack | solution.py:115
  59.2 2.3 %pad_maximum_fusion.1 = bf16[4,4,32,32,128]{4,3,2,1,0:T(8,128)(2,1)} fusion(bf16[1,4,32,32,128]{4,3,2,1,0:T(8,128)(2,1)S(1)} %bitcast.35, bf16[1,4,32,32,128]{4,3,2,1,0:T(8,128)(2,1)S(1)} %maximum_bitcast_fusion.1, bf16[1,4,32,32,128]{4,3,2,1,0:T(8,128)(2,1)S(1)} %bitcast.36, bf16[1,4,32,32,128]{4,3,2,1,0:T(8,128)(2,1)S(1)} %get-tuple-element.2), kind=kLoop, calls=%fused_computation.1 | loop fusion | flops 6291456 | bytes 8388608 | tf_op jit(solution)/shard_map/stack | solution.py:115
  61.4 0.1 collective-permute-done.7
  61.5 0.1 maximum_bitcast_fusion
  61.6 3.4 %pad_maximum_fusion = bf16[4,4,32,32,128]{4,3,2,1,0:T(8,128)(2,1)} fusion(bf16[1,4,32,32,128]{4,3,2,1,0:T(8,128)(2,1)} %bitcast.7, bf16[1,4,32,32,128]{4,3,2,1,0:T(8,128)(2,1)S(1)} %maximum_bitcast_fusion, bf16[1,4,32,32,128]{4,3,2,1,0:T(8,128)(2,1)} %bitcast.5, bf16[1,4,32,32,128]{4,3,2,1,0:T(8,128)(2,1)S(1)} %get-tuple-element.4), kind=kLoop, calls=%fused_computation | loop fusion | flops 6291456 | bytes 8388608 | tf_op jit(solution)/shard_map/stack | solution.py:115
  65.0 18.5 %shard_map.86 = f32[32,32,128]{2,1,0:T(8,128)} custom-call(s32[512]{0:T(512)} %add_select_fusion.6.index_ref, s32[512]{0:T(512)} %lag_ref.1, s32[512]{0:T(512)} %obs_ref.1, bf16[512,32,128]{2,1,0:T(8,128)(2,1)} %bitcast.34, bf16[512,32,128]{2,1,0:T(8,128)(2,1)} %bitcast.33, bf16[512,128,128]{2,1,0:T(8,128)(2,1)} %tiles_ref.1), custom_call_target="tpu_custom_call" | custom-call | tf_op jit(solution)/shard_map/pallas_call | solution.py:85
  83.5 1.1 copy.13
  84.6 0.3 copy.11
  84.9 25.7 %all_to_all.5 = f32[128,2,4,128]{3,2,1,0:T(4,128)S(1)} all-to-all(f32[128,2,4,128]{3,2,1,0:T(4,128)S(1)} %copy.11), channel_id=1, replica_groups=mesh['grp'=16,'lag'=8] {'grp','lag'}, dimensions={0} | all-to-all | bytes 1048576 | tf_op jit(solution)/shard_map/all_to_all | solution.py:141
  110.6 0.1 reduce_sum.9
  110.8 0.0 copy-start.3
  110.8 0.7 fusion.6
  (23 shorter events, 0.1 us)
Async XLA Ops:
  0.6 110.2 %copy-start = (bf16[2,128,128]{2,1,0:T(8,128)(2,1)S(1)}, bf16[2,128,128]{2,1,0:T(8,128)(2,1)}, u32[]{:S(2)}) copy-start(bf16[2,128,128]{2,1,0:T(8,128)(2,1)} %param.13) | copy-start | bytes 196612
  2.2 9.5 %collective-permute-start.9 = (bf16[32,32,128]{2,1,0:T(8,128)(2,1)S(1)}, bf16[32,32,128]{2,1,0:T(8,128)(2,1)S(1)}, u32[]{:S(2)}, u32[]{:S(2)}) collective-permute-start(bf16[32,32,128]{2,1,0:T(8,128)(2,1)S(1)} %get-tuple-element.8), channel_id=1, source_target_pairs={{0,32},{8,40},{16,48},{24,56},{32,64},{40,72},{48,80},{56,88},{64,... | collective-permute-start | bytes 786440 | tf_op jit(solution)/shard_map/ppermute | solution.py:108
  4.4 7.4 %collective-permute-start.8 = (bf16[32,32,128]{2,1,0:T(8,128)(2,1)S(1)}, bf16[32,32,128]{2,1,0:T(8,128)(2,1)S(1)}, u32[]{:S(2)}, u32[]{:S(2)}) collective-permute-start(bf16[32,32,128]{2,1,0:T(8,128)(2,1)S(1)} %get-tuple-element.8), channel_id=1, source_target_pairs={{0,96},{8,104},{16,112},{24,120},{32,0},{40,8},{48,16},{56,24},{64... | collective-permute-start | bytes 786440 | tf_op jit(solution)/shard_map/ppermute | solution.py:109
  5.9 9.3 %collective-permute-start.1 = (bf16[32,32,128]{2,1,0:T(8,128)(2,1)S(1)}, bf16[32,32,128]{2,1,0:T(8,128)(2,1)S(1)}, u32[]{:S(2)}, u32[]{:S(2)}) collective-permute-start(bf16[32,32,128]{2,1,0:T(8,128)(2,1)S(1)} %get-tuple-element.7), channel_id=1, source_target_pairs={{0,8},{8,16},{16,24},{24,0},{32,40},{40,48},{48,56},{56,32},{64,72... | collective-permute-start | bytes 786440 | tf_op jit(solution)/shard_map/ppermute | solution.py:108
  7.5 8.6 %collective-permute-start = (bf16[32,32,128]{2,1,0:T(8,128)(2,1)S(1)}, bf16[32,32,128]{2,1,0:T(8,128)(2,1)S(1)}, u32[]{:S(2)}, u32[]{:S(2)}) collective-permute-start(bf16[32,32,128]{2,1,0:T(8,128)(2,1)S(1)} %get-tuple-element.7), channel_id=1, source_target_pairs={{0,24},{8,0},{16,8},{24,16},{32,56},{40,32},{48,40},{56,48},{64,88... | collective-permute-start | bytes 786440 | tf_op jit(solution)/shard_map/ppermute | solution.py:109
  11.7 6.7 %collective-permute-start.10 = (bf16[16,32,128]{2,1,0:T(8,128)(2,1)S(1)}, bf16[16,32,128]{2,1,0:T(8,128)(2,1)S(1)}, u32[]{:S(2)}, u32[]{:S(2)}) collective-permute-start(bf16[16,32,128]{2,1,0:T(8,128)(2,1)S(1)} %slice.46), channel_id=1, source_target_pairs={{0,32},{8,40},{16,48},{24,56},{32,64},{40,72},{48,80},{56,88},{64,... | collective-permute-start | bytes 393224 | tf_op jit(solution)/shard_map/ppermute | solution.py:112
  11.8 6.6 %collective-permute-start.11 = (bf16[16,32,128]{2,1,0:T(8,128)(2,1)S(1)}, bf16[16,32,128]{2,1,0:T(8,128)(2,1)S(1)}, u32[]{:S(2)}, u32[]{:S(2)}) collective-permute-start(bf16[16,32,128]{2,1,0:T(8,128)(2,1)S(1)} %slice.47), channel_id=1, source_target_pairs={{0,96},{8,104},{16,112},{24,120},{32,0},{40,8},{48,16},{56,24},{64... | collective-permute-start | bytes 393224 | tf_op jit(solution)/shard_map/ppermute | solution.py:113
  15.2 6.2 %collective-permute-start.2 = (bf16[16,32,128]{2,1,0:T(8,128)(2,1)S(1)}, bf16[16,32,128]{2,1,0:T(8,128)(2,1)S(1)}, u32[]{:S(2)}, u32[]{:S(2)}) collective-permute-start(bf16[16,32,128]{2,1,0:T(8,128)(2,1)S(1)} %slice.41), channel_id=1, source_target_pairs={{0,8},{8,16},{16,24},{24,0},{32,40},{40,48},{48,56},{56,32},{64,72... | collective-permute-start | bytes 393224 | tf_op jit(solution)/shard_map/ppermute | solution.py:112
  16.2 5.2 %collective-permute-start.3 = (bf16[16,32,128]{2,1,0:T(8,128)(2,1)S(1)}, bf16[16,32,128]{2,1,0:T(8,128)(2,1)S(1)}, u32[]{:S(2)}, u32[]{:S(2)}) collective-permute-start(bf16[16,32,128]{2,1,0:T(8,128)(2,1)S(1)} %slice.42), channel_id=1, source_target_pairs={{0,24},{8,0},{16,8},{24,16},{32,56},{40,32},{48,40},{56,48},{64,88... | collective-permute-start | bytes 393224 | tf_op jit(solution)/shard_map/ppermute | solution.py:113
  18.6 35.2 %copy-start.4 = (s32[512]{0:T(512)S(1)}, s32[512]{0:T(512)}, u32[]{:S(2)}) copy-start(s32[512]{0:T(512)} %lag_ref.1) | copy-start | bytes 6148
  18.6 35.2 %copy-start.6 = (s32[512]{0:T(512)S(1)}, s32[512]{0:T(512)}, u32[]{:S(2)}) copy-start(s32[512]{0:T(512)} %param.9) | copy-start | bytes 6148
  18.6 24.8 %collective-permute-start.13 = (bf16[4,32,32,128]{3,2,1,0:T(8,128)(2,1)S(1)}, bf16[4,32,32,128]{3,2,1,0:T(8,128)(2,1)S(1)}, u32[]{:S(2)}, u32[]{:S(2)}) collective-permute-start(bf16[4,32,32,128]{3,2,1,0:T(8,128)(2,1)S(1)} %get-tuple-element.3), channel_id=1, source_target_pairs={{0,8},{8,16},{16,24},{24,0},{32,40},{40,48},{48,56},{56,32},{64,72... | collective-permute-start | bytes 3145736 | tf_op jit(solution)/shard_map/ppermute | solution.py:108
  18.7 25.7 %collective-permute-start.12 = (bf16[4,32,32,128]{3,2,1,0:T(8,128)(2,1)S(1)}, bf16[4,32,32,128]{3,2,1,0:T(8,128)(2,1)S(1)}, u32[]{:S(2)}, u32[]{:S(2)}) collective-permute-start(bf16[4,32,32,128]{3,2,1,0:T(8,128)(2,1)S(1)} %get-tuple-element.3), channel_id=1, source_target_pairs={{0,24},{8,0},{16,8},{24,16},{32,56},{40,32},{48,40},{56,48},{64,88... | collective-permute-start | bytes 3145736 | tf_op jit(solution)/shard_map/ppermute | solution.py:109
  22.6 26.1 %collective-permute-start.5 = (bf16[4,32,32,128]{3,2,1,0:T(8,128)(2,1)}, bf16[4,32,32,128]{3,2,1,0:T(8,128)(2,1)}, u32[]{:S(2)}, u32[]{:S(2)}) collective-permute-start(bf16[4,32,32,128]{3,2,1,0:T(8,128)(2,1)} %get-tuple-element.5), channel_id=1, source_target_pairs={{0,32},{8,40},{16,48},{24,56},{32,64},{40,72},{48,80},{56,88},{64,... | collective-permute-start | bytes 3145736 | tf_op jit(solution)/shard_map/ppermute | solution.py:108
  22.6 27.4 %collective-permute-start.4 = (bf16[4,32,32,128]{3,2,1,0:T(8,128)(2,1)}, bf16[4,32,32,128]{3,2,1,0:T(8,128)(2,1)}, u32[]{:S(2)}, u32[]{:S(2)}) collective-permute-start(bf16[4,32,32,128]{3,2,1,0:T(8,128)(2,1)} %get-tuple-element.5), channel_id=1, source_target_pairs={{0,96},{8,104},{16,112},{24,120},{32,0},{40,8},{48,16},{56,24},{64... | collective-permute-start | bytes 3145736 | tf_op jit(solution)/shard_map/ppermute | solution.py:109
  44.2 12.3 %collective-permute-start.14 = (bf16[2,32,32,128]{3,2,1,0:T(8,128)(2,1)}, bf16[2,32,32,128]{3,2,1,0:T(8,128)(2,1)}, u32[]{:S(2)}, u32[]{:S(2)}) collective-permute-start(bf16[2,32,32,128]{3,2,1,0:T(8,128)(2,1)} %slice.48), channel_id=1, source_target_pairs={{0,8},{8,16},{16,24},{24,0},{32,40},{40,48},{48,56},{56,32},{64,72... | collective-permute-start | bytes 1572872 | tf_op jit(solution)/shard_map/ppermute | solution.py:112
  44.4 1.0 copy-start.1
  46.2 11.6 %collective-permute-start.15 = (bf16[2,32,32,128]{3,2,1,0:T(8,128)(2,1)}, bf16[2,32,32,128]{3,2,1,0:T(8,128)(2,1)}, u32[]{:S(2)}, u32[]{:S(2)}) collective-permute-start(bf16[2,32,32,128]{3,2,1,0:T(8,128)(2,1)} %slice.49), channel_id=1, source_target_pairs={{0,24},{8,0},{16,8},{24,16},{32,56},{40,32},{48,40},{56,48},{64,88... | collective-permute-start | bytes 1572872 | tf_op jit(solution)/shard_map/ppermute | solution.py:113
  48.7 10.5 %copy-start.2 = (bf16[4,32,32,128]{3,2,1,0:T(8,128)(2,1)S(1)}, bf16[4,32,32,128]{3,2,1,0:T(8,128)(2,1)}, u32[]{:S(2)}) copy-start(bf16[4,32,32,128]{3,2,1,0:T(8,128)(2,1)} %copy-done.1) | copy-start | bytes 3145732
  49.9 11.6 %collective-permute-start.6 = (bf16[2,32,32,128]{3,2,1,0:T(8,128)(2,1)S(1)}, bf16[2,32,32,128]{3,2,1,0:T(8,128)(2,1)S(1)}, u32[]{:S(2)}, u32[]{:S(2)}) collective-permute-start(bf16[2,32,32,128]{3,2,1,0:T(8,128)(2,1)S(1)} %slice.43), channel_id=1, source_target_pairs={{0,32},{8,40},{16,48},{24,56},{32,64},{40,72},{48,80},{56,88},{64,... | collective-permute-start | bytes 1572872 | tf_op jit(solution)/shard_map/ppermute | solution.py:112
  51.0 10.5 %collective-permute-start.7 = (bf16[2,32,32,128]{3,2,1,0:T(8,128)(2,1)S(1)}, bf16[2,32,32,128]{3,2,1,0:T(8,128)(2,1)S(1)}, u32[]{:S(2)}, u32[]{:S(2)}) collective-permute-start(bf16[2,32,32,128]{3,2,1,0:T(8,128)(2,1)S(1)} %slice.44), channel_id=1, source_target_pairs={{0,96},{8,104},{16,112},{24,120},{32,0},{40,8},{48,16},{56,24},{64... | collective-permute-start | bytes 1572872 | tf_op jit(solution)/shard_map/ppermute | solution.py:113
  65.0 45.8 %copy-start.5 = (f32[2,4,128]{2,1,0:T(4,128)S(1)}, f32[2,4,128]{2,1,0:T(4,128)}, u32[]{:S(2)}) copy-start(f32[2,4,128]{2,1,0:T(4,128)} %param.12) | copy-start | bytes 12292
  110.8 0.8 copy-start.3

commit v11 on v10

--- a/solution.py
+++ b/solution.py
@@ -103,17 +103,20 @@
 
 def ring_gather(x, rows, cols, along_cols):
     n = cols if along_cols else rows
+    assert n == 4
+    n_lag = lax.axis_size("lag")
     plus = shift_pairs(rows, cols, 1, along_cols)
     minus = shift_pairs(rows, cols, -1, along_cols)
     from_behind = lax.ppermute(x, "grp", plus)
     from_ahead = lax.ppermute(x, "grp", minus)
-    assert n == 4
-    half = x.shape[0] // 2
-    far_a = lax.ppermute(from_behind[:half], "grp", plus)
-    far_b = lax.ppermute(from_ahead[half:], "grp", minus)
-    far = jnp.concatenate([far_a, far_b], axis=0)
+    odd = lax.axis_index("lag") % 2 == 1
+    send = jnp.where(odd, from_ahead, from_behind)
+    pairs = []
+    for l in range(n_lag):
+        for src, dst in (minus if l % 2 else plus):
+            pairs.append((src * n_lag + l, dst * n_lag + l))
+    far = lax.ppermute(send, ("grp", "lag"), pairs)
     return jnp.stack([x, from_ahead, far, from_behind])
-
 
 def body(history, tiles, tile_src, tile_obs, tile_lag, incident, near_inverse):
     n_grp = lax.axis_size("grp")

time: 112 us -> 115 us (1.027)
  waiting for transfers between devices: 24.4 us -> 37.8 us
  starting transfers between devices: 24.3 us -> 17 us
  local copies, waits for them, and re-layouts: 6.5 us -> 3.74 us
  other arithmetic: 10.6 us -> 12.7 us
  blocking collectives: 25.7 us -> 23.9 us
    ppermute x8 -> x4, starting transfers between devices: 11.4 us -> 3.89 us  [ring_gather(): far = lax.ppermute(send, ('grp', 'lag'), pairs)]
    ppermute x4, waiting for transfers between devices: 20.8 us -> 26.9 us  [ring_gather(): from_behind = lax.ppermute(x, 'grp', plus)]
    ppermute x8 -> x4, waiting for transfers between devices: 3.59 us -> 9.64 us  [ring_gather(): far = lax.ppermute(send, ('grp', 'lag'), pairs)]
    slice x8 -> x0, local copies, waits for them, and re-layouts: 3.93 us -> none  [the longest x4 2 us: ring_gather(): far_a = lax.ppermute(from_behind[:half], 'grp', plus)]
    ppermute x4, starting transfers between devices: 8.98 us -> 11.4 us  [ring_gather(): from_ahead = lax.ppermute(x, 'grp', minus)]
    select_n x0 -> x4, other arithmetic: none -> 2.39 us  [ring_gather(): send = jnp.where(odd, from_ahead, from_behind)]
    ppermute x4, starting transfers between devices: 3.91 us -> 1.71 us  [ring_gather(): from_behind = lax.ppermute(x, 'grp', plus)]
    all_to_all x1, blocking collectives: 25.7 us -> 23.9 us  [body(): received = lax.all_to_all(partial, ('grp', 'lag'), 0, 0, tiled=True)]
  transfers between devices with their start and end apart: 16 -> 12, of which waited for: 6 -> 6; matrix products, arithmetic and copies ran while one was open for 9% -> 7% of each run, Pallas kernels for 0% -> 0%
where the time goes in v11:
time: 115 us
  waiting for transfers between devices  37.8 us (33%)
  blocking collectives  23.9 us (21%)
  Pallas kernels  18.5 us (16%)
  starting transfers between devices  17 us (15%)
  other arithmetic  12.7 us (11%)
  local copies, waits for them, and re-layouts  3.74 us (3%)
    ppermute x4, waiting for transfers between devices, ring_gather(): from_behind = lax.ppermute(x, 'grp', plus)  26.9 us
    all_to_all x1, blocking collectives, body(): received = lax.all_to_all(partial, ('grp', 'lag'), 0, 0, tiled=True)  23.9 us
    pallas_call x1, Pallas kernels, field_partial(): pl.pallas_call(field_kernel, grid_spec=grid_spec, out_shape=jax.ShapeDtyp...  18.5 us
    ppermute x4, starting transfers between devices, ring_gather(): from_ahead = lax.ppermute(x, 'grp', minus)  11.4 us
    ppermute x4, waiting for transfers between devices, ring_gather(): far = lax.ppermute(send, ('grp', 'lag'), pairs)  9.64 us
    another operation x4, other arithmetic, ring_gather(): return jnp.stack([x, from_ahead, far, from_behind])  8.25 us
    ppermute x4, starting transfers between devices, ring_gather(): far = lax.ppermute(send, ('grp', 'lag'), pairs)  3.89 us
    select_n x4, other arithmetic, ring_gather(): send = jnp.where(odd, from_ahead, from_behind)  2.39 us
  transfers between devices with their start and end apart: 12, of which 6 were waited for; matrix products, arithmetic and copies ran while one was open for 7% of the time, Pallas kernels for 0%

profile of v11, /device:TPU:1, one launch (start us, length us, event | category | flops | bytes accessed | tf_op | source)
XLA Modules:
  0.0 115.2 jit_solution(9313618373946109938)
XLA Ops:
  0.6 0.0 copy-start
  0.6 1.3 %convert_element_type.6 = bf16[2,32,32,128]{3,2,1,0:T(8,128)(2,1)S(1)} convert(f32[2,32,32,128]{3,2,1,0:T(8,128)} %param.7) | non-fusion elementwise | flops 262144 | bytes 1572864 | tf_op jit(solution)/shard_map/convert_element_type | solution.py:126
  2.0 0.2 fusion.11
  2.2 3.6 %collective-permute-start.6 = (bf16[32,32,128]{2,1,0:T(8,128)(2,1)S(1)}, bf16[32,32,128]{2,1,0:T(8,128)(2,1)S(1)}, u32[]{:S(2)}, u32[]{:S(2)}) collective-permute-start(bf16[32,32,128]{2,1,0:T(8,128)(2,1)S(1)} %get-tuple-element.8), channel_id=1, source_target_pairs={{0,96},{8,104},{16,112},{24,120},{32,0},{40,8},{48,16},{56,24},{64... | collective-permute-start | bytes 786440 | tf_op jit(solution)/shard_map/ppermute | solution.py:111
  5.8 0.0 collective-permute-start.7
  5.8 3.8 %collective-permute-start = (bf16[32,32,128]{2,1,0:T(8,128)(2,1)S(1)}, bf16[32,32,128]{2,1,0:T(8,128)(2,1)S(1)}, u32[]{:S(2)}, u32[]{:S(2)}) collective-permute-start(bf16[32,32,128]{2,1,0:T(8,128)(2,1)S(1)} %get-tuple-element.7), channel_id=1, source_target_pairs={{0,24},{8,0},{16,8},{24,16},{32,56},{40,32},{48,40},{56,48},{64,88... | collective-permute-start | bytes 786440 | tf_op jit(solution)/shard_map/ppermute | solution.py:111
  9.6 0.0 collective-permute-start.1
  9.6 1.2 %collective-permute-done.6 = bf16[32,32,128]{2,1,0:T(8,128)(2,1)S(1)} collective-permute-done((bf16[32,32,128]{2,1,0:T(8,128)(2,1)S(1)}, bf16[32,32,128]{2,1,0:T(8,128)(2,1)S(1)}, u32[]{:S(2)}, u32[]{:S(2)}) %collective-permute-start.6) | collective-permute-done | bytes 262176 | tf_op jit(solution)/shard_map/ppermute | solution.py:111
  10.8 3.1 %collective-permute-done.7 = bf16[32,32,128]{2,1,0:T(8,128)(2,1)S(1)} collective-permute-done((bf16[32,32,128]{2,1,0:T(8,128)(2,1)S(1)}, bf16[32,32,128]{2,1,0:T(8,128)(2,1)S(1)}, u32[]{:S(2)}, u32[]{:S(2)}) %collective-permute-start.7) | collective-permute-done | bytes 262176 | tf_op jit(solution)/shard_map/ppermute | solution.py:110
  13.9 0.4 collective-permute-start.8
  14.3 0.0 collective-permute-done
  14.3 3.0 %collective-permute-done.1 = bf16[32,32,128]{2,1,0:T(8,128)(2,1)S(1)} collective-permute-done((bf16[32,32,128]{2,1,0:T(8,128)(2,1)S(1)}, bf16[32,32,128]{2,1,0:T(8,128)(2,1)S(1)}, u32[]{:S(2)}, u32[]{:S(2)}) %collective-permute-start.1) | collective-permute-done | bytes 262176 | tf_op jit(solution)/shard_map/ppermute | solution.py:110
  17.4 0.8 collective-permute-start.2
  18.2 1.0 collective-permute-done.8
  19.2 0.2 fusion.9
  19.4 1.7 %collective-permute-start.10 = (bf16[4,32,32,128]{3,2,1,0:T(8,128)(2,1)S(1)}, bf16[4,32,32,128]{3,2,1,0:T(8,128)(2,1)S(1)}, u32[]{:S(2)}, u32[]{:S(2)}) collective-permute-start(bf16[4,32,32,128]{3,2,1,0:T(8,128)(2,1)S(1)} %get-tuple-element.3), channel_id=1, source_target_pairs={{0,8},{8,16},{16,24},{24,0},{32,40},{40,48},{48,56},{56,32},{64,72... | collective-permute-start | bytes 3145736 | tf_op jit(solution)/shard_map/ppermute | solution.py:110
  21.1 2.5 %collective-permute-start.9 = (bf16[4,32,32,128]{3,2,1,0:T(8,128)(2,1)S(1)}, bf16[4,32,32,128]{3,2,1,0:T(8,128)(2,1)S(1)}, u32[]{:S(2)}, u32[]{:S(2)}) collective-permute-start(bf16[4,32,32,128]{3,2,1,0:T(8,128)(2,1)S(1)} %get-tuple-element.3), channel_id=1, source_target_pairs={{0,24},{8,0},{16,8},{24,16},{32,56},{40,32},{48,40},{56,48},{64,88... | collective-permute-start | bytes 3145736 | tf_op jit(solution)/shard_map/ppermute | solution.py:111
  23.6 0.0 collective-permute-done.2
  23.6 0.0 copy-done.7
  23.6 0.0 copy-start.9
  23.6 0.0 copy-start.11
  23.6 1.2 %fusion.10 = (bf16[1,4,32,32,128]{4,3,2,1,0:T(8,128)(2,1)S(1)}, bf16[4,32,32,128]{3,2,1,0:T(8,128)(2,1)S(1)}) fusion(bf16[1,32,32,128]{3,2,1,0:T(8,128)(2,1)} %bitcast.38, bf16[1,32,32,128]{3,2,1,0:T(8,128)(2,1)S(1)} %bitcast.41, bf16[1,32,32,128]{3,2,1,0:T(8,128)(2,1)} %bitcast.37, bf16[1,32,32,128]{3,2,1,0:T(8,128)(2,1)S(1)} %get-tuple-element.9), kind=kLoop, calls=%fused_computation.41 | loop fusion | flops 1572864 | bytes 3145728 | tf_op jit(solution)/shard_map/stack | solution.py:119
  24.8 1.5 %collective-permute-start.3 = (bf16[4,32,32,128]{3,2,1,0:T(8,128)(2,1)S(1)}, bf16[4,32,32,128]{3,2,1,0:T(8,128)(2,1)S(1)}, u32[]{:S(2)}, u32[]{:S(2)}) collective-permute-start(bf16[4,32,32,128]{3,2,1,0:T(8,128)(2,1)S(1)} %get-tuple-element.5), channel_id=1, source_target_pairs={{0,96},{8,104},{16,112},{24,120},{32,0},{40,8},{48,16},{56,24},{64... | collective-permute-start | bytes 3145736 | tf_op jit(solution)/shard_map/ppermute | solution.py:111
  26.4 0.0 collective-permute-start.4
  26.4 20.8 %collective-permute-done.10 = bf16[4,32,32,128]{3,2,1,0:T(8,128)(2,1)S(1)} collective-permute-done((bf16[4,32,32,128]{3,2,1,0:T(8,128)(2,1)S(1)}, bf16[4,32,32,128]{3,2,1,0:T(8,128)(2,1)S(1)}, u32[]{:S(2)}, u32[]{:S(2)}) %collective-permute-start.10) | collective-permute-done | bytes 1048608 | tf_op jit(solution)/shard_map/ppermute | solution.py:110
  47.2 0.0 collective-permute-done.9
  47.2 1.0 copy-done.1
  48.2 1.1 broadcast_select_fusion
  49.3 0.0 collective-permute-start.11
  49.3 0.0 collective-permute-done.3
  49.3 0.0 collective-permute-done.4
  49.3 1.0 copy-done.2
  50.3 1.2 %broadcast_select_fusion.1 = bf16[4,32,32,128]{3,2,1,0:T(8,128)(2,1)} fusion(bf16[4,32,32,128]{3,2,1,0:T(8,128)(2,1)S(1)} %collective-permute-done.3, bf16[4,32,32,128]{3,2,1,0:T(8,128)(2,1)S(1)} %collective-permute-done.4, pred[]{:T(512)S(6)} %eq.25), kind=kLoop, calls=%fused_computation.5 | loop fusion | flops 524288 | bytes 3145729 | tf_op jit(solution)/shard_map/jit(_where)/select_n | solution.py:113
  51.5 0.1 copy-done.4
  51.6 2.7 %collective-permute-start.5 = (bf16[4,32,32,128]{3,2,1,0:T(8,128)(2,1)}, bf16[4,32,32,128]{3,2,1,0:T(8,128)(2,1)}, u32[]{:S(2)}, u32[]{:S(2)}) collective-permute-start(bf16[4,32,32,128]{3,2,1,0:T(8,128)(2,1)} %broadcast_select_fusion.1), channel_id=1, source_target_pairs={{0,32},{8,40},{16,48},{24,56},{32,64},{40,72},{48,80},{56,88},{64,... | collective-permute-start | bytes 3145736 | tf_op jit(solution)/shard_map/ppermute | solution.py:118
  54.3 0.0 copy-done.9
  54.3 0.6 add_select_fusion.6.index_ref
  54.9 8.6 %collective-permute-done.11 = bf16[4,32,32,128]{3,2,1,0:T(8,128)(2,1)} collective-permute-done((bf16[4,32,32,128]{3,2,1,0:T(8,128)(2,1)}, bf16[4,32,32,128]{3,2,1,0:T(8,128)(2,1)}, u32[]{:S(2)}, u32[]{:S(2)}) %collective-permute-start.11) | collective-permute-done | bytes 1048608 | tf_op jit(solution)/shard_map/ppermute | solution.py:118
  63.6 3.6 %pad_maximum_fusion.1 = bf16[4,4,32,32,128]{4,3,2,1,0:T(8,128)(2,1)} fusion(bf16[1,4,32,32,128]{4,3,2,1,0:T(8,128)(2,1)S(1)} %bitcast.31, bf16[1,4,32,32,128]{4,3,2,1,0:T(8,128)(2,1)} %bitcast.15, bf16[1,4,32,32,128]{4,3,2,1,0:T(8,128)(2,1)} %bitcast.32, bf16[1,4,32,32,128]{4,3,2,1,0:T(8,128)(2,1)S(1)} %get-tuple-element.2), kind=kLoop, calls=%fused_computation.1 | loop fusion | flops 6291456 | bytes 8388608 | tf_op jit(solution)/shard_map/stack | solution.py:119
  67.1 0.0 collective-permute-done.5
  67.1 3.3 %pad_maximum_fusion = bf16[4,4,32,32,128]{4,3,2,1,0:T(8,128)(2,1)} fusion(bf16[1,4,32,32,128]{4,3,2,1,0:T(8,128)(2,1)S(1)} %bitcast.34, bf16[1,4,32,32,128]{4,3,2,1,0:T(8,128)(2,1)} %bitcast.6, bf16[1,4,32,32,128]{4,3,2,1,0:T(8,128)(2,1)S(1)} %bitcast.33, bf16[1,4,32,32,128]{4,3,2,1,0:T(8,128)(2,1)S(1)} %get-tuple-element.4), kind=kLoop, calls=%fused_computation | loop fusion | flops 6291456 | bytes 8388608 | tf_op jit(solution)/shard_map/stack | solution.py:119
  70.4 18.5 %shard_map.86 = f32[32,32,128]{2,1,0:T(8,128)} custom-call(s32[512]{0:T(512)} %add_select_fusion.6.index_ref, s32[512]{0:T(512)} %lag_ref.1, s32[512]{0:T(512)} %obs_ref.1, bf16[512,32,128]{2,1,0:T(8,128)(2,1)} %bitcast.30, bf16[512,32,128]{2,1,0:T(8,128)(2,1)} %bitcast.29, bf16[512,128,128]{2,1,0:T(8,128)(2,1)} %tiles_ref.1), custom_call_target="tpu_custom_call" | custom-call | tf_op jit(solution)/shard_map/pallas_call | solution.py:85
  88.9 1.1 copy.13
  90.0 0.3 copy.11
  90.4 23.9 %all_to_all.5 = f32[128,2,4,128]{3,2,1,0:T(4,128)S(1)} all-to-all(f32[128,2,4,128]{3,2,1,0:T(4,128)S(1)} %copy.11), channel_id=1, replica_groups=mesh['grp'=16,'lag'=8] {'grp','lag'}, dimensions={0} | all-to-all | bytes 1048576 | tf_op jit(solution)/shard_map/all_to_all | solution.py:144
  114.3 0.1 reduce_sum.9
  114.4 0.0 copy-start.8
  114.4 0.7 fusion.6
  (17 shorter events, 0.1 us)
Async XLA Ops:
  0.6 113.8 %copy-start = (bf16[2,128,128]{2,1,0:T(8,128)(2,1)S(1)}, bf16[2,128,128]{2,1,0:T(8,128)(2,1)}, u32[]{:S(2)}) copy-start(bf16[2,128,128]{2,1,0:T(8,128)(2,1)} %param.13) | copy-start | bytes 196612
  2.2 8.6 %collective-permute-start.6 = (bf16[32,32,128]{2,1,0:T(8,128)(2,1)S(1)}, bf16[32,32,128]{2,1,0:T(8,128)(2,1)S(1)}, u32[]{:S(2)}, u32[]{:S(2)}) collective-permute-start(bf16[32,32,128]{2,1,0:T(8,128)(2,1)S(1)} %get-tuple-element.8), channel_id=1, source_target_pairs={{0,96},{8,104},{16,112},{24,120},{32,0},{40,8},{48,16},{56,24},{64... | collective-permute-start | bytes 786440 | tf_op jit(solution)/shard_map/ppermute | solution.py:111
  5.8 8.1 %collective-permute-start.7 = (bf16[32,32,128]{2,1,0:T(8,128)(2,1)S(1)}, bf16[32,32,128]{2,1,0:T(8,128)(2,1)S(1)}, u32[]{:S(2)}, u32[]{:S(2)}) collective-permute-start(bf16[32,32,128]{2,1,0:T(8,128)(2,1)S(1)} %get-tuple-element.8), channel_id=1, source_target_pairs={{0,32},{8,40},{16,48},{24,56},{32,64},{40,72},{48,80},{56,88},{64,... | collective-permute-start | bytes 786440 | tf_op jit(solution)/shard_map/ppermute | solution.py:110
  5.8 8.5 %collective-permute-start = (bf16[32,32,128]{2,1,0:T(8,128)(2,1)S(1)}, bf16[32,32,128]{2,1,0:T(8,128)(2,1)S(1)}, u32[]{:S(2)}, u32[]{:S(2)}) collective-permute-start(bf16[32,32,128]{2,1,0:T(8,128)(2,1)S(1)} %get-tuple-element.7), channel_id=1, source_target_pairs={{0,24},{8,0},{16,8},{24,16},{32,56},{40,32},{48,40},{56,48},{64,88... | collective-permute-start | bytes 786440 | tf_op jit(solution)/shard_map/ppermute | solution.py:111
  9.6 7.8 %collective-permute-start.1 = (bf16[32,32,128]{2,1,0:T(8,128)(2,1)S(1)}, bf16[32,32,128]{2,1,0:T(8,128)(2,1)S(1)}, u32[]{:S(2)}, u32[]{:S(2)}) collective-permute-start(bf16[32,32,128]{2,1,0:T(8,128)(2,1)S(1)} %get-tuple-element.7), channel_id=1, source_target_pairs={{0,8},{8,16},{16,24},{24,0},{32,40},{40,48},{48,56},{56,32},{64,72... | collective-permute-start | bytes 786440 | tf_op jit(solution)/shard_map/ppermute | solution.py:110
  13.9 5.3 %collective-permute-start.8 = (bf16[32,32,128]{2,1,0:T(8,128)(2,1)S(1)}, bf16[32,32,128]{2,1,0:T(8,128)(2,1)S(1)}, u32[]{:S(2)}, u32[]{:S(2)}) collective-permute-start(bf16[32,32,128]{2,1,0:T(8,128)(2,1)S(1)} %broadcast_select_fusion.2), channel_id=1, source_target_pairs={{0,32},{8,40},{16,48},{24,56},{32,64},{40,72},{48,80},{56,88},{64,... | collective-permute-start | bytes 786440 | tf_op jit(solution)/shard_map/ppermute | solution.py:118
  14.3 9.3 %copy-start.6 = (bf16[32,32,128]{2,1,0:T(8,128)(2,1)}, bf16[32,32,128]{2,1,0:T(8,128)(2,1)S(1)}, u32[]{:S(2)}) copy-start(bf16[32,32,128]{2,1,0:T(8,128)(2,1)S(1)} %collective-permute-done) | copy-start | bytes 786436
  17.4 6.2 %copy-start.7 = (bf16[32,32,128]{2,1,0:T(8,128)(2,1)}, bf16[32,32,128]{2,1,0:T(8,128)(2,1)S(1)}, u32[]{:S(2)}) copy-start(bf16[32,32,128]{2,1,0:T(8,128)(2,1)S(1)} %collective-permute-done.1) | copy-start | bytes 786436
  17.4 6.2 %collective-permute-start.2 = (bf16[32,32,128]{2,1,0:T(8,128)(2,1)S(1)}, bf16[32,32,128]{2,1,0:T(8,128)(2,1)S(1)}, u32[]{:S(2)}, u32[]{:S(2)}) collective-permute-start(bf16[32,32,128]{2,1,0:T(8,128)(2,1)S(1)} %broadcast_select_fusion.3), channel_id=1, source_target_pairs={{0,8},{8,16},{16,24},{24,0},{32,40},{40,48},{48,56},{56,32},{64,72... | collective-permute-start | bytes 786440 | tf_op jit(solution)/shard_map/ppermute | solution.py:118
  19.4 27.8 %collective-permute-start.10 = (bf16[4,32,32,128]{3,2,1,0:T(8,128)(2,1)S(1)}, bf16[4,32,32,128]{3,2,1,0:T(8,128)(2,1)S(1)}, u32[]{:S(2)}, u32[]{:S(2)}) collective-permute-start(bf16[4,32,32,128]{3,2,1,0:T(8,128)(2,1)S(1)} %get-tuple-element.3), channel_id=1, source_target_pairs={{0,8},{8,16},{16,24},{24,0},{32,40},{40,48},{48,56},{56,32},{64,72... | collective-permute-start | bytes 3145736 | tf_op jit(solution)/shard_map/ppermute | solution.py:110
  21.1 26.1 %collective-permute-start.9 = (bf16[4,32,32,128]{3,2,1,0:T(8,128)(2,1)S(1)}, bf16[4,32,32,128]{3,2,1,0:T(8,128)(2,1)S(1)}, u32[]{:S(2)}, u32[]{:S(2)}) collective-permute-start(bf16[4,32,32,128]{3,2,1,0:T(8,128)(2,1)S(1)} %get-tuple-element.3), channel_id=1, source_target_pairs={{0,24},{8,0},{16,8},{24,16},{32,56},{40,32},{48,40},{56,48},{64,88... | collective-permute-start | bytes 3145736 | tf_op jit(solution)/shard_map/ppermute | solution.py:111
  23.6 30.7 %copy-start.9 = (s32[512]{0:T(512)S(1)}, s32[512]{0:T(512)}, u32[]{:S(2)}) copy-start(s32[512]{0:T(512)} %lag_ref.1) | copy-start | bytes 6148
  23.6 30.7 %copy-start.11 = (s32[512]{0:T(512)S(1)}, s32[512]{0:T(512)}, u32[]{:S(2)}) copy-start(s32[512]{0:T(512)} %param.9) | copy-start | bytes 6148
  24.8 24.5 %collective-permute-start.3 = (bf16[4,32,32,128]{3,2,1,0:T(8,128)(2,1)S(1)}, bf16[4,32,32,128]{3,2,1,0:T(8,128)(2,1)S(1)}, u32[]{:S(2)}, u32[]{:S(2)}) collective-permute-start(bf16[4,32,32,128]{3,2,1,0:T(8,128)(2,1)S(1)} %get-tuple-element.5), channel_id=1, source_target_pairs={{0,96},{8,104},{16,112},{24,120},{32,0},{40,8},{48,16},{56,24},{64... | collective-permute-start | bytes 3145736 | tf_op jit(solution)/shard_map/ppermute | solution.py:111
  26.4 22.9 %collective-permute-start.4 = (bf16[4,32,32,128]{3,2,1,0:T(8,128)(2,1)S(1)}, bf16[4,32,32,128]{3,2,1,0:T(8,128)(2,1)S(1)}, u32[]{:S(2)}, u32[]{:S(2)}) collective-permute-start(bf16[4,32,32,128]{3,2,1,0:T(8,128)(2,1)S(1)} %get-tuple-element.5), channel_id=1, source_target_pairs={{0,32},{8,40},{16,48},{24,56},{32,64},{40,72},{48,80},{56,88},{64,... | collective-permute-start | bytes 3145736 | tf_op jit(solution)/shard_map/ppermute | solution.py:110
  47.2 1.0 copy-start.1
  49.3 14.3 %collective-permute-start.11 = (bf16[4,32,32,128]{3,2,1,0:T(8,128)(2,1)}, bf16[4,32,32,128]{3,2,1,0:T(8,128)(2,1)}, u32[]{:S(2)}, u32[]{:S(2)}) collective-permute-start(bf16[4,32,32,128]{3,2,1,0:T(8,128)(2,1)} %broadcast_select_fusion), channel_id=1, source_target_pairs={{0,8},{8,16},{16,24},{24,0},{32,40},{40,48},{48,56},{56,32},{64,72... | collective-permute-start | bytes 3145736 | tf_op jit(solution)/shard_map/ppermute | solution.py:118
  49.3 1.0 copy-start.2
  50.3 1.3 %copy-start.4 = (bf16[4,32,32,128]{3,2,1,0:T(8,128)(2,1)}, bf16[4,32,32,128]{3,2,1,0:T(8,128)(2,1)S(1)}, u32[]{:S(2)}) copy-start(bf16[4,32,32,128]{3,2,1,0:T(8,128)(2,1)S(1)} %collective-permute-done.4) | copy-start | bytes 3145732
  51.6 15.5 %collective-permute-start.5 = (bf16[4,32,32,128]{3,2,1,0:T(8,128)(2,1)}, bf16[4,32,32,128]{3,2,1,0:T(8,128)(2,1)}, u32[]{:S(2)}, u32[]{:S(2)}) collective-permute-start(bf16[4,32,32,128]{3,2,1,0:T(8,128)(2,1)} %broadcast_select_fusion.1), channel_id=1, source_target_pairs={{0,32},{8,40},{16,48},{24,56},{32,64},{40,72},{48,80},{56,88},{64,... | collective-permute-start | bytes 3145736 | tf_op jit(solution)/shard_map/ppermute | solution.py:118
  63.6 3.6 %copy-start.3 = (bf16[4,32,32,128]{3,2,1,0:T(8,128)(2,1)S(1)}, bf16[4,32,32,128]{3,2,1,0:T(8,128)(2,1)}, u32[]{:S(2)}) copy-start(bf16[4,32,32,128]{3,2,1,0:T(8,128)(2,1)} %copy-done.2) | copy-start | bytes 3145732
  63.6 3.6 %copy-start.5 = (bf16[4,32,32,128]{3,2,1,0:T(8,128)(2,1)S(1)}, bf16[4,32,32,128]{3,2,1,0:T(8,128)(2,1)}, u32[]{:S(2)}) copy-start(bf16[4,32,32,128]{3,2,1,0:T(8,128)(2,1)} %copy-done.4) | copy-start | bytes 3145732
  70.4 44.0 %copy-start.10 = (f32[2,4,128]{2,1,0:T(4,128)S(1)}, f32[2,4,128]{2,1,0:T(4,128)}, u32[]{:S(2)}) copy-start(f32[2,4,128]{2,1,0:T(4,128)} %param.12) | copy-start | bytes 12292
  114.4 0.8 copy-start.8

commit v12 on v10

v12 whole, which is shorter than its diff:
```python
import jax
import jax.numpy as jnp
from jax import lax
from jax.experimental import pallas as pl
from jax.experimental.pallas import tpu as pltpu
from jax.sharding import PartitionSpec as P

BLOCK = 128


def field_kernel(source_ref, index_ref, obs_ref, *refs):
    tables = refs[:-5]
    tiles_ref, out_ref, rows, acc, sems = refs[-5:]
    step = pl.program_id(0)
    steps = pl.num_programs(0)
    block = tiles_ref.shape[0]

    def fetch(which, slot):
        def issue(t, carry):
            r = which * block + t
            i = index_ref[r]
            k = source_ref[r]
            for j, table in enumerate(tables):
                @pl.when(k == j)
                def _():
                    pltpu.make_async_copy(table.at[i], rows.at[slot, t], sems.at[slot]).start()

            return carry

        lax.fori_loop(0, block, issue, 0, unroll=4)

    def wait(slot):
        def one_wait(t, carry):
            pltpu.make_async_copy(tables[0].at[0], rows.at[slot, t], sems.at[slot]).wait()
            return carry

        lax.fori_loop(0, block, one_wait, 0, unroll=8)

    slot = step % 2

    @pl.when(step == 0)
    def _():
        acc[...] = jnp.zeros_like(acc)
        fetch(0, 0)

    wait(slot)

    @pl.when(step + 1 < steps)
    def _():
        fetch(step + 1, 1 - slot)

    def one(t, carry):
        term = lax.dot_general(rows[slot, t], tiles_ref[t], (((1,), (1,)), ((), ())),
                               preferred_element_type=jnp.float32)
        o = obs_ref[step * block + t]
        acc[o] = acc[o] + term
        return carry

    lax.fori_loop(0, block, one, 0, unroll=32)

    @pl.when(step == steps - 1)
    def _():
        groups, lags, obs_dev, ang_dev, _ = out_ref.shape
        for g in range(groups):
            for l in range(lags):
                out_ref[g, l] = acc[g * obs_dev:(g + 1) * obs_dev, l * ang_dev:(l + 1) * ang_dev]


def field_partial(tables, source, tile_index, tile_obs, tiles, groups, lags, obs_dev):
    _, angles, width = tables[0].shape
    n_tiles = tiles.shape[0]
    ang_dev = angles // lags
    out_shape = (groups, lags, obs_dev, ang_dev, width)
    grid_spec = pltpu.PrefetchScalarGridSpec(
        num_scalar_prefetch=3,
        grid=(n_tiles // BLOCK,),
        in_specs=[pl.BlockSpec(memory_space=pl.ANY) for _ in tables] + [
            pl.BlockSpec((BLOCK,) + tiles.shape[1:], lambda i, *_: (i, 0, 0)),
        ],
        out_specs=pl.BlockSpec(out_shape, lambda i, *_: (0, 0, 0, 0, 0)),
        scratch_shapes=[
            pltpu.VMEM((2, BLOCK, angles, width), tables[0].dtype),
            pltpu.VMEM((groups * obs_dev + 1, angles, width), jnp.float32),
            pltpu.SemaphoreType.DMA((2,)),
        ],
    )
    return pl.pallas_call(
        field_kernel,
        grid_spec=grid_spec,
        out_shape=jax.ShapeDtypeStruct(out_shape, jnp.float32),
        compiler_params=pltpu.CompilerParams(dimension_semantics=("arbitrary",)),
    )(source, tile_index, tile_obs, *tables, tiles)


def shift_pairs(rows, cols, step, along_cols):
    pairs = []
    for a in range(rows):
        for b in range(cols):
            if along_cols:
                pairs.append((a * cols + b, a * cols + (b + step) % cols))
            else:
                pairs.append((a * cols + b, ((a + step) % rows) * cols + b))
    return pairs


def ring_gather(x, rows, cols, along_cols, pieces=False):
    n = cols if along_cols else rows
    plus = shift_pairs(rows, cols, 1, along_cols)
    minus = shift_pairs(rows, cols, -1, along_cols)
    from_behind = lax.ppermute(x, "grp", plus)
    from_ahead = lax.ppermute(x, "grp", minus)
    assert n == 4
    half = x.shape[0] // 2
    far_a = lax.ppermute(from_behind[:half], "grp", plus)
    far_b = lax.ppermute(from_ahead[half:], "grp", minus)
    if pieces:
        return [x, from_ahead, far_a, far_b, from_behind]
    far = jnp.concatenate([far_a, far_b], axis=0)
    return jnp.stack([x, from_ahead, far, from_behind])


def body(history, tiles, tile_src, tile_obs, tile_lag, incident, near_inverse):
    n_grp = lax.axis_size("grp")
    n_lag = lax.axis_size("lag")
    obs_dev, ang_dev, width = incident.shape
    observers = obs_dev * n_grp
    hist16 = history.astype(jnp.bfloat16)
    lag_count, src_dev, angles, _ = hist16.shape
    rows = 4
    cols = n_grp // rows
    assert lag_count == 2 and rows * cols == n_grp
    first = ring_gather(ring_gather(hist16[0], rows, cols, True), rows, cols, False, pieces=True)
    second = ring_gather(ring_gather(hist16[1], rows, cols, False), rows, cols, True, pieces=True)
    tables = [p.reshape(-1, angles, width) for p in first + second]
    me = lax.axis_index("grp")
    owner = tile_src // src_dev
    local = tile_src % src_dev
    dy = (owner // cols - me // cols + rows) % rows
    dz = (owner % cols - me % cols + cols) % cols
    outer = jnp.where(tile_lag == 0, dy, dz)
    inner = jnp.where(tile_lag == 0, dz, dy)
    upper = (outer == 2) & (inner >= 2)
    piece = jnp.where(outer == 3, 4, outer + upper.astype(outer.dtype))
    source = piece + 5 * tile_lag
    tile_index = (inner - 2 * upper.astype(inner.dtype)) * src_dev + local
    partial = field_partial(tables, source, tile_index, tile_obs, tiles, n_grp, n_lag, obs_dev)
    partial = partial.reshape(n_grp * n_lag, obs_dev, ang_dev, width)
    received = lax.all_to_all(partial, ("grp", "lag"), 0, 0, tiled=True)
    field = jnp.sum(received, axis=0)
    rhs = (incident - field).astype(jnp.bfloat16)
    new_current = jnp.einsum("oag,ohg->oah", rhs, near_inverse, preferred_element_type=jnp.float32)
    return (field, new_current)


def solution(mesh):
    return jax.shard_map(
        body,
        mesh=mesh,
        in_specs=(
            P("lag", "grp", None, None),
            P(("grp", "lag"), None, None),
            P(("grp", "lag")),
            P(("grp", "lag")),
            P(("grp", "lag")),
            P("grp", "lag", None),
            P("grp", None, None),
        ),
        out_specs=(P("grp", "lag", None), P("grp", "lag", None)),
        check_vma=False,
    )
```

time: 112 us -> 111 us (level)
  other arithmetic: 10.6 us -> 4.38 us
  Pallas kernels: 18.5 us -> 22.9 us
  waiting for transfers between devices: 24.4 us -> 27.3 us
  local copies, waits for them, and re-layouts: 6.5 us -> 3.95 us
    another operation x8 -> x4, other arithmetic: 8.45 us -> 0.32 us  [ring_gather(): return jnp.stack([x, from_ahead, far, from_behind])]
    pallas_call x1, Pallas kernels: 18.5 us -> 22.9 us  [field_partial(): pl.pallas_call(field_kernel, grid_spec=grid_spec, out_shape=jax.ShapeDtyp...]
    ppermute x4, waiting for transfers between devices: 2.19 us -> 5.34 us  [ring_gather(): far_a = lax.ppermute(from_behind[:half], 'grp', plus)]
    add x0 -> x2, other arithmetic: none -> 2.57 us  [the longest x1 1.31 us: body(): tile_index = (inner - 2 * upper.astype(inner.dtype)) * src_dev + local]
    reshape x2 -> x0, local copies, waits for them, and re-layouts: 1.42 us -> none  [the longest x1 1.08 us: body(): partial = partial.reshape(n_grp, obs_dev, n_lag, ang_dev, width)]
    ppermute x4, waiting for transfers between devices: 1.4 us -> 0.21 us  [ring_gather(): far_b = lax.ppermute(from_ahead[half:], 'grp', minus)]
  transfers between devices with their start and end apart: 16 -> 16, of which waited for: 6 -> 6; matrix products, arithmetic and copies ran while one was open for 9% -> 6% of each run, Pallas kernels for 0% -> 0%
where the time goes in v12:
time: 111 us; the launch traced here: 110 us
  waiting for transfers between devices  27.3 us (25%)
  blocking collectives  25.8 us (23%)
  starting transfers between devices  24.3 us (22%)
  Pallas kernels  22.9 us (21%)
  other arithmetic  4.38 us (4%)
  local copies, waits for them, and re-layouts  3.95 us (4%)
    all_to_all x1, blocking collectives, body(): received = lax.all_to_all(partial, ('grp', 'lag'), 0, 0, tiled=True)  25.8 us
    pallas_call x1, Pallas kernels, field_partial(): pl.pallas_call(field_kernel, grid_spec=grid_spec, out_shape=jax.ShapeDtyp...  22.9 us
    ppermute x4, waiting for transfers between devices, ring_gather(): from_behind = lax.ppermute(x, 'grp', plus)  21.8 us
    ppermute x4, starting transfers between devices, ring_gather(): far_b = lax.ppermute(from_ahead[half:], 'grp', minus)  10.1 us
    ppermute x4, starting transfers between devices, ring_gather(): from_ahead = lax.ppermute(x, 'grp', minus)  8.97 us
    ppermute x4, waiting for transfers between devices, ring_gather(): far_a = lax.ppermute(from_behind[:half], 'grp', plus)  5.34 us
    ppermute x4, starting transfers between devices, ring_gather(): from_behind = lax.ppermute(x, 'grp', plus)  3.98 us
  transfers between devices with their start and end apart: 16, of which 6 were waited for; matrix products, arithmetic and copies ran while one was open for 6% of the time, Pallas kernels for 0%

profile of v12, /device:TPU:1, one launch (start us, length us, event | category | flops | bytes accessed | tf_op | source)
XLA Modules:
  0.0 110.2 jit_solution(12213027788665423437)
XLA Ops:
  0.6 0.0 copy-start
  0.6 1.3 %convert_element_type.11 = bf16[2,32,32,128]{3,2,1,0:T(8,128)(2,1)S(1)} convert(f32[2,32,32,128]{3,2,1,0:T(8,128)} %param.7) | non-fusion elementwise | flops 262144 | bytes 1572864 | tf_op jit(solution)/shard_map/convert_element_type | solution.py:127
  2.0 0.2 fusion.10
  2.2 2.2 %collective-permute-start.9 = (bf16[32,32,128]{2,1,0:T(8,128)(2,1)S(1)}, bf16[32,32,128]{2,1,0:T(8,128)(2,1)S(1)}, u32[]{:S(2)}, u32[]{:S(2)}) collective-permute-start(bf16[32,32,128]{2,1,0:T(8,128)(2,1)S(1)} %get-tuple-element.7), channel_id=1, source_target_pairs={{0,32},{8,40},{16,48},{24,56},{32,64},{40,72},{48,80},{56,88},{64,... | collective-permute-start | bytes 786440 | tf_op jit(solution)/shard_map/ppermute | solution.py:110
  4.4 1.5 %collective-permute-start.8 = (bf16[32,32,128]{2,1,0:T(8,128)(2,1)S(1)}, bf16[32,32,128]{2,1,0:T(8,128)(2,1)S(1)}, u32[]{:S(2)}, u32[]{:S(2)}) collective-permute-start(bf16[32,32,128]{2,1,0:T(8,128)(2,1)S(1)} %get-tuple-element.7), channel_id=1, source_target_pairs={{0,96},{8,104},{16,112},{24,120},{32,0},{40,8},{48,16},{56,24},{64... | collective-permute-start | bytes 786440 | tf_op jit(solution)/shard_map/ppermute | solution.py:111
  5.9 1.6 %collective-permute-start.1 = (bf16[32,32,128]{2,1,0:T(8,128)(2,1)S(1)}, bf16[32,32,128]{2,1,0:T(8,128)(2,1)S(1)}, u32[]{:S(2)}, u32[]{:S(2)}) collective-permute-start(bf16[32,32,128]{2,1,0:T(8,128)(2,1)S(1)} %get-tuple-element.6), channel_id=1, source_target_pairs={{0,8},{8,16},{16,24},{24,0},{32,40},{40,48},{48,56},{56,32},{64,72... | collective-permute-start | bytes 786440 | tf_op jit(solution)/shard_map/ppermute | solution.py:110
  7.5 2.1 %collective-permute-start = (bf16[32,32,128]{2,1,0:T(8,128)(2,1)S(1)}, bf16[32,32,128]{2,1,0:T(8,128)(2,1)S(1)}, u32[]{:S(2)}, u32[]{:S(2)}) collective-permute-start(bf16[32,32,128]{2,1,0:T(8,128)(2,1)S(1)} %get-tuple-element.6), channel_id=1, source_target_pairs={{0,24},{8,0},{16,8},{24,16},{32,56},{40,32},{48,40},{56,48},{64,88... | collective-permute-start | bytes 786440 | tf_op jit(solution)/shard_map/ppermute | solution.py:111
  9.7 2.0 %collective-permute-done.9 = bf16[32,32,128]{2,1,0:T(8,128)(2,1)S(1)} collective-permute-done((bf16[32,32,128]{2,1,0:T(8,128)(2,1)S(1)}, bf16[32,32,128]{2,1,0:T(8,128)(2,1)S(1)}, u32[]{:S(2)}, u32[]{:S(2)}) %collective-permute-start.9) | collective-permute-done | bytes 262176 | tf_op jit(solution)/shard_map/ppermute | solution.py:110
  11.7 0.1 collective-permute-start.10
  11.8 0.0 collective-permute-done.8
  11.8 2.7 %collective-permute-start.11 = (bf16[16,32,128]{2,1,0:T(8,128)(2,1)S(1)}, bf16[16,32,128]{2,1,0:T(8,128)(2,1)S(1)}, u32[]{:S(2)}, u32[]{:S(2)}) collective-permute-start(bf16[16,32,128]{2,1,0:T(8,128)(2,1)S(1)} %slice.47), channel_id=1, source_target_pairs={{0,96},{8,104},{16,112},{24,120},{32,0},{40,8},{48,16},{56,24},{64... | collective-permute-start | bytes 393224 | tf_op jit(solution)/shard_map/ppermute | solution.py:115
  14.5 0.7 collective-permute-done.1
  15.2 1.0 collective-permute-start.2
  16.2 0.0 collective-permute-done
  16.2 2.2 %collective-permute-start.3 = (bf16[16,32,128]{2,1,0:T(8,128)(2,1)S(1)}, bf16[16,32,128]{2,1,0:T(8,128)(2,1)S(1)}, u32[]{:S(2)}, u32[]{:S(2)}) collective-permute-start(bf16[16,32,128]{2,1,0:T(8,128)(2,1)S(1)} %slice.42), channel_id=1, source_target_pairs={{0,24},{8,0},{16,8},{24,16},{32,56},{40,32},{48,40},{56,48},{64,88... | collective-permute-start | bytes 393224 | tf_op jit(solution)/shard_map/ppermute | solution.py:115
  18.4 0.0 collective-permute-done.10
  18.4 0.0 collective-permute-done.11
  18.4 0.1 pad_maximum_fusion.1
  18.6 0.1 collective-permute-start.13
  18.7 2.7 %collective-permute-start.12 = (bf16[4,32,32,128]{3,2,1,0:T(8,128)(2,1)S(1)}, bf16[4,32,32,128]{3,2,1,0:T(8,128)(2,1)S(1)}, u32[]{:S(2)}, u32[]{:S(2)}) collective-permute-start(bf16[4,32,32,128]{3,2,1,0:T(8,128)(2,1)S(1)} %pad_maximum_fusion.1), channel_id=1, source_target_pairs={{0,24},{8,0},{16,8},{24,16},{32,56},{40,32},{48,40},{56,48},{64,88... | collective-permute-start | bytes 3145736 | tf_op jit(solution)/shard_map/ppermute | solution.py:111
  21.3 0.0 collective-permute-done.2
  21.3 0.0 collective-permute-done.3
  21.4 0.0 copy-start.8
  21.4 0.1 pad_maximum_fusion
  21.5 0.1 collective-permute-start.5
  21.6 2.7 %collective-permute-start.4 = (bf16[4,32,32,128]{3,2,1,0:T(8,128)(2,1)S(1)}, bf16[4,32,32,128]{3,2,1,0:T(8,128)(2,1)S(1)}, u32[]{:S(2)}, u32[]{:S(2)}) collective-permute-start(bf16[4,32,32,128]{3,2,1,0:T(8,128)(2,1)S(1)} %pad_maximum_fusion), channel_id=1, source_target_pairs={{0,96},{8,104},{16,112},{24,120},{32,0},{40,8},{48,16},{56,24},{64... | collective-permute-start | bytes 3145736 | tf_op jit(solution)/shard_map/ppermute | solution.py:111
  24.3 19.1 %collective-permute-done.13 = bf16[4,32,32,128]{3,2,1,0:T(8,128)(2,1)S(1)} collective-permute-done((bf16[4,32,32,128]{3,2,1,0:T(8,128)(2,1)S(1)}, bf16[4,32,32,128]{3,2,1,0:T(8,128)(2,1)S(1)}, u32[]{:S(2)}, u32[]{:S(2)}) %collective-permute-start.13) | collective-permute-done | bytes 1048608 | tf_op jit(solution)/shard_map/ppermute | solution.py:110
  43.4 1.0 slice.48
  44.3 0.2 collective-permute-start.14
  44.5 0.0 collective-permute-done.12
  44.5 0.9 slice.49
  45.4 2.5 %collective-permute-start.15 = (bf16[2,32,32,128]{3,2,1,0:T(8,128)(2,1)}, bf16[2,32,32,128]{3,2,1,0:T(8,128)(2,1)}, u32[]{:S(2)}, u32[]{:S(2)}) collective-permute-start(bf16[2,32,32,128]{3,2,1,0:T(8,128)(2,1)} %slice.49), channel_id=1, source_target_pairs={{0,24},{8,0},{16,8},{24,16},{32,56},{40,32},{48,40},{56,48},{64,88... | collective-permute-start | bytes 1572872 | tf_op jit(solution)/shard_map/ppermute | solution.py:115
  47.9 0.0 collective-permute-done.5
  47.9 0.9 slice.43
  48.8 0.0 collective-permute-start.6
  48.8 0.9 slice.44
  49.8 2.7 %collective-permute-start.7 = (bf16[2,32,32,128]{3,2,1,0:T(8,128)(2,1)}, bf16[2,32,32,128]{3,2,1,0:T(8,128)(2,1)}, u32[]{:S(2)}, u32[]{:S(2)}) collective-permute-start(bf16[2,32,32,128]{3,2,1,0:T(8,128)(2,1)} %slice.44), channel_id=1, source_target_pairs={{0,96},{8,104},{16,112},{24,120},{32,0},{40,8},{48,16},{56,24},{64... | collective-permute-start | bytes 1572872 | tf_op jit(solution)/shard_map/ppermute | solution.py:115
  52.4 1.3 %fusion.6 = (s32[512]{0:T(512)}, s32[512]{0:T(512)S(1)}, s32[512]{0:T(512)S(1)}) fusion(s32[512]{0:T(512)} %param.9, s32[512]{0:T(512)} %param.11, s32[]{:T(128)S(6)} %select_n.49, s32[]{:T(128)S(6)} %select_n.52), kind=kLoop, calls=%fused_computation.27 | loop fusion | flops 37888 | bytes 10248 | tf_op jit(solution)/shard_map/add | solution.py:145
  53.7 1.3 %multiply_add_fusion.source_ref = s32[512]{0:T(512)} fusion(s32[512]{0:T(512)} %param.11, s32[512]{0:T(512)S(1)} %get-tuple-element.4, s32[512]{0:T(512)S(1)} %get-tuple-element.3), kind=kLoop, calls=%fused_computation.29 | loop fusion | flops 6144 | bytes 8192 | tf_op jit(solution)/shard_map/add | solution.py:144
  55.0 1.6 %collective-permute-done.14 = bf16[2,32,32,128]{3,2,1,0:T(8,128)(2,1)} collective-permute-done((bf16[2,32,32,128]{3,2,1,0:T(8,128)(2,1)}, bf16[2,32,32,128]{3,2,1,0:T(8,128)(2,1)}, u32[]{:S(2)}, u32[]{:S(2)}) %collective-permute-start.14) | collective-permute-done | bytes 524320 | tf_op jit(solution)/shard_map/ppermute | solution.py:114
  56.6 0.2 collective-permute-done.15
  56.8 3.7 %collective-permute-done.6 = bf16[2,32,32,128]{3,2,1,0:T(8,128)(2,1)} collective-permute-done((bf16[2,32,32,128]{3,2,1,0:T(8,128)(2,1)}, bf16[2,32,32,128]{3,2,1,0:T(8,128)(2,1)}, u32[]{:S(2)}, u32[]{:S(2)}) %collective-permute-start.6) | collective-permute-done | bytes 524320 | tf_op jit(solution)/shard_map/ppermute | solution.py:114
  60.5 0.0 collective-permute-done.7
  60.6 22.9 %shard_map.86 = f32[16,8,2,4,128]{4,3,2,1,0:T(4,128)} custom-call(s32[512]{0:T(512)} %multiply_add_fusion.source_ref, s32[512]{0:T(512)} %get-tuple-element.2.index_ref, s32[512]{0:T(512)} %obs_ref.1, bf16[128,32,128]{2,1,0:T(8,128)(2,1)} %bitcast.25, bf16[128,32,128]{2,1,0:T(8,128)(2,1)} %bitcast.29, bf16[64,32,128]{2,1,0:T(8,128)(2,1)} %bitcast.6.refs_2_, ...), custom_call_target="tpu_custom_call" | custom-call | tf_op jit(solution)/shard_map/pallas_call | solution.py:87
  83.5 25.8 %all_to_all.5 = f32[128,2,4,128]{3,2,1,0:T(4,128)S(1)} all-to-all(f32[128,2,4,128]{3,2,1,0:T(4,128)} %bitcast.30), channel_id=1, replica_groups=mesh['grp'=16,'lag'=8] {'grp','lag'}, dimensions={0} | all-to-all | bytes 1048576 | tf_op jit(solution)/shard_map/all_to_all | solution.py:148
  109.3 0.1 reduce_sum.9
  109.4 0.0 copy-start.7
  109.4 0.7 fusion.7
  (22 shorter events, 0.1 us)
Async XLA Ops:
  0.6 108.8 %copy-start = (bf16[2,128,128]{2,1,0:T(8,128)(2,1)S(1)}, bf16[2,128,128]{2,1,0:T(8,128)(2,1)}, u32[]{:S(2)}) copy-start(bf16[2,128,128]{2,1,0:T(8,128)(2,1)} %param.13) | copy-start | bytes 196612
  2.2 9.5 %collective-permute-start.9 = (bf16[32,32,128]{2,1,0:T(8,128)(2,1)S(1)}, bf16[32,32,128]{2,1,0:T(8,128)(2,1)S(1)}, u32[]{:S(2)}, u32[]{:S(2)}) collective-permute-start(bf16[32,32,128]{2,1,0:T(8,128)(2,1)S(1)} %get-tuple-element.7), channel_id=1, source_target_pairs={{0,32},{8,40},{16,48},{24,56},{32,64},{40,72},{48,80},{56,88},{64,... | collective-permute-start | bytes 786440 | tf_op jit(solution)/shard_map/ppermute | solution.py:110
  4.4 7.4 %collective-permute-start.8 = (bf16[32,32,128]{2,1,0:T(8,128)(2,1)S(1)}, bf16[32,32,128]{2,1,0:T(8,128)(2,1)S(1)}, u32[]{:S(2)}, u32[]{:S(2)}) collective-permute-start(bf16[32,32,128]{2,1,0:T(8,128)(2,1)S(1)} %get-tuple-element.7), channel_id=1, source_target_pairs={{0,96},{8,104},{16,112},{24,120},{32,0},{40,8},{48,16},{56,24},{64... | collective-permute-start | bytes 786440 | tf_op jit(solution)/shard_map/ppermute | solution.py:111
  5.9 9.3 %collective-permute-start.1 = (bf16[32,32,128]{2,1,0:T(8,128)(2,1)S(1)}, bf16[32,32,128]{2,1,0:T(8,128)(2,1)S(1)}, u32[]{:S(2)}, u32[]{:S(2)}) collective-permute-start(bf16[32,32,128]{2,1,0:T(8,128)(2,1)S(1)} %get-tuple-element.6), channel_id=1, source_target_pairs={{0,8},{8,16},{16,24},{24,0},{32,40},{40,48},{48,56},{56,32},{64,72... | collective-permute-start | bytes 786440 | tf_op jit(solution)/shard_map/ppermute | solution.py:110
  7.5 8.6 %collective-permute-start = (bf16[32,32,128]{2,1,0:T(8,128)(2,1)S(1)}, bf16[32,32,128]{2,1,0:T(8,128)(2,1)S(1)}, u32[]{:S(2)}, u32[]{:S(2)}) collective-permute-start(bf16[32,32,128]{2,1,0:T(8,128)(2,1)S(1)} %get-tuple-element.6), channel_id=1, source_target_pairs={{0,24},{8,0},{16,8},{24,16},{32,56},{40,32},{48,40},{56,48},{64,88... | collective-permute-start | bytes 786440 | tf_op jit(solution)/shard_map/ppermute | solution.py:111
  11.7 6.7 %collective-permute-start.10 = (bf16[16,32,128]{2,1,0:T(8,128)(2,1)S(1)}, bf16[16,32,128]{2,1,0:T(8,128)(2,1)S(1)}, u32[]{:S(2)}, u32[]{:S(2)}) collective-permute-start(bf16[16,32,128]{2,1,0:T(8,128)(2,1)S(1)} %slice.46), channel_id=1, source_target_pairs={{0,32},{8,40},{16,48},{24,56},{32,64},{40,72},{48,80},{56,88},{64,... | collective-permute-start | bytes 393224 | tf_op jit(solution)/shard_map/ppermute | solution.py:114
  11.8 6.6 %collective-permute-start.11 = (bf16[16,32,128]{2,1,0:T(8,128)(2,1)S(1)}, bf16[16,32,128]{2,1,0:T(8,128)(2,1)S(1)}, u32[]{:S(2)}, u32[]{:S(2)}) collective-permute-start(bf16[16,32,128]{2,1,0:T(8,128)(2,1)S(1)} %slice.47), channel_id=1, source_target_pairs={{0,96},{8,104},{16,112},{24,120},{32,0},{40,8},{48,16},{56,24},{64... | collective-permute-start | bytes 393224 | tf_op jit(solution)/shard_map/ppermute | solution.py:115
  15.2 6.1 %collective-permute-start.2 = (bf16[16,32,128]{2,1,0:T(8,128)(2,1)S(1)}, bf16[16,32,128]{2,1,0:T(8,128)(2,1)S(1)}, u32[]{:S(2)}, u32[]{:S(2)}) collective-permute-start(bf16[16,32,128]{2,1,0:T(8,128)(2,1)S(1)} %slice.41), channel_id=1, source_target_pairs={{0,8},{8,16},{16,24},{24,0},{32,40},{40,48},{48,56},{56,32},{64,72... | collective-permute-start | bytes 393224 | tf_op jit(solution)/shard_map/ppermute | solution.py:114
  16.2 5.2 %collective-permute-start.3 = (bf16[16,32,128]{2,1,0:T(8,128)(2,1)S(1)}, bf16[16,32,128]{2,1,0:T(8,128)(2,1)S(1)}, u32[]{:S(2)}, u32[]{:S(2)}) collective-permute-start(bf16[16,32,128]{2,1,0:T(8,128)(2,1)S(1)} %slice.42), channel_id=1, source_target_pairs={{0,24},{8,0},{16,8},{24,16},{32,56},{40,32},{48,40},{56,48},{64,88... | collective-permute-start | bytes 393224 | tf_op jit(solution)/shard_map/ppermute | solution.py:115
  18.6 42.0 %copy-start.1 = (bf16[4,32,32,128]{3,2,1,0:T(8,128)(2,1)}, bf16[4,32,32,128]{3,2,1,0:T(8,128)(2,1)S(1)}, u32[]{:S(2)}) copy-start(bf16[4,32,32,128]{3,2,1,0:T(8,128)(2,1)S(1)} %pad_maximum_fusion.1) | copy-start | bytes 3145732
  18.6 24.8 %collective-permute-start.13 = (bf16[4,32,32,128]{3,2,1,0:T(8,128)(2,1)S(1)}, bf16[4,32,32,128]{3,2,1,0:T(8,128)(2,1)S(1)}, u32[]{:S(2)}, u32[]{:S(2)}) collective-permute-start(bf16[4,32,32,128]{3,2,1,0:T(8,128)(2,1)S(1)} %pad_maximum_fusion.1), channel_id=1, source_target_pairs={{0,8},{8,16},{16,24},{24,0},{32,40},{40,48},{48,56},{56,32},{64,72... | collective-permute-start | bytes 3145736 | tf_op jit(solution)/shard_map/ppermute | solution.py:110
  18.7 25.8 %collective-permute-start.12 = (bf16[4,32,32,128]{3,2,1,0:T(8,128)(2,1)S(1)}, bf16[4,32,32,128]{3,2,1,0:T(8,128)(2,1)S(1)}, u32[]{:S(2)}, u32[]{:S(2)}) collective-permute-start(bf16[4,32,32,128]{3,2,1,0:T(8,128)(2,1)S(1)} %pad_maximum_fusion.1), channel_id=1, source_target_pairs={{0,24},{8,0},{16,8},{24,16},{32,56},{40,32},{48,40},{56,48},{64,88... | collective-permute-start | bytes 3145736 | tf_op jit(solution)/shard_map/ppermute | solution.py:111
  21.4 88.0 %copy-start.8 = (f32[2,4,128]{2,1,0:T(4,128)S(1)}, f32[2,4,128]{2,1,0:T(4,128)}, u32[]{:S(2)}) copy-start(f32[2,4,128]{2,1,0:T(4,128)} %param.12) | copy-start | bytes 12292
  21.5 39.0 %copy-start.2 = (bf16[4,32,32,128]{3,2,1,0:T(8,128)(2,1)}, bf16[4,32,32,128]{3,2,1,0:T(8,128)(2,1)S(1)}, u32[]{:S(2)}) copy-start(bf16[4,32,32,128]{3,2,1,0:T(8,128)(2,1)S(1)} %pad_maximum_fusion) | copy-start | bytes 3145732
  21.5 26.4 %collective-permute-start.5 = (bf16[4,32,32,128]{3,2,1,0:T(8,128)(2,1)S(1)}, bf16[4,32,32,128]{3,2,1,0:T(8,128)(2,1)S(1)}, u32[]{:S(2)}, u32[]{:S(2)}) collective-permute-start(bf16[4,32,32,128]{3,2,1,0:T(8,128)(2,1)S(1)} %pad_maximum_fusion), channel_id=1, source_target_pairs={{0,32},{8,40},{16,48},{24,56},{32,64},{40,72},{48,80},{56,88},{64,... | collective-permute-start | bytes 3145736 | tf_op jit(solution)/shard_map/ppermute | solution.py:110
  21.6 27.2 %collective-permute-start.4 = (bf16[4,32,32,128]{3,2,1,0:T(8,128)(2,1)S(1)}, bf16[4,32,32,128]{3,2,1,0:T(8,128)(2,1)S(1)}, u32[]{:S(2)}, u32[]{:S(2)}) collective-permute-start(bf16[4,32,32,128]{3,2,1,0:T(8,128)(2,1)S(1)} %pad_maximum_fusion), channel_id=1, source_target_pairs={{0,96},{8,104},{16,112},{24,120},{32,0},{40,8},{48,16},{56,24},{64... | collective-permute-start | bytes 3145736 | tf_op jit(solution)/shard_map/ppermute | solution.py:111
  43.4 17.2 %copy-start.3 = (bf16[4,32,32,128]{3,2,1,0:T(8,128)(2,1)}, bf16[4,32,32,128]{3,2,1,0:T(8,128)(2,1)S(1)}, u32[]{:S(2)}) copy-start(bf16[4,32,32,128]{3,2,1,0:T(8,128)(2,1)S(1)} %collective-permute-done.13) | copy-start | bytes 3145732
  44.3 12.3 %collective-permute-start.14 = (bf16[2,32,32,128]{3,2,1,0:T(8,128)(2,1)}, bf16[2,32,32,128]{3,2,1,0:T(8,128)(2,1)}, u32[]{:S(2)}, u32[]{:S(2)}) collective-permute-start(bf16[2,32,32,128]{3,2,1,0:T(8,128)(2,1)} %slice.48), channel_id=1, source_target_pairs={{0,8},{8,16},{16,24},{24,0},{32,40},{40,48},{48,56},{56,32},{64,72... | collective-permute-start | bytes 1572872 | tf_op jit(solution)/shard_map/ppermute | solution.py:114
  44.5 4.3 %copy-start.4 = (bf16[4,32,32,128]{3,2,1,0:T(8,128)(2,1)}, bf16[4,32,32,128]{3,2,1,0:T(8,128)(2,1)S(1)}, u32[]{:S(2)}) copy-start(bf16[4,32,32,128]{3,2,1,0:T(8,128)(2,1)S(1)} %collective-permute-done.12) | copy-start | bytes 3145732
  45.4 11.4 %collective-permute-start.15 = (bf16[2,32,32,128]{3,2,1,0:T(8,128)(2,1)}, bf16[2,32,32,128]{3,2,1,0:T(8,128)(2,1)}, u32[]{:S(2)}, u32[]{:S(2)}) collective-permute-start(bf16[2,32,32,128]{3,2,1,0:T(8,128)(2,1)} %slice.49), channel_id=1, source_target_pairs={{0,24},{8,0},{16,8},{24,16},{32,56},{40,32},{48,40},{56,48},{64,88... | collective-permute-start | bytes 1572872 | tf_op jit(solution)/shard_map/ppermute | solution.py:115
  47.9 1.8 %copy-start.5 = (bf16[4,32,32,128]{3,2,1,0:T(8,128)(2,1)}, bf16[4,32,32,128]{3,2,1,0:T(8,128)(2,1)S(1)}, u32[]{:S(2)}) copy-start(bf16[4,32,32,128]{3,2,1,0:T(8,128)(2,1)S(1)} %collective-permute-done.5) | copy-start | bytes 3145732
  48.8 11.7 %collective-permute-start.6 = (bf16[2,32,32,128]{3,2,1,0:T(8,128)(2,1)}, bf16[2,32,32,128]{3,2,1,0:T(8,128)(2,1)}, u32[]{:S(2)}, u32[]{:S(2)}) collective-permute-start(bf16[2,32,32,128]{3,2,1,0:T(8,128)(2,1)} %slice.43), channel_id=1, source_target_pairs={{0,32},{8,40},{16,48},{24,56},{32,64},{40,72},{48,80},{56,88},{64,... | collective-permute-start | bytes 1572872 | tf_op jit(solution)/shard_map/ppermute | solution.py:114
  48.8 3.6 %copy-start.6 = (bf16[4,32,32,128]{3,2,1,0:T(8,128)(2,1)}, bf16[4,32,32,128]{3,2,1,0:T(8,128)(2,1)S(1)}, u32[]{:S(2)}) copy-start(bf16[4,32,32,128]{3,2,1,0:T(8,128)(2,1)S(1)} %collective-permute-done.4) | copy-start | bytes 3145732
  49.8 10.8 %collective-permute-start.7 = (bf16[2,32,32,128]{3,2,1,0:T(8,128)(2,1)}, bf16[2,32,32,128]{3,2,1,0:T(8,128)(2,1)}, u32[]{:S(2)}, u32[]{:S(2)}) collective-permute-start(bf16[2,32,32,128]{3,2,1,0:T(8,128)(2,1)} %slice.44), channel_id=1, source_target_pairs={{0,96},{8,104},{16,112},{24,120},{32,0},{40,8},{48,16},{56,24},{64... | collective-permute-start | bytes 1572872 | tf_op jit(solution)/shard_map/ppermute | solution.py:115
  109.4 0.8 copy-start.7

commit v13 on v12

--- a/solution.py
+++ b/solution.py
@@ -103,13 +103,16 @@
     return pairs
 
 
-def ring_gather(x, rows, cols, along_cols, pieces=False):
+def ring_gather(x, rows, cols, along_cols, pieces=False, direct=False):
     n = cols if along_cols else rows
     plus = shift_pairs(rows, cols, 1, along_cols)
     minus = shift_pairs(rows, cols, -1, along_cols)
     from_behind = lax.ppermute(x, "grp", plus)
     from_ahead = lax.ppermute(x, "grp", minus)
     assert n == 4
+    if direct:
+        far = lax.ppermute(x, "grp", shift_pairs(rows, cols, 2, along_cols))
+        return jnp.stack([x, from_ahead, far, from_behind])
     half = x.shape[0] // 2
     far_a = lax.ppermute(from_behind[:half], "grp", plus)
     far_b = lax.ppermute(from_ahead[half:], "grp", minus)
@@ -129,8 +132,8 @@
     rows = 4
     cols = n_grp // rows
     assert lag_count == 2 and rows * cols == n_grp
-    first = ring_gather(ring_gather(hist16[0], rows, cols, True), rows, cols, False, pieces=True)
-    second = ring_gather(ring_gather(hist16[1], rows, cols, False), rows, cols, True, pieces=True)
+    first = ring_gather(ring_gather(hist16[0], rows, cols, True, direct=True), rows, cols, False, pieces=True)
+    second = ring_gather(ring_gather(hist16[1], rows, cols, False, direct=True), rows, cols, True, pieces=True)
     tables = [p.reshape(-1, angles, width) for p in first + second]
     me = lax.axis_index("grp")
     owner = tile_src // src_dev

time: 111 us -> 114 us (1.027)
  waiting for transfers between devices: 27.3 us -> 33 us
  blocking collectives: 25.8 us -> 23 us
    ppermute x0 -> x2, starting transfers between devices: none -> 5.92 us  [ring_gather(): far = lax.ppermute(x, 'grp', shift_pairs(rows, cols, 2, along_cols))]
    ppermute x4 -> x2, starting transfers between devices: 10.1 us -> 5.06 us  [ring_gather(): far_b = lax.ppermute(from_ahead[half:], 'grp', minus)]
    ppermute x0 -> x2, waiting for transfers between devices: none -> 4.02 us  [ring_gather(): far = lax.ppermute(x, 'grp', shift_pairs(rows, cols, 2, along_cols))]
    all_to_all x1, blocking collectives: 25.8 us -> 23 us  [body(): received = lax.all_to_all(partial, ('grp', 'lag'), 0, 0, tiled=True)]
    ppermute x4 -> x2, waiting for transfers between devices: 5.34 us -> 7.56 us  [ring_gather(): far_a = lax.ppermute(from_behind[:half], 'grp', plus)]
    ppermute x4, starting transfers between devices: 3.98 us -> 6 us  [ring_gather(): from_behind = lax.ppermute(x, 'grp', plus)]
  transfers between devices with their start and end apart: 16 -> 14, of which waited for: 6 -> 5; matrix products, arithmetic and copies ran while one was open for 6% -> 6% of each run, Pallas kernels for 0% -> 0%
where the time goes in v13:
time: 114 us
  waiting for transfers between devices  33 us (29%)
  starting transfers between devices  25.2 us (22%)
  blocking collectives  23 us (20%)
  Pallas kernels  22.9 us (20%)
  other arithmetic  4.33 us (4%)
  local copies, waits for them, and re-layouts  3.86 us (3%)
    all_to_all x1, blocking collectives, body(): received = lax.all_to_all(partial, ('grp', 'lag'), 0, 0, tiled=True)  23 us
    pallas_call x1, Pallas kernels, field_partial(): pl.pallas_call(field_kernel, grid_spec=grid_spec, out_shape=jax.ShapeDtyp...  22.9 us
    ppermute x4, waiting for transfers between devices, ring_gather(): from_behind = lax.ppermute(x, 'grp', plus)  21.4 us
    ppermute x4, starting transfers between devices, ring_gather(): from_ahead = lax.ppermute(x, 'grp', minus)  7.9 us
    ppermute x2, waiting for transfers between devices, ring_gather(): far_a = lax.ppermute(from_behind[:half], 'grp', plus)  7.56 us
    ppermute x4, starting transfers between devices, ring_gather(): from_behind = lax.ppermute(x, 'grp', plus)  6 us
    ppermute x2, starting transfers between devices, ring_gather(): far = lax.ppermute(x, 'grp', shift_pairs(rows, cols, 2, along_cols))  5.92 us
    ppermute x2, starting transfers between devices, ring_gather(): far_b = lax.ppermute(from_ahead[half:], 'grp', minus)  5.06 us
  transfers between devices with their start and end apart: 14, of which 5 were waited for; matrix products, arithmetic and copies ran while one was open for 6% of the time, Pallas kernels for 0%

profile of v13, /device:TPU:1, one launch (start us, length us, event | category | flops | bytes accessed | tf_op | source)
XLA Modules:
  0.0 113.8 jit_solution(11819366939997759439)
XLA Ops:
  0.6 0.0 copy-start
  0.6 1.3 %convert_element_type.11 = bf16[2,32,32,128]{3,2,1,0:T(8,128)(2,1)S(1)} convert(f32[2,32,32,128]{3,2,1,0:T(8,128)} %param.7) | non-fusion elementwise | flops 262144 | bytes 1572864 | tf_op jit(solution)/shard_map/convert_element_type | solution.py:130
  2.0 0.2 fusion.10
  2.2 2.2 %collective-permute-start.9 = (bf16[32,32,128]{2,1,0:T(8,128)(2,1)S(1)}, bf16[32,32,128]{2,1,0:T(8,128)(2,1)S(1)}, u32[]{:S(2)}, u32[]{:S(2)}) collective-permute-start(bf16[32,32,128]{2,1,0:T(8,128)(2,1)S(1)} %get-tuple-element.7), channel_id=1, source_target_pairs={{0,32},{8,40},{16,48},{24,56},{32,64},{40,72},{48,80},{56,88},{64,... | collective-permute-start | bytes 786440 | tf_op jit(solution)/shard_map/ppermute | solution.py:110
  4.4 2.6 %collective-permute-start.8 = (bf16[32,32,128]{2,1,0:T(8,128)(2,1)S(1)}, bf16[32,32,128]{2,1,0:T(8,128)(2,1)S(1)}, u32[]{:S(2)}, u32[]{:S(2)}) collective-permute-start(bf16[32,32,128]{2,1,0:T(8,128)(2,1)S(1)} %get-tuple-element.7), channel_id=1, source_target_pairs={{0,64},{8,72},{16,80},{24,88},{32,96},{40,104},{48,112},{56,120},{... | collective-permute-start | bytes 786440 | tf_op jit(solution)/shard_map/ppermute | solution.py:114
  7.0 1.1 collective-permute-start.7
  8.0 1.6 %collective-permute-start.2 = (bf16[32,32,128]{2,1,0:T(8,128)(2,1)S(1)}, bf16[32,32,128]{2,1,0:T(8,128)(2,1)S(1)}, u32[]{:S(2)}, u32[]{:S(2)}) collective-permute-start(bf16[32,32,128]{2,1,0:T(8,128)(2,1)S(1)} %get-tuple-element.6), channel_id=1, source_target_pairs={{0,8},{8,16},{16,24},{24,0},{32,40},{40,48},{48,56},{56,32},{64,72... | collective-permute-start | bytes 786440 | tf_op jit(solution)/shard_map/ppermute | solution.py:110
  9.7 3.3 %collective-permute-start.1 = (bf16[32,32,128]{2,1,0:T(8,128)(2,1)S(1)}, bf16[32,32,128]{2,1,0:T(8,128)(2,1)S(1)}, u32[]{:S(2)}, u32[]{:S(2)}) collective-permute-start(bf16[32,32,128]{2,1,0:T(8,128)(2,1)S(1)} %get-tuple-element.6), channel_id=1, source_target_pairs={{0,16},{8,24},{16,0},{24,8},{32,48},{40,56},{48,32},{56,40},{64,80... | collective-permute-start | bytes 786440 | tf_op jit(solution)/shard_map/ppermute | solution.py:114
  13.0 0.0 collective-permute-done.9
  13.0 2.3 %collective-permute-start = (bf16[32,32,128]{2,1,0:T(8,128)(2,1)S(1)}, bf16[32,32,128]{2,1,0:T(8,128)(2,1)S(1)}, u32[]{:S(2)}, u32[]{:S(2)}) collective-permute-start(bf16[32,32,128]{2,1,0:T(8,128)(2,1)S(1)} %get-tuple-element.6), channel_id=1, source_target_pairs={{0,24},{8,0},{16,8},{24,16},{32,56},{40,32},{48,40},{56,48},{64,88... | collective-permute-start | bytes 786440 | tf_op jit(solution)/shard_map/ppermute | solution.py:111
  15.3 3.0 %collective-permute-done.8 = bf16[32,32,128]{2,1,0:T(8,128)(2,1)S(1)} collective-permute-done((bf16[32,32,128]{2,1,0:T(8,128)(2,1)S(1)}, bf16[32,32,128]{2,1,0:T(8,128)(2,1)S(1)}, u32[]{:S(2)}, u32[]{:S(2)}) %collective-permute-start.8) | collective-permute-done | bytes 262176 | tf_op jit(solution)/shard_map/ppermute | solution.py:114
  18.3 0.0 collective-permute-done.7
  18.3 0.1 pad_maximum_fusion.1
  18.4 0.0 copy-start.1
  18.5 1.7 %collective-permute-start.11 = (bf16[4,32,32,128]{3,2,1,0:T(8,128)(2,1)S(1)}, bf16[4,32,32,128]{3,2,1,0:T(8,128)(2,1)S(1)}, u32[]{:S(2)}, u32[]{:S(2)}) collective-permute-start(bf16[4,32,32,128]{3,2,1,0:T(8,128)(2,1)S(1)} %pad_maximum_fusion.1), channel_id=1, source_target_pairs={{0,8},{8,16},{16,24},{24,0},{32,40},{40,48},{48,56},{56,32},{64,72... | collective-permute-start | bytes 3145736 | tf_op jit(solution)/shard_map/ppermute | solution.py:110
  20.2 2.2 %collective-permute-start.10 = (bf16[4,32,32,128]{3,2,1,0:T(8,128)(2,1)S(1)}, bf16[4,32,32,128]{3,2,1,0:T(8,128)(2,1)S(1)}, u32[]{:S(2)}, u32[]{:S(2)}) collective-permute-start(bf16[4,32,32,128]{3,2,1,0:T(8,128)(2,1)S(1)} %pad_maximum_fusion.1), channel_id=1, source_target_pairs={{0,24},{8,0},{16,8},{24,16},{32,56},{40,32},{48,40},{56,48},{64,88... | collective-permute-start | bytes 3145736 | tf_op jit(solution)/shard_map/ppermute | solution.py:111
  22.4 0.0 collective-permute-done.2
  22.4 1.1 collective-permute-done.1
  23.4 0.0 collective-permute-done
  23.4 0.1 pad_maximum_fusion
  23.6 0.5 collective-permute-start.4
  24.0 2.3 %collective-permute-start.3 = (bf16[4,32,32,128]{3,2,1,0:T(8,128)(2,1)S(1)}, bf16[4,32,32,128]{3,2,1,0:T(8,128)(2,1)S(1)}, u32[]{:S(2)}, u32[]{:S(2)}) collective-permute-start(bf16[4,32,32,128]{3,2,1,0:T(8,128)(2,1)S(1)} %pad_maximum_fusion), channel_id=1, source_target_pairs={{0,96},{8,104},{16,112},{24,120},{32,0},{40,8},{48,16},{56,24},{64... | collective-permute-start | bytes 3145736 | tf_op jit(solution)/shard_map/ppermute | solution.py:111
  26.3 21.4 %collective-permute-done.11 = bf16[4,32,32,128]{3,2,1,0:T(8,128)(2,1)S(1)} collective-permute-done((bf16[4,32,32,128]{3,2,1,0:T(8,128)(2,1)S(1)}, bf16[4,32,32,128]{3,2,1,0:T(8,128)(2,1)S(1)}, u32[]{:S(2)}, u32[]{:S(2)}) %collective-permute-start.11) | collective-permute-done | bytes 1048608 | tf_op jit(solution)/shard_map/ppermute | solution.py:110
  47.7 1.0 slice.28
  48.7 0.0 collective-permute-start.12
  48.7 0.0 collective-permute-done.10
  48.7 0.9 slice.29
  49.6 2.7 %collective-permute-start.13 = (bf16[2,32,32,128]{3,2,1,0:T(8,128)(2,1)}, bf16[2,32,32,128]{3,2,1,0:T(8,128)(2,1)}, u32[]{:S(2)}, u32[]{:S(2)}) collective-permute-start(bf16[2,32,32,128]{3,2,1,0:T(8,128)(2,1)} %slice.29), channel_id=1, source_target_pairs={{0,24},{8,0},{16,8},{24,16},{32,56},{40,32},{48,40},{56,48},{64,88... | collective-permute-start | bytes 1572872 | tf_op jit(solution)/shard_map/ppermute | solution.py:118
  52.2 0.0 collective-permute-done.4
  52.2 0.9 slice.25
  53.1 0.3 collective-permute-start.5
  53.4 0.0 collective-permute-done.3
  53.4 0.9 slice.26
  54.3 2.4 %collective-permute-start.6 = (bf16[2,32,32,128]{3,2,1,0:T(8,128)(2,1)}, bf16[2,32,32,128]{3,2,1,0:T(8,128)(2,1)}, u32[]{:S(2)}, u32[]{:S(2)}) collective-permute-start(bf16[2,32,32,128]{3,2,1,0:T(8,128)(2,1)} %slice.26), channel_id=1, source_target_pairs={{0,96},{8,104},{16,112},{24,120},{32,0},{40,8},{48,16},{56,24},{64... | collective-permute-start | bytes 1572872 | tf_op jit(solution)/shard_map/ppermute | solution.py:118
  56.7 0.0 copy-done.6
  56.7 1.3 %fusion.6 = (s32[512]{0:T(512)}, s32[512]{0:T(512)S(1)}, s32[512]{0:T(512)S(1)}) fusion(s32[512]{0:T(512)} %param.9, s32[512]{0:T(512)} %param.11, s32[]{:T(128)S(6)} %select_n.49, s32[]{:T(128)S(6)} %select_n.52), kind=kLoop, calls=%fused_computation.25 | loop fusion | flops 37888 | bytes 10248 | tf_op jit(solution)/shard_map/add | solution.py:148
  58.0 1.3 %multiply_add_fusion.source_ref = s32[512]{0:T(512)} fusion(s32[512]{0:T(512)} %param.11, s32[512]{0:T(512)S(1)} %get-tuple-element.4, s32[512]{0:T(512)S(1)} %get-tuple-element.3), kind=kLoop, calls=%fused_computation.27 | loop fusion | flops 6144 | bytes 8192 | tf_op jit(solution)/shard_map/add | solution.py:147
  59.3 3.7 %collective-permute-done.12 = bf16[2,32,32,128]{3,2,1,0:T(8,128)(2,1)} collective-permute-done((bf16[2,32,32,128]{3,2,1,0:T(8,128)(2,1)}, bf16[2,32,32,128]{3,2,1,0:T(8,128)(2,1)}, u32[]{:S(2)}, u32[]{:S(2)}) %collective-permute-start.12) | collective-permute-done | bytes 524320 | tf_op jit(solution)/shard_map/ppermute | solution.py:117
  63.0 0.0 collective-permute-done.13
  63.0 3.9 %collective-permute-done.5 = bf16[2,32,32,128]{3,2,1,0:T(8,128)(2,1)} collective-permute-done((bf16[2,32,32,128]{3,2,1,0:T(8,128)(2,1)}, bf16[2,32,32,128]{3,2,1,0:T(8,128)(2,1)}, u32[]{:S(2)}, u32[]{:S(2)}) %collective-permute-start.5) | collective-permute-done | bytes 524320 | tf_op jit(solution)/shard_map/ppermute | solution.py:117
  66.9 0.0 collective-permute-done.6
  66.9 0.0 copy-done.1
  66.9 22.9 %shard_map.86 = f32[16,8,2,4,128]{4,3,2,1,0:T(4,128)} custom-call(s32[512]{0:T(512)} %multiply_add_fusion.source_ref, s32[512]{0:T(512)} %get-tuple-element.2.index_ref, s32[512]{0:T(512)} %obs_ref.1, bf16[128,32,128]{2,1,0:T(8,128)(2,1)} %bitcast.23, bf16[128,32,128]{2,1,0:T(8,128)(2,1)} %bitcast.27, bf16[64,32,128]{2,1,0:T(8,128)(2,1)} %bitcast.6.refs_2_, ...), custom_call_target="tpu_custom_call" | custom-call | tf_op jit(solution)/shard_map/pallas_call | solution.py:87
  89.8 23.0 %all_to_all.5 = f32[128,2,4,128]{3,2,1,0:T(4,128)S(1)} all-to-all(f32[128,2,4,128]{3,2,1,0:T(4,128)} %bitcast.28), channel_id=1, replica_groups=mesh['grp'=16,'lag'=8] {'grp','lag'}, dimensions={0} | all-to-all | bytes 1048576 | tf_op jit(solution)/shard_map/all_to_all | solution.py:151
  112.8 0.1 reduce_sum.9
  113.0 0.0 copy-start.7
  113.0 0.7 fusion.7
  113.8 0.0 copy-done.7
  (12 shorter events, 0.0 us)
Async XLA Ops:
  0.6 112.4 %copy-start = (bf16[2,128,128]{2,1,0:T(8,128)(2,1)S(1)}, bf16[2,128,128]{2,1,0:T(8,128)(2,1)}, u32[]{:S(2)}) copy-start(bf16[2,128,128]{2,1,0:T(8,128)(2,1)} %param.13) | copy-start | bytes 196612
  2.2 10.8 %collective-permute-start.9 = (bf16[32,32,128]{2,1,0:T(8,128)(2,1)S(1)}, bf16[32,32,128]{2,1,0:T(8,128)(2,1)S(1)}, u32[]{:S(2)}, u32[]{:S(2)}) collective-permute-start(bf16[32,32,128]{2,1,0:T(8,128)(2,1)S(1)} %get-tuple-element.7), channel_id=1, source_target_pairs={{0,32},{8,40},{16,48},{24,56},{32,64},{40,72},{48,80},{56,88},{64,... | collective-permute-start | bytes 786440 | tf_op jit(solution)/shard_map/ppermute | solution.py:110
  4.4 13.9 %collective-permute-start.8 = (bf16[32,32,128]{2,1,0:T(8,128)(2,1)S(1)}, bf16[32,32,128]{2,1,0:T(8,128)(2,1)S(1)}, u32[]{:S(2)}, u32[]{:S(2)}) collective-permute-start(bf16[32,32,128]{2,1,0:T(8,128)(2,1)S(1)} %get-tuple-element.7), channel_id=1, source_target_pairs={{0,64},{8,72},{16,80},{24,88},{32,96},{40,104},{48,112},{56,120},{... | collective-permute-start | bytes 786440 | tf_op jit(solution)/shard_map/ppermute | solution.py:114
  7.0 11.3 %collective-permute-start.7 = (bf16[32,32,128]{2,1,0:T(8,128)(2,1)S(1)}, bf16[32,32,128]{2,1,0:T(8,128)(2,1)S(1)}, u32[]{:S(2)}, u32[]{:S(2)}) collective-permute-start(bf16[32,32,128]{2,1,0:T(8,128)(2,1)S(1)} %get-tuple-element.7), channel_id=1, source_target_pairs={{0,96},{8,104},{16,112},{24,120},{32,0},{40,8},{48,16},{56,24},{64... | collective-permute-start | bytes 786440 | tf_op jit(solution)/shard_map/ppermute | solution.py:111
  8.0 14.3 %collective-permute-start.2 = (bf16[32,32,128]{2,1,0:T(8,128)(2,1)S(1)}, bf16[32,32,128]{2,1,0:T(8,128)(2,1)S(1)}, u32[]{:S(2)}, u32[]{:S(2)}) collective-permute-start(bf16[32,32,128]{2,1,0:T(8,128)(2,1)S(1)} %get-tuple-element.6), channel_id=1, source_target_pairs={{0,8},{8,16},{16,24},{24,0},{32,40},{40,48},{48,56},{56,32},{64,72... | collective-permute-start | bytes 786440 | tf_op jit(solution)/shard_map/ppermute | solution.py:110
  9.7 13.7 %collective-permute-start.1 = (bf16[32,32,128]{2,1,0:T(8,128)(2,1)S(1)}, bf16[32,32,128]{2,1,0:T(8,128)(2,1)S(1)}, u32[]{:S(2)}, u32[]{:S(2)}) collective-permute-start(bf16[32,32,128]{2,1,0:T(8,128)(2,1)S(1)} %get-tuple-element.6), channel_id=1, source_target_pairs={{0,16},{8,24},{16,0},{24,8},{32,48},{40,56},{48,32},{56,40},{64,80... | collective-permute-start | bytes 786440 | tf_op jit(solution)/shard_map/ppermute | solution.py:114
  13.0 10.4 %collective-permute-start = (bf16[32,32,128]{2,1,0:T(8,128)(2,1)S(1)}, bf16[32,32,128]{2,1,0:T(8,128)(2,1)S(1)}, u32[]{:S(2)}, u32[]{:S(2)}) collective-permute-start(bf16[32,32,128]{2,1,0:T(8,128)(2,1)S(1)} %get-tuple-element.6), channel_id=1, source_target_pairs={{0,24},{8,0},{16,8},{24,16},{32,56},{40,32},{48,40},{56,48},{64,88... | collective-permute-start | bytes 786440 | tf_op jit(solution)/shard_map/ppermute | solution.py:111
  18.4 48.4 %copy-start.1 = (bf16[4,32,32,128]{3,2,1,0:T(8,128)(2,1)}, bf16[4,32,32,128]{3,2,1,0:T(8,128)(2,1)S(1)}, u32[]{:S(2)}) copy-start(bf16[4,32,32,128]{3,2,1,0:T(8,128)(2,1)S(1)} %pad_maximum_fusion.1) | copy-start | bytes 3145732
  18.5 29.2 %collective-permute-start.11 = (bf16[4,32,32,128]{3,2,1,0:T(8,128)(2,1)S(1)}, bf16[4,32,32,128]{3,2,1,0:T(8,128)(2,1)S(1)}, u32[]{:S(2)}, u32[]{:S(2)}) collective-permute-start(bf16[4,32,32,128]{3,2,1,0:T(8,128)(2,1)S(1)} %pad_maximum_fusion.1), channel_id=1, source_target_pairs={{0,8},{8,16},{16,24},{24,0},{32,40},{40,48},{48,56},{56,32},{64,72... | collective-permute-start | bytes 3145736 | tf_op jit(solution)/shard_map/ppermute | solution.py:110
  20.2 28.5 %collective-permute-start.10 = (bf16[4,32,32,128]{3,2,1,0:T(8,128)(2,1)S(1)}, bf16[4,32,32,128]{3,2,1,0:T(8,128)(2,1)S(1)}, u32[]{:S(2)}, u32[]{:S(2)}) collective-permute-start(bf16[4,32,32,128]{3,2,1,0:T(8,128)(2,1)S(1)} %pad_maximum_fusion.1), channel_id=1, source_target_pairs={{0,24},{8,0},{16,8},{24,16},{32,56},{40,32},{48,40},{56,48},{64,88... | collective-permute-start | bytes 3145736 | tf_op jit(solution)/shard_map/ppermute | solution.py:111
  23.4 89.6 %copy-start.8 = (f32[2,4,128]{2,1,0:T(4,128)S(1)}, f32[2,4,128]{2,1,0:T(4,128)}, u32[]{:S(2)}) copy-start(f32[2,4,128]{2,1,0:T(4,128)} %param.12) | copy-start | bytes 12292
  23.6 43.3 %copy-start.2 = (bf16[4,32,32,128]{3,2,1,0:T(8,128)(2,1)}, bf16[4,32,32,128]{3,2,1,0:T(8,128)(2,1)S(1)}, u32[]{:S(2)}) copy-start(bf16[4,32,32,128]{3,2,1,0:T(8,128)(2,1)S(1)} %pad_maximum_fusion) | copy-start | bytes 3145732
  23.6 28.7 %collective-permute-start.4 = (bf16[4,32,32,128]{3,2,1,0:T(8,128)(2,1)S(1)}, bf16[4,32,32,128]{3,2,1,0:T(8,128)(2,1)S(1)}, u32[]{:S(2)}, u32[]{:S(2)}) collective-permute-start(bf16[4,32,32,128]{3,2,1,0:T(8,128)(2,1)S(1)} %pad_maximum_fusion), channel_id=1, source_target_pairs={{0,32},{8,40},{16,48},{24,56},{32,64},{40,72},{48,80},{56,88},{64,... | collective-permute-start | bytes 3145736 | tf_op jit(solution)/shard_map/ppermute | solution.py:110
  24.0 29.4 %collective-permute-start.3 = (bf16[4,32,32,128]{3,2,1,0:T(8,128)(2,1)S(1)}, bf16[4,32,32,128]{3,2,1,0:T(8,128)(2,1)S(1)}, u32[]{:S(2)}, u32[]{:S(2)}) collective-permute-start(bf16[4,32,32,128]{3,2,1,0:T(8,128)(2,1)S(1)} %pad_maximum_fusion), channel_id=1, source_target_pairs={{0,96},{8,104},{16,112},{24,120},{32,0},{40,8},{48,16},{56,24},{64... | collective-permute-start | bytes 3145736 | tf_op jit(solution)/shard_map/ppermute | solution.py:111
  47.7 19.2 %copy-start.3 = (bf16[4,32,32,128]{3,2,1,0:T(8,128)(2,1)}, bf16[4,32,32,128]{3,2,1,0:T(8,128)(2,1)S(1)}, u32[]{:S(2)}) copy-start(bf16[4,32,32,128]{3,2,1,0:T(8,128)(2,1)S(1)} %collective-permute-done.11) | copy-start | bytes 3145732
  48.7 14.4 %collective-permute-start.12 = (bf16[2,32,32,128]{3,2,1,0:T(8,128)(2,1)}, bf16[2,32,32,128]{3,2,1,0:T(8,128)(2,1)}, u32[]{:S(2)}, u32[]{:S(2)}) collective-permute-start(bf16[2,32,32,128]{3,2,1,0:T(8,128)(2,1)} %slice.28), channel_id=1, source_target_pairs={{0,8},{8,16},{16,24},{24,0},{32,40},{40,48},{48,56},{56,32},{64,72... | collective-permute-start | bytes 1572872 | tf_op jit(solution)/shard_map/ppermute | solution.py:117
  48.7 4.8 %copy-start.4 = (bf16[4,32,32,128]{3,2,1,0:T(8,128)(2,1)}, bf16[4,32,32,128]{3,2,1,0:T(8,128)(2,1)S(1)}, u32[]{:S(2)}) copy-start(bf16[4,32,32,128]{3,2,1,0:T(8,128)(2,1)S(1)} %collective-permute-done.10) | copy-start | bytes 3145732
  49.6 13.5 %collective-permute-start.13 = (bf16[2,32,32,128]{3,2,1,0:T(8,128)(2,1)}, bf16[2,32,32,128]{3,2,1,0:T(8,128)(2,1)}, u32[]{:S(2)}, u32[]{:S(2)}) collective-permute-start(bf16[2,32,32,128]{3,2,1,0:T(8,128)(2,1)} %slice.29), channel_id=1, source_target_pairs={{0,24},{8,0},{16,8},{24,16},{32,56},{40,32},{48,40},{56,48},{64,88... | collective-permute-start | bytes 1572872 | tf_op jit(solution)/shard_map/ppermute | solution.py:118
  52.2 2.1 %copy-start.5 = (bf16[4,32,32,128]{3,2,1,0:T(8,128)(2,1)}, bf16[4,32,32,128]{3,2,1,0:T(8,128)(2,1)S(1)}, u32[]{:S(2)}) copy-start(bf16[4,32,32,128]{3,2,1,0:T(8,128)(2,1)S(1)} %collective-permute-done.4) | copy-start | bytes 3145732
  53.1 13.7 %collective-permute-start.5 = (bf16[2,32,32,128]{3,2,1,0:T(8,128)(2,1)}, bf16[2,32,32,128]{3,2,1,0:T(8,128)(2,1)}, u32[]{:S(2)}, u32[]{:S(2)}) collective-permute-start(bf16[2,32,32,128]{3,2,1,0:T(8,128)(2,1)} %slice.25), channel_id=1, source_target_pairs={{0,32},{8,40},{16,48},{24,56},{32,64},{40,72},{48,80},{56,88},{64,... | collective-permute-start | bytes 1572872 | tf_op jit(solution)/shard_map/ppermute | solution.py:117
  53.4 3.3 %copy-start.6 = (bf16[4,32,32,128]{3,2,1,0:T(8,128)(2,1)}, bf16[4,32,32,128]{3,2,1,0:T(8,128)(2,1)S(1)}, u32[]{:S(2)}) copy-start(bf16[4,32,32,128]{3,2,1,0:T(8,128)(2,1)S(1)} %collective-permute-done.3) | copy-start | bytes 3145732
  54.3 12.5 %collective-permute-start.6 = (bf16[2,32,32,128]{3,2,1,0:T(8,128)(2,1)}, bf16[2,32,32,128]{3,2,1,0:T(8,128)(2,1)}, u32[]{:S(2)}, u32[]{:S(2)}) collective-permute-start(bf16[2,32,32,128]{3,2,1,0:T(8,128)(2,1)} %slice.26), channel_id=1, source_target_pairs={{0,96},{8,104},{16,112},{24,120},{32,0},{40,8},{48,16},{56,24},{64... | collective-permute-start | bytes 1572872 | tf_op jit(solution)/shard_map/ppermute | solution.py:118
  113.0 0.8 copy-start.7

commit v14 on v12

--- a/solution.py
+++ b/solution.py
@@ -8,51 +8,32 @@
 BLOCK = 128
 
 
-def field_kernel(source_ref, index_ref, obs_ref, *refs):
-    tables = refs[:-5]
-    tiles_ref, out_ref, rows, acc, sems = refs[-5:]
+def field_kernel(index_ref, obs_ref, *refs):
+    pieces = refs[:-5]
+    tiles_ref, out_ref, table, acc, sems = refs[-5:]
     step = pl.program_id(0)
     steps = pl.num_programs(0)
     block = tiles_ref.shape[0]
 
-    def fetch(which, slot):
-        def issue(t, carry):
-            r = which * block + t
-            i = index_ref[r]
-            k = source_ref[r]
-            for j, table in enumerate(tables):
-                @pl.when(k == j)
-                def _():
-                    pltpu.make_async_copy(table.at[i], rows.at[slot, t], sems.at[slot]).start()
-
-            return carry
-
-        lax.fori_loop(0, block, issue, 0, unroll=4)
-
-    def wait(slot):
-        def one_wait(t, carry):
-            pltpu.make_async_copy(tables[0].at[0], rows.at[slot, t], sems.at[slot]).wait()
-            return carry
-
-        lax.fori_loop(0, block, one_wait, 0, unroll=8)
-
-    slot = step % 2
-
     @pl.when(step == 0)
     def _():
+        copies = []
+        offset = 0
+        for j, piece in enumerate(pieces):
+            size = piece.shape[0]
+            copy = pltpu.make_async_copy(piece, table.at[pl.ds(offset, size)], sems.at[j])
+            copy.start()
+            copies.append(copy)
+            offset += size
         acc[...] = jnp.zeros_like(acc)
-        fetch(0, 0)
-
-    wait(slot)
-
-    @pl.when(step + 1 < steps)
-    def _():
-        fetch(step + 1, 1 - slot)
+        for copy in copies:
+            copy.wait()
 
     def one(t, carry):
-        term = lax.dot_general(rows[slot, t], tiles_ref[t], (((1,), (1,)), ((), ())),
+        r = step * block + t
+        term = lax.dot_general(table[index_ref[r]], tiles_ref[t], (((1,), (1,)), ((), ())),
                                preferred_element_type=jnp.float32)
-        o = obs_ref[step * block + t]
+        o = obs_ref[r]
         acc[o] = acc[o] + term
         return carry
 
@@ -66,22 +47,23 @@
                 out_ref[g, l] = acc[g * obs_dev:(g + 1) * obs_dev, l * ang_dev:(l + 1) * ang_dev]
 
 
-def field_partial(tables, source, tile_index, tile_obs, tiles, groups, lags, obs_dev):
-    _, angles, width = tables[0].shape
+def field_partial(pieces, tile_index, tile_obs, tiles, groups, lags, obs_dev):
+    _, angles, width = pieces[0].shape
+    total = sum(piece.shape[0] for piece in pieces)
     n_tiles = tiles.shape[0]
     ang_dev = angles // lags
     out_shape = (groups, lags, obs_dev, ang_dev, width)
     grid_spec = pltpu.PrefetchScalarGridSpec(
-        num_scalar_prefetch=3,
+        num_scalar_prefetch=2,
         grid=(n_tiles // BLOCK,),
-        in_specs=[pl.BlockSpec(memory_space=pl.ANY) for _ in tables] + [
+        in_specs=[pl.BlockSpec(memory_space=pl.ANY) for _ in pieces] + [
             pl.BlockSpec((BLOCK,) + tiles.shape[1:], lambda i, *_: (i, 0, 0)),
         ],
         out_specs=pl.BlockSpec(out_shape, lambda i, *_: (0, 0, 0, 0, 0)),
         scratch_shapes=[
-            pltpu.VMEM((2, BLOCK, angles, width), tables[0].dtype),
+            pltpu.VMEM((total, angles, width), pieces[0].dtype),
             pltpu.VMEM((groups * obs_dev + 1, angles, width), jnp.float32),
-            pltpu.SemaphoreType.DMA((2,)),
+            pltpu.SemaphoreType.DMA((len(pieces),)),
         ],
     )
     return pl.pallas_call(
@@ -89,7 +71,7 @@
         grid_spec=grid_spec,
         out_shape=jax.ShapeDtypeStruct(out_shape, jnp.float32),
         compiler_params=pltpu.CompilerParams(dimension_semantics=("arbitrary",)),
-    )(source, tile_index, tile_obs, *tables, tiles)
+    )(tile_index, tile_obs, *pieces, tiles)
 
 
 def shift_pairs(rows, cols, step, along_cols):
@@ -142,8 +124,12 @@
     upper = (outer == 2) & (inner >= 2)
     piece = jnp.where(outer == 3, 4, outer + upper.astype(outer.dtype))
     source = piece + 5 * tile_lag
-    tile_index = (inner - 2 * upper.astype(inner.dtype)) * src_dev + local
-    partial = field_partial(tables, source, tile_index, tile_obs, tiles, n_grp, n_lag, obs_dev)
+    starts = [0]
+    for table in tables[:-1]:
+        starts.append(starts[-1] + table.shape[0])
+    start = jnp.asarray(starts, jnp.int32)[source]
+    tile_index = start + (inner - 2 * upper.astype(inner.dtype)) * src_dev + local
+    partial = field_partial(tables, tile_index, tile_obs, tiles, n_grp, n_lag, obs_dev)
     partial = partial.reshape(n_grp * n_lag, obs_dev, ang_dev, width)
     received = lax.all_to_all(partial, ("grp", "lag"), 0, 0, tiled=True)
     field = jnp.sum(received, axis=0)

time: 111 us -> 106 us (0.955)
  Pallas kernels: 22.9 us -> 18.4 us
  waiting for transfers between devices: 27.3 us -> 28.6 us
  other arithmetic: 4.38 us -> 3.13 us
    pallas_call x1, Pallas kernels: 22.9 us -> 18.4 us  [field_partial(): pl.pallas_call(field_kernel, grid_spec=grid_spec, out_shape=jax.ShapeDtyp...]
    ppermute x4, waiting for transfers between devices: 5.34 us -> 6.64 us  [ring_gather(): far_a = lax.ppermute(from_behind[:half], 'grp', plus)]
    add x2 -> x1, other arithmetic: 2.57 us -> 1.32 us  [body(): start + (inner - 2 * upper.astype(inner.dtype)) * src_dev + local]
  transfers between devices with their start and end apart: 16 -> 16, of which waited for: 6 -> 6; matrix products, arithmetic and copies ran while one was open for 6% -> 5% of each run, Pallas kernels for 0% -> 0%
where the time goes in v14:
time: 106 us
  waiting for transfers between devices  28.6 us (27%)
  blocking collectives  25.8 us (24%)
  starting transfers between devices  24.2 us (23%)
  Pallas kernels  18.4 us (17%)
  local copies, waits for them, and re-layouts  3.87 us (4%)
  other arithmetic  3.13 us (3%)
    all_to_all x1, blocking collectives, body(): received = lax.all_to_all(partial, ('grp', 'lag'), 0, 0, tiled=True)  25.8 us
    ppermute x4, waiting for transfers between devices, ring_gather(): from_behind = lax.ppermute(x, 'grp', plus)  21.8 us
    pallas_call x1, Pallas kernels, field_partial(): pl.pallas_call(field_kernel, grid_spec=grid_spec, out_shape=jax.ShapeDtyp...  18.4 us
    ppermute x4, starting transfers between devices, ring_gather(): far_b = lax.ppermute(from_ahead[half:], 'grp', minus)  10.1 us
    ppermute x4, starting transfers between devices, ring_gather(): from_ahead = lax.ppermute(x, 'grp', minus)  8.97 us
    ppermute x4, waiting for transfers between devices, ring_gather(): far_a = lax.ppermute(from_behind[:half], 'grp', plus)  6.64 us
    ppermute x4, starting transfers between devices, ring_gather(): from_behind = lax.ppermute(x, 'grp', plus)  3.98 us
  transfers between devices with their start and end apart: 16, of which 6 were waited for; matrix products, arithmetic and copies ran while one was open for 5% of the time, Pallas kernels for 0%

profile of v14, /device:TPU:1, one launch (start us, length us, event | category | flops | bytes accessed | tf_op | source)
XLA Modules:
  0.0 105.6 jit_solution(17130911010657506017)
XLA Ops:
  0.6 0.0 copy-start
  0.6 1.3 %convert_element_type.11 = bf16[2,32,32,128]{3,2,1,0:T(8,128)(2,1)S(1)} convert(f32[2,32,32,128]{3,2,1,0:T(8,128)} %param.8) | non-fusion elementwise | flops 262144 | bytes 1572864 | tf_op jit(solution)/shard_map/convert_element_type | solution.py:109
  2.0 0.2 fusion.10
  2.2 2.2 %collective-permute-start.9 = (bf16[32,32,128]{2,1,0:T(8,128)(2,1)S(1)}, bf16[32,32,128]{2,1,0:T(8,128)(2,1)S(1)}, u32[]{:S(2)}, u32[]{:S(2)}) collective-permute-start(bf16[32,32,128]{2,1,0:T(8,128)(2,1)S(1)} %get-tuple-element.4), channel_id=1, source_target_pairs={{0,32},{8,40},{16,48},{24,56},{32,64},{40,72},{48,80},{56,88},{64,... | collective-permute-start | bytes 786440 | tf_op jit(solution)/shard_map/ppermute | solution.py:92
  4.4 1.5 %collective-permute-start.8 = (bf16[32,32,128]{2,1,0:T(8,128)(2,1)S(1)}, bf16[32,32,128]{2,1,0:T(8,128)(2,1)S(1)}, u32[]{:S(2)}, u32[]{:S(2)}) collective-permute-start(bf16[32,32,128]{2,1,0:T(8,128)(2,1)S(1)} %get-tuple-element.4), channel_id=1, source_target_pairs={{0,96},{8,104},{16,112},{24,120},{32,0},{40,8},{48,16},{56,24},{64... | collective-permute-start | bytes 786440 | tf_op jit(solution)/shard_map/ppermute | solution.py:93
  5.9 1.6 %collective-permute-start.1 = (bf16[32,32,128]{2,1,0:T(8,128)(2,1)S(1)}, bf16[32,32,128]{2,1,0:T(8,128)(2,1)S(1)}, u32[]{:S(2)}, u32[]{:S(2)}) collective-permute-start(bf16[32,32,128]{2,1,0:T(8,128)(2,1)S(1)} %get-tuple-element.3), channel_id=1, source_target_pairs={{0,8},{8,16},{16,24},{24,0},{32,40},{40,48},{48,56},{56,32},{64,72... | collective-permute-start | bytes 786440 | tf_op jit(solution)/shard_map/ppermute | solution.py:92
  7.5 2.1 %collective-permute-start = (bf16[32,32,128]{2,1,0:T(8,128)(2,1)S(1)}, bf16[32,32,128]{2,1,0:T(8,128)(2,1)S(1)}, u32[]{:S(2)}, u32[]{:S(2)}) collective-permute-start(bf16[32,32,128]{2,1,0:T(8,128)(2,1)S(1)} %get-tuple-element.3), channel_id=1, source_target_pairs={{0,24},{8,0},{16,8},{24,16},{32,56},{40,32},{48,40},{56,48},{64,88... | collective-permute-start | bytes 786440 | tf_op jit(solution)/shard_map/ppermute | solution.py:93
  9.6 2.0 %collective-permute-done.9 = bf16[32,32,128]{2,1,0:T(8,128)(2,1)S(1)} collective-permute-done((bf16[32,32,128]{2,1,0:T(8,128)(2,1)S(1)}, bf16[32,32,128]{2,1,0:T(8,128)(2,1)S(1)}, u32[]{:S(2)}, u32[]{:S(2)}) %collective-permute-start.9) | collective-permute-done | bytes 262176 | tf_op jit(solution)/shard_map/ppermute | solution.py:92
  11.7 0.1 collective-permute-start.10
  11.8 0.0 collective-permute-done.8
  11.8 2.7 %collective-permute-start.11 = (bf16[16,32,128]{2,1,0:T(8,128)(2,1)S(1)}, bf16[16,32,128]{2,1,0:T(8,128)(2,1)S(1)}, u32[]{:S(2)}, u32[]{:S(2)}) collective-permute-start(bf16[16,32,128]{2,1,0:T(8,128)(2,1)S(1)} %slice.58), channel_id=1, source_target_pairs={{0,96},{8,104},{16,112},{24,120},{32,0},{40,8},{48,16},{56,24},{64... | collective-permute-start | bytes 393224 | tf_op jit(solution)/shard_map/ppermute | solution.py:97
  14.5 0.7 collective-permute-done.1
  15.2 1.0 collective-permute-start.2
  16.2 0.0 collective-permute-done
  16.2 2.2 %collective-permute-start.3 = (bf16[16,32,128]{2,1,0:T(8,128)(2,1)S(1)}, bf16[16,32,128]{2,1,0:T(8,128)(2,1)S(1)}, u32[]{:S(2)}, u32[]{:S(2)}) collective-permute-start(bf16[16,32,128]{2,1,0:T(8,128)(2,1)S(1)} %slice.53), channel_id=1, source_target_pairs={{0,24},{8,0},{16,8},{24,16},{32,56},{40,32},{48,40},{56,48},{64,88... | collective-permute-start | bytes 393224 | tf_op jit(solution)/shard_map/ppermute | solution.py:97
  18.4 0.0 collective-permute-done.10
  18.4 0.0 collective-permute-done.11
  18.4 0.1 pad_maximum_fusion.1
  18.6 0.1 collective-permute-start.13
  18.7 2.7 %collective-permute-start.12 = (bf16[4,32,32,128]{3,2,1,0:T(8,128)(2,1)S(1)}, bf16[4,32,32,128]{3,2,1,0:T(8,128)(2,1)S(1)}, u32[]{:S(2)}, u32[]{:S(2)}) collective-permute-start(bf16[4,32,32,128]{3,2,1,0:T(8,128)(2,1)S(1)} %pad_maximum_fusion.1), channel_id=1, source_target_pairs={{0,24},{8,0},{16,8},{24,16},{32,56},{40,32},{48,40},{56,48},{64,88... | collective-permute-start | bytes 3145736 | tf_op jit(solution)/shard_map/ppermute | solution.py:93
  21.3 0.0 collective-permute-done.2
  21.3 0.0 collective-permute-done.3
  21.4 0.0 copy-start.8
  21.4 0.1 pad_maximum_fusion
  21.5 0.1 collective-permute-start.5
  21.6 2.7 %collective-permute-start.4 = (bf16[4,32,32,128]{3,2,1,0:T(8,128)(2,1)S(1)}, bf16[4,32,32,128]{3,2,1,0:T(8,128)(2,1)S(1)}, u32[]{:S(2)}, u32[]{:S(2)}) collective-permute-start(bf16[4,32,32,128]{3,2,1,0:T(8,128)(2,1)S(1)} %pad_maximum_fusion), channel_id=1, source_target_pairs={{0,96},{8,104},{16,112},{24,120},{32,0},{40,8},{48,16},{56,24},{64... | collective-permute-start | bytes 3145736 | tf_op jit(solution)/shard_map/ppermute | solution.py:93
  24.3 19.1 %collective-permute-done.13 = bf16[4,32,32,128]{3,2,1,0:T(8,128)(2,1)S(1)} collective-permute-done((bf16[4,32,32,128]{3,2,1,0:T(8,128)(2,1)S(1)}, bf16[4,32,32,128]{3,2,1,0:T(8,128)(2,1)S(1)}, u32[]{:S(2)}, u32[]{:S(2)}) %collective-permute-start.13) | collective-permute-done | bytes 1048608 | tf_op jit(solution)/shard_map/ppermute | solution.py:92
  43.3 0.9 slice.59
  44.3 0.2 collective-permute-start.14
  44.5 0.0 collective-permute-done.12
  44.5 0.9 slice.60
  45.4 2.5 %collective-permute-start.15 = (bf16[2,32,32,128]{3,2,1,0:T(8,128)(2,1)}, bf16[2,32,32,128]{3,2,1,0:T(8,128)(2,1)}, u32[]{:S(2)}, u32[]{:S(2)}) collective-permute-start(bf16[2,32,32,128]{3,2,1,0:T(8,128)(2,1)} %slice.60), channel_id=1, source_target_pairs={{0,24},{8,0},{16,8},{24,16},{32,56},{40,32},{48,40},{56,48},{64,88... | collective-permute-start | bytes 1572872 | tf_op jit(solution)/shard_map/ppermute | solution.py:97
  47.9 0.0 collective-permute-done.5
  47.9 0.9 slice.54
  48.7 0.0 collective-permute-start.6
  48.7 0.0 collective-permute-done.4
  48.8 0.9 slice.55
  49.7 2.7 %collective-permute-start.7 = (bf16[2,32,32,128]{3,2,1,0:T(8,128)(2,1)}, bf16[2,32,32,128]{3,2,1,0:T(8,128)(2,1)}, u32[]{:S(2)}, u32[]{:S(2)}) collective-permute-start(bf16[2,32,32,128]{3,2,1,0:T(8,128)(2,1)} %slice.55), channel_id=1, source_target_pairs={{0,96},{8,104},{16,112},{24,120},{32,0},{40,8},{48,16},{56,24},{64... | collective-permute-start | bytes 1572872 | tf_op jit(solution)/shard_map/ppermute | solution.py:97
  52.3 1.3 %fusion.6.index_ref = s32[512]{0:T(512)} fusion(s32[512]{0:T(512)} %param.12, s32[512]{0:T(512)} %param.10, s32[]{:T(128)S(6)} %select_n.55, s32[]{:T(128)S(6)} %select_n.52), kind=kLoop, calls=%fused_computation.28 | loop fusion | flops 52224 | bytes 6152 | tf_op jit(solution)/shard_map/add | solution.py:131
  53.7 2.9 %collective-permute-done.14 = bf16[2,32,32,128]{3,2,1,0:T(8,128)(2,1)} collective-permute-done((bf16[2,32,32,128]{3,2,1,0:T(8,128)(2,1)}, bf16[2,32,32,128]{3,2,1,0:T(8,128)(2,1)}, u32[]{:S(2)}, u32[]{:S(2)}) %collective-permute-start.14) | collective-permute-done | bytes 524320 | tf_op jit(solution)/shard_map/ppermute | solution.py:96
  56.6 0.2 collective-permute-done.15
  56.7 3.7 %collective-permute-done.6 = bf16[2,32,32,128]{3,2,1,0:T(8,128)(2,1)} collective-permute-done((bf16[2,32,32,128]{3,2,1,0:T(8,128)(2,1)}, bf16[2,32,32,128]{3,2,1,0:T(8,128)(2,1)}, u32[]{:S(2)}, u32[]{:S(2)}) %collective-permute-start.6) | collective-permute-done | bytes 524320 | tf_op jit(solution)/shard_map/ppermute | solution.py:96
  60.5 0.0 collective-permute-done.7
  60.5 18.4 %shard_map.95 = f32[16,8,2,4,128]{4,3,2,1,0:T(4,128)} custom-call(s32[512]{0:T(512)} %fusion.6.index_ref, s32[512]{0:T(512)} %obs_ref.1, bf16[128,32,128]{2,1,0:T(8,128)(2,1)} %bitcast.25, bf16[128,32,128]{2,1,0:T(8,128)(2,1)} %bitcast.29, bf16[64,32,128]{2,1,0:T(8,128)(2,1)} %bitcast.6.refs_2_, bf16[64,32,128]{2,1,0:T(8,128)(2,1)} %bitcast.7.refs_3_, ...), custom_call_target="tpu_custom_call" | custom-call | tf_op jit(solution)/shard_map/pallas_call | solution.py:69
  78.9 25.8 %all_to_all.5 = f32[128,2,4,128]{3,2,1,0:T(4,128)S(1)} all-to-all(f32[128,2,4,128]{3,2,1,0:T(4,128)} %bitcast.30), channel_id=1, replica_groups=mesh['grp'=16,'lag'=8] {'grp','lag'}, dimensions={0} | all-to-all | bytes 1048576 | tf_op jit(solution)/shard_map/all_to_all | solution.py:134
  104.7 0.1 reduce_sum.9
  104.9 0.0 copy-start.7
  104.9 0.7 fusion.7
  (21 shorter events, 0.1 us)
Async XLA Ops:
  0.6 104.2 %copy-start = (bf16[2,128,128]{2,1,0:T(8,128)(2,1)S(1)}, bf16[2,128,128]{2,1,0:T(8,128)(2,1)}, u32[]{:S(2)}) copy-start(bf16[2,128,128]{2,1,0:T(8,128)(2,1)} %param.14) | copy-start | bytes 196612
  2.2 9.5 %collective-permute-start.9 = (bf16[32,32,128]{2,1,0:T(8,128)(2,1)S(1)}, bf16[32,32,128]{2,1,0:T(8,128)(2,1)S(1)}, u32[]{:S(2)}, u32[]{:S(2)}) collective-permute-start(bf16[32,32,128]{2,1,0:T(8,128)(2,1)S(1)} %get-tuple-element.4), channel_id=1, source_target_pairs={{0,32},{8,40},{16,48},{24,56},{32,64},{40,72},{48,80},{56,88},{64,... | collective-permute-start | bytes 786440 | tf_op jit(solution)/shard_map/ppermute | solution.py:92
  4.4 7.4 %collective-permute-start.8 = (bf16[32,32,128]{2,1,0:T(8,128)(2,1)S(1)}, bf16[32,32,128]{2,1,0:T(8,128)(2,1)S(1)}, u32[]{:S(2)}, u32[]{:S(2)}) collective-permute-start(bf16[32,32,128]{2,1,0:T(8,128)(2,1)S(1)} %get-tuple-element.4), channel_id=1, source_target_pairs={{0,96},{8,104},{16,112},{24,120},{32,0},{40,8},{48,16},{56,24},{64... | collective-permute-start | bytes 786440 | tf_op jit(solution)/shard_map/ppermute | solution.py:93
  5.9 9.3 %collective-permute-start.1 = (bf16[32,32,128]{2,1,0:T(8,128)(2,1)S(1)}, bf16[32,32,128]{2,1,0:T(8,128)(2,1)S(1)}, u32[]{:S(2)}, u32[]{:S(2)}) collective-permute-start(bf16[32,32,128]{2,1,0:T(8,128)(2,1)S(1)} %get-tuple-element.3), channel_id=1, source_target_pairs={{0,8},{8,16},{16,24},{24,0},{32,40},{40,48},{48,56},{56,32},{64,72... | collective-permute-start | bytes 786440 | tf_op jit(solution)/shard_map/ppermute | solution.py:92
  7.5 8.6 %collective-permute-start = (bf16[32,32,128]{2,1,0:T(8,128)(2,1)S(1)}, bf16[32,32,128]{2,1,0:T(8,128)(2,1)S(1)}, u32[]{:S(2)}, u32[]{:S(2)}) collective-permute-start(bf16[32,32,128]{2,1,0:T(8,128)(2,1)S(1)} %get-tuple-element.3), channel_id=1, source_target_pairs={{0,24},{8,0},{16,8},{24,16},{32,56},{40,32},{48,40},{56,48},{64,88... | collective-permute-start | bytes 786440 | tf_op jit(solution)/shard_map/ppermute | solution.py:93
  11.7 6.7 %collective-permute-start.10 = (bf16[16,32,128]{2,1,0:T(8,128)(2,1)S(1)}, bf16[16,32,128]{2,1,0:T(8,128)(2,1)S(1)}, u32[]{:S(2)}, u32[]{:S(2)}) collective-permute-start(bf16[16,32,128]{2,1,0:T(8,128)(2,1)S(1)} %slice.57), channel_id=1, source_target_pairs={{0,32},{8,40},{16,48},{24,56},{32,64},{40,72},{48,80},{56,88},{64,... | collective-permute-start | bytes 393224 | tf_op jit(solution)/shard_map/ppermute | solution.py:96
  11.8 6.6 %collective-permute-start.11 = (bf16[16,32,128]{2,1,0:T(8,128)(2,1)S(1)}, bf16[16,32,128]{2,1,0:T(8,128)(2,1)S(1)}, u32[]{:S(2)}, u32[]{:S(2)}) collective-permute-start(bf16[16,32,128]{2,1,0:T(8,128)(2,1)S(1)} %slice.58), channel_id=1, source_target_pairs={{0,96},{8,104},{16,112},{24,120},{32,0},{40,8},{48,16},{56,24},{64... | collective-permute-start | bytes 393224 | tf_op jit(solution)/shard_map/ppermute | solution.py:97
  15.2 6.1 %collective-permute-start.2 = (bf16[16,32,128]{2,1,0:T(8,128)(2,1)S(1)}, bf16[16,32,128]{2,1,0:T(8,128)(2,1)S(1)}, u32[]{:S(2)}, u32[]{:S(2)}) collective-permute-start(bf16[16,32,128]{2,1,0:T(8,128)(2,1)S(1)} %slice.52), channel_id=1, source_target_pairs={{0,8},{8,16},{16,24},{24,0},{32,40},{40,48},{48,56},{56,32},{64,72... | collective-permute-start | bytes 393224 | tf_op jit(solution)/shard_map/ppermute | solution.py:96
  16.2 5.2 %collective-permute-start.3 = (bf16[16,32,128]{2,1,0:T(8,128)(2,1)S(1)}, bf16[16,32,128]{2,1,0:T(8,128)(2,1)S(1)}, u32[]{:S(2)}, u32[]{:S(2)}) collective-permute-start(bf16[16,32,128]{2,1,0:T(8,128)(2,1)S(1)} %slice.53), channel_id=1, source_target_pairs={{0,24},{8,0},{16,8},{24,16},{32,56},{40,32},{48,40},{56,48},{64,88... | collective-permute-start | bytes 393224 | tf_op jit(solution)/shard_map/ppermute | solution.py:97
  18.6 41.9 %copy-start.1 = (bf16[4,32,32,128]{3,2,1,0:T(8,128)(2,1)}, bf16[4,32,32,128]{3,2,1,0:T(8,128)(2,1)S(1)}, u32[]{:S(2)}) copy-start(bf16[4,32,32,128]{3,2,1,0:T(8,128)(2,1)S(1)} %pad_maximum_fusion.1) | copy-start | bytes 3145732
  18.6 24.8 %collective-permute-start.13 = (bf16[4,32,32,128]{3,2,1,0:T(8,128)(2,1)S(1)}, bf16[4,32,32,128]{3,2,1,0:T(8,128)(2,1)S(1)}, u32[]{:S(2)}, u32[]{:S(2)}) collective-permute-start(bf16[4,32,32,128]{3,2,1,0:T(8,128)(2,1)S(1)} %pad_maximum_fusion.1), channel_id=1, source_target_pairs={{0,8},{8,16},{16,24},{24,0},{32,40},{40,48},{48,56},{56,32},{64,72... | collective-permute-start | bytes 3145736 | tf_op jit(solution)/shard_map/ppermute | solution.py:92
  18.7 25.8 %collective-permute-start.12 = (bf16[4,32,32,128]{3,2,1,0:T(8,128)(2,1)S(1)}, bf16[4,32,32,128]{3,2,1,0:T(8,128)(2,1)S(1)}, u32[]{:S(2)}, u32[]{:S(2)}) collective-permute-start(bf16[4,32,32,128]{3,2,1,0:T(8,128)(2,1)S(1)} %pad_maximum_fusion.1), channel_id=1, source_target_pairs={{0,24},{8,0},{16,8},{24,16},{32,56},{40,32},{48,40},{56,48},{64,88... | collective-permute-start | bytes 3145736 | tf_op jit(solution)/shard_map/ppermute | solution.py:93
  21.4 83.5 %copy-start.8 = (f32[2,4,128]{2,1,0:T(4,128)S(1)}, f32[2,4,128]{2,1,0:T(4,128)}, u32[]{:S(2)}) copy-start(f32[2,4,128]{2,1,0:T(4,128)} %param.13) | copy-start | bytes 12292
  21.5 39.0 %copy-start.2 = (bf16[4,32,32,128]{3,2,1,0:T(8,128)(2,1)}, bf16[4,32,32,128]{3,2,1,0:T(8,128)(2,1)S(1)}, u32[]{:S(2)}) copy-start(bf16[4,32,32,128]{3,2,1,0:T(8,128)(2,1)S(1)} %pad_maximum_fusion) | copy-start | bytes 3145732
  21.5 26.3 %collective-permute-start.5 = (bf16[4,32,32,128]{3,2,1,0:T(8,128)(2,1)S(1)}, bf16[4,32,32,128]{3,2,1,0:T(8,128)(2,1)S(1)}, u32[]{:S(2)}, u32[]{:S(2)}) collective-permute-start(bf16[4,32,32,128]{3,2,1,0:T(8,128)(2,1)S(1)} %pad_maximum_fusion), channel_id=1, source_target_pairs={{0,32},{8,40},{16,48},{24,56},{32,64},{40,72},{48,80},{56,88},{64,... | collective-permute-start | bytes 3145736 | tf_op jit(solution)/shard_map/ppermute | solution.py:92
  21.6 27.2 %collective-permute-start.4 = (bf16[4,32,32,128]{3,2,1,0:T(8,128)(2,1)S(1)}, bf16[4,32,32,128]{3,2,1,0:T(8,128)(2,1)S(1)}, u32[]{:S(2)}, u32[]{:S(2)}) collective-permute-start(bf16[4,32,32,128]{3,2,1,0:T(8,128)(2,1)S(1)} %pad_maximum_fusion), channel_id=1, source_target_pairs={{0,96},{8,104},{16,112},{24,120},{32,0},{40,8},{48,16},{56,24},{64... | collective-permute-start | bytes 3145736 | tf_op jit(solution)/shard_map/ppermute | solution.py:93
  43.3 17.1 %copy-start.3 = (bf16[4,32,32,128]{3,2,1,0:T(8,128)(2,1)}, bf16[4,32,32,128]{3,2,1,0:T(8,128)(2,1)S(1)}, u32[]{:S(2)}) copy-start(bf16[4,32,32,128]{3,2,1,0:T(8,128)(2,1)S(1)} %collective-permute-done.13) | copy-start | bytes 3145732
  44.3 12.3 %collective-permute-start.14 = (bf16[2,32,32,128]{3,2,1,0:T(8,128)(2,1)}, bf16[2,32,32,128]{3,2,1,0:T(8,128)(2,1)}, u32[]{:S(2)}, u32[]{:S(2)}) collective-permute-start(bf16[2,32,32,128]{3,2,1,0:T(8,128)(2,1)} %slice.59), channel_id=1, source_target_pairs={{0,8},{8,16},{16,24},{24,0},{32,40},{40,48},{48,56},{56,32},{64,72... | collective-permute-start | bytes 1572872 | tf_op jit(solution)/shard_map/ppermute | solution.py:96
  44.5 4.3 %copy-start.4 = (bf16[4,32,32,128]{3,2,1,0:T(8,128)(2,1)}, bf16[4,32,32,128]{3,2,1,0:T(8,128)(2,1)S(1)}, u32[]{:S(2)}) copy-start(bf16[4,32,32,128]{3,2,1,0:T(8,128)(2,1)S(1)} %collective-permute-done.12) | copy-start | bytes 3145732
  45.4 11.4 %collective-permute-start.15 = (bf16[2,32,32,128]{3,2,1,0:T(8,128)(2,1)}, bf16[2,32,32,128]{3,2,1,0:T(8,128)(2,1)}, u32[]{:S(2)}, u32[]{:S(2)}) collective-permute-start(bf16[2,32,32,128]{3,2,1,0:T(8,128)(2,1)} %slice.60), channel_id=1, source_target_pairs={{0,24},{8,0},{16,8},{24,16},{32,56},{40,32},{48,40},{56,48},{64,88... | collective-permute-start | bytes 1572872 | tf_op jit(solution)/shard_map/ppermute | solution.py:97
  47.9 1.8 %copy-start.5 = (bf16[4,32,32,128]{3,2,1,0:T(8,128)(2,1)}, bf16[4,32,32,128]{3,2,1,0:T(8,128)(2,1)S(1)}, u32[]{:S(2)}) copy-start(bf16[4,32,32,128]{3,2,1,0:T(8,128)(2,1)S(1)} %collective-permute-done.5) | copy-start | bytes 3145732
  48.7 11.7 %collective-permute-start.6 = (bf16[2,32,32,128]{3,2,1,0:T(8,128)(2,1)}, bf16[2,32,32,128]{3,2,1,0:T(8,128)(2,1)}, u32[]{:S(2)}, u32[]{:S(2)}) collective-permute-start(bf16[2,32,32,128]{3,2,1,0:T(8,128)(2,1)} %slice.54), channel_id=1, source_target_pairs={{0,32},{8,40},{16,48},{24,56},{32,64},{40,72},{48,80},{56,88},{64,... | collective-permute-start | bytes 1572872 | tf_op jit(solution)/shard_map/ppermute | solution.py:96
  48.8 3.6 %copy-start.6 = (bf16[4,32,32,128]{3,2,1,0:T(8,128)(2,1)}, bf16[4,32,32,128]{3,2,1,0:T(8,128)(2,1)S(1)}, u32[]{:S(2)}) copy-start(bf16[4,32,32,128]{3,2,1,0:T(8,128)(2,1)S(1)} %collective-permute-done.4) | copy-start | bytes 3145732
  49.7 10.8 %collective-permute-start.7 = (bf16[2,32,32,128]{3,2,1,0:T(8,128)(2,1)}, bf16[2,32,32,128]{3,2,1,0:T(8,128)(2,1)}, u32[]{:S(2)}, u32[]{:S(2)}) collective-permute-start(bf16[2,32,32,128]{3,2,1,0:T(8,128)(2,1)} %slice.55), channel_id=1, source_target_pairs={{0,96},{8,104},{16,112},{24,120},{32,0},{40,8},{48,16},{56,24},{64... | collective-permute-start | bytes 1572872 | tf_op jit(solution)/shard_map/ppermute | solution.py:97
  104.9 0.8 copy-start.7

commit v15 on v14

--- a/solution.py
+++ b/solution.py
@@ -41,10 +41,10 @@
 
     @pl.when(step == steps - 1)
     def _():
-        groups, lags, obs_dev, ang_dev, _ = out_ref.shape
+        lags, groups, obs_dev, ang_dev, _ = out_ref.shape
         for g in range(groups):
             for l in range(lags):
-                out_ref[g, l] = acc[g * obs_dev:(g + 1) * obs_dev, l * ang_dev:(l + 1) * ang_dev]
+                out_ref[l, g] = acc[g * obs_dev:(g + 1) * obs_dev, l * ang_dev:(l + 1) * ang_dev]
 
 
 def field_partial(pieces, tile_index, tile_obs, tiles, groups, lags, obs_dev):
@@ -52,7 +52,7 @@
     total = sum(piece.shape[0] for piece in pieces)
     n_tiles = tiles.shape[0]
     ang_dev = angles // lags
-    out_shape = (groups, lags, obs_dev, ang_dev, width)
+    out_shape = (lags, groups, obs_dev, ang_dev, width)
     grid_spec = pltpu.PrefetchScalarGridSpec(
         num_scalar_prefetch=2,
         grid=(n_tiles // BLOCK,),
@@ -131,7 +131,7 @@
     tile_index = start + (inner - 2 * upper.astype(inner.dtype)) * src_dev + local
     partial = field_partial(tables, tile_index, tile_obs, tiles, n_grp, n_lag, obs_dev)
     partial = partial.reshape(n_grp * n_lag, obs_dev, ang_dev, width)
-    received = lax.all_to_all(partial, ("grp", "lag"), 0, 0, tiled=True)
+    received = lax.all_to_all(partial, ("lag", "grp"), 0, 0, tiled=True)
     field = jnp.sum(received, axis=0)
     rhs = (incident - field).astype(jnp.bfloat16)
     new_current = jnp.einsum("oag,ohg->oah", rhs, near_inverse, preferred_element_type=jnp.float32)

time: 106 us -> 106 us (level)
  no operation moved by 1% of the time
where the time goes in v15:
time: 106 us
  waiting for transfers between devices  28.6 us (27%)
  blocking collectives  25.9 us (24%)
  starting transfers between devices  24.2 us (23%)
  Pallas kernels  18.4 us (17%)
  local copies, waits for them, and re-layouts  3.87 us (4%)
  other arithmetic  3.13 us (3%)
    all_to_all x1, blocking collectives, body(): received = lax.all_to_all(partial, ('lag', 'grp'), 0, 0, tiled=True)  25.9 us
    ppermute x4, waiting for transfers between devices, ring_gather(): from_behind = lax.ppermute(x, 'grp', plus)  21.8 us
    pallas_call x1, Pallas kernels, field_partial(): pl.pallas_call(field_kernel, grid_spec=grid_spec, out_shape=jax.ShapeDtyp...  18.4 us
    ppermute x4, starting transfers between devices, ring_gather(): far_b = lax.ppermute(from_ahead[half:], 'grp', minus)  10.1 us
    ppermute x4, starting transfers between devices, ring_gather(): from_ahead = lax.ppermute(x, 'grp', minus)  8.97 us
    ppermute x4, waiting for transfers between devices, ring_gather(): far_a = lax.ppermute(from_behind[:half], 'grp', plus)  6.64 us
    ppermute x4, starting transfers between devices, ring_gather(): from_behind = lax.ppermute(x, 'grp', plus)  3.98 us
  transfers between devices with their start and end apart: 16, of which 6 were waited for; matrix products, arithmetic and copies ran while one was open for 5% of the time, Pallas kernels for 0%

profile of v15, /device:TPU:1, one launch (start us, length us, event | category | flops | bytes accessed | tf_op | source)
XLA Modules:
  0.0 105.8 jit_solution(13835873897812882650)
XLA Ops:
  0.6 0.0 copy-start
  0.6 1.3 %convert_element_type.11 = bf16[2,32,32,128]{3,2,1,0:T(8,128)(2,1)S(1)} convert(f32[2,32,32,128]{3,2,1,0:T(8,128)} %param.8) | non-fusion elementwise | flops 262144 | bytes 1572864 | tf_op jit(solution)/shard_map/convert_element_type | solution.py:109
  2.0 0.2 fusion.10
  2.2 2.2 %collective-permute-start.9 = (bf16[32,32,128]{2,1,0:T(8,128)(2,1)S(1)}, bf16[32,32,128]{2,1,0:T(8,128)(2,1)S(1)}, u32[]{:S(2)}, u32[]{:S(2)}) collective-permute-start(bf16[32,32,128]{2,1,0:T(8,128)(2,1)S(1)} %get-tuple-element.4), channel_id=1, source_target_pairs={{0,32},{8,40},{16,48},{24,56},{32,64},{40,72},{48,80},{56,88},{64,... | collective-permute-start | bytes 786440 | tf_op jit(solution)/shard_map/ppermute | solution.py:92
  4.4 1.5 %collective-permute-start.8 = (bf16[32,32,128]{2,1,0:T(8,128)(2,1)S(1)}, bf16[32,32,128]{2,1,0:T(8,128)(2,1)S(1)}, u32[]{:S(2)}, u32[]{:S(2)}) collective-permute-start(bf16[32,32,128]{2,1,0:T(8,128)(2,1)S(1)} %get-tuple-element.4), channel_id=1, source_target_pairs={{0,96},{8,104},{16,112},{24,120},{32,0},{40,8},{48,16},{56,24},{64... | collective-permute-start | bytes 786440 | tf_op jit(solution)/shard_map/ppermute | solution.py:93
  5.9 1.6 %collective-permute-start.1 = (bf16[32,32,128]{2,1,0:T(8,128)(2,1)S(1)}, bf16[32,32,128]{2,1,0:T(8,128)(2,1)S(1)}, u32[]{:S(2)}, u32[]{:S(2)}) collective-permute-start(bf16[32,32,128]{2,1,0:T(8,128)(2,1)S(1)} %get-tuple-element.3), channel_id=1, source_target_pairs={{0,8},{8,16},{16,24},{24,0},{32,40},{40,48},{48,56},{56,32},{64,72... | collective-permute-start | bytes 786440 | tf_op jit(solution)/shard_map/ppermute | solution.py:92
  7.5 2.1 %collective-permute-start = (bf16[32,32,128]{2,1,0:T(8,128)(2,1)S(1)}, bf16[32,32,128]{2,1,0:T(8,128)(2,1)S(1)}, u32[]{:S(2)}, u32[]{:S(2)}) collective-permute-start(bf16[32,32,128]{2,1,0:T(8,128)(2,1)S(1)} %get-tuple-element.3), channel_id=1, source_target_pairs={{0,24},{8,0},{16,8},{24,16},{32,56},{40,32},{48,40},{56,48},{64,88... | collective-permute-start | bytes 786440 | tf_op jit(solution)/shard_map/ppermute | solution.py:93
  9.6 2.0 %collective-permute-done.9 = bf16[32,32,128]{2,1,0:T(8,128)(2,1)S(1)} collective-permute-done((bf16[32,32,128]{2,1,0:T(8,128)(2,1)S(1)}, bf16[32,32,128]{2,1,0:T(8,128)(2,1)S(1)}, u32[]{:S(2)}, u32[]{:S(2)}) %collective-permute-start.9) | collective-permute-done | bytes 262176 | tf_op jit(solution)/shard_map/ppermute | solution.py:92
  11.7 0.1 collective-permute-start.10
  11.8 0.0 collective-permute-done.8
  11.8 2.7 %collective-permute-start.11 = (bf16[16,32,128]{2,1,0:T(8,128)(2,1)S(1)}, bf16[16,32,128]{2,1,0:T(8,128)(2,1)S(1)}, u32[]{:S(2)}, u32[]{:S(2)}) collective-permute-start(bf16[16,32,128]{2,1,0:T(8,128)(2,1)S(1)} %slice.58), channel_id=1, source_target_pairs={{0,96},{8,104},{16,112},{24,120},{32,0},{40,8},{48,16},{56,24},{64... | collective-permute-start | bytes 393224 | tf_op jit(solution)/shard_map/ppermute | solution.py:97
  14.5 0.7 collective-permute-done.1
  15.2 1.0 collective-permute-start.2
  16.2 0.0 collective-permute-done
  16.2 2.2 %collective-permute-start.3 = (bf16[16,32,128]{2,1,0:T(8,128)(2,1)S(1)}, bf16[16,32,128]{2,1,0:T(8,128)(2,1)S(1)}, u32[]{:S(2)}, u32[]{:S(2)}) collective-permute-start(bf16[16,32,128]{2,1,0:T(8,128)(2,1)S(1)} %slice.53), channel_id=1, source_target_pairs={{0,24},{8,0},{16,8},{24,16},{32,56},{40,32},{48,40},{56,48},{64,88... | collective-permute-start | bytes 393224 | tf_op jit(solution)/shard_map/ppermute | solution.py:97
  18.4 0.0 collective-permute-done.10
  18.4 0.0 collective-permute-done.11
  18.4 0.1 pad_maximum_fusion.1
  18.6 0.1 collective-permute-start.13
  18.7 2.7 %collective-permute-start.12 = (bf16[4,32,32,128]{3,2,1,0:T(8,128)(2,1)S(1)}, bf16[4,32,32,128]{3,2,1,0:T(8,128)(2,1)S(1)}, u32[]{:S(2)}, u32[]{:S(2)}) collective-permute-start(bf16[4,32,32,128]{3,2,1,0:T(8,128)(2,1)S(1)} %pad_maximum_fusion.1), channel_id=1, source_target_pairs={{0,24},{8,0},{16,8},{24,16},{32,56},{40,32},{48,40},{56,48},{64,88... | collective-permute-start | bytes 3145736 | tf_op jit(solution)/shard_map/ppermute | solution.py:93
  21.3 0.0 collective-permute-done.2
  21.3 0.0 collective-permute-done.3
  21.4 0.0 copy-start.8
  21.4 0.1 pad_maximum_fusion
  21.5 0.1 collective-permute-start.5
  21.6 2.7 %collective-permute-start.4 = (bf16[4,32,32,128]{3,2,1,0:T(8,128)(2,1)S(1)}, bf16[4,32,32,128]{3,2,1,0:T(8,128)(2,1)S(1)}, u32[]{:S(2)}, u32[]{:S(2)}) collective-permute-start(bf16[4,32,32,128]{3,2,1,0:T(8,128)(2,1)S(1)} %pad_maximum_fusion), channel_id=1, source_target_pairs={{0,96},{8,104},{16,112},{24,120},{32,0},{40,8},{48,16},{56,24},{64... | collective-permute-start | bytes 3145736 | tf_op jit(solution)/shard_map/ppermute | solution.py:93
  24.3 19.1 %collective-permute-done.13 = bf16[4,32,32,128]{3,2,1,0:T(8,128)(2,1)S(1)} collective-permute-done((bf16[4,32,32,128]{3,2,1,0:T(8,128)(2,1)S(1)}, bf16[4,32,32,128]{3,2,1,0:T(8,128)(2,1)S(1)}, u32[]{:S(2)}, u32[]{:S(2)}) %collective-permute-start.13) | collective-permute-done | bytes 1048608 | tf_op jit(solution)/shard_map/ppermute | solution.py:92
  43.3 0.9 slice.59
  44.3 0.2 collective-permute-start.14
  44.5 0.0 collective-permute-done.12
  44.5 0.9 slice.60
  45.4 2.5 %collective-permute-start.15 = (bf16[2,32,32,128]{3,2,1,0:T(8,128)(2,1)}, bf16[2,32,32,128]{3,2,1,0:T(8,128)(2,1)}, u32[]{:S(2)}, u32[]{:S(2)}) collective-permute-start(bf16[2,32,32,128]{3,2,1,0:T(8,128)(2,1)} %slice.60), channel_id=1, source_target_pairs={{0,24},{8,0},{16,8},{24,16},{32,56},{40,32},{48,40},{56,48},{64,88... | collective-permute-start | bytes 1572872 | tf_op jit(solution)/shard_map/ppermute | solution.py:97
  47.9 0.0 collective-permute-done.5
  47.9 0.9 slice.54
  48.7 0.0 collective-permute-start.6
  48.7 0.0 collective-permute-done.4
  48.8 0.9 slice.55
  49.7 2.7 %collective-permute-start.7 = (bf16[2,32,32,128]{3,2,1,0:T(8,128)(2,1)}, bf16[2,32,32,128]{3,2,1,0:T(8,128)(2,1)}, u32[]{:S(2)}, u32[]{:S(2)}) collective-permute-start(bf16[2,32,32,128]{3,2,1,0:T(8,128)(2,1)} %slice.55), channel_id=1, source_target_pairs={{0,96},{8,104},{16,112},{24,120},{32,0},{40,8},{48,16},{56,24},{64... | collective-permute-start | bytes 1572872 | tf_op jit(solution)/shard_map/ppermute | solution.py:97
  52.3 1.3 %fusion.6.index_ref = s32[512]{0:T(512)} fusion(s32[512]{0:T(512)} %param.12, s32[512]{0:T(512)} %param.10, s32[]{:T(128)S(6)} %select_n.55, s32[]{:T(128)S(6)} %select_n.52), kind=kLoop, calls=%fused_computation.28 | loop fusion | flops 52224 | bytes 6152 | tf_op jit(solution)/shard_map/add | solution.py:131
  53.7 2.9 %collective-permute-done.14 = bf16[2,32,32,128]{3,2,1,0:T(8,128)(2,1)} collective-permute-done((bf16[2,32,32,128]{3,2,1,0:T(8,128)(2,1)}, bf16[2,32,32,128]{3,2,1,0:T(8,128)(2,1)}, u32[]{:S(2)}, u32[]{:S(2)}) %collective-permute-start.14) | collective-permute-done | bytes 524320 | tf_op jit(solution)/shard_map/ppermute | solution.py:96
  56.6 0.2 collective-permute-done.15
  56.7 3.7 %collective-permute-done.6 = bf16[2,32,32,128]{3,2,1,0:T(8,128)(2,1)} collective-permute-done((bf16[2,32,32,128]{3,2,1,0:T(8,128)(2,1)}, bf16[2,32,32,128]{3,2,1,0:T(8,128)(2,1)}, u32[]{:S(2)}, u32[]{:S(2)}) %collective-permute-start.6) | collective-permute-done | bytes 524320 | tf_op jit(solution)/shard_map/ppermute | solution.py:96
  60.5 0.0 collective-permute-done.7
  60.5 18.4 %shard_map.95 = f32[8,16,2,4,128]{4,3,2,1,0:T(4,128)} custom-call(s32[512]{0:T(512)} %fusion.6.index_ref, s32[512]{0:T(512)} %obs_ref.1, bf16[128,32,128]{2,1,0:T(8,128)(2,1)} %bitcast.25, bf16[128,32,128]{2,1,0:T(8,128)(2,1)} %bitcast.29, bf16[64,32,128]{2,1,0:T(8,128)(2,1)} %bitcast.6.refs_2_, bf16[64,32,128]{2,1,0:T(8,128)(2,1)} %bitcast.7.refs_3_, ...), custom_call_target="tpu_custom_call" | custom-call | tf_op jit(solution)/shard_map/pallas_call | solution.py:69
  78.9 25.9 %all_to_all.5 = f32[128,2,4,128]{3,2,1,0:T(4,128)S(1)} all-to-all(f32[128,2,4,128]{3,2,1,0:T(4,128)} %bitcast.30), channel_id=1, replica_groups=mesh['grp'=16,'lag'=8] {'lag','grp'}, dimensions={0} | all-to-all | bytes 1048576 | tf_op jit(solution)/shard_map/all_to_all | solution.py:134
  104.8 0.1 reduce_sum.9
  105.0 0.0 copy-start.7
  105.0 0.7 fusion.7
  (21 shorter events, 0.1 us)
Async XLA Ops:
  0.6 104.4 %copy-start = (bf16[2,128,128]{2,1,0:T(8,128)(2,1)S(1)}, bf16[2,128,128]{2,1,0:T(8,128)(2,1)}, u32[]{:S(2)}) copy-start(bf16[2,128,128]{2,1,0:T(8,128)(2,1)} %param.14) | copy-start | bytes 196612
  2.2 9.5 %collective-permute-start.9 = (bf16[32,32,128]{2,1,0:T(8,128)(2,1)S(1)}, bf16[32,32,128]{2,1,0:T(8,128)(2,1)S(1)}, u32[]{:S(2)}, u32[]{:S(2)}) collective-permute-start(bf16[32,32,128]{2,1,0:T(8,128)(2,1)S(1)} %get-tuple-element.4), channel_id=1, source_target_pairs={{0,32},{8,40},{16,48},{24,56},{32,64},{40,72},{48,80},{56,88},{64,... | collective-permute-start | bytes 786440 | tf_op jit(solution)/shard_map/ppermute | solution.py:92
  4.4 7.4 %collective-permute-start.8 = (bf16[32,32,128]{2,1,0:T(8,128)(2,1)S(1)}, bf16[32,32,128]{2,1,0:T(8,128)(2,1)S(1)}, u32[]{:S(2)}, u32[]{:S(2)}) collective-permute-start(bf16[32,32,128]{2,1,0:T(8,128)(2,1)S(1)} %get-tuple-element.4), channel_id=1, source_target_pairs={{0,96},{8,104},{16,112},{24,120},{32,0},{40,8},{48,16},{56,24},{64... | collective-permute-start | bytes 786440 | tf_op jit(solution)/shard_map/ppermute | solution.py:93
  5.9 9.3 %collective-permute-start.1 = (bf16[32,32,128]{2,1,0:T(8,128)(2,1)S(1)}, bf16[32,32,128]{2,1,0:T(8,128)(2,1)S(1)}, u32[]{:S(2)}, u32[]{:S(2)}) collective-permute-start(bf16[32,32,128]{2,1,0:T(8,128)(2,1)S(1)} %get-tuple-element.3), channel_id=1, source_target_pairs={{0,8},{8,16},{16,24},{24,0},{32,40},{40,48},{48,56},{56,32},{64,72... | collective-permute-start | bytes 786440 | tf_op jit(solution)/shard_map/ppermute | solution.py:92
  7.5 8.6 %collective-permute-start = (bf16[32,32,128]{2,1,0:T(8,128)(2,1)S(1)}, bf16[32,32,128]{2,1,0:T(8,128)(2,1)S(1)}, u32[]{:S(2)}, u32[]{:S(2)}) collective-permute-start(bf16[32,32,128]{2,1,0:T(8,128)(2,1)S(1)} %get-tuple-element.3), channel_id=1, source_target_pairs={{0,24},{8,0},{16,8},{24,16},{32,56},{40,32},{48,40},{56,48},{64,88... | collective-permute-start | bytes 786440 | tf_op jit(solution)/shard_map/ppermute | solution.py:93
  11.7 6.7 %collective-permute-start.10 = (bf16[16,32,128]{2,1,0:T(8,128)(2,1)S(1)}, bf16[16,32,128]{2,1,0:T(8,128)(2,1)S(1)}, u32[]{:S(2)}, u32[]{:S(2)}) collective-permute-start(bf16[16,32,128]{2,1,0:T(8,128)(2,1)S(1)} %slice.57), channel_id=1, source_target_pairs={{0,32},{8,40},{16,48},{24,56},{32,64},{40,72},{48,80},{56,88},{64,... | collective-permute-start | bytes 393224 | tf_op jit(solution)/shard_map/ppermute | solution.py:96
  11.8 6.6 %collective-permute-start.11 = (bf16[16,32,128]{2,1,0:T(8,128)(2,1)S(1)}, bf16[16,32,128]{2,1,0:T(8,128)(2,1)S(1)}, u32[]{:S(2)}, u32[]{:S(2)}) collective-permute-start(bf16[16,32,128]{2,1,0:T(8,128)(2,1)S(1)} %slice.58), channel_id=1, source_target_pairs={{0,96},{8,104},{16,112},{24,120},{32,0},{40,8},{48,16},{56,24},{64... | collective-permute-start | bytes 393224 | tf_op jit(solution)/shard_map/ppermute | solution.py:97
  15.2 6.1 %collective-permute-start.2 = (bf16[16,32,128]{2,1,0:T(8,128)(2,1)S(1)}, bf16[16,32,128]{2,1,0:T(8,128)(2,1)S(1)}, u32[]{:S(2)}, u32[]{:S(2)}) collective-permute-start(bf16[16,32,128]{2,1,0:T(8,128)(2,1)S(1)} %slice.52), channel_id=1, source_target_pairs={{0,8},{8,16},{16,24},{24,0},{32,40},{40,48},{48,56},{56,32},{64,72... | collective-permute-start | bytes 393224 | tf_op jit(solution)/shard_map/ppermute | solution.py:96
  16.2 5.2 %collective-permute-start.3 = (bf16[16,32,128]{2,1,0:T(8,128)(2,1)S(1)}, bf16[16,32,128]{2,1,0:T(8,128)(2,1)S(1)}, u32[]{:S(2)}, u32[]{:S(2)}) collective-permute-start(bf16[16,32,128]{2,1,0:T(8,128)(2,1)S(1)} %slice.53), channel_id=1, source_target_pairs={{0,24},{8,0},{16,8},{24,16},{32,56},{40,32},{48,40},{56,48},{64,88... | collective-permute-start | bytes 393224 | tf_op jit(solution)/shard_map/ppermute | solution.py:97
  18.6 41.9 %copy-start.1 = (bf16[4,32,32,128]{3,2,1,0:T(8,128)(2,1)}, bf16[4,32,32,128]{3,2,1,0:T(8,128)(2,1)S(1)}, u32[]{:S(2)}) copy-start(bf16[4,32,32,128]{3,2,1,0:T(8,128)(2,1)S(1)} %pad_maximum_fusion.1) | copy-start | bytes 3145732
  18.6 24.8 %collective-permute-start.13 = (bf16[4,32,32,128]{3,2,1,0:T(8,128)(2,1)S(1)}, bf16[4,32,32,128]{3,2,1,0:T(8,128)(2,1)S(1)}, u32[]{:S(2)}, u32[]{:S(2)}) collective-permute-start(bf16[4,32,32,128]{3,2,1,0:T(8,128)(2,1)S(1)} %pad_maximum_fusion.1), channel_id=1, source_target_pairs={{0,8},{8,16},{16,24},{24,0},{32,40},{40,48},{48,56},{56,32},{64,72... | collective-permute-start | bytes 3145736 | tf_op jit(solution)/shard_map/ppermute | solution.py:92
  18.7 25.8 %collective-permute-start.12 = (bf16[4,32,32,128]{3,2,1,0:T(8,128)(2,1)S(1)}, bf16[4,32,32,128]{3,2,1,0:T(8,128)(2,1)S(1)}, u32[]{:S(2)}, u32[]{:S(2)}) collective-permute-start(bf16[4,32,32,128]{3,2,1,0:T(8,128)(2,1)S(1)} %pad_maximum_fusion.1), channel_id=1, source_target_pairs={{0,24},{8,0},{16,8},{24,16},{32,56},{40,32},{48,40},{56,48},{64,88... | collective-permute-start | bytes 3145736 | tf_op jit(solution)/shard_map/ppermute | solution.py:93
  21.4 83.6 %copy-start.8 = (f32[2,4,128]{2,1,0:T(4,128)S(1)}, f32[2,4,128]{2,1,0:T(4,128)}, u32[]{:S(2)}) copy-start(f32[2,4,128]{2,1,0:T(4,128)} %param.13) | copy-start | bytes 12292
  21.5 39.0 %copy-start.2 = (bf16[4,32,32,128]{3,2,1,0:T(8,128)(2,1)}, bf16[4,32,32,128]{3,2,1,0:T(8,128)(2,1)S(1)}, u32[]{:S(2)}) copy-start(bf16[4,32,32,128]{3,2,1,0:T(8,128)(2,1)S(1)} %pad_maximum_fusion) | copy-start | bytes 3145732
  21.5 26.3 %collective-permute-start.5 = (bf16[4,32,32,128]{3,2,1,0:T(8,128)(2,1)S(1)}, bf16[4,32,32,128]{3,2,1,0:T(8,128)(2,1)S(1)}, u32[]{:S(2)}, u32[]{:S(2)}) collective-permute-start(bf16[4,32,32,128]{3,2,1,0:T(8,128)(2,1)S(1)} %pad_maximum_fusion), channel_id=1, source_target_pairs={{0,32},{8,40},{16,48},{24,56},{32,64},{40,72},{48,80},{56,88},{64,... | collective-permute-start | bytes 3145736 | tf_op jit(solution)/shard_map/ppermute | solution.py:92
  21.6 27.2 %collective-permute-start.4 = (bf16[4,32,32,128]{3,2,1,0:T(8,128)(2,1)S(1)}, bf16[4,32,32,128]{3,2,1,0:T(8,128)(2,1)S(1)}, u32[]{:S(2)}, u32[]{:S(2)}) collective-permute-start(bf16[4,32,32,128]{3,2,1,0:T(8,128)(2,1)S(1)} %pad_maximum_fusion), channel_id=1, source_target_pairs={{0,96},{8,104},{16,112},{24,120},{32,0},{40,8},{48,16},{56,24},{64... | collective-permute-start | bytes 3145736 | tf_op jit(solution)/shard_map/ppermute | solution.py:93
  43.3 17.1 %copy-start.3 = (bf16[4,32,32,128]{3,2,1,0:T(8,128)(2,1)}, bf16[4,32,32,128]{3,2,1,0:T(8,128)(2,1)S(1)}, u32[]{:S(2)}) copy-start(bf16[4,32,32,128]{3,2,1,0:T(8,128)(2,1)S(1)} %collective-permute-done.13) | copy-start | bytes 3145732
  44.3 12.3 %collective-permute-start.14 = (bf16[2,32,32,128]{3,2,1,0:T(8,128)(2,1)}, bf16[2,32,32,128]{3,2,1,0:T(8,128)(2,1)}, u32[]{:S(2)}, u32[]{:S(2)}) collective-permute-start(bf16[2,32,32,128]{3,2,1,0:T(8,128)(2,1)} %slice.59), channel_id=1, source_target_pairs={{0,8},{8,16},{16,24},{24,0},{32,40},{40,48},{48,56},{56,32},{64,72... | collective-permute-start | bytes 1572872 | tf_op jit(solution)/shard_map/ppermute | solution.py:96
  44.5 4.3 %copy-start.4 = (bf16[4,32,32,128]{3,2,1,0:T(8,128)(2,1)}, bf16[4,32,32,128]{3,2,1,0:T(8,128)(2,1)S(1)}, u32[]{:S(2)}) copy-start(bf16[4,32,32,128]{3,2,1,0:T(8,128)(2,1)S(1)} %collective-permute-done.12) | copy-start | bytes 3145732
  45.4 11.4 %collective-permute-start.15 = (bf16[2,32,32,128]{3,2,1,0:T(8,128)(2,1)}, bf16[2,32,32,128]{3,2,1,0:T(8,128)(2,1)}, u32[]{:S(2)}, u32[]{:S(2)}) collective-permute-start(bf16[2,32,32,128]{3,2,1,0:T(8,128)(2,1)} %slice.60), channel_id=1, source_target_pairs={{0,24},{8,0},{16,8},{24,16},{32,56},{40,32},{48,40},{56,48},{64,88... | collective-permute-start | bytes 1572872 | tf_op jit(solution)/shard_map/ppermute | solution.py:97
  47.9 1.8 %copy-start.5 = (bf16[4,32,32,128]{3,2,1,0:T(8,128)(2,1)}, bf16[4,32,32,128]{3,2,1,0:T(8,128)(2,1)S(1)}, u32[]{:S(2)}) copy-start(bf16[4,32,32,128]{3,2,1,0:T(8,128)(2,1)S(1)} %collective-permute-done.5) | copy-start | bytes 3145732
  48.7 11.7 %collective-permute-start.6 = (bf16[2,32,32,128]{3,2,1,0:T(8,128)(2,1)}, bf16[2,32,32,128]{3,2,1,0:T(8,128)(2,1)}, u32[]{:S(2)}, u32[]{:S(2)}) collective-permute-start(bf16[2,32,32,128]{3,2,1,0:T(8,128)(2,1)} %slice.54), channel_id=1, source_target_pairs={{0,32},{8,40},{16,48},{24,56},{32,64},{40,72},{48,80},{56,88},{64,... | collective-permute-start | bytes 1572872 | tf_op jit(solution)/shard_map/ppermute | solution.py:96
  48.8 3.6 %copy-start.6 = (bf16[4,32,32,128]{3,2,1,0:T(8,128)(2,1)}, bf16[4,32,32,128]{3,2,1,0:T(8,128)(2,1)S(1)}, u32[]{:S(2)}) copy-start(bf16[4,32,32,128]{3,2,1,0:T(8,128)(2,1)S(1)} %collective-permute-done.4) | copy-start | bytes 3145732
  49.7 10.8 %collective-permute-start.7 = (bf16[2,32,32,128]{3,2,1,0:T(8,128)(2,1)}, bf16[2,32,32,128]{3,2,1,0:T(8,128)(2,1)}, u32[]{:S(2)}, u32[]{:S(2)}) collective-permute-start(bf16[2,32,32,128]{3,2,1,0:T(8,128)(2,1)} %slice.55), channel_id=1, source_target_pairs={{0,96},{8,104},{16,112},{24,120},{32,0},{40,8},{48,16},{56,24},{64... | collective-permute-start | bytes 1572872 | tf_op jit(solution)/shard_map/ppermute | solution.py:97
  105.0 0.8 copy-start.7

commit v16 on v15

--- a/solution.py
+++ b/solution.py
@@ -106,13 +106,12 @@
     n_lag = lax.axis_size("lag")
     obs_dev, ang_dev, width = incident.shape
     observers = obs_dev * n_grp
-    hist16 = history.astype(jnp.bfloat16)
-    lag_count, src_dev, angles, _ = hist16.shape
+    lag_count, src_dev, angles, _ = history.shape
     rows = 4
     cols = n_grp // rows
     assert lag_count == 2 and rows * cols == n_grp
-    first = ring_gather(ring_gather(hist16[0], rows, cols, True), rows, cols, False, pieces=True)
-    second = ring_gather(ring_gather(hist16[1], rows, cols, False), rows, cols, True, pieces=True)
+    first = ring_gather(ring_gather(history[0].astype(jnp.bfloat16), rows, cols, True), rows, cols, False, pieces=True)
+    second = ring_gather(ring_gather(history[1].astype(jnp.bfloat16), rows, cols, False), rows, cols, True, pieces=True)
     tables = [p.reshape(-1, angles, width) for p in first + second]
     me = lax.axis_index("grp")
     owner = tile_src // src_dev

time: 106 us -> 106 us (level)
  other arithmetic: 3.13 us -> 1.78 us
  local copies, waits for them, and re-layouts: 3.87 us -> 5.03 us
    convert_element_type x1 -> x0, other arithmetic: 1.35 us -> none  [body(): hist16 = history.astype(jnp.bfloat16)]
    slice x1, local copies, waits for them, and re-layouts: 0.16 us -> 1.32 us  [body(): history[1].astype(jnp.bfloat16)]
where the time goes in v16:
time: 106 us
  waiting for transfers between devices  28.6 us (27%)
  blocking collectives  25.9 us (24%)
  starting transfers between devices  24.2 us (23%)
  Pallas kernels  18.4 us (17%)
  local copies, waits for them, and re-layouts  5.03 us (5%)
  other arithmetic  1.78 us (2%)
    all_to_all x1, blocking collectives, body(): received = lax.all_to_all(partial, ('lag', 'grp'), 0, 0, tiled=True)  25.9 us
    ppermute x4, waiting for transfers between devices, ring_gather(): from_behind = lax.ppermute(x, 'grp', plus)  21.8 us
    pallas_call x1, Pallas kernels, field_partial(): pl.pallas_call(field_kernel, grid_spec=grid_spec, out_shape=jax.ShapeDtyp...  18.4 us
    ppermute x4, starting transfers between devices, ring_gather(): far_b = lax.ppermute(from_ahead[half:], 'grp', minus)  10.1 us
    ppermute x4, starting transfers between devices, ring_gather(): from_ahead = lax.ppermute(x, 'grp', minus)  8.97 us
    ppermute x4, waiting for transfers between devices, ring_gather(): far_a = lax.ppermute(from_behind[:half], 'grp', plus)  6.64 us
    ppermute x4, starting transfers between devices, ring_gather(): from_behind = lax.ppermute(x, 'grp', plus)  3.98 us
  transfers between devices with their start and end apart: 16, of which 6 were waited for; matrix products, arithmetic and copies ran while one was open for 5% of the time, Pallas kernels for 0%

profile of v16, /device:TPU:1, one launch (start us, length us, event | category | flops | bytes accessed | tf_op | source)
XLA Modules:
  0.0 105.6 jit_solution(4437698837518821106)
XLA Ops:
  0.6 0.0 copy-start
  0.6 1.3 %fusion.10 = (bf16[1,32,32,128]{3,2,1,0:T(8,128)(2,1)S(1)}, bf16[1,32,32,128]{3,2,1,0:T(8,128)(2,1)S(1)}) fusion(f32[2,32,32,128]{3,2,1,0:T(8,128)} %param.8), kind=kLoop, calls=%fused_computation.38 | loop fusion | bytes 1048576 | tf_op jit(solution)/shard_map/slice | solution.py:114
  2.0 2.2 %collective-permute-start.9 = (bf16[32,32,128]{2,1,0:T(8,128)(2,1)S(1)}, bf16[32,32,128]{2,1,0:T(8,128)(2,1)S(1)}, u32[]{:S(2)}, u32[]{:S(2)}) collective-permute-start(bf16[32,32,128]{2,1,0:T(8,128)(2,1)S(1)} %bitcast.31), channel_id=1, source_target_pairs={{0,32},{8,40},{16,48},{24,56},{32,64},{40,72},{48,80},{56,88},{64,... | collective-permute-start | bytes 786440 | tf_op jit(solution)/shard_map/ppermute | solution.py:92
  4.2 1.5 %collective-permute-start.8 = (bf16[32,32,128]{2,1,0:T(8,128)(2,1)S(1)}, bf16[32,32,128]{2,1,0:T(8,128)(2,1)S(1)}, u32[]{:S(2)}, u32[]{:S(2)}) collective-permute-start(bf16[32,32,128]{2,1,0:T(8,128)(2,1)S(1)} %bitcast.32), channel_id=1, source_target_pairs={{0,96},{8,104},{16,112},{24,120},{32,0},{40,8},{48,16},{56,24},{64... | collective-permute-start | bytes 786440 | tf_op jit(solution)/shard_map/ppermute | solution.py:93
  5.7 1.6 %collective-permute-start.1 = (bf16[32,32,128]{2,1,0:T(8,128)(2,1)S(1)}, bf16[32,32,128]{2,1,0:T(8,128)(2,1)S(1)}, u32[]{:S(2)}, u32[]{:S(2)}) collective-permute-start(bf16[32,32,128]{2,1,0:T(8,128)(2,1)S(1)} %bitcast.29), channel_id=1, source_target_pairs={{0,8},{8,16},{16,24},{24,0},{32,40},{40,48},{48,56},{56,32},{64,72... | collective-permute-start | bytes 786440 | tf_op jit(solution)/shard_map/ppermute | solution.py:92
  7.3 2.1 %collective-permute-start = (bf16[32,32,128]{2,1,0:T(8,128)(2,1)S(1)}, bf16[32,32,128]{2,1,0:T(8,128)(2,1)S(1)}, u32[]{:S(2)}, u32[]{:S(2)}) collective-permute-start(bf16[32,32,128]{2,1,0:T(8,128)(2,1)S(1)} %bitcast.30), channel_id=1, source_target_pairs={{0,24},{8,0},{16,8},{24,16},{32,56},{40,32},{48,40},{56,48},{64,88... | collective-permute-start | bytes 786440 | tf_op jit(solution)/shard_map/ppermute | solution.py:93
  9.4 2.0 %collective-permute-done.9 = bf16[32,32,128]{2,1,0:T(8,128)(2,1)S(1)} collective-permute-done((bf16[32,32,128]{2,1,0:T(8,128)(2,1)S(1)}, bf16[32,32,128]{2,1,0:T(8,128)(2,1)S(1)}, u32[]{:S(2)}, u32[]{:S(2)}) %collective-permute-start.9) | collective-permute-done | bytes 262176 | tf_op jit(solution)/shard_map/ppermute | solution.py:92
  11.5 0.1 collective-permute-start.10
  11.6 0.0 collective-permute-done.8
  11.6 2.7 %collective-permute-start.11 = (bf16[16,32,128]{2,1,0:T(8,128)(2,1)S(1)}, bf16[16,32,128]{2,1,0:T(8,128)(2,1)S(1)}, u32[]{:S(2)}, u32[]{:S(2)}) collective-permute-start(bf16[16,32,128]{2,1,0:T(8,128)(2,1)S(1)} %slice.56), channel_id=1, source_target_pairs={{0,96},{8,104},{16,112},{24,120},{32,0},{40,8},{48,16},{56,24},{64... | collective-permute-start | bytes 393224 | tf_op jit(solution)/shard_map/ppermute | solution.py:97
  14.3 0.7 collective-permute-done.1
  15.0 1.0 collective-permute-start.2
  16.0 0.0 collective-permute-done
  16.0 2.2 %collective-permute-start.3 = (bf16[16,32,128]{2,1,0:T(8,128)(2,1)S(1)}, bf16[16,32,128]{2,1,0:T(8,128)(2,1)S(1)}, u32[]{:S(2)}, u32[]{:S(2)}) collective-permute-start(bf16[16,32,128]{2,1,0:T(8,128)(2,1)S(1)} %slice.52), channel_id=1, source_target_pairs={{0,24},{8,0},{16,8},{24,16},{32,56},{40,32},{48,40},{56,48},{64,88... | collective-permute-start | bytes 393224 | tf_op jit(solution)/shard_map/ppermute | solution.py:97
  18.2 0.0 collective-permute-done.10
  18.2 0.0 collective-permute-done.11
  18.2 0.1 pad_maximum_fusion.1
  18.4 0.1 collective-permute-start.13
  18.5 2.7 %collective-permute-start.12 = (bf16[4,32,32,128]{3,2,1,0:T(8,128)(2,1)S(1)}, bf16[4,32,32,128]{3,2,1,0:T(8,128)(2,1)S(1)}, u32[]{:S(2)}, u32[]{:S(2)}) collective-permute-start(bf16[4,32,32,128]{3,2,1,0:T(8,128)(2,1)S(1)} %pad_maximum_fusion.1), channel_id=1, source_target_pairs={{0,24},{8,0},{16,8},{24,16},{32,56},{40,32},{48,40},{56,48},{64,88... | collective-permute-start | bytes 3145736 | tf_op jit(solution)/shard_map/ppermute | solution.py:93
  21.1 0.0 collective-permute-done.2
  21.1 0.0 collective-permute-done.3
  21.2 0.0 copy-start.8
  21.2 0.1 pad_maximum_fusion
  21.3 0.1 collective-permute-start.5
  21.4 2.7 %collective-permute-start.4 = (bf16[4,32,32,128]{3,2,1,0:T(8,128)(2,1)S(1)}, bf16[4,32,32,128]{3,2,1,0:T(8,128)(2,1)S(1)}, u32[]{:S(2)}, u32[]{:S(2)}) collective-permute-start(bf16[4,32,32,128]{3,2,1,0:T(8,128)(2,1)S(1)} %pad_maximum_fusion), channel_id=1, source_target_pairs={{0,96},{8,104},{16,112},{24,120},{32,0},{40,8},{48,16},{56,24},{64... | collective-permute-start | bytes 3145736 | tf_op jit(solution)/shard_map/ppermute | solution.py:93
  24.1 19.1 %collective-permute-done.13 = bf16[4,32,32,128]{3,2,1,0:T(8,128)(2,1)S(1)} collective-permute-done((bf16[4,32,32,128]{3,2,1,0:T(8,128)(2,1)S(1)}, bf16[4,32,32,128]{3,2,1,0:T(8,128)(2,1)S(1)}, u32[]{:S(2)}, u32[]{:S(2)}) %collective-permute-start.13) | collective-permute-done | bytes 1048608 | tf_op jit(solution)/shard_map/ppermute | solution.py:92
  43.2 0.9 slice.57
  44.1 0.2 collective-permute-start.14
  44.3 0.0 collective-permute-done.12
  44.3 0.9 slice.58
  45.2 2.5 %collective-permute-start.15 = (bf16[2,32,32,128]{3,2,1,0:T(8,128)(2,1)}, bf16[2,32,32,128]{3,2,1,0:T(8,128)(2,1)}, u32[]{:S(2)}, u32[]{:S(2)}) collective-permute-start(bf16[2,32,32,128]{3,2,1,0:T(8,128)(2,1)} %slice.58), channel_id=1, source_target_pairs={{0,24},{8,0},{16,8},{24,16},{32,56},{40,32},{48,40},{56,48},{64,88... | collective-permute-start | bytes 1572872 | tf_op jit(solution)/shard_map/ppermute | solution.py:97
  47.7 0.0 collective-permute-done.5
  47.7 0.9 slice.53
  48.6 0.0 collective-permute-start.6
  48.6 0.0 collective-permute-done.4
  48.6 0.0 copy-done.4
  48.6 0.9 slice.54
  49.5 2.7 %collective-permute-start.7 = (bf16[2,32,32,128]{3,2,1,0:T(8,128)(2,1)}, bf16[2,32,32,128]{3,2,1,0:T(8,128)(2,1)}, u32[]{:S(2)}, u32[]{:S(2)}) collective-permute-start(bf16[2,32,32,128]{3,2,1,0:T(8,128)(2,1)} %slice.54), channel_id=1, source_target_pairs={{0,96},{8,104},{16,112},{24,120},{32,0},{40,8},{48,16},{56,24},{64... | collective-permute-start | bytes 1572872 | tf_op jit(solution)/shard_map/ppermute | solution.py:97
  52.1 1.3 %fusion.6.index_ref = s32[512]{0:T(512)} fusion(s32[512]{0:T(512)} %param.12, s32[512]{0:T(512)} %param.10, s32[]{:T(128)S(6)} %select_n.55, s32[]{:T(128)S(6)} %select_n.52), kind=kLoop, calls=%fused_computation.30 | loop fusion | flops 52224 | bytes 6152 | tf_op jit(solution)/shard_map/add | solution.py:130
  53.5 2.9 %collective-permute-done.14 = bf16[2,32,32,128]{3,2,1,0:T(8,128)(2,1)} collective-permute-done((bf16[2,32,32,128]{3,2,1,0:T(8,128)(2,1)}, bf16[2,32,32,128]{3,2,1,0:T(8,128)(2,1)}, u32[]{:S(2)}, u32[]{:S(2)}) %collective-permute-start.14) | collective-permute-done | bytes 524320 | tf_op jit(solution)/shard_map/ppermute | solution.py:96
  56.4 0.2 collective-permute-done.15
  56.6 3.7 %collective-permute-done.6 = bf16[2,32,32,128]{3,2,1,0:T(8,128)(2,1)} collective-permute-done((bf16[2,32,32,128]{3,2,1,0:T(8,128)(2,1)}, bf16[2,32,32,128]{3,2,1,0:T(8,128)(2,1)}, u32[]{:S(2)}, u32[]{:S(2)}) %collective-permute-start.6) | collective-permute-done | bytes 524320 | tf_op jit(solution)/shard_map/ppermute | solution.py:96
  60.3 0.0 collective-permute-done.7
  60.3 18.4 %shard_map.95 = f32[8,16,2,4,128]{4,3,2,1,0:T(4,128)} custom-call(s32[512]{0:T(512)} %fusion.6.index_ref, s32[512]{0:T(512)} %obs_ref.1, bf16[128,32,128]{2,1,0:T(8,128)(2,1)} %bitcast.23, bf16[128,32,128]{2,1,0:T(8,128)(2,1)} %bitcast.27, bf16[64,32,128]{2,1,0:T(8,128)(2,1)} %bitcast.6.refs_2_, bf16[64,32,128]{2,1,0:T(8,128)(2,1)} %bitcast.7.refs_3_, ...), custom_call_target="tpu_custom_call" | custom-call | tf_op jit(solution)/shard_map/pallas_call | solution.py:69
  78.7 25.9 %all_to_all.5 = f32[128,2,4,128]{3,2,1,0:T(4,128)S(1)} all-to-all(f32[128,2,4,128]{3,2,1,0:T(4,128)} %bitcast.28), channel_id=1, replica_groups=mesh['grp'=16,'lag'=8] {'lag','grp'}, dimensions={0} | all-to-all | bytes 1048576 | tf_op jit(solution)/shard_map/all_to_all | solution.py:133
  104.7 0.1 reduce_sum.9
  104.8 0.0 copy-start.7
  104.8 0.7 fusion.7
  (20 shorter events, 0.1 us)
Async XLA Ops:
  0.6 104.2 %copy-start = (bf16[2,128,128]{2,1,0:T(8,128)(2,1)S(1)}, bf16[2,128,128]{2,1,0:T(8,128)(2,1)}, u32[]{:S(2)}) copy-start(bf16[2,128,128]{2,1,0:T(8,128)(2,1)} %param.14) | copy-start | bytes 196612
  2.0 9.5 %collective-permute-start.9 = (bf16[32,32,128]{2,1,0:T(8,128)(2,1)S(1)}, bf16[32,32,128]{2,1,0:T(8,128)(2,1)S(1)}, u32[]{:S(2)}, u32[]{:S(2)}) collective-permute-start(bf16[32,32,128]{2,1,0:T(8,128)(2,1)S(1)} %bitcast.31), channel_id=1, source_target_pairs={{0,32},{8,40},{16,48},{24,56},{32,64},{40,72},{48,80},{56,88},{64,... | collective-permute-start | bytes 786440 | tf_op jit(solution)/shard_map/ppermute | solution.py:92
  4.2 7.4 %collective-permute-start.8 = (bf16[32,32,128]{2,1,0:T(8,128)(2,1)S(1)}, bf16[32,32,128]{2,1,0:T(8,128)(2,1)S(1)}, u32[]{:S(2)}, u32[]{:S(2)}) collective-permute-start(bf16[32,32,128]{2,1,0:T(8,128)(2,1)S(1)} %bitcast.32), channel_id=1, source_target_pairs={{0,96},{8,104},{16,112},{24,120},{32,0},{40,8},{48,16},{56,24},{64... | collective-permute-start | bytes 786440 | tf_op jit(solution)/shard_map/ppermute | solution.py:93
  5.7 9.3 %collective-permute-start.1 = (bf16[32,32,128]{2,1,0:T(8,128)(2,1)S(1)}, bf16[32,32,128]{2,1,0:T(8,128)(2,1)S(1)}, u32[]{:S(2)}, u32[]{:S(2)}) collective-permute-start(bf16[32,32,128]{2,1,0:T(8,128)(2,1)S(1)} %bitcast.29), channel_id=1, source_target_pairs={{0,8},{8,16},{16,24},{24,0},{32,40},{40,48},{48,56},{56,32},{64,72... | collective-permute-start | bytes 786440 | tf_op jit(solution)/shard_map/ppermute | solution.py:92
  7.3 8.6 %collective-permute-start = (bf16[32,32,128]{2,1,0:T(8,128)(2,1)S(1)}, bf16[32,32,128]{2,1,0:T(8,128)(2,1)S(1)}, u32[]{:S(2)}, u32[]{:S(2)}) collective-permute-start(bf16[32,32,128]{2,1,0:T(8,128)(2,1)S(1)} %bitcast.30), channel_id=1, source_target_pairs={{0,24},{8,0},{16,8},{24,16},{32,56},{40,32},{48,40},{56,48},{64,88... | collective-permute-start | bytes 786440 | tf_op jit(solution)/shard_map/ppermute | solution.py:93
  11.5 6.7 %collective-permute-start.10 = (bf16[16,32,128]{2,1,0:T(8,128)(2,1)S(1)}, bf16[16,32,128]{2,1,0:T(8,128)(2,1)S(1)}, u32[]{:S(2)}, u32[]{:S(2)}) collective-permute-start(bf16[16,32,128]{2,1,0:T(8,128)(2,1)S(1)} %slice.55), channel_id=1, source_target_pairs={{0,32},{8,40},{16,48},{24,56},{32,64},{40,72},{48,80},{56,88},{64,... | collective-permute-start | bytes 393224 | tf_op jit(solution)/shard_map/ppermute | solution.py:96
  11.6 6.6 %collective-permute-start.11 = (bf16[16,32,128]{2,1,0:T(8,128)(2,1)S(1)}, bf16[16,32,128]{2,1,0:T(8,128)(2,1)S(1)}, u32[]{:S(2)}, u32[]{:S(2)}) collective-permute-start(bf16[16,32,128]{2,1,0:T(8,128)(2,1)S(1)} %slice.56), channel_id=1, source_target_pairs={{0,96},{8,104},{16,112},{24,120},{32,0},{40,8},{48,16},{56,24},{64... | collective-permute-start | bytes 393224 | tf_op jit(solution)/shard_map/ppermute | solution.py:97
  15.0 6.1 %collective-permute-start.2 = (bf16[16,32,128]{2,1,0:T(8,128)(2,1)S(1)}, bf16[16,32,128]{2,1,0:T(8,128)(2,1)S(1)}, u32[]{:S(2)}, u32[]{:S(2)}) collective-permute-start(bf16[16,32,128]{2,1,0:T(8,128)(2,1)S(1)} %slice.51), channel_id=1, source_target_pairs={{0,8},{8,16},{16,24},{24,0},{32,40},{40,48},{48,56},{56,32},{64,72... | collective-permute-start | bytes 393224 | tf_op jit(solution)/shard_map/ppermute | solution.py:96
  16.0 5.2 %collective-permute-start.3 = (bf16[16,32,128]{2,1,0:T(8,128)(2,1)S(1)}, bf16[16,32,128]{2,1,0:T(8,128)(2,1)S(1)}, u32[]{:S(2)}, u32[]{:S(2)}) collective-permute-start(bf16[16,32,128]{2,1,0:T(8,128)(2,1)S(1)} %slice.52), channel_id=1, source_target_pairs={{0,24},{8,0},{16,8},{24,16},{32,56},{40,32},{48,40},{56,48},{64,88... | collective-permute-start | bytes 393224 | tf_op jit(solution)/shard_map/ppermute | solution.py:97
  18.4 41.9 %copy-start.1 = (bf16[4,32,32,128]{3,2,1,0:T(8,128)(2,1)}, bf16[4,32,32,128]{3,2,1,0:T(8,128)(2,1)S(1)}, u32[]{:S(2)}) copy-start(bf16[4,32,32,128]{3,2,1,0:T(8,128)(2,1)S(1)} %pad_maximum_fusion.1) | copy-start | bytes 3145732
  18.4 24.8 %collective-permute-start.13 = (bf16[4,32,32,128]{3,2,1,0:T(8,128)(2,1)S(1)}, bf16[4,32,32,128]{3,2,1,0:T(8,128)(2,1)S(1)}, u32[]{:S(2)}, u32[]{:S(2)}) collective-permute-start(bf16[4,32,32,128]{3,2,1,0:T(8,128)(2,1)S(1)} %pad_maximum_fusion.1), channel_id=1, source_target_pairs={{0,8},{8,16},{16,24},{24,0},{32,40},{40,48},{48,56},{56,32},{64,72... | collective-permute-start | bytes 3145736 | tf_op jit(solution)/shard_map/ppermute | solution.py:92
  18.5 25.8 %collective-permute-start.12 = (bf16[4,32,32,128]{3,2,1,0:T(8,128)(2,1)S(1)}, bf16[4,32,32,128]{3,2,1,0:T(8,128)(2,1)S(1)}, u32[]{:S(2)}, u32[]{:S(2)}) collective-permute-start(bf16[4,32,32,128]{3,2,1,0:T(8,128)(2,1)S(1)} %pad_maximum_fusion.1), channel_id=1, source_target_pairs={{0,24},{8,0},{16,8},{24,16},{32,56},{40,32},{48,40},{56,48},{64,88... | collective-permute-start | bytes 3145736 | tf_op jit(solution)/shard_map/ppermute | solution.py:93
  21.2 83.7 %copy-start.8 = (f32[2,4,128]{2,1,0:T(4,128)S(1)}, f32[2,4,128]{2,1,0:T(4,128)}, u32[]{:S(2)}) copy-start(f32[2,4,128]{2,1,0:T(4,128)} %param.13) | copy-start | bytes 12292
  21.3 39.0 %copy-start.2 = (bf16[4,32,32,128]{3,2,1,0:T(8,128)(2,1)}, bf16[4,32,32,128]{3,2,1,0:T(8,128)(2,1)S(1)}, u32[]{:S(2)}) copy-start(bf16[4,32,32,128]{3,2,1,0:T(8,128)(2,1)S(1)} %pad_maximum_fusion) | copy-start | bytes 3145732
  21.3 26.3 %collective-permute-start.5 = (bf16[4,32,32,128]{3,2,1,0:T(8,128)(2,1)S(1)}, bf16[4,32,32,128]{3,2,1,0:T(8,128)(2,1)S(1)}, u32[]{:S(2)}, u32[]{:S(2)}) collective-permute-start(bf16[4,32,32,128]{3,2,1,0:T(8,128)(2,1)S(1)} %pad_maximum_fusion), channel_id=1, source_target_pairs={{0,32},{8,40},{16,48},{24,56},{32,64},{40,72},{48,80},{56,88},{64,... | collective-permute-start | bytes 3145736 | tf_op jit(solution)/shard_map/ppermute | solution.py:92
  21.4 27.2 %collective-permute-start.4 = (bf16[4,32,32,128]{3,2,1,0:T(8,128)(2,1)S(1)}, bf16[4,32,32,128]{3,2,1,0:T(8,128)(2,1)S(1)}, u32[]{:S(2)}, u32[]{:S(2)}) collective-permute-start(bf16[4,32,32,128]{3,2,1,0:T(8,128)(2,1)S(1)} %pad_maximum_fusion), channel_id=1, source_target_pairs={{0,96},{8,104},{16,112},{24,120},{32,0},{40,8},{48,16},{56,24},{64... | collective-permute-start | bytes 3145736 | tf_op jit(solution)/shard_map/ppermute | solution.py:93
  43.1 17.1 %copy-start.3 = (bf16[4,32,32,128]{3,2,1,0:T(8,128)(2,1)}, bf16[4,32,32,128]{3,2,1,0:T(8,128)(2,1)S(1)}, u32[]{:S(2)}) copy-start(bf16[4,32,32,128]{3,2,1,0:T(8,128)(2,1)S(1)} %collective-permute-done.13) | copy-start | bytes 3145732
  44.1 12.3 %collective-permute-start.14 = (bf16[2,32,32,128]{3,2,1,0:T(8,128)(2,1)}, bf16[2,32,32,128]{3,2,1,0:T(8,128)(2,1)}, u32[]{:S(2)}, u32[]{:S(2)}) collective-permute-start(bf16[2,32,32,128]{3,2,1,0:T(8,128)(2,1)} %slice.57), channel_id=1, source_target_pairs={{0,8},{8,16},{16,24},{24,0},{32,40},{40,48},{48,56},{56,32},{64,72... | collective-permute-start | bytes 1572872 | tf_op jit(solution)/shard_map/ppermute | solution.py:96
  44.3 4.3 %copy-start.4 = (bf16[4,32,32,128]{3,2,1,0:T(8,128)(2,1)}, bf16[4,32,32,128]{3,2,1,0:T(8,128)(2,1)S(1)}, u32[]{:S(2)}) copy-start(bf16[4,32,32,128]{3,2,1,0:T(8,128)(2,1)S(1)} %collective-permute-done.12) | copy-start | bytes 3145732
  45.2 11.4 %collective-permute-start.15 = (bf16[2,32,32,128]{3,2,1,0:T(8,128)(2,1)}, bf16[2,32,32,128]{3,2,1,0:T(8,128)(2,1)}, u32[]{:S(2)}, u32[]{:S(2)}) collective-permute-start(bf16[2,32,32,128]{3,2,1,0:T(8,128)(2,1)} %slice.58), channel_id=1, source_target_pairs={{0,24},{8,0},{16,8},{24,16},{32,56},{40,32},{48,40},{56,48},{64,88... | collective-permute-start | bytes 1572872 | tf_op jit(solution)/shard_map/ppermute | solution.py:97
  47.7 1.8 %copy-start.5 = (bf16[4,32,32,128]{3,2,1,0:T(8,128)(2,1)}, bf16[4,32,32,128]{3,2,1,0:T(8,128)(2,1)S(1)}, u32[]{:S(2)}) copy-start(bf16[4,32,32,128]{3,2,1,0:T(8,128)(2,1)S(1)} %collective-permute-done.5) | copy-start | bytes 3145732
  48.6 11.7 %collective-permute-start.6 = (bf16[2,32,32,128]{3,2,1,0:T(8,128)(2,1)}, bf16[2,32,32,128]{3,2,1,0:T(8,128)(2,1)}, u32[]{:S(2)}, u32[]{:S(2)}) collective-permute-start(bf16[2,32,32,128]{3,2,1,0:T(8,128)(2,1)} %slice.53), channel_id=1, source_target_pairs={{0,32},{8,40},{16,48},{24,56},{32,64},{40,72},{48,80},{56,88},{64,... | collective-permute-start | bytes 1572872 | tf_op jit(solution)/shard_map/ppermute | solution.py:96
  48.6 3.6 %copy-start.6 = (bf16[4,32,32,128]{3,2,1,0:T(8,128)(2,1)}, bf16[4,32,32,128]{3,2,1,0:T(8,128)(2,1)S(1)}, u32[]{:S(2)}) copy-start(bf16[4,32,32,128]{3,2,1,0:T(8,128)(2,1)S(1)} %collective-permute-done.4) | copy-start | bytes 3145732
  49.5 10.8 %collective-permute-start.7 = (bf16[2,32,32,128]{3,2,1,0:T(8,128)(2,1)}, bf16[2,32,32,128]{3,2,1,0:T(8,128)(2,1)}, u32[]{:S(2)}, u32[]{:S(2)}) collective-permute-start(bf16[2,32,32,128]{3,2,1,0:T(8,128)(2,1)} %slice.54), channel_id=1, source_target_pairs={{0,96},{8,104},{16,112},{24,120},{32,0},{40,8},{48,16},{56,24},{64... | collective-permute-start | bytes 1572872 | tf_op jit(solution)/shard_map/ppermute | solution.py:97
  104.8 0.8 copy-start.7

commit v17 on v16

--- a/solution.py
+++ b/solution.py
@@ -9,14 +9,19 @@
 
 
 def field_kernel(index_ref, obs_ref, *refs):
-    pieces = refs[:-5]
-    tiles_ref, out_ref, table, acc, sems = refs[-5:]
+    pieces = refs[:-6]
+    tiles_hbm, out_ref, table, tiles_ref, acc, sems = refs[-6:]
     step = pl.program_id(0)
     steps = pl.num_programs(0)
-    block = tiles_ref.shape[0]
+    block = tiles_ref.shape[1]
+    slot = step % 2
+
+    def tiles_copy(which, into):
+        return pltpu.make_async_copy(tiles_hbm.at[pl.ds(which * block, block)], tiles_ref.at[into], sems.at[len(pieces) + into])
 
     @pl.when(step == 0)
     def _():
+        tiles_copy(0, 0).start()
         copies = []
         offset = 0
         for j, piece in enumerate(pieces):
@@ -29,9 +34,15 @@
         for copy in copies:
             copy.wait()
 
+    tiles_copy(step, slot).wait()
+
+    @pl.when(step + 1 < steps)
+    def _():
+        tiles_copy(step + 1, 1 - slot).start()
+
     def one(t, carry):
         r = step * block + t
-        term = lax.dot_general(table[index_ref[r]], tiles_ref[t], (((1,), (1,)), ((), ())),
+        term = lax.dot_general(table[index_ref[r]], tiles_ref[slot, t], (((1,), (1,)), ((), ())),
                                preferred_element_type=jnp.float32)
         o = obs_ref[r]
         acc[o] = acc[o] + term
@@ -56,14 +67,13 @@
     grid_spec = pltpu.PrefetchScalarGridSpec(
         num_scalar_prefetch=2,
         grid=(n_tiles // BLOCK,),
-        in_specs=[pl.BlockSpec(memory_space=pl.ANY) for _ in pieces] + [
-            pl.BlockSpec((BLOCK,) + tiles.shape[1:], lambda i, *_: (i, 0, 0)),
-        ],
+        in_specs=[pl.BlockSpec(memory_space=pl.ANY) for _ in pieces] + [pl.BlockSpec(memory_space=pl.ANY)],
         out_specs=pl.BlockSpec(out_shape, lambda i, *_: (0, 0, 0, 0, 0)),
         scratch_shapes=[
             pltpu.VMEM((total, angles, width), pieces[0].dtype),
+            pltpu.VMEM((2, BLOCK) + tiles.shape[1:], tiles.dtype),
             pltpu.VMEM((groups * obs_dev + 1, angles, width), jnp.float32),
-            pltpu.SemaphoreType.DMA((len(pieces),)),
+            pltpu.SemaphoreType.DMA((len(pieces) + 2,)),
         ],
     )
     return pl.pallas_call(

time: 106 us -> 104 us (0.981)
  Pallas kernels: 18.4 us -> 17 us
    pallas_call x1, Pallas kernels: 18.4 us -> 17 us  [field_partial(): pl.pallas_call(field_kernel, grid_spec=grid_spec, out_shape=jax.ShapeDtyp...]
where the time goes in v17:
time: 104 us
  waiting for transfers between devices  28.6 us (28%)
  blocking collectives  25.9 us (25%)
  starting transfers between devices  24.2 us (23%)
  Pallas kernels  17 us (16%)
  local copies, waits for them, and re-layouts  5.03 us (5%)
  other arithmetic  1.78 us (2%)
    all_to_all x1, blocking collectives, body(): received = lax.all_to_all(partial, ('lag', 'grp'), 0, 0, tiled=True)  25.9 us
    ppermute x4, waiting for transfers between devices, ring_gather(): from_behind = lax.ppermute(x, 'grp', plus)  21.8 us
    pallas_call x1, Pallas kernels, field_partial(): pl.pallas_call(field_kernel, grid_spec=grid_spec, out_shape=jax.ShapeDtyp...  17 us
    ppermute x4, starting transfers between devices, ring_gather(): far_b = lax.ppermute(from_ahead[half:], 'grp', minus)  10.1 us
    ppermute x4, starting transfers between devices, ring_gather(): from_ahead = lax.ppermute(x, 'grp', minus)  8.97 us
    ppermute x4, waiting for transfers between devices, ring_gather(): far_a = lax.ppermute(from_behind[:half], 'grp', plus)  6.64 us
    ppermute x4, starting transfers between devices, ring_gather(): from_behind = lax.ppermute(x, 'grp', plus)  3.98 us
  transfers between devices with their start and end apart: 16, of which 6 were waited for; matrix products, arithmetic and copies ran while one was open for 5% of the time, Pallas kernels for 0%

profile of v17, /device:TPU:1, one launch (start us, length us, event | category | flops | bytes accessed | tf_op | source)
XLA Modules:
  0.0 104.2 jit_solution(15733655316841911220)
XLA Ops:
  0.6 0.0 copy-start
  0.6 1.3 %fusion.10 = (bf16[1,32,32,128]{3,2,1,0:T(8,128)(2,1)S(1)}, bf16[1,32,32,128]{3,2,1,0:T(8,128)(2,1)S(1)}) fusion(f32[2,32,32,128]{3,2,1,0:T(8,128)} %param.8), kind=kLoop, calls=%fused_computation.38 | loop fusion | bytes 1048576 | tf_op jit(solution)/shard_map/slice | solution.py:124
  2.0 2.2 %collective-permute-start.9 = (bf16[32,32,128]{2,1,0:T(8,128)(2,1)S(1)}, bf16[32,32,128]{2,1,0:T(8,128)(2,1)S(1)}, u32[]{:S(2)}, u32[]{:S(2)}) collective-permute-start(bf16[32,32,128]{2,1,0:T(8,128)(2,1)S(1)} %bitcast.31), channel_id=1, source_target_pairs={{0,32},{8,40},{16,48},{24,56},{32,64},{40,72},{48,80},{56,88},{64,... | collective-permute-start | bytes 786440 | tf_op jit(solution)/shard_map/ppermute | solution.py:102
  4.2 1.5 %collective-permute-start.8 = (bf16[32,32,128]{2,1,0:T(8,128)(2,1)S(1)}, bf16[32,32,128]{2,1,0:T(8,128)(2,1)S(1)}, u32[]{:S(2)}, u32[]{:S(2)}) collective-permute-start(bf16[32,32,128]{2,1,0:T(8,128)(2,1)S(1)} %bitcast.32), channel_id=1, source_target_pairs={{0,96},{8,104},{16,112},{24,120},{32,0},{40,8},{48,16},{56,24},{64... | collective-permute-start | bytes 786440 | tf_op jit(solution)/shard_map/ppermute | solution.py:103
  5.7 1.6 %collective-permute-start.1 = (bf16[32,32,128]{2,1,0:T(8,128)(2,1)S(1)}, bf16[32,32,128]{2,1,0:T(8,128)(2,1)S(1)}, u32[]{:S(2)}, u32[]{:S(2)}) collective-permute-start(bf16[32,32,128]{2,1,0:T(8,128)(2,1)S(1)} %bitcast.29), channel_id=1, source_target_pairs={{0,8},{8,16},{16,24},{24,0},{32,40},{40,48},{48,56},{56,32},{64,72... | collective-permute-start | bytes 786440 | tf_op jit(solution)/shard_map/ppermute | solution.py:102
  7.3 2.1 %collective-permute-start = (bf16[32,32,128]{2,1,0:T(8,128)(2,1)S(1)}, bf16[32,32,128]{2,1,0:T(8,128)(2,1)S(1)}, u32[]{:S(2)}, u32[]{:S(2)}) collective-permute-start(bf16[32,32,128]{2,1,0:T(8,128)(2,1)S(1)} %bitcast.30), channel_id=1, source_target_pairs={{0,24},{8,0},{16,8},{24,16},{32,56},{40,32},{48,40},{56,48},{64,88... | collective-permute-start | bytes 786440 | tf_op jit(solution)/shard_map/ppermute | solution.py:103
  9.4 2.0 %collective-permute-done.9 = bf16[32,32,128]{2,1,0:T(8,128)(2,1)S(1)} collective-permute-done((bf16[32,32,128]{2,1,0:T(8,128)(2,1)S(1)}, bf16[32,32,128]{2,1,0:T(8,128)(2,1)S(1)}, u32[]{:S(2)}, u32[]{:S(2)}) %collective-permute-start.9) | collective-permute-done | bytes 262176 | tf_op jit(solution)/shard_map/ppermute | solution.py:102
  11.5 0.1 collective-permute-start.10
  11.6 0.0 collective-permute-done.8
  11.6 2.7 %collective-permute-start.11 = (bf16[16,32,128]{2,1,0:T(8,128)(2,1)S(1)}, bf16[16,32,128]{2,1,0:T(8,128)(2,1)S(1)}, u32[]{:S(2)}, u32[]{:S(2)}) collective-permute-start(bf16[16,32,128]{2,1,0:T(8,128)(2,1)S(1)} %slice.56), channel_id=1, source_target_pairs={{0,96},{8,104},{16,112},{24,120},{32,0},{40,8},{48,16},{56,24},{64... | collective-permute-start | bytes 393224 | tf_op jit(solution)/shard_map/ppermute | solution.py:107
  14.3 0.7 collective-permute-done.1
  15.0 1.0 collective-permute-start.2
  16.0 0.0 collective-permute-done
  16.0 2.2 %collective-permute-start.3 = (bf16[16,32,128]{2,1,0:T(8,128)(2,1)S(1)}, bf16[16,32,128]{2,1,0:T(8,128)(2,1)S(1)}, u32[]{:S(2)}, u32[]{:S(2)}) collective-permute-start(bf16[16,32,128]{2,1,0:T(8,128)(2,1)S(1)} %slice.52), channel_id=1, source_target_pairs={{0,24},{8,0},{16,8},{24,16},{32,56},{40,32},{48,40},{56,48},{64,88... | collective-permute-start | bytes 393224 | tf_op jit(solution)/shard_map/ppermute | solution.py:107
  18.2 0.0 collective-permute-done.10
  18.2 0.0 collective-permute-done.11
  18.2 0.1 pad_maximum_fusion.1
  18.4 0.1 collective-permute-start.13
  18.5 2.7 %collective-permute-start.12 = (bf16[4,32,32,128]{3,2,1,0:T(8,128)(2,1)S(1)}, bf16[4,32,32,128]{3,2,1,0:T(8,128)(2,1)S(1)}, u32[]{:S(2)}, u32[]{:S(2)}) collective-permute-start(bf16[4,32,32,128]{3,2,1,0:T(8,128)(2,1)S(1)} %pad_maximum_fusion.1), channel_id=1, source_target_pairs={{0,24},{8,0},{16,8},{24,16},{32,56},{40,32},{48,40},{56,48},{64,88... | collective-permute-start | bytes 3145736 | tf_op jit(solution)/shard_map/ppermute | solution.py:103
  21.1 0.0 collective-permute-done.2
  21.1 0.0 collective-permute-done.3
  21.2 0.0 copy-start.8
  21.2 0.1 pad_maximum_fusion
  21.3 0.1 collective-permute-start.5
  21.4 2.7 %collective-permute-start.4 = (bf16[4,32,32,128]{3,2,1,0:T(8,128)(2,1)S(1)}, bf16[4,32,32,128]{3,2,1,0:T(8,128)(2,1)S(1)}, u32[]{:S(2)}, u32[]{:S(2)}) collective-permute-start(bf16[4,32,32,128]{3,2,1,0:T(8,128)(2,1)S(1)} %pad_maximum_fusion), channel_id=1, source_target_pairs={{0,96},{8,104},{16,112},{24,120},{32,0},{40,8},{48,16},{56,24},{64... | collective-permute-start | bytes 3145736 | tf_op jit(solution)/shard_map/ppermute | solution.py:103
  24.1 19.1 %collective-permute-done.13 = bf16[4,32,32,128]{3,2,1,0:T(8,128)(2,1)S(1)} collective-permute-done((bf16[4,32,32,128]{3,2,1,0:T(8,128)(2,1)S(1)}, bf16[4,32,32,128]{3,2,1,0:T(8,128)(2,1)S(1)}, u32[]{:S(2)}, u32[]{:S(2)}) %collective-permute-start.13) | collective-permute-done | bytes 1048608 | tf_op jit(solution)/shard_map/ppermute | solution.py:102
  43.2 0.9 slice.57
  44.1 0.2 collective-permute-start.14
  44.3 0.0 collective-permute-done.12
  44.3 0.9 slice.58
  45.2 2.5 %collective-permute-start.15 = (bf16[2,32,32,128]{3,2,1,0:T(8,128)(2,1)}, bf16[2,32,32,128]{3,2,1,0:T(8,128)(2,1)}, u32[]{:S(2)}, u32[]{:S(2)}) collective-permute-start(bf16[2,32,32,128]{3,2,1,0:T(8,128)(2,1)} %slice.58), channel_id=1, source_target_pairs={{0,24},{8,0},{16,8},{24,16},{32,56},{40,32},{48,40},{56,48},{64,88... | collective-permute-start | bytes 1572872 | tf_op jit(solution)/shard_map/ppermute | solution.py:107
  47.7 0.0 collective-permute-done.5
  47.7 0.9 slice.53
  48.6 0.0 collective-permute-start.6
  48.6 0.0 collective-permute-done.4
  48.6 0.0 copy-done.4
  48.6 0.9 slice.54
  49.5 2.7 %collective-permute-start.7 = (bf16[2,32,32,128]{3,2,1,0:T(8,128)(2,1)}, bf16[2,32,32,128]{3,2,1,0:T(8,128)(2,1)}, u32[]{:S(2)}, u32[]{:S(2)}) collective-permute-start(bf16[2,32,32,128]{3,2,1,0:T(8,128)(2,1)} %slice.54), channel_id=1, source_target_pairs={{0,96},{8,104},{16,112},{24,120},{32,0},{40,8},{48,16},{56,24},{64... | collective-permute-start | bytes 1572872 | tf_op jit(solution)/shard_map/ppermute | solution.py:107
  52.1 1.3 %fusion.6.index_ref = s32[512]{0:T(512)} fusion(s32[512]{0:T(512)} %param.12, s32[512]{0:T(512)} %param.10, s32[]{:T(128)S(6)} %select_n.55, s32[]{:T(128)S(6)} %select_n.52), kind=kLoop, calls=%fused_computation.30 | loop fusion | flops 52224 | bytes 6152 | tf_op jit(solution)/shard_map/add | solution.py:140
  53.5 2.9 %collective-permute-done.14 = bf16[2,32,32,128]{3,2,1,0:T(8,128)(2,1)} collective-permute-done((bf16[2,32,32,128]{3,2,1,0:T(8,128)(2,1)}, bf16[2,32,32,128]{3,2,1,0:T(8,128)(2,1)}, u32[]{:S(2)}, u32[]{:S(2)}) %collective-permute-start.14) | collective-permute-done | bytes 524320 | tf_op jit(solution)/shard_map/ppermute | solution.py:106
  56.4 0.2 collective-permute-done.15
  56.6 3.7 %collective-permute-done.6 = bf16[2,32,32,128]{3,2,1,0:T(8,128)(2,1)} collective-permute-done((bf16[2,32,32,128]{3,2,1,0:T(8,128)(2,1)}, bf16[2,32,32,128]{3,2,1,0:T(8,128)(2,1)}, u32[]{:S(2)}, u32[]{:S(2)}) %collective-permute-start.6) | collective-permute-done | bytes 524320 | tf_op jit(solution)/shard_map/ppermute | solution.py:106
  60.3 0.0 collective-permute-done.7
  60.3 17.0 %shard_map.95 = f32[8,16,2,4,128]{4,3,2,1,0:T(4,128)} custom-call(s32[512]{0:T(512)} %fusion.6.index_ref, s32[512]{0:T(512)} %obs_ref.1, bf16[128,32,128]{2,1,0:T(8,128)(2,1)} %bitcast.23, bf16[128,32,128]{2,1,0:T(8,128)(2,1)} %bitcast.27, bf16[64,32,128]{2,1,0:T(8,128)(2,1)} %bitcast.6.refs_2_, bf16[64,32,128]{2,1,0:T(8,128)(2,1)} %bitcast.7.refs_3_, ...), custom_call_target="tpu_custom_call" | custom-call | tf_op jit(solution)/shard_map/pallas_call | solution.py:79
  77.3 25.9 %all_to_all.5 = f32[128,2,4,128]{3,2,1,0:T(4,128)S(1)} all-to-all(f32[128,2,4,128]{3,2,1,0:T(4,128)} %bitcast.28), channel_id=1, replica_groups=mesh['grp'=16,'lag'=8] {'lag','grp'}, dimensions={0} | all-to-all | bytes 1048576 | tf_op jit(solution)/shard_map/all_to_all | solution.py:143
  103.3 0.1 reduce_sum.9
  103.4 0.0 copy-start.7
  103.4 0.7 fusion.7
  (20 shorter events, 0.1 us)
Async XLA Ops:
  0.6 102.8 %copy-start = (bf16[2,128,128]{2,1,0:T(8,128)(2,1)S(1)}, bf16[2,128,128]{2,1,0:T(8,128)(2,1)}, u32[]{:S(2)}) copy-start(bf16[2,128,128]{2,1,0:T(8,128)(2,1)} %param.14) | copy-start | bytes 196612
  2.0 9.5 %collective-permute-start.9 = (bf16[32,32,128]{2,1,0:T(8,128)(2,1)S(1)}, bf16[32,32,128]{2,1,0:T(8,128)(2,1)S(1)}, u32[]{:S(2)}, u32[]{:S(2)}) collective-permute-start(bf16[32,32,128]{2,1,0:T(8,128)(2,1)S(1)} %bitcast.31), channel_id=1, source_target_pairs={{0,32},{8,40},{16,48},{24,56},{32,64},{40,72},{48,80},{56,88},{64,... | collective-permute-start | bytes 786440 | tf_op jit(solution)/shard_map/ppermute | solution.py:102
  4.2 7.4 %collective-permute-start.8 = (bf16[32,32,128]{2,1,0:T(8,128)(2,1)S(1)}, bf16[32,32,128]{2,1,0:T(8,128)(2,1)S(1)}, u32[]{:S(2)}, u32[]{:S(2)}) collective-permute-start(bf16[32,32,128]{2,1,0:T(8,128)(2,1)S(1)} %bitcast.32), channel_id=1, source_target_pairs={{0,96},{8,104},{16,112},{24,120},{32,0},{40,8},{48,16},{56,24},{64... | collective-permute-start | bytes 786440 | tf_op jit(solution)/shard_map/ppermute | solution.py:103
  5.7 9.3 %collective-permute-start.1 = (bf16[32,32,128]{2,1,0:T(8,128)(2,1)S(1)}, bf16[32,32,128]{2,1,0:T(8,128)(2,1)S(1)}, u32[]{:S(2)}, u32[]{:S(2)}) collective-permute-start(bf16[32,32,128]{2,1,0:T(8,128)(2,1)S(1)} %bitcast.29), channel_id=1, source_target_pairs={{0,8},{8,16},{16,24},{24,0},{32,40},{40,48},{48,56},{56,32},{64,72... | collective-permute-start | bytes 786440 | tf_op jit(solution)/shard_map/ppermute | solution.py:102
  7.3 8.6 %collective-permute-start = (bf16[32,32,128]{2,1,0:T(8,128)(2,1)S(1)}, bf16[32,32,128]{2,1,0:T(8,128)(2,1)S(1)}, u32[]{:S(2)}, u32[]{:S(2)}) collective-permute-start(bf16[32,32,128]{2,1,0:T(8,128)(2,1)S(1)} %bitcast.30), channel_id=1, source_target_pairs={{0,24},{8,0},{16,8},{24,16},{32,56},{40,32},{48,40},{56,48},{64,88... | collective-permute-start | bytes 786440 | tf_op jit(solution)/shard_map/ppermute | solution.py:103
  11.5 6.7 %collective-permute-start.10 = (bf16[16,32,128]{2,1,0:T(8,128)(2,1)S(1)}, bf16[16,32,128]{2,1,0:T(8,128)(2,1)S(1)}, u32[]{:S(2)}, u32[]{:S(2)}) collective-permute-start(bf16[16,32,128]{2,1,0:T(8,128)(2,1)S(1)} %slice.55), channel_id=1, source_target_pairs={{0,32},{8,40},{16,48},{24,56},{32,64},{40,72},{48,80},{56,88},{64,... | collective-permute-start | bytes 393224 | tf_op jit(solution)/shard_map/ppermute | solution.py:106
  11.6 6.6 %collective-permute-start.11 = (bf16[16,32,128]{2,1,0:T(8,128)(2,1)S(1)}, bf16[16,32,128]{2,1,0:T(8,128)(2,1)S(1)}, u32[]{:S(2)}, u32[]{:S(2)}) collective-permute-start(bf16[16,32,128]{2,1,0:T(8,128)(2,1)S(1)} %slice.56), channel_id=1, source_target_pairs={{0,96},{8,104},{16,112},{24,120},{32,0},{40,8},{48,16},{56,24},{64... | collective-permute-start | bytes 393224 | tf_op jit(solution)/shard_map/ppermute | solution.py:107
  15.0 6.1 %collective-permute-start.2 = (bf16[16,32,128]{2,1,0:T(8,128)(2,1)S(1)}, bf16[16,32,128]{2,1,0:T(8,128)(2,1)S(1)}, u32[]{:S(2)}, u32[]{:S(2)}) collective-permute-start(bf16[16,32,128]{2,1,0:T(8,128)(2,1)S(1)} %slice.51), channel_id=1, source_target_pairs={{0,8},{8,16},{16,24},{24,0},{32,40},{40,48},{48,56},{56,32},{64,72... | collective-permute-start | bytes 393224 | tf_op jit(solution)/shard_map/ppermute | solution.py:106
  16.0 5.2 %collective-permute-start.3 = (bf16[16,32,128]{2,1,0:T(8,128)(2,1)S(1)}, bf16[16,32,128]{2,1,0:T(8,128)(2,1)S(1)}, u32[]{:S(2)}, u32[]{:S(2)}) collective-permute-start(bf16[16,32,128]{2,1,0:T(8,128)(2,1)S(1)} %slice.52), channel_id=1, source_target_pairs={{0,24},{8,0},{16,8},{24,16},{32,56},{40,32},{48,40},{56,48},{64,88... | collective-permute-start | bytes 393224 | tf_op jit(solution)/shard_map/ppermute | solution.py:107
  18.4 41.9 %copy-start.1 = (bf16[4,32,32,128]{3,2,1,0:T(8,128)(2,1)}, bf16[4,32,32,128]{3,2,1,0:T(8,128)(2,1)S(1)}, u32[]{:S(2)}) copy-start(bf16[4,32,32,128]{3,2,1,0:T(8,128)(2,1)S(1)} %pad_maximum_fusion.1) | copy-start | bytes 3145732
  18.4 24.8 %collective-permute-start.13 = (bf16[4,32,32,128]{3,2,1,0:T(8,128)(2,1)S(1)}, bf16[4,32,32,128]{3,2,1,0:T(8,128)(2,1)S(1)}, u32[]{:S(2)}, u32[]{:S(2)}) collective-permute-start(bf16[4,32,32,128]{3,2,1,0:T(8,128)(2,1)S(1)} %pad_maximum_fusion.1), channel_id=1, source_target_pairs={{0,8},{8,16},{16,24},{24,0},{32,40},{40,48},{48,56},{56,32},{64,72... | collective-permute-start | bytes 3145736 | tf_op jit(solution)/shard_map/ppermute | solution.py:102
  18.5 25.8 %collective-permute-start.12 = (bf16[4,32,32,128]{3,2,1,0:T(8,128)(2,1)S(1)}, bf16[4,32,32,128]{3,2,1,0:T(8,128)(2,1)S(1)}, u32[]{:S(2)}, u32[]{:S(2)}) collective-permute-start(bf16[4,32,32,128]{3,2,1,0:T(8,128)(2,1)S(1)} %pad_maximum_fusion.1), channel_id=1, source_target_pairs={{0,24},{8,0},{16,8},{24,16},{32,56},{40,32},{48,40},{56,48},{64,88... | collective-permute-start | bytes 3145736 | tf_op jit(solution)/shard_map/ppermute | solution.py:103
  21.2 82.3 %copy-start.8 = (f32[2,4,128]{2,1,0:T(4,128)S(1)}, f32[2,4,128]{2,1,0:T(4,128)}, u32[]{:S(2)}) copy-start(f32[2,4,128]{2,1,0:T(4,128)} %param.13) | copy-start | bytes 12292
  21.3 39.0 %copy-start.2 = (bf16[4,32,32,128]{3,2,1,0:T(8,128)(2,1)}, bf16[4,32,32,128]{3,2,1,0:T(8,128)(2,1)S(1)}, u32[]{:S(2)}) copy-start(bf16[4,32,32,128]{3,2,1,0:T(8,128)(2,1)S(1)} %pad_maximum_fusion) | copy-start | bytes 3145732
  21.3 26.3 %collective-permute-start.5 = (bf16[4,32,32,128]{3,2,1,0:T(8,128)(2,1)S(1)}, bf16[4,32,32,128]{3,2,1,0:T(8,128)(2,1)S(1)}, u32[]{:S(2)}, u32[]{:S(2)}) collective-permute-start(bf16[4,32,32,128]{3,2,1,0:T(8,128)(2,1)S(1)} %pad_maximum_fusion), channel_id=1, source_target_pairs={{0,32},{8,40},{16,48},{24,56},{32,64},{40,72},{48,80},{56,88},{64,... | collective-permute-start | bytes 3145736 | tf_op jit(solution)/shard_map/ppermute | solution.py:102
  21.4 27.2 %collective-permute-start.4 = (bf16[4,32,32,128]{3,2,1,0:T(8,128)(2,1)S(1)}, bf16[4,32,32,128]{3,2,1,0:T(8,128)(2,1)S(1)}, u32[]{:S(2)}, u32[]{:S(2)}) collective-permute-start(bf16[4,32,32,128]{3,2,1,0:T(8,128)(2,1)S(1)} %pad_maximum_fusion), channel_id=1, source_target_pairs={{0,96},{8,104},{16,112},{24,120},{32,0},{40,8},{48,16},{56,24},{64... | collective-permute-start | bytes 3145736 | tf_op jit(solution)/shard_map/ppermute | solution.py:103
  43.1 17.1 %copy-start.3 = (bf16[4,32,32,128]{3,2,1,0:T(8,128)(2,1)}, bf16[4,32,32,128]{3,2,1,0:T(8,128)(2,1)S(1)}, u32[]{:S(2)}) copy-start(bf16[4,32,32,128]{3,2,1,0:T(8,128)(2,1)S(1)} %collective-permute-done.13) | copy-start | bytes 3145732
  44.1 12.3 %collective-permute-start.14 = (bf16[2,32,32,128]{3,2,1,0:T(8,128)(2,1)}, bf16[2,32,32,128]{3,2,1,0:T(8,128)(2,1)}, u32[]{:S(2)}, u32[]{:S(2)}) collective-permute-start(bf16[2,32,32,128]{3,2,1,0:T(8,128)(2,1)} %slice.57), channel_id=1, source_target_pairs={{0,8},{8,16},{16,24},{24,0},{32,40},{40,48},{48,56},{56,32},{64,72... | collective-permute-start | bytes 1572872 | tf_op jit(solution)/shard_map/ppermute | solution.py:106
  44.3 4.3 %copy-start.4 = (bf16[4,32,32,128]{3,2,1,0:T(8,128)(2,1)}, bf16[4,32,32,128]{3,2,1,0:T(8,128)(2,1)S(1)}, u32[]{:S(2)}) copy-start(bf16[4,32,32,128]{3,2,1,0:T(8,128)(2,1)S(1)} %collective-permute-done.12) | copy-start | bytes 3145732
  45.2 11.4 %collective-permute-start.15 = (bf16[2,32,32,128]{3,2,1,0:T(8,128)(2,1)}, bf16[2,32,32,128]{3,2,1,0:T(8,128)(2,1)}, u32[]{:S(2)}, u32[]{:S(2)}) collective-permute-start(bf16[2,32,32,128]{3,2,1,0:T(8,128)(2,1)} %slice.58), channel_id=1, source_target_pairs={{0,24},{8,0},{16,8},{24,16},{32,56},{40,32},{48,40},{56,48},{64,88... | collective-permute-start | bytes 1572872 | tf_op jit(solution)/shard_map/ppermute | solution.py:107
  47.7 1.8 %copy-start.5 = (bf16[4,32,32,128]{3,2,1,0:T(8,128)(2,1)}, bf16[4,32,32,128]{3,2,1,0:T(8,128)(2,1)S(1)}, u32[]{:S(2)}) copy-start(bf16[4,32,32,128]{3,2,1,0:T(8,128)(2,1)S(1)} %collective-permute-done.5) | copy-start | bytes 3145732
  48.6 11.7 %collective-permute-start.6 = (bf16[2,32,32,128]{3,2,1,0:T(8,128)(2,1)}, bf16[2,32,32,128]{3,2,1,0:T(8,128)(2,1)}, u32[]{:S(2)}, u32[]{:S(2)}) collective-permute-start(bf16[2,32,32,128]{3,2,1,0:T(8,128)(2,1)} %slice.53), channel_id=1, source_target_pairs={{0,32},{8,40},{16,48},{24,56},{32,64},{40,72},{48,80},{56,88},{64,... | collective-permute-start | bytes 1572872 | tf_op jit(solution)/shard_map/ppermute | solution.py:106
  48.6 3.6 %copy-start.6 = (bf16[4,32,32,128]{3,2,1,0:T(8,128)(2,1)}, bf16[4,32,32,128]{3,2,1,0:T(8,128)(2,1)S(1)}, u32[]{:S(2)}) copy-start(bf16[4,32,32,128]{3,2,1,0:T(8,128)(2,1)S(1)} %collective-permute-done.4) | copy-start | bytes 3145732
  49.5 10.8 %collective-permute-start.7 = (bf16[2,32,32,128]{3,2,1,0:T(8,128)(2,1)}, bf16[2,32,32,128]{3,2,1,0:T(8,128)(2,1)}, u32[]{:S(2)}, u32[]{:S(2)}) collective-permute-start(bf16[2,32,32,128]{3,2,1,0:T(8,128)(2,1)} %slice.54), channel_id=1, source_target_pairs={{0,96},{8,104},{16,112},{24,120},{32,0},{40,8},{48,16},{56,24},{64... | collective-permute-start | bytes 1572872 | tf_op jit(solution)/shard_map/ppermute | solution.py:107
  103.4 0.8 copy-start.7

commit v18 on v17

--- a/solution.py
+++ b/solution.py
@@ -48,7 +48,7 @@
         acc[o] = acc[o] + term
         return carry
 
-    lax.fori_loop(0, block, one, 0, unroll=32)
+    lax.fori_loop(0, block, one, 0, unroll=block)
 
     @pl.when(step == steps - 1)
     def _():

time: 104 us -> 103 us (level)
  Pallas kernels: 17 us -> 15.6 us
    pallas_call x1, Pallas kernels: 17 us -> 15.6 us  [field_partial(): pl.pallas_call(field_kernel, grid_spec=grid_spec, out_shape=jax.ShapeDtyp...]
where the time goes in v18:
time: 103 us
  waiting for transfers between devices  28.6 us (28%)
  blocking collectives  25.9 us (25%)
  starting transfers between devices  24.2 us (23%)
  Pallas kernels  15.6 us (15%)
  local copies, waits for them, and re-layouts  5.03 us (5%)
  other arithmetic  1.78 us (2%)
    all_to_all x1, blocking collectives, body(): received = lax.all_to_all(partial, ('lag', 'grp'), 0, 0, tiled=True)  25.9 us
    ppermute x4, waiting for transfers between devices, ring_gather(): from_behind = lax.ppermute(x, 'grp', plus)  21.8 us
    pallas_call x1, Pallas kernels, field_partial(): pl.pallas_call(field_kernel, grid_spec=grid_spec, out_shape=jax.ShapeDtyp...  15.6 us
    ppermute x4, starting transfers between devices, ring_gather(): far_b = lax.ppermute(from_ahead[half:], 'grp', minus)  10.1 us
    ppermute x4, starting transfers between devices, ring_gather(): from_ahead = lax.ppermute(x, 'grp', minus)  8.97 us
    ppermute x4, waiting for transfers between devices, ring_gather(): far_a = lax.ppermute(from_behind[:half], 'grp', plus)  6.64 us
    ppermute x4, starting transfers between devices, ring_gather(): from_behind = lax.ppermute(x, 'grp', plus)  3.98 us
  transfers between devices with their start and end apart: 16, of which 6 were waited for; matrix products, arithmetic and copies ran while one was open for 5% of the time, Pallas kernels for 0%

profile of v18, /device:TPU:1, one launch (start us, length us, event | category | flops | bytes accessed | tf_op | source)
XLA Modules:
  0.0 102.8 jit_solution(6634360425105907228)
XLA Ops:
  0.6 0.0 copy-start
  0.6 1.3 %fusion.10 = (bf16[1,32,32,128]{3,2,1,0:T(8,128)(2,1)S(1)}, bf16[1,32,32,128]{3,2,1,0:T(8,128)(2,1)S(1)}) fusion(f32[2,32,32,128]{3,2,1,0:T(8,128)} %param.8), kind=kLoop, calls=%fused_computation.38 | loop fusion | bytes 1048576 | tf_op jit(solution)/shard_map/slice | solution.py:124
  2.0 2.2 %collective-permute-start.9 = (bf16[32,32,128]{2,1,0:T(8,128)(2,1)S(1)}, bf16[32,32,128]{2,1,0:T(8,128)(2,1)S(1)}, u32[]{:S(2)}, u32[]{:S(2)}) collective-permute-start(bf16[32,32,128]{2,1,0:T(8,128)(2,1)S(1)} %bitcast.31), channel_id=1, source_target_pairs={{0,32},{8,40},{16,48},{24,56},{32,64},{40,72},{48,80},{56,88},{64,... | collective-permute-start | bytes 786440 | tf_op jit(solution)/shard_map/ppermute | solution.py:102
  4.2 1.5 %collective-permute-start.8 = (bf16[32,32,128]{2,1,0:T(8,128)(2,1)S(1)}, bf16[32,32,128]{2,1,0:T(8,128)(2,1)S(1)}, u32[]{:S(2)}, u32[]{:S(2)}) collective-permute-start(bf16[32,32,128]{2,1,0:T(8,128)(2,1)S(1)} %bitcast.32), channel_id=1, source_target_pairs={{0,96},{8,104},{16,112},{24,120},{32,0},{40,8},{48,16},{56,24},{64... | collective-permute-start | bytes 786440 | tf_op jit(solution)/shard_map/ppermute | solution.py:103
  5.7 1.6 %collective-permute-start.1 = (bf16[32,32,128]{2,1,0:T(8,128)(2,1)S(1)}, bf16[32,32,128]{2,1,0:T(8,128)(2,1)S(1)}, u32[]{:S(2)}, u32[]{:S(2)}) collective-permute-start(bf16[32,32,128]{2,1,0:T(8,128)(2,1)S(1)} %bitcast.29), channel_id=1, source_target_pairs={{0,8},{8,16},{16,24},{24,0},{32,40},{40,48},{48,56},{56,32},{64,72... | collective-permute-start | bytes 786440 | tf_op jit(solution)/shard_map/ppermute | solution.py:102
  7.3 2.1 %collective-permute-start = (bf16[32,32,128]{2,1,0:T(8,128)(2,1)S(1)}, bf16[32,32,128]{2,1,0:T(8,128)(2,1)S(1)}, u32[]{:S(2)}, u32[]{:S(2)}) collective-permute-start(bf16[32,32,128]{2,1,0:T(8,128)(2,1)S(1)} %bitcast.30), channel_id=1, source_target_pairs={{0,24},{8,0},{16,8},{24,16},{32,56},{40,32},{48,40},{56,48},{64,88... | collective-permute-start | bytes 786440 | tf_op jit(solution)/shard_map/ppermute | solution.py:103
  9.4 2.0 %collective-permute-done.9 = bf16[32,32,128]{2,1,0:T(8,128)(2,1)S(1)} collective-permute-done((bf16[32,32,128]{2,1,0:T(8,128)(2,1)S(1)}, bf16[32,32,128]{2,1,0:T(8,128)(2,1)S(1)}, u32[]{:S(2)}, u32[]{:S(2)}) %collective-permute-start.9) | collective-permute-done | bytes 262176 | tf_op jit(solution)/shard_map/ppermute | solution.py:102
  11.5 0.1 collective-permute-start.10
  11.6 0.0 collective-permute-done.8
  11.6 2.7 %collective-permute-start.11 = (bf16[16,32,128]{2,1,0:T(8,128)(2,1)S(1)}, bf16[16,32,128]{2,1,0:T(8,128)(2,1)S(1)}, u32[]{:S(2)}, u32[]{:S(2)}) collective-permute-start(bf16[16,32,128]{2,1,0:T(8,128)(2,1)S(1)} %slice.56), channel_id=1, source_target_pairs={{0,96},{8,104},{16,112},{24,120},{32,0},{40,8},{48,16},{56,24},{64... | collective-permute-start | bytes 393224 | tf_op jit(solution)/shard_map/ppermute | solution.py:107
  14.3 0.7 collective-permute-done.1
  15.0 1.0 collective-permute-start.2
  16.0 0.0 collective-permute-done
  16.0 2.2 %collective-permute-start.3 = (bf16[16,32,128]{2,1,0:T(8,128)(2,1)S(1)}, bf16[16,32,128]{2,1,0:T(8,128)(2,1)S(1)}, u32[]{:S(2)}, u32[]{:S(2)}) collective-permute-start(bf16[16,32,128]{2,1,0:T(8,128)(2,1)S(1)} %slice.52), channel_id=1, source_target_pairs={{0,24},{8,0},{16,8},{24,16},{32,56},{40,32},{48,40},{56,48},{64,88... | collective-permute-start | bytes 393224 | tf_op jit(solution)/shard_map/ppermute | solution.py:107
  18.2 0.0 collective-permute-done.10
  18.2 0.0 collective-permute-done.11
  18.2 0.1 pad_maximum_fusion.1
  18.4 0.1 collective-permute-start.13
  18.5 2.7 %collective-permute-start.12 = (bf16[4,32,32,128]{3,2,1,0:T(8,128)(2,1)S(1)}, bf16[4,32,32,128]{3,2,1,0:T(8,128)(2,1)S(1)}, u32[]{:S(2)}, u32[]{:S(2)}) collective-permute-start(bf16[4,32,32,128]{3,2,1,0:T(8,128)(2,1)S(1)} %pad_maximum_fusion.1), channel_id=1, source_target_pairs={{0,24},{8,0},{16,8},{24,16},{32,56},{40,32},{48,40},{56,48},{64,88... | collective-permute-start | bytes 3145736 | tf_op jit(solution)/shard_map/ppermute | solution.py:103
  21.1 0.0 collective-permute-done.2
  21.1 0.0 collective-permute-done.3
  21.2 0.0 copy-start.8
  21.2 0.1 pad_maximum_fusion
  21.3 0.1 collective-permute-start.5
  21.4 2.7 %collective-permute-start.4 = (bf16[4,32,32,128]{3,2,1,0:T(8,128)(2,1)S(1)}, bf16[4,32,32,128]{3,2,1,0:T(8,128)(2,1)S(1)}, u32[]{:S(2)}, u32[]{:S(2)}) collective-permute-start(bf16[4,32,32,128]{3,2,1,0:T(8,128)(2,1)S(1)} %pad_maximum_fusion), channel_id=1, source_target_pairs={{0,96},{8,104},{16,112},{24,120},{32,0},{40,8},{48,16},{56,24},{64... | collective-permute-start | bytes 3145736 | tf_op jit(solution)/shard_map/ppermute | solution.py:103
  24.1 19.1 %collective-permute-done.13 = bf16[4,32,32,128]{3,2,1,0:T(8,128)(2,1)S(1)} collective-permute-done((bf16[4,32,32,128]{3,2,1,0:T(8,128)(2,1)S(1)}, bf16[4,32,32,128]{3,2,1,0:T(8,128)(2,1)S(1)}, u32[]{:S(2)}, u32[]{:S(2)}) %collective-permute-start.13) | collective-permute-done | bytes 1048608 | tf_op jit(solution)/shard_map/ppermute | solution.py:102
  43.2 0.9 slice.57
  44.1 0.2 collective-permute-start.14
  44.3 0.0 collective-permute-done.12
  44.3 0.9 slice.58
  45.2 2.5 %collective-permute-start.15 = (bf16[2,32,32,128]{3,2,1,0:T(8,128)(2,1)}, bf16[2,32,32,128]{3,2,1,0:T(8,128)(2,1)}, u32[]{:S(2)}, u32[]{:S(2)}) collective-permute-start(bf16[2,32,32,128]{3,2,1,0:T(8,128)(2,1)} %slice.58), channel_id=1, source_target_pairs={{0,24},{8,0},{16,8},{24,16},{32,56},{40,32},{48,40},{56,48},{64,88... | collective-permute-start | bytes 1572872 | tf_op jit(solution)/shard_map/ppermute | solution.py:107
  47.7 0.0 collective-permute-done.5
  47.7 0.9 slice.53
  48.6 0.0 collective-permute-start.6
  48.6 0.0 collective-permute-done.4
  48.6 0.0 copy-done.4
  48.6 0.9 slice.54
  49.5 2.7 %collective-permute-start.7 = (bf16[2,32,32,128]{3,2,1,0:T(8,128)(2,1)}, bf16[2,32,32,128]{3,2,1,0:T(8,128)(2,1)}, u32[]{:S(2)}, u32[]{:S(2)}) collective-permute-start(bf16[2,32,32,128]{3,2,1,0:T(8,128)(2,1)} %slice.54), channel_id=1, source_target_pairs={{0,96},{8,104},{16,112},{24,120},{32,0},{40,8},{48,16},{56,24},{64... | collective-permute-start | bytes 1572872 | tf_op jit(solution)/shard_map/ppermute | solution.py:107
  52.1 1.3 %fusion.6.index_ref = s32[512]{0:T(512)} fusion(s32[512]{0:T(512)} %param.12, s32[512]{0:T(512)} %param.10, s32[]{:T(128)S(6)} %select_n.55, s32[]{:T(128)S(6)} %select_n.52), kind=kLoop, calls=%fused_computation.30 | loop fusion | flops 52224 | bytes 6152 | tf_op jit(solution)/shard_map/add | solution.py:140
  53.5 2.9 %collective-permute-done.14 = bf16[2,32,32,128]{3,2,1,0:T(8,128)(2,1)} collective-permute-done((bf16[2,32,32,128]{3,2,1,0:T(8,128)(2,1)}, bf16[2,32,32,128]{3,2,1,0:T(8,128)(2,1)}, u32[]{:S(2)}, u32[]{:S(2)}) %collective-permute-start.14) | collective-permute-done | bytes 524320 | tf_op jit(solution)/shard_map/ppermute | solution.py:106
  56.4 0.2 collective-permute-done.15
  56.6 3.7 %collective-permute-done.6 = bf16[2,32,32,128]{3,2,1,0:T(8,128)(2,1)} collective-permute-done((bf16[2,32,32,128]{3,2,1,0:T(8,128)(2,1)}, bf16[2,32,32,128]{3,2,1,0:T(8,128)(2,1)}, u32[]{:S(2)}, u32[]{:S(2)}) %collective-permute-start.6) | collective-permute-done | bytes 524320 | tf_op jit(solution)/shard_map/ppermute | solution.py:106
  60.3 0.0 collective-permute-done.7
  60.3 15.6 %shard_map.95 = f32[8,16,2,4,128]{4,3,2,1,0:T(4,128)} custom-call(s32[512]{0:T(512)} %fusion.6.index_ref, s32[512]{0:T(512)} %obs_ref.1, bf16[128,32,128]{2,1,0:T(8,128)(2,1)} %bitcast.23, bf16[128,32,128]{2,1,0:T(8,128)(2,1)} %bitcast.27, bf16[64,32,128]{2,1,0:T(8,128)(2,1)} %bitcast.6.refs_2_, bf16[64,32,128]{2,1,0:T(8,128)(2,1)} %bitcast.7.refs_3_, ...), custom_call_target="tpu_custom_call" | custom-call | tf_op jit(solution)/shard_map/pallas_call | solution.py:79
  75.9 25.9 %all_to_all.5 = f32[128,2,4,128]{3,2,1,0:T(4,128)S(1)} all-to-all(f32[128,2,4,128]{3,2,1,0:T(4,128)} %bitcast.28), channel_id=1, replica_groups=mesh['grp'=16,'lag'=8] {'lag','grp'}, dimensions={0} | all-to-all | bytes 1048576 | tf_op jit(solution)/shard_map/all_to_all | solution.py:143
  101.9 0.1 reduce_sum.9
  102.0 0.0 copy-start.7
  102.0 0.7 fusion.7
  (20 shorter events, 0.1 us)
Async XLA Ops:
  0.6 101.4 %copy-start = (bf16[2,128,128]{2,1,0:T(8,128)(2,1)S(1)}, bf16[2,128,128]{2,1,0:T(8,128)(2,1)}, u32[]{:S(2)}) copy-start(bf16[2,128,128]{2,1,0:T(8,128)(2,1)} %param.14) | copy-start | bytes 196612
  2.0 9.5 %collective-permute-start.9 = (bf16[32,32,128]{2,1,0:T(8,128)(2,1)S(1)}, bf16[32,32,128]{2,1,0:T(8,128)(2,1)S(1)}, u32[]{:S(2)}, u32[]{:S(2)}) collective-permute-start(bf16[32,32,128]{2,1,0:T(8,128)(2,1)S(1)} %bitcast.31), channel_id=1, source_target_pairs={{0,32},{8,40},{16,48},{24,56},{32,64},{40,72},{48,80},{56,88},{64,... | collective-permute-start | bytes 786440 | tf_op jit(solution)/shard_map/ppermute | solution.py:102
  4.2 7.4 %collective-permute-start.8 = (bf16[32,32,128]{2,1,0:T(8,128)(2,1)S(1)}, bf16[32,32,128]{2,1,0:T(8,128)(2,1)S(1)}, u32[]{:S(2)}, u32[]{:S(2)}) collective-permute-start(bf16[32,32,128]{2,1,0:T(8,128)(2,1)S(1)} %bitcast.32), channel_id=1, source_target_pairs={{0,96},{8,104},{16,112},{24,120},{32,0},{40,8},{48,16},{56,24},{64... | collective-permute-start | bytes 786440 | tf_op jit(solution)/shard_map/ppermute | solution.py:103
  5.7 9.3 %collective-permute-start.1 = (bf16[32,32,128]{2,1,0:T(8,128)(2,1)S(1)}, bf16[32,32,128]{2,1,0:T(8,128)(2,1)S(1)}, u32[]{:S(2)}, u32[]{:S(2)}) collective-permute-start(bf16[32,32,128]{2,1,0:T(8,128)(2,1)S(1)} %bitcast.29), channel_id=1, source_target_pairs={{0,8},{8,16},{16,24},{24,0},{32,40},{40,48},{48,56},{56,32},{64,72... | collective-permute-start | bytes 786440 | tf_op jit(solution)/shard_map/ppermute | solution.py:102
  7.3 8.6 %collective-permute-start = (bf16[32,32,128]{2,1,0:T(8,128)(2,1)S(1)}, bf16[32,32,128]{2,1,0:T(8,128)(2,1)S(1)}, u32[]{:S(2)}, u32[]{:S(2)}) collective-permute-start(bf16[32,32,128]{2,1,0:T(8,128)(2,1)S(1)} %bitcast.30), channel_id=1, source_target_pairs={{0,24},{8,0},{16,8},{24,16},{32,56},{40,32},{48,40},{56,48},{64,88... | collective-permute-start | bytes 786440 | tf_op jit(solution)/shard_map/ppermute | solution.py:103
  11.5 6.7 %collective-permute-start.10 = (bf16[16,32,128]{2,1,0:T(8,128)(2,1)S(1)}, bf16[16,32,128]{2,1,0:T(8,128)(2,1)S(1)}, u32[]{:S(2)}, u32[]{:S(2)}) collective-permute-start(bf16[16,32,128]{2,1,0:T(8,128)(2,1)S(1)} %slice.55), channel_id=1, source_target_pairs={{0,32},{8,40},{16,48},{24,56},{32,64},{40,72},{48,80},{56,88},{64,... | collective-permute-start | bytes 393224 | tf_op jit(solution)/shard_map/ppermute | solution.py:106
  11.6 6.6 %collective-permute-start.11 = (bf16[16,32,128]{2,1,0:T(8,128)(2,1)S(1)}, bf16[16,32,128]{2,1,0:T(8,128)(2,1)S(1)}, u32[]{:S(2)}, u32[]{:S(2)}) collective-permute-start(bf16[16,32,128]{2,1,0:T(8,128)(2,1)S(1)} %slice.56), channel_id=1, source_target_pairs={{0,96},{8,104},{16,112},{24,120},{32,0},{40,8},{48,16},{56,24},{64... | collective-permute-start | bytes 393224 | tf_op jit(solution)/shard_map/ppermute | solution.py:107
  15.0 6.1 %collective-permute-start.2 = (bf16[16,32,128]{2,1,0:T(8,128)(2,1)S(1)}, bf16[16,32,128]{2,1,0:T(8,128)(2,1)S(1)}, u32[]{:S(2)}, u32[]{:S(2)}) collective-permute-start(bf16[16,32,128]{2,1,0:T(8,128)(2,1)S(1)} %slice.51), channel_id=1, source_target_pairs={{0,8},{8,16},{16,24},{24,0},{32,40},{40,48},{48,56},{56,32},{64,72... | collective-permute-start | bytes 393224 | tf_op jit(solution)/shard_map/ppermute | solution.py:106
  16.0 5.2 %collective-permute-start.3 = (bf16[16,32,128]{2,1,0:T(8,128)(2,1)S(1)}, bf16[16,32,128]{2,1,0:T(8,128)(2,1)S(1)}, u32[]{:S(2)}, u32[]{:S(2)}) collective-permute-start(bf16[16,32,128]{2,1,0:T(8,128)(2,1)S(1)} %slice.52), channel_id=1, source_target_pairs={{0,24},{8,0},{16,8},{24,16},{32,56},{40,32},{48,40},{56,48},{64,88... | collective-permute-start | bytes 393224 | tf_op jit(solution)/shard_map/ppermute | solution.py:107
  18.4 41.9 %copy-start.1 = (bf16[4,32,32,128]{3,2,1,0:T(8,128)(2,1)}, bf16[4,32,32,128]{3,2,1,0:T(8,128)(2,1)S(1)}, u32[]{:S(2)}) copy-start(bf16[4,32,32,128]{3,2,1,0:T(8,128)(2,1)S(1)} %pad_maximum_fusion.1) | copy-start | bytes 3145732
  18.4 24.8 %collective-permute-start.13 = (bf16[4,32,32,128]{3,2,1,0:T(8,128)(2,1)S(1)}, bf16[4,32,32,128]{3,2,1,0:T(8,128)(2,1)S(1)}, u32[]{:S(2)}, u32[]{:S(2)}) collective-permute-start(bf16[4,32,32,128]{3,2,1,0:T(8,128)(2,1)S(1)} %pad_maximum_fusion.1), channel_id=1, source_target_pairs={{0,8},{8,16},{16,24},{24,0},{32,40},{40,48},{48,56},{56,32},{64,72... | collective-permute-start | bytes 3145736 | tf_op jit(solution)/shard_map/ppermute | solution.py:102
  18.5 25.8 %collective-permute-start.12 = (bf16[4,32,32,128]{3,2,1,0:T(8,128)(2,1)S(1)}, bf16[4,32,32,128]{3,2,1,0:T(8,128)(2,1)S(1)}, u32[]{:S(2)}, u32[]{:S(2)}) collective-permute-start(bf16[4,32,32,128]{3,2,1,0:T(8,128)(2,1)S(1)} %pad_maximum_fusion.1), channel_id=1, source_target_pairs={{0,24},{8,0},{16,8},{24,16},{32,56},{40,32},{48,40},{56,48},{64,88... | collective-permute-start | bytes 3145736 | tf_op jit(solution)/shard_map/ppermute | solution.py:103
  21.2 80.9 %copy-start.8 = (f32[2,4,128]{2,1,0:T(4,128)S(1)}, f32[2,4,128]{2,1,0:T(4,128)}, u32[]{:S(2)}) copy-start(f32[2,4,128]{2,1,0:T(4,128)} %param.13) | copy-start | bytes 12292
  21.3 39.0 %copy-start.2 = (bf16[4,32,32,128]{3,2,1,0:T(8,128)(2,1)}, bf16[4,32,32,128]{3,2,1,0:T(8,128)(2,1)S(1)}, u32[]{:S(2)}) copy-start(bf16[4,32,32,128]{3,2,1,0:T(8,128)(2,1)S(1)} %pad_maximum_fusion) | copy-start | bytes 3145732
  21.3 26.3 %collective-permute-start.5 = (bf16[4,32,32,128]{3,2,1,0:T(8,128)(2,1)S(1)}, bf16[4,32,32,128]{3,2,1,0:T(8,128)(2,1)S(1)}, u32[]{:S(2)}, u32[]{:S(2)}) collective-permute-start(bf16[4,32,32,128]{3,2,1,0:T(8,128)(2,1)S(1)} %pad_maximum_fusion), channel_id=1, source_target_pairs={{0,32},{8,40},{16,48},{24,56},{32,64},{40,72},{48,80},{56,88},{64,... | collective-permute-start | bytes 3145736 | tf_op jit(solution)/shard_map/ppermute | solution.py:102
  21.4 27.2 %collective-permute-start.4 = (bf16[4,32,32,128]{3,2,1,0:T(8,128)(2,1)S(1)}, bf16[4,32,32,128]{3,2,1,0:T(8,128)(2,1)S(1)}, u32[]{:S(2)}, u32[]{:S(2)}) collective-permute-start(bf16[4,32,32,128]{3,2,1,0:T(8,128)(2,1)S(1)} %pad_maximum_fusion), channel_id=1, source_target_pairs={{0,96},{8,104},{16,112},{24,120},{32,0},{40,8},{48,16},{56,24},{64... | collective-permute-start | bytes 3145736 | tf_op jit(solution)/shard_map/ppermute | solution.py:103
  43.1 17.1 %copy-start.3 = (bf16[4,32,32,128]{3,2,1,0:T(8,128)(2,1)}, bf16[4,32,32,128]{3,2,1,0:T(8,128)(2,1)S(1)}, u32[]{:S(2)}) copy-start(bf16[4,32,32,128]{3,2,1,0:T(8,128)(2,1)S(1)} %collective-permute-done.13) | copy-start | bytes 3145732
  44.1 12.3 %collective-permute-start.14 = (bf16[2,32,32,128]{3,2,1,0:T(8,128)(2,1)}, bf16[2,32,32,128]{3,2,1,0:T(8,128)(2,1)}, u32[]{:S(2)}, u32[]{:S(2)}) collective-permute-start(bf16[2,32,32,128]{3,2,1,0:T(8,128)(2,1)} %slice.57), channel_id=1, source_target_pairs={{0,8},{8,16},{16,24},{24,0},{32,40},{40,48},{48,56},{56,32},{64,72... | collective-permute-start | bytes 1572872 | tf_op jit(solution)/shard_map/ppermute | solution.py:106
  44.3 4.3 %copy-start.4 = (bf16[4,32,32,128]{3,2,1,0:T(8,128)(2,1)}, bf16[4,32,32,128]{3,2,1,0:T(8,128)(2,1)S(1)}, u32[]{:S(2)}) copy-start(bf16[4,32,32,128]{3,2,1,0:T(8,128)(2,1)S(1)} %collective-permute-done.12) | copy-start | bytes 3145732
  45.2 11.4 %collective-permute-start.15 = (bf16[2,32,32,128]{3,2,1,0:T(8,128)(2,1)}, bf16[2,32,32,128]{3,2,1,0:T(8,128)(2,1)}, u32[]{:S(2)}, u32[]{:S(2)}) collective-permute-start(bf16[2,32,32,128]{3,2,1,0:T(8,128)(2,1)} %slice.58), channel_id=1, source_target_pairs={{0,24},{8,0},{16,8},{24,16},{32,56},{40,32},{48,40},{56,48},{64,88... | collective-permute-start | bytes 1572872 | tf_op jit(solution)/shard_map/ppermute | solution.py:107
  47.7 1.8 %copy-start.5 = (bf16[4,32,32,128]{3,2,1,0:T(8,128)(2,1)}, bf16[4,32,32,128]{3,2,1,0:T(8,128)(2,1)S(1)}, u32[]{:S(2)}) copy-start(bf16[4,32,32,128]{3,2,1,0:T(8,128)(2,1)S(1)} %collective-permute-done.5) | copy-start | bytes 3145732
  48.6 11.7 %collective-permute-start.6 = (bf16[2,32,32,128]{3,2,1,0:T(8,128)(2,1)}, bf16[2,32,32,128]{3,2,1,0:T(8,128)(2,1)}, u32[]{:S(2)}, u32[]{:S(2)}) collective-permute-start(bf16[2,32,32,128]{3,2,1,0:T(8,128)(2,1)} %slice.53), channel_id=1, source_target_pairs={{0,32},{8,40},{16,48},{24,56},{32,64},{40,72},{48,80},{56,88},{64,... | collective-permute-start | bytes 1572872 | tf_op jit(solution)/shard_map/ppermute | solution.py:106
  48.6 3.6 %copy-start.6 = (bf16[4,32,32,128]{3,2,1,0:T(8,128)(2,1)}, bf16[4,32,32,128]{3,2,1,0:T(8,128)(2,1)S(1)}, u32[]{:S(2)}) copy-start(bf16[4,32,32,128]{3,2,1,0:T(8,128)(2,1)S(1)} %collective-permute-done.4) | copy-start | bytes 3145732
  49.5 10.8 %collective-permute-start.7 = (bf16[2,32,32,128]{3,2,1,0:T(8,128)(2,1)}, bf16[2,32,32,128]{3,2,1,0:T(8,128)(2,1)}, u32[]{:S(2)}, u32[]{:S(2)}) collective-permute-start(bf16[2,32,32,128]{3,2,1,0:T(8,128)(2,1)} %slice.54), channel_id=1, source_target_pairs={{0,96},{8,104},{16,112},{24,120},{32,0},{40,8},{48,16},{56,24},{64... | collective-permute-start | bytes 1572872 | tf_op jit(solution)/shard_map/ppermute | solution.py:107
  102.0 0.8 copy-start.7
